TPU v7x, 512 devices: a whole 4x4x16 slice. The times are simulated.
512 devices in a mesh: col: 32 (over y, x, core), row: 16 (over z).
Axes of the slice: x: 4, y: 4, z: 16, core: 2. Of those that a mesh axis runs over, the one named last changes fastest.
Arguments:
- normal_matrix: float32 [4, 16, 128, 2, 32, 128], P(None, 'row', None, None, 'col'), may hold values from -3 to 5.5, as said below
- right_sides: float32 [256, 4, 16, 128], P('col', None, 'row'), may hold values from -6 to 6
Outputs:
- reduced_matrix: float32 [4, 16, 128, 2, 32, 128], P(None, 'row', None, None, 'col')
- reduced_sides: float32 [256, 4, 16, 128], P('col', None, 'row')
Inputs may be any that keep to these rules, and one draw needn't show every extreme that they name: `normal_matrix`: A is symmetric; its leading 128 x 128 block is strictly diagonally dominant with a positive diagonal.
All inputs are finite; a program needn't handle non-finite values.
Results may differ from a plain program's by a relative error of at most 0.00005.
Values sent between devices are 32-bit elements; how exact they have to be, the bound alone decides.
No kernel may reach another device: no remote copies, remote signals or barrier semaphores. Data moves between devices by JAX's collectives and lax.ppermute only.
A program may use at most 64 MiB of HBM per device.

v0:
```python
import jax
import jax.numpy as jnp
from jax import lax
from jax.sharding import PartitionSpec as P


def spread(block, axis, holder):
    block = jnp.where(lax.axis_index(axis) == holder, block, jnp.zeros_like(block))
    return lax.psum(block, axis)


def on_device(normal_matrix, right_sides):
    row_blocks, _, block, col_blocks, _, _ = normal_matrix.shape
    col_id = lax.axis_index("col")
    row_id = lax.axis_index("row")
    col_count = lax.axis_size("col")
    row_count = lax.axis_size("row")
    local = normal_matrix.reshape(row_blocks * block, col_blocks * block)
    first = local[:, :block]
    corner_raw = spread(first[:block], "row", 0)
    identity = jnp.eye(block, dtype=jnp.float32)
    corner_raw = jnp.where(col_id == 0, corner_raw, identity)
    corner_own = jnp.linalg.cholesky(corner_raw)
    rows_own = jax.scipy.linalg.solve_triangular(corner_own, first.T, lower=True).T
    stacked = jnp.concatenate([corner_own, rows_own], axis=0)
    stacked = spread(stacked, "col", 0)
    corner = stacked[:block]
    rows_factor = stacked[block:]
    picked = []
    for index in range(col_blocks):
        start = (index * col_count + col_id) // row_count * block
        picked.append(lax.dynamic_slice_in_dim(rows_factor, start, block, 0))
    selected = jnp.concatenate(picked, axis=0)
    cols_factor = spread(selected, "row", col_id % row_count)
    change = jnp.dot(
        rows_factor,
        cols_factor.T,
        precision=lax.Precision.HIGHEST,
        preferred_element_type=jnp.float32,
    )
    trailing = (local - change).reshape(row_blocks, block, col_blocks, block)
    global_rows = row_id + row_count * jnp.arange(row_blocks, dtype=jnp.int32)
    global_cols = col_id + col_count * jnp.arange(col_blocks, dtype=jnp.int32)
    inner = (global_rows[:, None, None, None] >= 1) & (global_cols[None, None, :, None] >= 1)
    result = jnp.where(inner, trailing, jnp.float32(0.0))
    column = jnp.where(
        global_rows[:, None, None] == 0, corner[None], rows_factor.reshape(row_blocks, block, block)
    )
    result = jnp.where((global_cols == 0)[None, None, :, None], column[:, :, None, :], result)
    result = result.reshape(normal_matrix.shape)
    side_count = right_sides.shape[0]
    top_sides = spread(right_sides[:, 0, 0, :], "row", 0)
    lead = jax.scipy.linalg.solve_triangular(corner, top_sides.T, lower=True).T
    flat = right_sides.reshape(side_count, row_blocks * block)
    reduced = flat - jnp.dot(
        lead, rows_factor.T, precision=lax.Precision.HIGHEST, preferred_element_type=jnp.float32
    )
    reduced = reduced.reshape(side_count, row_blocks, block)
    reduced = jnp.where((global_rows == 0)[None, :, None], lead[:, None, :], reduced)
    return (result, reduced.reshape(right_sides.shape))


def solution(mesh):
    placed = (P(None, "row", None, None, "col", None), P("col", None, "row", None))
    return jax.shard_map(
        on_device,
        mesh=mesh,
        in_specs=placed,
        out_specs=(P(None, "row", None, None, "col", None), P("col", None, "row", None)),
        check_vma=False,
    )
```

profile of v0, /device:TPU:1, one launch (start us, length us, event | category | flops | bytes accessed | tf_op | source)
XLA Modules:
  0.0 450.4 jit_solution(13755997180216444617)
XLA Ops:
  7.2 1.1 copy.16
  8.3 0.6 slice_select_fusion
  9.0 0.6 copy-done.3
  9.7 129.1 %all-reduce.4.cloned.1.call-done = f32[128,128]{1,0:T(8,128)} async-done(((f32[128,128]{1,0:T(8,128)}), f32[128,128]{1,0:T(8,128)}) %all-reduce.4.cloned.1.call-update) | async-done | bytes 65552 | tf_op jit(solution)/shard_map/psum | solution.py:9
  138.9 0.7 copy-done.2
  139.7 11.7 %cholesky.19 = f32[128,128]{1,0:T(8,128)S(1)} custom-call(f32[128,128]{1,0:T(8,128)S(1)} %fusion.5), custom_call_target="Cholesky" | custom-call | tf_op jit(solution)/shard_map/jit(cholesky)/cholesky | solution.py:23
  151.4 0.6 compare_reduce_fusion
  152.1 0.7 select_bitcast_fusion.1
  152.7 9.8 %custom-call.11 = f32[1,128,128]{1,2,0:T(8,128)S(1)} custom-call(f32[1,128,128]{2,1,0:T(8,128)S(1)} %get-tuple-element.2), custom_call_target="InvertDiagBlocksLowerTriangular" | custom-call | tf_op jit(solution)/shard_map/jit(_solve_triangular)/triangular_solve | solution.py:24
  162.6 0.4 convolution_bitcast_fusion
  162.9 0.7 maximum_select_fusion
  163.8 21.4 %psum.31 = f32[8,128]{1,0:T(8,128)S(1)} all-reduce(f32[8,128]{1,0:T(8,128)S(1)} %bitcast.46), channel_id=1, replica_groups=mesh['col'=32,'row'=16] {'row'}, use_global_device_ids=true, to_apply=%region_5.6 | all-reduce | flops 1024 | bytes 8192 | tf_op jit(solution)/shard_map/psum | solution.py:9
  185.2 118.3 %all-reduce.6.cloned.1.call-done = f32[640,128]{1,0:T(8,128)} async-done(((f32[640,128]{1,0:T(8,128)}), f32[640,128]{1,0:T(8,128)}) %all-reduce.6.cloned.1.call-update) | async-done | bytes 327696 | tf_op jit(solution)/shard_map/psum | solution.py:9
  303.4 0.8 select_bitcast_fusion
  304.3 9.8 %custom-call.12 = f32[1,128,128]{1,2,0:T(8,128)S(1)} custom-call(f32[1,128,128]{2,1,0:T(8,128)S(1)} %get-tuple-element.4), custom_call_target="InvertDiagBlocksLowerTriangular" | custom-call | tf_op jit(solution)/shard_map/jit(_solve_triangular)/triangular_solve | solution.py:53
  314.1 1.0 slice.42
  315.1 0.7 maximum_select_fusion.1
  316.1 0.7 copy-done
  316.8 0.3 fusion
  317.1 0.7 broadcast_select_fusion.3
  317.8 122.8 %all-reduce.8.cloned.1.call-done = f32[256,128]{1,0:T(8,128)} async-done(((f32[256,128]{1,0:T(8,128)}), f32[256,128]{1,0:T(8,128)}) %all-reduce.8.cloned.1.call-update) | async-done | bytes 131088 | tf_op jit(solution)/shard_map/psum | solution.py:9
  440.6 1.5 convolution_subtract_fusion
  442.1 0.3 reshape.136
  442.4 1.5 broadcast_select_fusion
  (24 shorter events, 0.7 us)
Async XLA Ops:
  7.2 131.6 %all-reduce.4.cloned.1.call-start = ((), (), s32[]{:S(2)}) async-start(), calls=%async_computation | async-start | bytes 131072 | tf_op jit(solution)/shard_map/psum | solution.py:9
  8.9 0.7 copy-start.3
  9.0 294.5 %all-reduce.6.cloned.1.call-start = ((), (), s32[]{:S(2)}) async-start(), calls=%async_computation.1 | async-start | bytes 655360 | tf_op jit(solution)/shard_map/psum | solution.py:9
  138.8 0.8 copy-start.2
  163.7 276.9 %all-reduce.8.cloned.1.call-start = ((), (), s32[]{:S(2)}) async-start(), calls=%async_computation.2 | async-start | bytes 262144 | tf_op jit(solution)/shard_map/psum | solution.py:9
  315.8 1.0 copy-start
  315.8 124.8 %copy-start.1 = (f32[4,1,128,2,1,128]{5,4,3,2,1,0:T(1,128)S(1)}, f32[4,1,128,2,1,128]{5,4,3,2,1,0:T(1,128)}, u32[]{:S(2)}) copy-start(f32[4,1,128,2,1,128]{5,4,3,2,1,0:T(1,128)} %param.2) | copy-start | bytes 1572868
Sparse Core Ops, SparseCore 0:
  10.9 127.8 all-reduce.3
  163.8 139.5 all-reduce.5
  315.9 124.6 all-reduce.7
where the time goes:
time: 459 us; the launch traced here: 450 us
  waiting for transfers between devices  370 us (81%)
  other arithmetic  38 us (8%)
  blocking collectives  21.4 us (5%)
  between operations  13.9 us (3%)
    psum x3, waiting for transfers between devices, spread(): return lax.psum(block, axis)  370 us
    psum x1, blocking collectives, spread(): return lax.psum(block, axis)  21.4 us
    another operation x3, other arithmetic, on_device(): corner_own = jnp.linalg.cholesky(corner_raw)  12.4 us
    another operation x2, other arithmetic, on_device(): lead = jax.scipy.linalg.solve_triangular(corner, top_sides.T, lower=True).T  10.7 us
    another operation x2, other arithmetic, on_device(): jax.scipy.linalg.solve_triangular(corner_own, first.T, lower=True)  10.5 us
  transfers between devices with their start and end apart: 3, of which 3 were waited for; matrix products, arithmetic and copies ran while one was open for 0% of the time, Pallas kernels for 0%

commit v1 on v0

--- a/solution.py
+++ b/solution.py
@@ -4,9 +4,16 @@
 from jax.sharding import PartitionSpec as P
 
 
-def spread(block, axis, holder):
-    block = jnp.where(lax.axis_index(axis) == holder, block, jnp.zeros_like(block))
-    return lax.psum(block, axis)
+def spread(block, axis):
+    count = lax.axis_size(axis)
+    index = lax.axis_index(axis)
+    step = 1
+    while step < count:
+        pairs = [(i, i + step) for i in range(step) if i + step < count]
+        arrived = lax.ppermute(block, axis, pairs)
+        block = jnp.where((index >= step) & (index < 2 * step), arrived, block)
+        step *= 2
+    return block
 
 
 def on_device(normal_matrix, right_sides):
@@ -15,23 +22,21 @@
     row_id = lax.axis_index("row")
     col_count = lax.axis_size("col")
     row_count = lax.axis_size("row")
+    side_count = right_sides.shape[0]
     local = normal_matrix.reshape(row_blocks * block, col_blocks * block)
-    first = local[:, :block]
-    corner_raw = spread(first[:block], "row", 0)
-    identity = jnp.eye(block, dtype=jnp.float32)
-    corner_raw = jnp.where(col_id == 0, corner_raw, identity)
-    corner_own = jnp.linalg.cholesky(corner_raw)
-    rows_own = jax.scipy.linalg.solve_triangular(corner_own, first.T, lower=True).T
-    stacked = jnp.concatenate([corner_own, rows_own], axis=0)
-    stacked = spread(stacked, "col", 0)
-    corner = stacked[:block]
-    rows_factor = stacked[block:]
-    picked = []
-    for index in range(col_blocks):
-        start = (index * col_count + col_id) // row_count * block
-        picked.append(lax.dynamic_slice_in_dim(rows_factor, start, block, 0))
-    selected = jnp.concatenate(picked, axis=0)
-    cols_factor = spread(selected, "row", col_id % row_count)
+
+    corner_raw = spread(spread(local[:block, :block], "row"), "col")
+    left = spread(local[:, :block], "col")
+    top = jnp.concatenate([local[:block], right_sides[:, 0, 0, :].T], axis=1)
+    top = spread(top, "row")
+
+    corner = jnp.linalg.cholesky(corner_raw)
+    rhs = jnp.concatenate([left.T, top], axis=1)
+    solved = jax.scipy.linalg.solve_triangular(corner, rhs, lower=True).T
+    rows_factor = solved[: row_blocks * block]
+    cols_factor = solved[row_blocks * block: (row_blocks + col_blocks) * block]
+    lead = solved[(row_blocks + col_blocks) * block:]
+
     change = jnp.dot(
         rows_factor,
         cols_factor.T,
@@ -48,9 +53,7 @@
     )
     result = jnp.where((global_cols == 0)[None, None, :, None], column[:, :, None, :], result)
     result = result.reshape(normal_matrix.shape)
-    side_count = right_sides.shape[0]
-    top_sides = spread(right_sides[:, 0, 0, :], "row", 0)
-    lead = jax.scipy.linalg.solve_triangular(corner, top_sides.T, lower=True).T
+
     flat = right_sides.reshape(side_count, row_blocks * block)
     reduced = flat - jnp.dot(
         lead, rows_factor.T, precision=lax.Precision.HIGHEST, preferred_element_type=jnp.float32

time: 459 us -> 110 us (0.24)
  the two profiles are of different devices: /device:TPU:1 before, /device:TPU:100 now
where the time goes in v1:
time: 110 us; the launch traced here: 109 us
  waiting for transfers between devices  48.9 us (44%)
  starting transfers between devices  27.6 us (25%)
  other arithmetic  25.7 us (23%)
  local copies, waits for them, and re-layouts  4.4 us (4%)
  matrix products  1.81 us (2%)
  between operations  1.12 us (1%)
    ppermute x18, waiting for transfers between devices, spread(): arrived = lax.ppermute(block, axis, pairs)  48.9 us
    ppermute x18, starting transfers between devices, spread(): arrived = lax.ppermute(block, axis, pairs)  27.6 us
    another operation x3, other arithmetic, on_device(): corner = jnp.linalg.cholesky(corner_raw)  12.4 us
    another operation x2, other arithmetic, on_device(): solved = jax.scipy.linalg.solve_triangular(corner, rhs, lower=True).T  10.5 us
  transfers between devices with their start and end apart: 18, of which 7 were waited for; matrix products, arithmetic and copies ran while one was open for 23% of the time, Pallas kernels for 0%

profile of v1, /device:TPU:100, one launch (start us, length us, event | category | flops | bytes accessed | tf_op | source)
XLA Modules:
  0.0 109.4 jit_solution(5456579011354896550)
XLA Ops:
  0.6 1.1 copy.20
  2.6 1.3 %slice_reduce_fusion = f32[128,2,128]{2,1,0:T(2,128)S(1)} fusion(f32[4,1,128,2,1,128]{5,4,3,2,1,0:T(1,128)} %param.2), kind=kLoop, calls=%fused_computation.14 | loop fusion | bytes 262144 | tf_op jit(solution)/shard_map/slice | solution.py:30
  6.2 1.3 %collective-permute-start.1 = (f32[128,128]{0,1:T(8,128)S(1)}, f32[128,128]{0,1:T(8,128)S(1)}, u32[]{:S(2)}, u32[]{:S(2)}) collective-permute-start(f32[128,128]{0,1:T(8,128)S(1)} %broadcast_select_fusion.12), channel_id=1, source_target_pairs={{0,2},{1,3},{16,18},{17,19},{32,34},{33,35},{48,50},{49,51},{64,66... | collective-permute-start | bytes 196616 | tf_op jit(solution)/shard_map/ppermute | solution.py:13
  7.5 6.1 %collective-permute-done.1 = f32[128,128]{0,1:T(8,128)S(1)} collective-permute-done((f32[128,128]{0,1:T(8,128)S(1)}, f32[128,128]{0,1:T(8,128)S(1)}, u32[]{:S(2)}, u32[]{:S(2)}) %collective-permute-start.1) | collective-permute-done | bytes 65568 | tf_op jit(solution)/shard_map/ppermute | solution.py:13
  13.6 2.4 %collective-permute-start.2 = (f32[128,128]{0,1:T(8,128)S(1)}, f32[128,128]{0,1:T(8,128)S(1)}, u32[]{:S(2)}, u32[]{:S(2)}) collective-permute-start(f32[128,128]{0,1:T(8,128)S(1)} %broadcast_select_fusion.13), channel_id=1, source_target_pairs={{0,4},{1,5},{2,6},{3,7},{16,20},{17,21},{18,22},{19,23},{32,36},{3... | collective-permute-start | bytes 196616 | tf_op jit(solution)/shard_map/ppermute | solution.py:13
  16.0 4.2 %collective-permute-done.2 = f32[128,128]{0,1:T(8,128)S(1)} collective-permute-done((f32[128,128]{0,1:T(8,128)S(1)}, f32[128,128]{0,1:T(8,128)S(1)}, u32[]{:S(2)}, u32[]{:S(2)}) %collective-permute-start.2) | collective-permute-done | bytes 65568 | tf_op jit(solution)/shard_map/ppermute | solution.py:13
  20.2 1.3 %collective-permute-start.3 = (f32[128,128]{0,1:T(8,128)S(1)}, f32[128,128]{0,1:T(8,128)S(1)}, u32[]{:S(2)}, u32[]{:S(2)}) collective-permute-start(f32[128,128]{0,1:T(8,128)S(1)} %broadcast_select_fusion.14), channel_id=1, source_target_pairs={{0,8},{1,9},{2,10},{3,11},{4,12},{5,13},{6,14},{7,15},{16,24},{17,... | collective-permute-start | bytes 196616 | tf_op jit(solution)/shard_map/ppermute | solution.py:13
  21.6 2.4 %collective-permute-done.3 = f32[128,128]{0,1:T(8,128)S(1)} collective-permute-done((f32[128,128]{0,1:T(8,128)S(1)}, f32[128,128]{0,1:T(8,128)S(1)}, u32[]{:S(2)}, u32[]{:S(2)}) %collective-permute-start.3) | collective-permute-done | bytes 65568 | tf_op jit(solution)/shard_map/ppermute | solution.py:13
  24.7 1.3 %collective-permute-start.15 = (f32[128,264]{1,0:T(8,128)S(1)}, f32[128,264]{1,0:T(8,128)S(1)}, u32[]{:S(2)}, u32[]{:S(2)}) collective-permute-start(f32[128,264]{1,0:T(8,128)S(1)} %broadcast_select_fusion.7), channel_id=1, source_target_pairs={{0,2},{1,3},{16,18},{17,19},{32,34},{33,35},{48,50},{49,51},{64,66... | collective-permute-start | bytes 405512 | tf_op jit(solution)/shard_map/ppermute | solution.py:13
  27.5 1.3 %collective-permute-start.6 = (f32[128,128]{0,1:T(8,128)S(1)}, f32[128,128]{0,1:T(8,128)S(1)}, u32[]{:S(2)}, u32[]{:S(2)}) collective-permute-start(f32[128,128]{0,1:T(8,128)S(1)} %broadcast_select_fusion.17), channel_id=1, source_target_pairs={{0,64},{16,80},{32,96},{48,112},{1,65},{17,81},{33,97},{49,113},{2... | collective-permute-start | bytes 196616 | tf_op jit(solution)/shard_map/ppermute | solution.py:13
  28.8 12.4 %collective-permute-done.15 = f32[128,264]{1,0:T(8,128)S(1)} collective-permute-done((f32[128,264]{1,0:T(8,128)S(1)}, f32[128,264]{1,0:T(8,128)S(1)}, u32[]{:S(2)}, u32[]{:S(2)}) %collective-permute-start.15) | collective-permute-done | bytes 135200 | tf_op jit(solution)/shard_map/ppermute | solution.py:13
  41.3 1.3 %collective-permute-start.16 = (f32[128,264]{1,0:T(8,128)S(1)}, f32[128,264]{1,0:T(8,128)S(1)}, u32[]{:S(2)}, u32[]{:S(2)}) collective-permute-start(f32[128,264]{1,0:T(8,128)S(1)} %broadcast_select_fusion.8), channel_id=1, source_target_pairs={{0,4},{1,5},{2,6},{3,7},{16,20},{17,21},{18,22},{19,23},{32,36},{3... | collective-permute-start | bytes 405512 | tf_op jit(solution)/shard_map/ppermute | solution.py:13
  42.6 4.0 %collective-permute-start.7 = (f32[128,128]{0,1:T(8,128)S(1)}, f32[128,128]{0,1:T(8,128)S(1)}, u32[]{:S(2)}, u32[]{:S(2)}) collective-permute-start(f32[128,128]{0,1:T(8,128)S(1)} %broadcast_select_fusion.18), channel_id=1, source_target_pairs={{0,128},{16,144},{32,160},{48,176},{64,192},{80,208},{96,224},{112... | collective-permute-start | bytes 196616 | tf_op jit(solution)/shard_map/ppermute | solution.py:13
  46.6 13.8 %collective-permute-done.16 = f32[128,264]{1,0:T(8,128)S(1)} collective-permute-done((f32[128,264]{1,0:T(8,128)S(1)}, f32[128,264]{1,0:T(8,128)S(1)}, u32[]{:S(2)}, u32[]{:S(2)}) %collective-permute-start.16) | collective-permute-done | bytes 135200 | tf_op jit(solution)/shard_map/ppermute | solution.py:13
  60.5 1.3 %collective-permute-start.17 = (f32[128,264]{1,0:T(8,128)S(1)}, f32[128,264]{1,0:T(8,128)S(1)}, u32[]{:S(2)}, u32[]{:S(2)}) collective-permute-start(f32[128,264]{1,0:T(8,128)S(1)} %broadcast_select_fusion.9), channel_id=1, source_target_pairs={{0,8},{1,9},{2,10},{3,11},{4,12},{5,13},{6,14},{7,15},{16,24},{17,... | collective-permute-start | bytes 405512 | tf_op jit(solution)/shard_map/ppermute | solution.py:13
  61.8 5.4 %collective-permute-start.8 = (f32[128,128]{0,1:T(8,128)S(1)}, f32[128,128]{0,1:T(8,128)S(1)}, u32[]{:S(2)}, u32[]{:S(2)}) collective-permute-start(f32[128,128]{0,1:T(8,128)S(1)} %broadcast_select_fusion.19), channel_id=1, source_target_pairs={{0,256},{16,272},{32,288},{48,304},{64,320},{80,336},{96,352},{112... | collective-permute-start | bytes 196616 | tf_op jit(solution)/shard_map/ppermute | solution.py:13
  67.4 1.3 %collective-permute-start.11 = (f32[512,128]{0,1:T(8,128)S(1)}, f32[512,128]{0,1:T(8,128)S(1)}, u32[]{:S(2)}, u32[]{:S(2)}) collective-permute-start(f32[512,128]{0,1:T(8,128)S(1)} %broadcast_select_fusion.4), channel_id=1, source_target_pairs={{0,64},{16,80},{32,96},{48,112},{1,65},{17,81},{33,97},{49,113},{2... | collective-permute-start | bytes 786440 | tf_op jit(solution)/shard_map/ppermute | solution.py:13
  69.3 9.4 %collective-permute-done.11 = f32[512,128]{0,1:T(8,128)S(1)} collective-permute-done((f32[512,128]{0,1:T(8,128)S(1)}, f32[512,128]{0,1:T(8,128)S(1)}, u32[]{:S(2)}, u32[]{:S(2)}) %collective-permute-start.11) | collective-permute-done | bytes 262176 | tf_op jit(solution)/shard_map/ppermute | solution.py:13
  78.7 1.3 %collective-permute-start.12 = (f32[512,128]{0,1:T(8,128)S(1)}, f32[512,128]{0,1:T(8,128)S(1)}, u32[]{:S(2)}, u32[]{:S(2)}) collective-permute-start(f32[512,128]{0,1:T(8,128)S(1)} %broadcast_select_fusion.5), channel_id=1, source_target_pairs={{0,128},{16,144},{32,160},{48,176},{64,192},{80,208},{96,224},{112... | collective-permute-start | bytes 786440 | tf_op jit(solution)/shard_map/ppermute | solution.py:13
  80.1 11.7 %cholesky.18 = f32[128,128]{1,0:T(8,128)S(1)} custom-call(f32[128,128]{1,0:T(8,128)S(1)} %fusion.7), custom_call_target="Cholesky" | custom-call | tf_op jit(solution)/shard_map/jit(cholesky)/cholesky | solution.py:33
  91.9 1.3 %collective-permute-start.13 = (f32[512,128]{0,1:T(8,128)S(1)}, f32[512,128]{0,1:T(8,128)S(1)}, u32[]{:S(2)}, u32[]{:S(2)}) collective-permute-start(f32[512,128]{0,1:T(8,128)S(1)} %broadcast_select_fusion.6), channel_id=1, source_target_pairs={{0,256},{16,272},{32,288},{48,304},{64,320},{80,336},{96,352},{112... | collective-permute-start | bytes 786440 | tf_op jit(solution)/shard_map/ppermute | solution.py:13
  94.5 9.8 %custom-call.7 = f32[1,128,128]{1,2,0:T(8,128)S(1)} custom-call(f32[1,128,128]{2,1,0:T(8,128)S(1)} %get-tuple-element.2), custom_call_target="InvertDiagBlocksLowerTriangular" | custom-call | tf_op jit(solution)/shard_map/jit(_solve_triangular)/triangular_solve | solution.py:35
  104.4 0.9 fusion.1
  107.9 1.5 %broadcast_select_fusion = f32[4,1,128,2,1,128]{5,4,3,2,1,0:T(1,128)} fusion(pred[2]{0:T(512)(128)(4,1)S(1)} %get-tuple-element.5, f32[4,1,128,2,1,128]{5,4,3,2,1,0:T(1,128)S(1)} %copy.8, pred[4,2]{1,0:T(4,128)(4,1)S(1)} %broadcast_and_fusion, f32[4,128,128]{2,1,0:T(8,128)S(1)} %broadcast_select_fusion.2), kind=kLoop, calls=%fused_computation.3 | loop fusion | flops 262144 | bytes 1310730 | tf_op jit(solution)/shard_map/jit(_where)/select_n | solution.py:54
  (62 shorter events, 10.1 us)
Async XLA Ops:
  1.9 4.2 %collective-permute-start = (f32[128,128]{0,1:T(8,128)S(1)}, f32[128,128]{0,1:T(8,128)S(1)}, u32[]{:S(2)}, u32[]{:S(2)}) collective-permute-start(f32[128,128]{0,1:T(8,128)S(1)} %slice.44), channel_id=1, source_target_pairs={{0,1},{16,17},{32,33},{48,49},{64,65},{80,81},{96,97},{112,113},{1... | collective-permute-start | bytes 196616 | tf_op jit(solution)/shard_map/ppermute | solution.py:13
  3.9 0.7 slice-start
  4.7 19.9 %collective-permute-start.14 = (f32[128,264]{1,0:T(8,128)S(1)}, f32[128,264]{1,0:T(8,128)S(1)}, u32[]{:S(2)}, u32[]{:S(2)}) collective-permute-start(f32[128,264]{1,0:T(8,128)S(1)} %pad_maximum_fusion), channel_id=1, source_target_pairs={{0,1},{16,17},{32,33},{48,49},{64,65},{80,81},{96,97},{112,113},{1... | collective-permute-start | bytes 405512 | tf_op jit(solution)/shard_map/ppermute | solution.py:13
  5.5 21.3 %collective-permute-start.9 = (f32[512,128]{0,1:T(8,128)S(1)}, f32[512,128]{0,1:T(8,128)S(1)}, u32[]{:S(2)}, u32[]{:S(2)}) collective-permute-start(f32[512,128]{0,1:T(8,128)S(1)} %slice.45), channel_id=1, source_target_pairs={{0,16},{1,17},{2,18},{3,19},{4,20},{5,21},{6,22},{7,23},{8,24},{9,... | collective-permute-start | bytes 786440 | tf_op jit(solution)/shard_map/ppermute | solution.py:13
  6.2 7.4 %collective-permute-start.1 = (f32[128,128]{0,1:T(8,128)S(1)}, f32[128,128]{0,1:T(8,128)S(1)}, u32[]{:S(2)}, u32[]{:S(2)}) collective-permute-start(f32[128,128]{0,1:T(8,128)S(1)} %broadcast_select_fusion.12), channel_id=1, source_target_pairs={{0,2},{1,3},{16,18},{17,19},{32,34},{33,35},{48,50},{49,51},{64,66... | collective-permute-start | bytes 196616 | tf_op jit(solution)/shard_map/ppermute | solution.py:13
  13.6 6.6 %collective-permute-start.2 = (f32[128,128]{0,1:T(8,128)S(1)}, f32[128,128]{0,1:T(8,128)S(1)}, u32[]{:S(2)}, u32[]{:S(2)}) collective-permute-start(f32[128,128]{0,1:T(8,128)S(1)} %broadcast_select_fusion.13), channel_id=1, source_target_pairs={{0,4},{1,5},{2,6},{3,7},{16,20},{17,21},{18,22},{19,23},{32,36},{3... | collective-permute-start | bytes 196616 | tf_op jit(solution)/shard_map/ppermute | solution.py:13
  20.2 3.8 %collective-permute-start.3 = (f32[128,128]{0,1:T(8,128)S(1)}, f32[128,128]{0,1:T(8,128)S(1)}, u32[]{:S(2)}, u32[]{:S(2)}) collective-permute-start(f32[128,128]{0,1:T(8,128)S(1)} %broadcast_select_fusion.14), channel_id=1, source_target_pairs={{0,8},{1,9},{2,10},{3,11},{4,12},{5,13},{6,14},{7,15},{16,24},{17,... | collective-permute-start | bytes 196616 | tf_op jit(solution)/shard_map/ppermute | solution.py:13
  24.0 2.0 %collective-permute-start.4 = (f32[128,128]{0,1:T(8,128)S(1)}, f32[128,128]{0,1:T(8,128)S(1)}, u32[]{:S(2)}, u32[]{:S(2)}) collective-permute-start(f32[128,128]{0,1:T(8,128)S(1)} %broadcast_select_fusion.15), channel_id=1, source_target_pairs={{0,16},{1,17},{2,18},{3,19},{4,20},{5,21},{6,22},{7,23},{8,24},{9,... | collective-permute-start | bytes 196616 | tf_op jit(solution)/shard_map/ppermute | solution.py:13
  24.7 16.5 %collective-permute-start.15 = (f32[128,264]{1,0:T(8,128)S(1)}, f32[128,264]{1,0:T(8,128)S(1)}, u32[]{:S(2)}, u32[]{:S(2)}) collective-permute-start(f32[128,264]{1,0:T(8,128)S(1)} %broadcast_select_fusion.7), channel_id=1, source_target_pairs={{0,2},{1,3},{16,18},{17,19},{32,34},{33,35},{48,50},{49,51},{64,66... | collective-permute-start | bytes 405512 | tf_op jit(solution)/shard_map/ppermute | solution.py:13
  26.1 1.4 %collective-permute-start.5 = (f32[128,128]{0,1:T(8,128)S(1)}, f32[128,128]{0,1:T(8,128)S(1)}, u32[]{:S(2)}, u32[]{:S(2)}) collective-permute-start(f32[128,128]{0,1:T(8,128)S(1)} %broadcast_select_fusion.16), channel_id=1, source_target_pairs={{0,32},{16,48},{1,33},{17,49},{2,34},{18,50},{3,35},{19,51},{4,36}... | collective-permute-start | bytes 196616 | tf_op jit(solution)/shard_map/ppermute | solution.py:13
  26.8 40.5 %collective-permute-start.10 = (f32[512,128]{0,1:T(8,128)S(1)}, f32[512,128]{0,1:T(8,128)S(1)}, u32[]{:S(2)}, u32[]{:S(2)}) collective-permute-start(f32[512,128]{0,1:T(8,128)S(1)} %broadcast_select_fusion.3), channel_id=1, source_target_pairs={{0,32},{16,48},{1,33},{17,49},{2,34},{18,50},{3,35},{19,51},{4,36}... | collective-permute-start | bytes 786440 | tf_op jit(solution)/shard_map/ppermute | solution.py:13
  27.5 15.1 %collective-permute-start.6 = (f32[128,128]{0,1:T(8,128)S(1)}, f32[128,128]{0,1:T(8,128)S(1)}, u32[]{:S(2)}, u32[]{:S(2)}) collective-permute-start(f32[128,128]{0,1:T(8,128)S(1)} %broadcast_select_fusion.17), channel_id=1, source_target_pairs={{0,64},{16,80},{32,96},{48,112},{1,65},{17,81},{33,97},{49,113},{2... | collective-permute-start | bytes 196616 | tf_op jit(solution)/shard_map/ppermute | solution.py:13
  41.3 19.2 %collective-permute-start.16 = (f32[128,264]{1,0:T(8,128)S(1)}, f32[128,264]{1,0:T(8,128)S(1)}, u32[]{:S(2)}, u32[]{:S(2)}) collective-permute-start(f32[128,264]{1,0:T(8,128)S(1)} %broadcast_select_fusion.8), channel_id=1, source_target_pairs={{0,4},{1,5},{2,6},{3,7},{16,20},{17,21},{18,22},{19,23},{32,36},{3... | collective-permute-start | bytes 405512 | tf_op jit(solution)/shard_map/ppermute | solution.py:13
  42.6 19.2 %collective-permute-start.7 = (f32[128,128]{0,1:T(8,128)S(1)}, f32[128,128]{0,1:T(8,128)S(1)}, u32[]{:S(2)}, u32[]{:S(2)}) collective-permute-start(f32[128,128]{0,1:T(8,128)S(1)} %broadcast_select_fusion.18), channel_id=1, source_target_pairs={{0,128},{16,144},{32,160},{48,176},{64,192},{80,208},{96,224},{112... | collective-permute-start | bytes 196616 | tf_op jit(solution)/shard_map/ppermute | solution.py:13
  60.5 8.2 %collective-permute-start.17 = (f32[128,264]{1,0:T(8,128)S(1)}, f32[128,264]{1,0:T(8,128)S(1)}, u32[]{:S(2)}, u32[]{:S(2)}) collective-permute-start(f32[128,264]{1,0:T(8,128)S(1)} %broadcast_select_fusion.9), channel_id=1, source_target_pairs={{0,8},{1,9},{2,10},{3,11},{4,12},{5,13},{6,14},{7,15},{16,24},{17,... | collective-permute-start | bytes 405512 | tf_op jit(solution)/shard_map/ppermute | solution.py:13
  61.8 7.3 %collective-permute-start.8 = (f32[128,128]{0,1:T(8,128)S(1)}, f32[128,128]{0,1:T(8,128)S(1)}, u32[]{:S(2)}, u32[]{:S(2)}) collective-permute-start(f32[128,128]{0,1:T(8,128)S(1)} %broadcast_select_fusion.19), channel_id=1, source_target_pairs={{0,256},{16,272},{32,288},{48,304},{64,320},{80,336},{96,352},{112... | collective-permute-start | bytes 196616 | tf_op jit(solution)/shard_map/ppermute | solution.py:13
  67.4 11.3 %collective-permute-start.11 = (f32[512,128]{0,1:T(8,128)S(1)}, f32[512,128]{0,1:T(8,128)S(1)}, u32[]{:S(2)}, u32[]{:S(2)}) collective-permute-start(f32[512,128]{0,1:T(8,128)S(1)} %broadcast_select_fusion.4), channel_id=1, source_target_pairs={{0,64},{16,80},{32,96},{48,112},{1,65},{17,81},{33,97},{49,113},{2... | collective-permute-start | bytes 786440 | tf_op jit(solution)/shard_map/ppermute | solution.py:13
  78.7 13.1 %collective-permute-start.12 = (f32[512,128]{0,1:T(8,128)S(1)}, f32[512,128]{0,1:T(8,128)S(1)}, u32[]{:S(2)}, u32[]{:S(2)}) collective-permute-start(f32[512,128]{0,1:T(8,128)S(1)} %broadcast_select_fusion.5), channel_id=1, source_target_pairs={{0,128},{16,144},{32,160},{48,176},{64,192},{80,208},{96,224},{112... | collective-permute-start | bytes 786440 | tf_op jit(solution)/shard_map/ppermute | solution.py:13
  91.9 12.4 %collective-permute-start.13 = (f32[512,128]{0,1:T(8,128)S(1)}, f32[512,128]{0,1:T(8,128)S(1)}, u32[]{:S(2)}, u32[]{:S(2)}) collective-permute-start(f32[512,128]{0,1:T(8,128)S(1)} %broadcast_select_fusion.6), channel_id=1, source_target_pairs={{0,256},{16,272},{32,288},{48,304},{64,320},{80,336},{96,352},{112... | collective-permute-start | bytes 786440 | tf_op jit(solution)/shard_map/ppermute | solution.py:13
  106.1 0.7 copy-start

commit v2 on v1

--- a/solution.py
+++ b/solution.py
@@ -25,10 +25,10 @@
     side_count = right_sides.shape[0]
     local = normal_matrix.reshape(row_blocks * block, col_blocks * block)
 
-    corner_raw = spread(spread(local[:block, :block], "row"), "col")
     left = spread(local[:, :block], "col")
     top = jnp.concatenate([local[:block], right_sides[:, 0, 0, :].T], axis=1)
     top = spread(top, "row")
+    corner_raw = spread(top[:, :block], "col")
 
     corner = jnp.linalg.cholesky(corner_raw)
     rhs = jnp.concatenate([left.T, top], axis=1)

time: 110 us -> 98.8 us (0.90)
  the two profiles are of different devices: /device:TPU:100 before, /device:TPU:494 now
where the time goes in v2:
time: 98.8 us; the launch traced here: 98.3 us
  waiting for transfers between devices  50.2 us (51%)
  other arithmetic  25.6 us (26%)
  starting transfers between devices  17.1 us (17%)
  local copies, waits for them, and re-layouts  2.69 us (3%)
  matrix products  1.66 us (2%)
  between operations  1.09 us (1%)
    ppermute x14, waiting for transfers between devices, spread(): arrived = lax.ppermute(block, axis, pairs)  50.2 us
    ppermute x14, starting transfers between devices, spread(): arrived = lax.ppermute(block, axis, pairs)  17.1 us
    another operation x3, other arithmetic, on_device(): corner = jnp.linalg.cholesky(corner_raw)  12.4 us
    another operation x2, other arithmetic, on_device(): solved = jax.scipy.linalg.solve_triangular(corner, rhs, lower=True).T  10.5 us
  transfers between devices with their start and end apart: 14, of which 3 were waited for; matrix products, arithmetic and copies ran while one was open for 24% of the time, Pallas kernels for 0%

profile of v2, /device:TPU:494, one launch (start us, length us, event | category | flops | bytes accessed | tf_op | source)
XLA Modules:
  0.0 98.3 jit_solution(3707076940299518582)
XLA Ops:
  0.6 0.7 slice.38
  1.3 0.9 slice-done.2
  2.3 0.7 collective-permute-start
  3.1 0.8 collective-permute-start.1
  3.9 0.7 collective-permute-start.2
  4.7 1.3 %collective-permute-start.3 = (f32[128,264]{0,1:T(8,128)S(1)}, f32[128,264]{0,1:T(8,128)S(1)}, u32[]{:S(2)}, u32[]{:S(2)}) collective-permute-start(f32[128,264]{0,1:T(8,128)S(1)} %broadcast_select_fusion.9), channel_id=1, source_target_pairs={{0,8},{1,9},{2,10},{3,11},{4,12},{5,13},{6,14},{7,15},{16,24},{17,... | collective-permute-start | bytes 405512 | tf_op jit(solution)/shard_map/ppermute | solution.py:13
  6.0 0.7 collective-permute-start.9
  6.8 33.5 %collective-permute-done.3 = f32[128,264]{0,1:T(8,128)S(1)} collective-permute-done((f32[128,264]{0,1:T(8,128)S(1)}, f32[128,264]{0,1:T(8,128)S(1)}, u32[]{:S(2)}, u32[]{:S(2)}) %collective-permute-start.3) | collective-permute-done | bytes 135200 | tf_op jit(solution)/shard_map/ppermute | solution.py:13
  40.2 0.7 collective-permute-start.4
  41.0 0.7 collective-permute-start.10
  41.7 0.7 collective-permute-start.5
  42.4 0.7 collective-permute-start.6
  43.1 0.7 collective-permute-start.11
  43.9 1.3 %collective-permute-start.7 = (f32[128,128]{0,1:T(8,128)S(1)}, f32[128,128]{0,1:T(8,128)S(1)}, u32[]{:S(2)}, u32[]{:S(2)}) collective-permute-start(f32[128,128]{0,1:T(8,128)S(1)} %broadcast_select_fusion.14), channel_id=1, source_target_pairs={{0,128},{16,144},{32,160},{48,176},{64,192},{80,208},{96,224},{112... | collective-permute-start | bytes 196616 | tf_op jit(solution)/shard_map/ppermute | solution.py:13
  45.2 16.2 %collective-permute-done.7 = f32[128,128]{0,1:T(8,128)S(1)} collective-permute-done((f32[128,128]{0,1:T(8,128)S(1)}, f32[128,128]{0,1:T(8,128)S(1)}, u32[]{:S(2)}, u32[]{:S(2)}) %collective-permute-start.7) | collective-permute-done | bytes 65568 | tf_op jit(solution)/shard_map/ppermute | solution.py:13
  61.4 1.3 %collective-permute-start.8 = (f32[128,128]{0,1:T(8,128)S(1)}, f32[128,128]{0,1:T(8,128)S(1)}, u32[]{:S(2)}, u32[]{:S(2)}) collective-permute-start(f32[128,128]{0,1:T(8,128)S(1)} %broadcast_select_fusion.15), channel_id=1, source_target_pairs={{0,256},{16,272},{32,288},{48,304},{64,320},{80,336},{96,352},{112... | collective-permute-start | bytes 196616 | tf_op jit(solution)/shard_map/ppermute | solution.py:13
  62.8 1.3 %collective-permute-start.12 = (f32[512,128]{1,0:T(8,128)S(1)}, f32[512,128]{1,0:T(8,128)S(1)}, u32[]{:S(2)}, u32[]{:S(2)}) collective-permute-start(f32[512,128]{1,0:T(8,128)S(1)} %broadcast_select_fusion.5), channel_id=1, source_target_pairs={{0,128},{16,144},{32,160},{48,176},{64,192},{80,208},{96,224},{112... | collective-permute-start | bytes 786440 | tf_op jit(solution)/shard_map/ppermute | solution.py:13
  64.7 11.7 %cholesky.18 = f32[128,128]{1,0:T(8,128)S(1)} custom-call(f32[128,128]{1,0:T(8,128)S(1)} %fusion.7), custom_call_target="Cholesky" | custom-call | tf_op jit(solution)/shard_map/jit(cholesky)/cholesky | solution.py:33
  76.5 5.8 %collective-permute-start.13 = (f32[512,128]{1,0:T(8,128)S(1)}, f32[512,128]{1,0:T(8,128)S(1)}, u32[]{:S(2)}, u32[]{:S(2)}) collective-permute-start(f32[512,128]{1,0:T(8,128)S(1)} %broadcast_select_fusion.6), channel_id=1, source_target_pairs={{0,256},{16,272},{32,288},{48,304},{64,320},{80,336},{96,352},{112... | collective-permute-start | bytes 786440 | tf_op jit(solution)/shard_map/ppermute | solution.py:13
  83.0 0.7 select_bitcast_fusion.1
  83.6 9.8 %custom-call.7 = f32[1,128,128]{1,2,0:T(8,128)S(1)} custom-call(f32[1,128,128]{2,1,0:T(8,128)S(1)} %get-tuple-element.2), custom_call_target="InvertDiagBlocksLowerTriangular" | custom-call | tf_op jit(solution)/shard_map/jit(_solve_triangular)/triangular_solve | solution.py:35
  93.5 0.8 fusion.1
  96.0 0.7 broadcast_select_fusion.11
  96.8 1.5 %broadcast_select_fusion = f32[4,1,128,2,1,128]{5,4,3,2,1,0:T(1,128)} fusion(pred[2]{0:T(512)(128)(4,1)S(1)} %get-tuple-element.5, f32[4,1,128,2,1,128]{5,4,3,2,1,0:T(1,128)S(1)} %bitcast.39, pred[4,2]{1,0:T(4,128)(4,1)S(1)} %broadcast_and_fusion, f32[4,128,128]{2,1,0:T(8,128)S(1)} %broadcast_select_fusion.2), kind=kLoop, calls=%fused_computation.3 | loop fusion | flops 262144 | bytes 1310730 | tf_op jit(solution)/shard_map/jit(_where)/select_n | solution.py:54
  (53 shorter events, 3.8 us)
Async XLA Ops:
  1.3 0.9 slice-start.2
  2.3 0.7 collective-permute-start
  3.0 2.9 %copy-start.1 = (f32[4,1,128,2,1,128]{5,4,3,2,1,0:T(1,128)S(1)}, f32[4,1,128,2,1,128]{5,4,3,2,1,0:T(1,128)}, u32[]{:S(2)}) copy-start(f32[4,1,128,2,1,128]{5,4,3,2,1,0:T(1,128)} %param.2) | copy-start | bytes 1572868
  3.1 0.8 collective-permute-start.1
  3.9 0.7 collective-permute-start.2
  4.7 35.6 %collective-permute-start.3 = (f32[128,264]{0,1:T(8,128)S(1)}, f32[128,264]{0,1:T(8,128)S(1)}, u32[]{:S(2)}, u32[]{:S(2)}) collective-permute-start(f32[128,264]{0,1:T(8,128)S(1)} %broadcast_select_fusion.9), channel_id=1, source_target_pairs={{0,8},{1,9},{2,10},{3,11},{4,12},{5,13},{6,14},{7,15},{16,24},{17,... | collective-permute-start | bytes 405512 | tf_op jit(solution)/shard_map/ppermute | solution.py:13
  6.0 34.9 %collective-permute-start.9 = (f32[512,128]{1,0:T(8,128)S(1)}, f32[512,128]{1,0:T(8,128)S(1)}, u32[]{:S(2)}, u32[]{:S(2)}) collective-permute-start(f32[512,128]{1,0:T(8,128)S(1)} %slice.45), channel_id=1, source_target_pairs={{0,16},{1,17},{2,18},{3,19},{4,20},{5,21},{6,22},{7,23},{8,24},{9,... | collective-permute-start | bytes 786440 | tf_op jit(solution)/shard_map/ppermute | solution.py:13
  40.2 1.4 %collective-permute-start.4 = (f32[128,128]{0,1:T(8,128)S(1)}, f32[128,128]{0,1:T(8,128)S(1)}, u32[]{:S(2)}, u32[]{:S(2)}) collective-permute-start(f32[128,128]{0,1:T(8,128)S(1)} %slice.44), channel_id=1, source_target_pairs={{0,16},{1,17},{2,18},{3,19},{4,20},{5,21},{6,22},{7,23},{8,24},{9,... | collective-permute-start | bytes 196616 | tf_op jit(solution)/shard_map/ppermute | solution.py:13
  41.0 2.1 %collective-permute-start.10 = (f32[512,128]{1,0:T(8,128)S(1)}, f32[512,128]{1,0:T(8,128)S(1)}, u32[]{:S(2)}, u32[]{:S(2)}) collective-permute-start(f32[512,128]{1,0:T(8,128)S(1)} %broadcast_select_fusion.3), channel_id=1, source_target_pairs={{0,32},{16,48},{1,33},{17,49},{2,34},{18,50},{3,35},{19,51},{4,36}... | collective-permute-start | bytes 786440 | tf_op jit(solution)/shard_map/ppermute | solution.py:13
  41.7 0.7 collective-permute-start.5
  42.4 1.4 %collective-permute-start.6 = (f32[128,128]{0,1:T(8,128)S(1)}, f32[128,128]{0,1:T(8,128)S(1)}, u32[]{:S(2)}, u32[]{:S(2)}) collective-permute-start(f32[128,128]{0,1:T(8,128)S(1)} %broadcast_select_fusion.13), channel_id=1, source_target_pairs={{0,64},{16,80},{32,96},{48,112},{1,65},{17,81},{33,97},{49,113},{2... | collective-permute-start | bytes 196616 | tf_op jit(solution)/shard_map/ppermute | solution.py:13
  43.1 19.6 %collective-permute-start.11 = (f32[512,128]{1,0:T(8,128)S(1)}, f32[512,128]{1,0:T(8,128)S(1)}, u32[]{:S(2)}, u32[]{:S(2)}) collective-permute-start(f32[512,128]{1,0:T(8,128)S(1)} %broadcast_select_fusion.4), channel_id=1, source_target_pairs={{0,64},{16,80},{32,96},{48,112},{1,65},{17,81},{33,97},{49,113},{2... | collective-permute-start | bytes 786440 | tf_op jit(solution)/shard_map/ppermute | solution.py:13
  43.9 17.5 %collective-permute-start.7 = (f32[128,128]{0,1:T(8,128)S(1)}, f32[128,128]{0,1:T(8,128)S(1)}, u32[]{:S(2)}, u32[]{:S(2)}) collective-permute-start(f32[128,128]{0,1:T(8,128)S(1)} %broadcast_select_fusion.14), channel_id=1, source_target_pairs={{0,128},{16,144},{32,160},{48,176},{64,192},{80,208},{96,224},{112... | collective-permute-start | bytes 196616 | tf_op jit(solution)/shard_map/ppermute | solution.py:13
  61.4 3.2 %collective-permute-start.8 = (f32[128,128]{0,1:T(8,128)S(1)}, f32[128,128]{0,1:T(8,128)S(1)}, u32[]{:S(2)}, u32[]{:S(2)}) collective-permute-start(f32[128,128]{0,1:T(8,128)S(1)} %broadcast_select_fusion.15), channel_id=1, source_target_pairs={{0,256},{16,272},{32,288},{48,304},{64,320},{80,336},{96,352},{112... | collective-permute-start | bytes 196616 | tf_op jit(solution)/shard_map/ppermute | solution.py:13
  62.8 13.7 %collective-permute-start.12 = (f32[512,128]{1,0:T(8,128)S(1)}, f32[512,128]{1,0:T(8,128)S(1)}, u32[]{:S(2)}, u32[]{:S(2)}) collective-permute-start(f32[512,128]{1,0:T(8,128)S(1)} %broadcast_select_fusion.5), channel_id=1, source_target_pairs={{0,128},{16,144},{32,160},{48,176},{64,192},{80,208},{96,224},{112... | collective-permute-start | bytes 786440 | tf_op jit(solution)/shard_map/ppermute | solution.py:13
  76.5 16.9 %collective-permute-start.13 = (f32[512,128]{1,0:T(8,128)S(1)}, f32[512,128]{1,0:T(8,128)S(1)}, u32[]{:S(2)}, u32[]{:S(2)}) collective-permute-start(f32[512,128]{1,0:T(8,128)S(1)} %broadcast_select_fusion.6), channel_id=1, source_target_pairs={{0,256},{16,272},{32,288},{48,304},{64,320},{80,336},{96,352},{112... | collective-permute-start | bytes 786440 | tf_op jit(solution)/shard_map/ppermute | solution.py:13
  94.3 0.8 copy-start
  94.3 0.7 copy-start.2
  95.3 0.7 slice-start
  95.3 1.4 %slice-start.1 = ((f32[776,128]{1,0:T(8,128)}), f32[512,128]{1,0:T(8,128)S(1)}, s32[]{:S(2)}) async-start(f32[776,128]{1,0:T(8,128)} %copy-done), calls=%async_computation.1 | async-start | bytes 524288 | tf_op jit(solution)/shard_map/slice | solution.py:36

commit v3 on v2

--- a/solution.py
+++ b/solution.py
@@ -8,11 +8,13 @@
     count = lax.axis_size(axis)
     index = lax.axis_index(axis)
     step = 1
-    while step < count:
-        pairs = [(i, i + step) for i in range(step) if i + step < count]
+    while 2 * step < count:
+        step *= 2
+    while step >= 1:
+        pairs = [(i, i + step) for i in range(0, count, 2 * step) if i + step < count]
         arrived = lax.ppermute(block, axis, pairs)
-        block = jnp.where((index >= step) & (index < 2 * step), arrived, block)
-        step *= 2
+        block = jnp.where(index % (2 * step) == step, arrived, block)
+        step //= 2
     return block
 
 

time: 98.8 us -> 93.9 us (0.950)
  the two profiles are of different devices: /device:TPU:494 before, /device:TPU:472 now
where the time goes in v3:
time: 93.9 us; the launch traced here: 93.4 us
  waiting for transfers between devices  43.5 us (46%)
  other arithmetic  25.6 us (27%)
  starting transfers between devices  18.9 us (20%)
  local copies, waits for them, and re-layouts  2.69 us (3%)
  matrix products  1.66 us (2%)
  between operations  1.1 us (1%)
    ppermute x14, waiting for transfers between devices, spread(): arrived = lax.ppermute(block, axis, pairs)  43.5 us
    ppermute x14, starting transfers between devices, spread(): arrived = lax.ppermute(block, axis, pairs)  18.9 us
    another operation x3, other arithmetic, on_device(): corner = jnp.linalg.cholesky(corner_raw)  12.4 us
    another operation x2, other arithmetic, on_device(): solved = jax.scipy.linalg.solve_triangular(corner, rhs, lower=True).T  10.5 us
  transfers between devices with their start and end apart: 14, of which 5 were waited for; matrix products, arithmetic and copies ran while one was open for 25% of the time, Pallas kernels for 0%

profile of v3, /device:TPU:472, one launch (start us, length us, event | category | flops | bytes accessed | tf_op | source)
XLA Modules:
  0.0 93.4 jit_solution(55565897210837272)
XLA Ops:
  0.6 0.7 slice.38
  1.3 0.9 slice-done.2
  2.3 0.7 collective-permute-start
  3.1 0.8 collective-permute-start.1
  3.9 1.3 %collective-permute-start.2 = (f32[128,264]{0,1:T(8,128)S(1)}, f32[128,264]{0,1:T(8,128)S(1)}, u32[]{:S(2)}, u32[]{:S(2)}) collective-permute-start(f32[128,264]{0,1:T(8,128)S(1)} %broadcast_select_fusion.8), channel_id=1, source_target_pairs={{0,2},{4,6},{8,10},{12,14},{16,18},{20,22},{24,26},{28,30},{32,34}... | collective-permute-start | bytes 405512 | tf_op jit(solution)/shard_map/ppermute | solution.py:15
  5.3 27.5 %collective-permute-done.2 = f32[128,264]{0,1:T(8,128)S(1)} collective-permute-done((f32[128,264]{0,1:T(8,128)S(1)}, f32[128,264]{0,1:T(8,128)S(1)}, u32[]{:S(2)}, u32[]{:S(2)}) %collective-permute-start.2) | collective-permute-done | bytes 135200 | tf_op jit(solution)/shard_map/ppermute | solution.py:15
  32.8 1.3 %collective-permute-start.3 = (f32[128,264]{0,1:T(8,128)S(1)}, f32[128,264]{0,1:T(8,128)S(1)}, u32[]{:S(2)}, u32[]{:S(2)}) collective-permute-start(f32[128,264]{0,1:T(8,128)S(1)} %broadcast_select_fusion.9), channel_id=1, source_target_pairs={{0,1},{2,3},{4,5},{6,7},{8,9},{10,11},{12,13},{14,15},{16,17},{18,... | collective-permute-start | bytes 405512 | tf_op jit(solution)/shard_map/ppermute | solution.py:15
  34.2 0.7 collective-permute-start.9
  34.9 1.7 %collective-permute-done.3 = f32[128,264]{0,1:T(8,128)S(1)} collective-permute-done((f32[128,264]{0,1:T(8,128)S(1)}, f32[128,264]{0,1:T(8,128)S(1)}, u32[]{:S(2)}, u32[]{:S(2)}) %collective-permute-start.3) | collective-permute-done | bytes 135200 | tf_op jit(solution)/shard_map/ppermute | solution.py:15
  37.4 1.3 %collective-permute-start.10 = (f32[512,128]{1,0:T(8,128)S(1)}, f32[512,128]{1,0:T(8,128)S(1)}, u32[]{:S(2)}, u32[]{:S(2)}) collective-permute-start(f32[512,128]{1,0:T(8,128)S(1)} %broadcast_select_fusion.3), channel_id=1, source_target_pairs={{0,128},{256,384},{1,129},{257,385},{2,130},{258,386},{3,131},{259... | collective-permute-start | bytes 786440 | tf_op jit(solution)/shard_map/ppermute | solution.py:15
  38.7 1.3 %collective-permute-start.5 = (f32[128,128]{0,1:T(8,128)S(1)}, f32[128,128]{0,1:T(8,128)S(1)}, u32[]{:S(2)}, u32[]{:S(2)}) collective-permute-start(f32[128,128]{0,1:T(8,128)S(1)} %broadcast_select_fusion.12), channel_id=1, source_target_pairs={{0,128},{256,384},{1,129},{257,385},{2,130},{258,386},{3,131},{259... | collective-permute-start | bytes 196616 | tf_op jit(solution)/shard_map/ppermute | solution.py:15
  40.1 11.0 %collective-permute-done.5 = f32[128,128]{0,1:T(8,128)S(1)} collective-permute-done((f32[128,128]{0,1:T(8,128)S(1)}, f32[128,128]{0,1:T(8,128)S(1)}, u32[]{:S(2)}, u32[]{:S(2)}) %collective-permute-start.5) | collective-permute-done | bytes 65568 | tf_op jit(solution)/shard_map/ppermute | solution.py:15
  51.1 1.3 %collective-permute-start.6 = (f32[128,128]{0,1:T(8,128)S(1)}, f32[128,128]{0,1:T(8,128)S(1)}, u32[]{:S(2)}, u32[]{:S(2)}) collective-permute-start(f32[128,128]{0,1:T(8,128)S(1)} %broadcast_select_fusion.13), channel_id=1, source_target_pairs={{0,64},{128,192},{256,320},{384,448},{1,65},{129,193},{257,321},{3... | collective-permute-start | bytes 196616 | tf_op jit(solution)/shard_map/ppermute | solution.py:15
  52.5 1.3 %collective-permute-start.11 = (f32[512,128]{1,0:T(8,128)S(1)}, f32[512,128]{1,0:T(8,128)S(1)}, u32[]{:S(2)}, u32[]{:S(2)}) collective-permute-start(f32[512,128]{1,0:T(8,128)S(1)} %broadcast_select_fusion.4), channel_id=1, source_target_pairs={{0,64},{128,192},{256,320},{384,448},{1,65},{129,193},{257,321},{3... | collective-permute-start | bytes 786440 | tf_op jit(solution)/shard_map/ppermute | solution.py:15
  54.3 1.3 %collective-permute-start.7 = (f32[128,128]{0,1:T(8,128)S(1)}, f32[128,128]{0,1:T(8,128)S(1)}, u32[]{:S(2)}, u32[]{:S(2)}) collective-permute-start(f32[128,128]{0,1:T(8,128)S(1)} %broadcast_select_fusion.14), channel_id=1, source_target_pairs={{0,32},{64,96},{128,160},{192,224},{256,288},{320,352},{384,416},{... | collective-permute-start | bytes 196616 | tf_op jit(solution)/shard_map/ppermute | solution.py:15
  55.7 2.7 %collective-permute-done.7 = f32[128,128]{0,1:T(8,128)S(1)} collective-permute-done((f32[128,128]{0,1:T(8,128)S(1)}, f32[128,128]{0,1:T(8,128)S(1)}, u32[]{:S(2)}, u32[]{:S(2)}) %collective-permute-start.7) | collective-permute-done | bytes 65568 | tf_op jit(solution)/shard_map/ppermute | solution.py:15
  58.3 1.3 %collective-permute-start.8 = (f32[128,128]{0,1:T(8,128)S(1)}, f32[128,128]{0,1:T(8,128)S(1)}, u32[]{:S(2)}, u32[]{:S(2)}) collective-permute-start(f32[128,128]{0,1:T(8,128)S(1)} %broadcast_select_fusion.15), channel_id=1, source_target_pairs={{0,16},{32,48},{64,80},{96,112},{128,144},{160,176},{192,208},{224... | collective-permute-start | bytes 196616 | tf_op jit(solution)/shard_map/ppermute | solution.py:15
  59.7 4.4 %collective-permute-start.12 = (f32[512,128]{1,0:T(8,128)S(1)}, f32[512,128]{1,0:T(8,128)S(1)}, u32[]{:S(2)}, u32[]{:S(2)}) collective-permute-start(f32[512,128]{1,0:T(8,128)S(1)} %broadcast_select_fusion.5), channel_id=1, source_target_pairs={{0,32},{64,96},{128,160},{192,224},{256,288},{320,352},{384,416},{... | collective-permute-start | bytes 786440 | tf_op jit(solution)/shard_map/ppermute | solution.py:15
  64.2 11.7 %cholesky.18 = f32[128,128]{1,0:T(8,128)S(1)} custom-call(f32[128,128]{1,0:T(8,128)S(1)} %fusion.7), custom_call_target="Cholesky" | custom-call | tf_op jit(solution)/shard_map/jit(cholesky)/cholesky | solution.py:35
  76.0 1.3 %collective-permute-start.13 = (f32[512,128]{1,0:T(8,128)S(1)}, f32[512,128]{1,0:T(8,128)S(1)}, u32[]{:S(2)}, u32[]{:S(2)}) collective-permute-start(f32[512,128]{1,0:T(8,128)S(1)} %broadcast_select_fusion.6), channel_id=1, source_target_pairs={{0,16},{32,48},{64,80},{96,112},{128,144},{160,176},{192,208},{224... | collective-permute-start | bytes 786440 | tf_op jit(solution)/shard_map/ppermute | solution.py:15
  78.7 9.8 %custom-call.7 = f32[1,128,128]{1,2,0:T(8,128)S(1)} custom-call(f32[1,128,128]{2,1,0:T(8,128)S(1)} %get-tuple-element.2), custom_call_target="InvertDiagBlocksLowerTriangular" | custom-call | tf_op jit(solution)/shard_map/jit(_solve_triangular)/triangular_solve | solution.py:37
  88.5 0.8 fusion.1
  91.1 0.7 broadcast_select_fusion.11
  91.8 1.5 %broadcast_select_fusion = f32[4,1,128,2,1,128]{5,4,3,2,1,0:T(1,128)} fusion(pred[2]{0:T(512)(128)(4,1)S(1)} %get-tuple-element.5, f32[4,1,128,2,1,128]{5,4,3,2,1,0:T(1,128)S(1)} %bitcast.39, pred[4,2]{1,0:T(4,128)(4,1)S(1)} %broadcast_and_fusion, f32[4,128,128]{2,1,0:T(8,128)S(1)} %broadcast_select_fusion.2), kind=kLoop, calls=%fused_computation.3 | loop fusion | flops 262144 | bytes 1310730 | tf_op jit(solution)/shard_map/jit(_where)/select_n | solution.py:56
  (53 shorter events, 5.0 us)
Async XLA Ops:
  1.3 0.9 slice-start.2
  2.3 0.7 collective-permute-start
  3.1 31.1 %copy-start.1 = (f32[4,1,128,2,1,128]{5,4,3,2,1,0:T(1,128)S(1)}, f32[4,1,128,2,1,128]{5,4,3,2,1,0:T(1,128)}, u32[]{:S(2)}) copy-start(f32[4,1,128,2,1,128]{5,4,3,2,1,0:T(1,128)} %param.2) | copy-start | bytes 1572868
  3.1 0.8 collective-permute-start.1
  3.9 28.9 %collective-permute-start.2 = (f32[128,264]{0,1:T(8,128)S(1)}, f32[128,264]{0,1:T(8,128)S(1)}, u32[]{:S(2)}, u32[]{:S(2)}) collective-permute-start(f32[128,264]{0,1:T(8,128)S(1)} %broadcast_select_fusion.8), channel_id=1, source_target_pairs={{0,2},{4,6},{8,10},{12,14},{16,18},{20,22},{24,26},{28,30},{32,34}... | collective-permute-start | bytes 405512 | tf_op jit(solution)/shard_map/ppermute | solution.py:15
  32.8 3.8 %collective-permute-start.3 = (f32[128,264]{0,1:T(8,128)S(1)}, f32[128,264]{0,1:T(8,128)S(1)}, u32[]{:S(2)}, u32[]{:S(2)}) collective-permute-start(f32[128,264]{0,1:T(8,128)S(1)} %broadcast_select_fusion.9), channel_id=1, source_target_pairs={{0,1},{2,3},{4,5},{6,7},{8,9},{10,11},{12,13},{14,15},{16,17},{18,... | collective-permute-start | bytes 405512 | tf_op jit(solution)/shard_map/ppermute | solution.py:15
  34.2 3.2 %collective-permute-start.9 = (f32[512,128]{1,0:T(8,128)S(1)}, f32[512,128]{1,0:T(8,128)S(1)}, u32[]{:S(2)}, u32[]{:S(2)}) collective-permute-start(f32[512,128]{1,0:T(8,128)S(1)} %slice.45), channel_id=1, source_target_pairs={{0,256},{1,257},{2,258},{3,259},{4,260},{5,261},{6,262},{7,263},{8... | collective-permute-start | bytes 786440 | tf_op jit(solution)/shard_map/ppermute | solution.py:15
  36.7 2.0 %collective-permute-start.4 = (f32[128,128]{0,1:T(8,128)S(1)}, f32[128,128]{0,1:T(8,128)S(1)}, u32[]{:S(2)}, u32[]{:S(2)}) collective-permute-start(f32[128,128]{0,1:T(8,128)S(1)} %slice.44), channel_id=1, source_target_pairs={{0,256},{1,257},{2,258},{3,259},{4,260},{5,261},{6,262},{7,263},{8... | collective-permute-start | bytes 196616 | tf_op jit(solution)/shard_map/ppermute | solution.py:15
  37.4 15.0 %collective-permute-start.10 = (f32[512,128]{1,0:T(8,128)S(1)}, f32[512,128]{1,0:T(8,128)S(1)}, u32[]{:S(2)}, u32[]{:S(2)}) collective-permute-start(f32[512,128]{1,0:T(8,128)S(1)} %broadcast_select_fusion.3), channel_id=1, source_target_pairs={{0,128},{256,384},{1,129},{257,385},{2,130},{258,386},{3,131},{259... | collective-permute-start | bytes 786440 | tf_op jit(solution)/shard_map/ppermute | solution.py:15
  38.7 12.3 %collective-permute-start.5 = (f32[128,128]{0,1:T(8,128)S(1)}, f32[128,128]{0,1:T(8,128)S(1)}, u32[]{:S(2)}, u32[]{:S(2)}) collective-permute-start(f32[128,128]{0,1:T(8,128)S(1)} %broadcast_select_fusion.12), channel_id=1, source_target_pairs={{0,128},{256,384},{1,129},{257,385},{2,130},{258,386},{3,131},{259... | collective-permute-start | bytes 196616 | tf_op jit(solution)/shard_map/ppermute | solution.py:15
  51.1 3.2 %collective-permute-start.6 = (f32[128,128]{0,1:T(8,128)S(1)}, f32[128,128]{0,1:T(8,128)S(1)}, u32[]{:S(2)}, u32[]{:S(2)}) collective-permute-start(f32[128,128]{0,1:T(8,128)S(1)} %broadcast_select_fusion.13), channel_id=1, source_target_pairs={{0,64},{128,192},{256,320},{384,448},{1,65},{129,193},{257,321},{3... | collective-permute-start | bytes 196616 | tf_op jit(solution)/shard_map/ppermute | solution.py:15
  52.5 7.2 %collective-permute-start.11 = (f32[512,128]{1,0:T(8,128)S(1)}, f32[512,128]{1,0:T(8,128)S(1)}, u32[]{:S(2)}, u32[]{:S(2)}) collective-permute-start(f32[512,128]{1,0:T(8,128)S(1)} %broadcast_select_fusion.4), channel_id=1, source_target_pairs={{0,64},{128,192},{256,320},{384,448},{1,65},{129,193},{257,321},{3... | collective-permute-start | bytes 786440 | tf_op jit(solution)/shard_map/ppermute | solution.py:15
  54.3 4.0 %collective-permute-start.7 = (f32[128,128]{0,1:T(8,128)S(1)}, f32[128,128]{0,1:T(8,128)S(1)}, u32[]{:S(2)}, u32[]{:S(2)}) collective-permute-start(f32[128,128]{0,1:T(8,128)S(1)} %broadcast_select_fusion.14), channel_id=1, source_target_pairs={{0,32},{64,96},{128,160},{192,224},{256,288},{320,352},{384,416},{... | collective-permute-start | bytes 196616 | tf_op jit(solution)/shard_map/ppermute | solution.py:15
  58.3 5.8 %collective-permute-start.8 = (f32[128,128]{0,1:T(8,128)S(1)}, f32[128,128]{0,1:T(8,128)S(1)}, u32[]{:S(2)}, u32[]{:S(2)}) collective-permute-start(f32[128,128]{0,1:T(8,128)S(1)} %broadcast_select_fusion.15), channel_id=1, source_target_pairs={{0,16},{32,48},{64,80},{96,112},{128,144},{160,176},{192,208},{224... | collective-permute-start | bytes 196616 | tf_op jit(solution)/shard_map/ppermute | solution.py:15
  59.7 16.3 %collective-permute-start.12 = (f32[512,128]{1,0:T(8,128)S(1)}, f32[512,128]{1,0:T(8,128)S(1)}, u32[]{:S(2)}, u32[]{:S(2)}) collective-permute-start(f32[512,128]{1,0:T(8,128)S(1)} %broadcast_select_fusion.5), channel_id=1, source_target_pairs={{0,32},{64,96},{128,160},{192,224},{256,288},{320,352},{384,416},{... | collective-permute-start | bytes 786440 | tf_op jit(solution)/shard_map/ppermute | solution.py:15
  76.0 12.4 %collective-permute-start.13 = (f32[512,128]{1,0:T(8,128)S(1)}, f32[512,128]{1,0:T(8,128)S(1)}, u32[]{:S(2)}, u32[]{:S(2)}) collective-permute-start(f32[512,128]{1,0:T(8,128)S(1)} %broadcast_select_fusion.6), channel_id=1, source_target_pairs={{0,16},{32,48},{64,80},{96,112},{128,144},{160,176},{192,208},{224... | collective-permute-start | bytes 786440 | tf_op jit(solution)/shard_map/ppermute | solution.py:15
  89.3 0.8 copy-start
  89.3 0.7 copy-start.2
  90.4 0.7 slice-start
  90.4 1.4 %slice-start.1 = ((f32[776,128]{1,0:T(8,128)}), f32[512,128]{1,0:T(8,128)S(1)}, s32[]{:S(2)}) async-start(f32[776,128]{1,0:T(8,128)} %copy-done), calls=%async_computation.1 | async-start | bytes 524288 | tf_op jit(solution)/shard_map/slice | solution.py:38

commit v4 on v3

--- a/solution.py
+++ b/solution.py
@@ -18,6 +18,28 @@
     return block
 
 
+def spread_wide(block, axis):
+    count = lax.axis_size(axis)
+    index = lax.axis_index(axis)
+    radices = []
+    rest = count
+    while rest > 1:
+        radix = 4 if rest % 4 == 0 else rest
+        radices.append(radix)
+        rest //= radix
+    span = count
+    for radix in radices:
+        span //= radix
+        got = block
+        for digit in range(1, radix):
+            pairs = [(i, i + digit * span) for i in range(0, count, span * radix)]
+            arrived = lax.ppermute(block, axis, pairs)
+            mine = (index % (span * radix)) == digit * span
+            got = jnp.where(mine, arrived, got)
+        block = got
+    return block
+
+
 def on_device(normal_matrix, right_sides):
     row_blocks, _, block, col_blocks, _, _ = normal_matrix.shape
     col_id = lax.axis_index("col")
@@ -29,8 +51,8 @@
 
     left = spread(local[:, :block], "col")
     top = jnp.concatenate([local[:block], right_sides[:, 0, 0, :].T], axis=1)
-    top = spread(top, "row")
-    corner_raw = spread(top[:, :block], "col")
+    top = spread_wide(top, "row")
+    corner_raw = spread_wide(top[:, :block], "col")
 
     corner = jnp.linalg.cholesky(corner_raw)
     rhs = jnp.concatenate([left.T, top], axis=1)

time: 93.9 us -> 89.5 us (0.953)
  the two profiles are of different devices: /device:TPU:472 before, /device:TPU:28 now
where the time goes in v4:
time: 89.5 us; the launch traced here: 89 us
  starting transfers between devices  32.9 us (37%)
  other arithmetic  25.6 us (29%)
  waiting for transfers between devices  25.1 us (28%)
  local copies, waits for them, and re-layouts  2.69 us (3%)
  matrix products  1.66 us (2%)
  between operations  1.1 us (1%)
    ppermute x13, starting transfers between devices, spread_wide(): arrived = lax.ppermute(block, axis, pairs)  27.6 us
    ppermute x13, waiting for transfers between devices, spread_wide(): arrived = lax.ppermute(block, axis, pairs)  16.8 us
    another operation x3, other arithmetic, on_device(): corner = jnp.linalg.cholesky(corner_raw)  12.4 us
    another operation x2, other arithmetic, on_device(): solved = jax.scipy.linalg.solve_triangular(corner, rhs, lower=True).T  10.5 us
    ppermute x5, waiting for transfers between devices, spread(): arrived = lax.ppermute(block, axis, pairs)  8.29 us
    ppermute x5, starting transfers between devices, spread(): arrived = lax.ppermute(block, axis, pairs)  5.26 us
  transfers between devices with their start and end apart: 18, of which 7 were waited for; matrix products, arithmetic and copies ran while one was open for 26% of the time, Pallas kernels for 0%

profile of v4, /device:TPU:28, one launch (start us, length us, event | category | flops | bytes accessed | tf_op | source)
XLA Modules:
  0.0 89.0 jit_solution(2170603934798160183)
XLA Ops:
  0.6 0.7 slice.38
  1.3 0.9 %slice-done.2 = f32[1,1,128,2,1,128]{5,4,3,2,1,0:T(1,128)S(1)} async-done(((f32[4,1,128,2,1,128]{5,4,3,2,1,0:T(1,128)}), f32[1,1,128,2,1,128]{5,4,3,2,1,0:T(1,128)S(1)}, s32[]{:S(2)}) %slice-start.2) | async-done | bytes 131096 | tf_op jit(solution)/shard_map/slice | solution.py:53
  2.4 9.2 %collective-permute-start.2 = (f32[128,264]{0,1:T(8,128)S(1)}, f32[128,264]{0,1:T(8,128)S(1)}, u32[]{:S(2)}, u32[]{:S(2)}) collective-permute-start(f32[128,264]{0,1:T(8,128)S(1)} %pad_maximum_fusion), channel_id=1, source_target_pairs={{0,4},{16,20},{32,36},{48,52},{64,68},{80,84},{96,100},{112,116},{... | collective-permute-start | bytes 405512 | tf_op jit(solution)/shard_map/ppermute | solution.py:36
  11.6 7.3 %collective-permute-start.1 = (f32[128,264]{0,1:T(8,128)S(1)}, f32[128,264]{0,1:T(8,128)S(1)}, u32[]{:S(2)}, u32[]{:S(2)}) collective-permute-start(f32[128,264]{0,1:T(8,128)S(1)} %pad_maximum_fusion), channel_id=1, source_target_pairs={{0,8},{16,24},{32,40},{48,56},{64,72},{80,88},{96,104},{112,120},{... | collective-permute-start | bytes 405512 | tf_op jit(solution)/shard_map/ppermute | solution.py:36
  18.9 1.3 %collective-permute-start = (f32[128,264]{0,1:T(8,128)S(1)}, f32[128,264]{0,1:T(8,128)S(1)}, u32[]{:S(2)}, u32[]{:S(2)}) collective-permute-start(f32[128,264]{0,1:T(8,128)S(1)} %pad_maximum_fusion), channel_id=1, source_target_pairs={{0,12},{16,28},{32,44},{48,60},{64,76},{80,92},{96,108},{112,124},... | collective-permute-start | bytes 405512 | tf_op jit(solution)/shard_map/ppermute | solution.py:36
  20.2 1.5 %collective-permute-done.1 = f32[128,264]{0,1:T(8,128)S(1)} collective-permute-done((f32[128,264]{0,1:T(8,128)S(1)}, f32[128,264]{0,1:T(8,128)S(1)}, u32[]{:S(2)}, u32[]{:S(2)}) %collective-permute-start.1) | collective-permute-done | bytes 135200 | tf_op jit(solution)/shard_map/ppermute | solution.py:36
  21.7 1.3 %collective-permute-done = f32[128,264]{0,1:T(8,128)S(1)} collective-permute-done((f32[128,264]{0,1:T(8,128)S(1)}, f32[128,264]{0,1:T(8,128)S(1)}, u32[]{:S(2)}, u32[]{:S(2)}) %collective-permute-start) | collective-permute-done | bytes 135200 | tf_op jit(solution)/shard_map/ppermute | solution.py:36
  23.1 1.3 %collective-permute-start.5 = (f32[128,264]{0,1:T(8,128)S(1)}, f32[128,264]{0,1:T(8,128)S(1)}, u32[]{:S(2)}, u32[]{:S(2)}) collective-permute-start(f32[128,264]{0,1:T(8,128)S(1)} %select_select_fusion.1), channel_id=1, source_target_pairs={{0,1},{4,5},{8,9},{12,13},{16,17},{20,21},{24,25},{28,29},{32,33},... | collective-permute-start | bytes 405512 | tf_op jit(solution)/shard_map/ppermute | solution.py:36
  24.4 1.3 %collective-permute-start.4 = (f32[128,264]{0,1:T(8,128)S(1)}, f32[128,264]{0,1:T(8,128)S(1)}, u32[]{:S(2)}, u32[]{:S(2)}) collective-permute-start(f32[128,264]{0,1:T(8,128)S(1)} %select_select_fusion.1), channel_id=1, source_target_pairs={{0,2},{4,6},{8,10},{12,14},{16,18},{20,22},{24,26},{28,30},{32,34}... | collective-permute-start | bytes 405512 | tf_op jit(solution)/shard_map/ppermute | solution.py:36
  25.7 1.3 %collective-permute-start.3 = (f32[128,264]{0,1:T(8,128)S(1)}, f32[128,264]{0,1:T(8,128)S(1)}, u32[]{:S(2)}, u32[]{:S(2)}) collective-permute-start(f32[128,264]{0,1:T(8,128)S(1)} %select_select_fusion.1), channel_id=1, source_target_pairs={{0,3},{4,7},{8,11},{12,15},{16,19},{20,23},{24,27},{28,31},{32,35}... | collective-permute-start | bytes 405512 | tf_op jit(solution)/shard_map/ppermute | solution.py:36
  28.4 2.6 %collective-permute-done.4 = f32[128,264]{0,1:T(8,128)S(1)} collective-permute-done((f32[128,264]{0,1:T(8,128)S(1)}, f32[128,264]{0,1:T(8,128)S(1)}, u32[]{:S(2)}, u32[]{:S(2)}) %collective-permute-start.4) | collective-permute-done | bytes 135200 | tf_op jit(solution)/shard_map/ppermute | solution.py:36
  31.0 1.4 %collective-permute-done.3 = f32[128,264]{0,1:T(8,128)S(1)} collective-permute-done((f32[128,264]{0,1:T(8,128)S(1)}, f32[128,264]{0,1:T(8,128)S(1)}, u32[]{:S(2)}, u32[]{:S(2)}) %collective-permute-start.3) | collective-permute-done | bytes 135200 | tf_op jit(solution)/shard_map/ppermute | solution.py:36
  35.9 1.3 %collective-permute-start.10 = (f32[128,128]{0,1:T(8,128)S(1)}, f32[128,128]{0,1:T(8,128)S(1)}, u32[]{:S(2)}, u32[]{:S(2)}) collective-permute-start(f32[128,128]{0,1:T(8,128)S(1)} %select_select_fusion.4), channel_id=1, source_target_pairs={{0,64},{128,192},{256,320},{384,448},{1,65},{129,193},{257,321},{3... | collective-permute-start | bytes 196616 | tf_op jit(solution)/shard_map/ppermute | solution.py:36
  38.0 9.4 %collective-permute-done.10 = f32[128,128]{0,1:T(8,128)S(1)} collective-permute-done((f32[128,128]{0,1:T(8,128)S(1)}, f32[128,128]{0,1:T(8,128)S(1)}, u32[]{:S(2)}, u32[]{:S(2)}) %collective-permute-start.10) | collective-permute-done | bytes 65568 | tf_op jit(solution)/shard_map/ppermute | solution.py:36
  47.4 1.3 %collective-permute-start.12 = (f32[128,128]{0,1:T(8,128)S(1)}, f32[128,128]{0,1:T(8,128)S(1)}, u32[]{:S(2)}, u32[]{:S(2)}) collective-permute-start(f32[128,128]{0,1:T(8,128)S(1)} %select_select_fusion.3), channel_id=1, source_target_pairs={{0,16},{32,48},{64,80},{96,112},{128,144},{160,176},{192,208},{224... | collective-permute-start | bytes 196616 | tf_op jit(solution)/shard_map/ppermute | solution.py:36
  48.7 1.3 %collective-permute-start.15 = (f32[512,128]{1,0:T(8,128)S(1)}, f32[512,128]{1,0:T(8,128)S(1)}, u32[]{:S(2)}, u32[]{:S(2)}) collective-permute-start(f32[512,128]{1,0:T(8,128)S(1)} %broadcast_select_fusion.4), channel_id=1, source_target_pairs={{0,64},{128,192},{256,320},{384,448},{1,65},{129,193},{257,321},{3... | collective-permute-start | bytes 786440 | tf_op jit(solution)/shard_map/ppermute | solution.py:15
  50.2 8.3 %collective-permute-done.15 = f32[512,128]{1,0:T(8,128)S(1)} collective-permute-done((f32[512,128]{1,0:T(8,128)S(1)}, f32[512,128]{1,0:T(8,128)S(1)}, u32[]{:S(2)}, u32[]{:S(2)}) %collective-permute-start.15) | collective-permute-done | bytes 262176 | tf_op jit(solution)/shard_map/ppermute | solution.py:15
  58.5 1.3 %collective-permute-start.16 = (f32[512,128]{1,0:T(8,128)S(1)}, f32[512,128]{1,0:T(8,128)S(1)}, u32[]{:S(2)}, u32[]{:S(2)}) collective-permute-start(f32[512,128]{1,0:T(8,128)S(1)} %broadcast_select_fusion.5), channel_id=1, source_target_pairs={{0,32},{64,96},{128,160},{192,224},{256,288},{320,352},{384,416},{... | collective-permute-start | bytes 786440 | tf_op jit(solution)/shard_map/ppermute | solution.py:15
  59.8 11.7 %cholesky.18 = f32[128,128]{1,0:T(8,128)S(1)} custom-call(f32[128,128]{1,0:T(8,128)S(1)} %fusion.7), custom_call_target="Cholesky" | custom-call | tf_op jit(solution)/shard_map/jit(cholesky)/cholesky | solution.py:57
  71.6 1.3 %collective-permute-start.17 = (f32[512,128]{1,0:T(8,128)S(1)}, f32[512,128]{1,0:T(8,128)S(1)}, u32[]{:S(2)}, u32[]{:S(2)}) collective-permute-start(f32[512,128]{1,0:T(8,128)S(1)} %broadcast_select_fusion.6), channel_id=1, source_target_pairs={{0,16},{32,48},{64,80},{96,112},{128,144},{160,176},{192,208},{224... | collective-permute-start | bytes 786440 | tf_op jit(solution)/shard_map/ppermute | solution.py:15
  74.2 9.8 %custom-call.7 = f32[1,128,128]{1,2,0:T(8,128)S(1)} custom-call(f32[1,128,128]{2,1,0:T(8,128)S(1)} %get-tuple-element.2), custom_call_target="InvertDiagBlocksLowerTriangular" | custom-call | tf_op jit(solution)/shard_map/jit(_solve_triangular)/triangular_solve | solution.py:59
  84.1 0.8 fusion.1
  86.7 0.7 broadcast_select_fusion.7
  87.4 1.5 %broadcast_select_fusion = f32[4,1,128,2,1,128]{5,4,3,2,1,0:T(1,128)} fusion(pred[2]{0:T(512)(128)(4,1)S(1)} %get-tuple-element.5, f32[4,1,128,2,1,128]{5,4,3,2,1,0:T(1,128)S(1)} %bitcast.39, pred[4,2]{1,0:T(4,128)(4,1)S(1)} %broadcast_and_fusion, f32[4,128,128]{2,1,0:T(8,128)S(1)} %broadcast_select_fusion.2), kind=kLoop, calls=%fused_computation.3 | loop fusion | flops 262144 | bytes 1310730 | tf_op jit(solution)/shard_map/jit(_where)/select_n | solution.py:78
  (57 shorter events, 9.1 us)
Async XLA Ops:
  1.3 0.9 %slice-start.2 = ((f32[4,1,128,2,1,128]{5,4,3,2,1,0:T(1,128)}), f32[1,1,128,2,1,128]{5,4,3,2,1,0:T(1,128)S(1)}, s32[]{:S(2)}) async-start(f32[4,1,128,2,1,128]{5,4,3,2,1,0:T(1,128)} %param.2), calls=%async_computation.2 | async-start | bytes 262144 | tf_op jit(solution)/shard_map/slice | solution.py:53
  2.3 24.7 %copy-start.1 = (f32[4,1,128,2,1,128]{5,4,3,2,1,0:T(1,128)S(1)}, f32[4,1,128,2,1,128]{5,4,3,2,1,0:T(1,128)}, u32[]{:S(2)}) copy-start(f32[4,1,128,2,1,128]{5,4,3,2,1,0:T(1,128)} %param.2) | copy-start | bytes 1572868
  2.4 17.9 %collective-permute-start.2 = (f32[128,264]{0,1:T(8,128)S(1)}, f32[128,264]{0,1:T(8,128)S(1)}, u32[]{:S(2)}, u32[]{:S(2)}) collective-permute-start(f32[128,264]{0,1:T(8,128)S(1)} %pad_maximum_fusion), channel_id=1, source_target_pairs={{0,4},{16,20},{32,36},{48,52},{64,68},{80,84},{96,100},{112,116},{... | collective-permute-start | bytes 405512 | tf_op jit(solution)/shard_map/ppermute | solution.py:36
  11.6 10.1 %collective-permute-start.1 = (f32[128,264]{0,1:T(8,128)S(1)}, f32[128,264]{0,1:T(8,128)S(1)}, u32[]{:S(2)}, u32[]{:S(2)}) collective-permute-start(f32[128,264]{0,1:T(8,128)S(1)} %pad_maximum_fusion), channel_id=1, source_target_pairs={{0,8},{16,24},{32,40},{48,56},{64,72},{80,88},{96,104},{112,120},{... | collective-permute-start | bytes 405512 | tf_op jit(solution)/shard_map/ppermute | solution.py:36
  18.9 4.1 %collective-permute-start = (f32[128,264]{0,1:T(8,128)S(1)}, f32[128,264]{0,1:T(8,128)S(1)}, u32[]{:S(2)}, u32[]{:S(2)}) collective-permute-start(f32[128,264]{0,1:T(8,128)S(1)} %pad_maximum_fusion), channel_id=1, source_target_pairs={{0,12},{16,28},{32,44},{48,60},{64,76},{80,92},{96,108},{112,124},... | collective-permute-start | bytes 405512 | tf_op jit(solution)/shard_map/ppermute | solution.py:36
  23.1 5.3 %collective-permute-start.5 = (f32[128,264]{0,1:T(8,128)S(1)}, f32[128,264]{0,1:T(8,128)S(1)}, u32[]{:S(2)}, u32[]{:S(2)}) collective-permute-start(f32[128,264]{0,1:T(8,128)S(1)} %select_select_fusion.1), channel_id=1, source_target_pairs={{0,1},{4,5},{8,9},{12,13},{16,17},{20,21},{24,25},{28,29},{32,33},... | collective-permute-start | bytes 405512 | tf_op jit(solution)/shard_map/ppermute | solution.py:36
  24.4 6.6 %collective-permute-start.4 = (f32[128,264]{0,1:T(8,128)S(1)}, f32[128,264]{0,1:T(8,128)S(1)}, u32[]{:S(2)}, u32[]{:S(2)}) collective-permute-start(f32[128,264]{0,1:T(8,128)S(1)} %select_select_fusion.1), channel_id=1, source_target_pairs={{0,2},{4,6},{8,10},{12,14},{16,18},{20,22},{24,26},{28,30},{32,34}... | collective-permute-start | bytes 405512 | tf_op jit(solution)/shard_map/ppermute | solution.py:36
  25.7 6.7 %collective-permute-start.3 = (f32[128,264]{0,1:T(8,128)S(1)}, f32[128,264]{0,1:T(8,128)S(1)}, u32[]{:S(2)}, u32[]{:S(2)}) collective-permute-start(f32[128,264]{0,1:T(8,128)S(1)} %select_select_fusion.1), channel_id=1, source_target_pairs={{0,3},{4,7},{8,11},{12,15},{16,19},{20,23},{24,27},{28,31},{32,35}... | collective-permute-start | bytes 405512 | tf_op jit(solution)/shard_map/ppermute | solution.py:36
  27.1 7.4 %collective-permute-start.13 = (f32[512,128]{1,0:T(8,128)S(1)}, f32[512,128]{1,0:T(8,128)S(1)}, u32[]{:S(2)}, u32[]{:S(2)}) collective-permute-start(f32[512,128]{1,0:T(8,128)S(1)} %slice.45), channel_id=1, source_target_pairs={{0,256},{1,257},{2,258},{3,259},{4,260},{5,261},{6,262},{7,263},{8... | collective-permute-start | bytes 786440 | tf_op jit(solution)/shard_map/ppermute | solution.py:15
  32.5 2.8 %collective-permute-start.8 = (f32[128,128]{0,1:T(8,128)S(1)}, f32[128,128]{0,1:T(8,128)S(1)}, u32[]{:S(2)}, u32[]{:S(2)}) collective-permute-start(f32[128,128]{0,1:T(8,128)S(1)} %slice.44), channel_id=1, source_target_pairs={{0,128},{1,129},{2,130},{3,131},{4,132},{5,133},{6,134},{7,135},{8... | collective-permute-start | bytes 196616 | tf_op jit(solution)/shard_map/ppermute | solution.py:36
  33.1 2.1 %collective-permute-start.7 = (f32[128,128]{0,1:T(8,128)S(1)}, f32[128,128]{0,1:T(8,128)S(1)}, u32[]{:S(2)}, u32[]{:S(2)}) collective-permute-start(f32[128,128]{0,1:T(8,128)S(1)} %slice.44), channel_id=1, source_target_pairs={{0,256},{1,257},{2,258},{3,259},{4,260},{5,261},{6,262},{7,263},{8... | collective-permute-start | bytes 196616 | tf_op jit(solution)/shard_map/ppermute | solution.py:36
  33.8 1.4 %collective-permute-start.6 = (f32[128,128]{0,1:T(8,128)S(1)}, f32[128,128]{0,1:T(8,128)S(1)}, u32[]{:S(2)}, u32[]{:S(2)}) collective-permute-start(f32[128,128]{0,1:T(8,128)S(1)} %slice.44), channel_id=1, source_target_pairs={{0,384},{1,385},{2,386},{3,387},{4,388},{5,389},{6,390},{7,391},{8... | collective-permute-start | bytes 196616 | tf_op jit(solution)/shard_map/ppermute | solution.py:36
  34.5 14.1 %collective-permute-start.14 = (f32[512,128]{1,0:T(8,128)S(1)}, f32[512,128]{1,0:T(8,128)S(1)}, u32[]{:S(2)}, u32[]{:S(2)}) collective-permute-start(f32[512,128]{1,0:T(8,128)S(1)} %broadcast_select_fusion.3), channel_id=1, source_target_pairs={{0,128},{256,384},{1,129},{257,385},{2,130},{258,386},{3,131},{259... | collective-permute-start | bytes 786440 | tf_op jit(solution)/shard_map/ppermute | solution.py:15
  35.3 2.7 %collective-permute-start.11 = (f32[128,128]{0,1:T(8,128)S(1)}, f32[128,128]{0,1:T(8,128)S(1)}, u32[]{:S(2)}, u32[]{:S(2)}) collective-permute-start(f32[128,128]{0,1:T(8,128)S(1)} %select_select_fusion.4), channel_id=1, source_target_pairs={{0,32},{128,160},{256,288},{384,416},{1,33},{129,161},{257,289},{3... | collective-permute-start | bytes 196616 | tf_op jit(solution)/shard_map/ppermute | solution.py:36
  35.9 11.4 %collective-permute-start.10 = (f32[128,128]{0,1:T(8,128)S(1)}, f32[128,128]{0,1:T(8,128)S(1)}, u32[]{:S(2)}, u32[]{:S(2)}) collective-permute-start(f32[128,128]{0,1:T(8,128)S(1)} %select_select_fusion.4), channel_id=1, source_target_pairs={{0,64},{128,192},{256,320},{384,448},{1,65},{129,193},{257,321},{3... | collective-permute-start | bytes 196616 | tf_op jit(solution)/shard_map/ppermute | solution.py:36
  37.2 10.1 %collective-permute-start.9 = (f32[128,128]{0,1:T(8,128)S(1)}, f32[128,128]{0,1:T(8,128)S(1)}, u32[]{:S(2)}, u32[]{:S(2)}) collective-permute-start(f32[128,128]{0,1:T(8,128)S(1)} %select_select_fusion.4), channel_id=1, source_target_pairs={{0,96},{128,224},{256,352},{384,480},{1,97},{129,225},{257,353},{3... | collective-permute-start | bytes 196616 | tf_op jit(solution)/shard_map/ppermute | solution.py:36
  47.4 2.7 %collective-permute-start.12 = (f32[128,128]{0,1:T(8,128)S(1)}, f32[128,128]{0,1:T(8,128)S(1)}, u32[]{:S(2)}, u32[]{:S(2)}) collective-permute-start(f32[128,128]{0,1:T(8,128)S(1)} %select_select_fusion.3), channel_id=1, source_target_pairs={{0,16},{32,48},{64,80},{96,112},{128,144},{160,176},{192,208},{224... | collective-permute-start | bytes 196616 | tf_op jit(solution)/shard_map/ppermute | solution.py:36
  48.7 9.8 %collective-permute-start.15 = (f32[512,128]{1,0:T(8,128)S(1)}, f32[512,128]{1,0:T(8,128)S(1)}, u32[]{:S(2)}, u32[]{:S(2)}) collective-permute-start(f32[512,128]{1,0:T(8,128)S(1)} %broadcast_select_fusion.4), channel_id=1, source_target_pairs={{0,64},{128,192},{256,320},{384,448},{1,65},{129,193},{257,321},{3... | collective-permute-start | bytes 786440 | tf_op jit(solution)/shard_map/ppermute | solution.py:15
  58.5 13.1 %collective-permute-start.16 = (f32[512,128]{1,0:T(8,128)S(1)}, f32[512,128]{1,0:T(8,128)S(1)}, u32[]{:S(2)}, u32[]{:S(2)}) collective-permute-start(f32[512,128]{1,0:T(8,128)S(1)} %broadcast_select_fusion.5), channel_id=1, source_target_pairs={{0,32},{64,96},{128,160},{192,224},{256,288},{320,352},{384,416},{... | collective-permute-start | bytes 786440 | tf_op jit(solution)/shard_map/ppermute | solution.py:15
  71.6 12.4 %collective-permute-start.17 = (f32[512,128]{1,0:T(8,128)S(1)}, f32[512,128]{1,0:T(8,128)S(1)}, u32[]{:S(2)}, u32[]{:S(2)}) collective-permute-start(f32[512,128]{1,0:T(8,128)S(1)} %broadcast_select_fusion.6), channel_id=1, source_target_pairs={{0,16},{32,48},{64,80},{96,112},{128,144},{160,176},{192,208},{224... | collective-permute-start | bytes 786440 | tf_op jit(solution)/shard_map/ppermute | solution.py:15
  84.9 0.8 copy-start
  84.9 0.7 copy-start.2
  86.0 0.7 slice-start
  86.0 1.4 %slice-start.1 = ((f32[776,128]{1,0:T(8,128)}), f32[512,128]{1,0:T(8,128)S(1)}, s32[]{:S(2)}) async-start(f32[776,128]{1,0:T(8,128)} %copy-done), calls=%async_computation.1 | async-start | bytes 524288 | tf_op jit(solution)/shard_map/slice | solution.py:60

commit v5 on v4

--- a/solution.py
+++ b/solution.py
@@ -4,27 +4,13 @@
 from jax.sharding import PartitionSpec as P
 
 
-def spread(block, axis):
-    count = lax.axis_size(axis)
-    index = lax.axis_index(axis)
-    step = 1
-    while 2 * step < count:
-        step *= 2
-    while step >= 1:
-        pairs = [(i, i + step) for i in range(0, count, 2 * step) if i + step < count]
-        arrived = lax.ppermute(block, axis, pairs)
-        block = jnp.where(index % (2 * step) == step, arrived, block)
-        step //= 2
-    return block
-
-
-def spread_wide(block, axis):
+def tree(block, axis, wide):
     count = lax.axis_size(axis)
     index = lax.axis_index(axis)
     radices = []
     rest = count
     while rest > 1:
-        radix = 4 if rest % 4 == 0 else rest
+        radix = (4 if rest % 4 == 0 else rest) if wide else 2
         radices.append(radix)
         rest //= radix
     span = count
@@ -32,12 +18,59 @@
         span //= radix
         got = block
         for digit in range(1, radix):
-            pairs = [(i, i + digit * span) for i in range(0, count, span * radix)]
+            pairs = [
+                (i, i + digit * span)
+                for i in range(0, count, span * radix)
+                if i + digit * span < count
+            ]
             arrived = lax.ppermute(block, axis, pairs)
             mine = (index % (span * radix)) == digit * span
             got = jnp.where(mine, arrived, got)
-        block = got
+        block = yield got
     return block
+
+
+def lockstep(*trees):
+    held = [None] * len(trees)
+    results = [None] * len(trees)
+    live = []
+    for k, t in enumerate(trees):
+        try:
+            held[k] = next(t)
+            live.append(k)
+        except StopIteration as stop:
+            results[k] = stop.value
+    while live:
+        tied = lax.optimization_barrier(tuple(held[k] for k in live))
+        still = []
+        for k, value in zip(live, tied):
+            try:
+                held[k] = trees[k].send(value)
+                still.append(k)
+            except StopIteration as stop:
+                results[k] = stop.value
+        live = still
+    return results
+
+
+def pause(gen, rounds):
+    got = next(gen)
+    for step in range(rounds):
+        tied = yield got
+        if step < rounds - 1:
+            got = gen.send(tied)
+    return tied, gen
+
+
+def resume(paused):
+    value, gen = paused
+    try:
+        got = gen.send(value)
+        while True:
+            tied = yield got
+            got = gen.send(tied)
+    except StopIteration as stop:
+        return stop.value
 
 
 def on_device(normal_matrix, right_sides):
@@ -49,10 +82,11 @@
     side_count = right_sides.shape[0]
     local = normal_matrix.reshape(row_blocks * block, col_blocks * block)
 
-    left = spread(local[:, :block], "col")
     top = jnp.concatenate([local[:block], right_sides[:, 0, 0, :].T], axis=1)
-    top = spread_wide(top, "row")
-    corner_raw = spread_wide(top[:, :block], "col")
+    row_tree = tree(top, "row", True)
+    col_tree = tree(local[:, :block], "col", False)
+    top, paused = lockstep(row_tree, pause(col_tree, 2))
+    corner_raw, left = lockstep(tree(top[:, :block], "col", True), resume(paused))
 
     corner = jnp.linalg.cholesky(corner_raw)
     rhs = jnp.concatenate([left.T, top], axis=1)

time: 89.5 us -> 98.6 us (1.10)
  the two profiles are of different devices: /device:TPU:28 before, /device:TPU:1 now
where the time goes in v5:
time: 98.6 us; the launch traced here: 97.8 us
  waiting for transfers between devices  35.4 us (36%)
  starting transfers between devices  31.4 us (32%)
  other arithmetic  25.6 us (26%)
  local copies, waits for them, and re-layouts  2.69 us (3%)
  matrix products  1.66 us (2%)
  between operations  1.13 us (1%)
    ppermute x18, waiting for transfers between devices, tree(): arrived = lax.ppermute(block, axis, pairs)  35.4 us
    ppermute x18, starting transfers between devices, tree(): arrived = lax.ppermute(block, axis, pairs)  31.4 us
    another operation x3, other arithmetic, on_device(): corner = jnp.linalg.cholesky(corner_raw)  12.4 us
    another operation x2, other arithmetic, on_device(): solved = jax.scipy.linalg.solve_triangular(corner, rhs, lower=True).T  10.5 us
  transfers between devices with their start and end apart: 18, of which 5 were waited for; matrix products, arithmetic and copies ran while one was open for 0% of the time, Pallas kernels for 0%

profile of v5, /device:TPU:1, one launch (start us, length us, event | category | flops | bytes accessed | tf_op | source)
XLA Modules:
  0.0 97.8 jit_solution(15865897818798810407)
XLA Ops:
  0.6 0.7 slice.38
  1.3 0.9 slice-done.2
  2.3 9.7 %collective-permute-start.2 = (f32[128,264]{0,1:T(8,128)S(1)}, f32[128,264]{0,1:T(8,128)S(1)}, u32[]{:S(2)}, u32[]{:S(2)}) collective-permute-start(f32[128,264]{0,1:T(8,128)S(1)} %pad_maximum_fusion), channel_id=1, source_target_pairs={{0,4},{16,20},{32,36},{48,52},{64,68},{80,84},{96,100},{112,116},{... | collective-permute-start | bytes 405512 | tf_op jit(solution)/shard_map/ppermute | solution.py:26
  12.0 7.3 %collective-permute-start.1 = (f32[128,264]{0,1:T(8,128)S(1)}, f32[128,264]{0,1:T(8,128)S(1)}, u32[]{:S(2)}, u32[]{:S(2)}) collective-permute-start(f32[128,264]{0,1:T(8,128)S(1)} %pad_maximum_fusion), channel_id=1, source_target_pairs={{0,8},{16,24},{32,40},{48,56},{64,72},{80,88},{96,104},{112,120},{... | collective-permute-start | bytes 405512 | tf_op jit(solution)/shard_map/ppermute | solution.py:26
  19.3 1.3 %collective-permute-start = (f32[128,264]{0,1:T(8,128)S(1)}, f32[128,264]{0,1:T(8,128)S(1)}, u32[]{:S(2)}, u32[]{:S(2)}) collective-permute-start(f32[128,264]{0,1:T(8,128)S(1)} %pad_maximum_fusion), channel_id=1, source_target_pairs={{0,12},{16,28},{32,44},{48,60},{64,76},{80,92},{96,108},{112,124},... | collective-permute-start | bytes 405512 | tf_op jit(solution)/shard_map/ppermute | solution.py:26
  20.7 0.7 collective-permute-start.3
  21.5 1.3 %collective-permute-done = f32[128,264]{0,1:T(8,128)S(1)} collective-permute-done((f32[128,264]{0,1:T(8,128)S(1)}, f32[128,264]{0,1:T(8,128)S(1)}, u32[]{:S(2)}, u32[]{:S(2)}) %collective-permute-start) | collective-permute-done | bytes 135200 | tf_op jit(solution)/shard_map/ppermute | solution.py:26
  22.9 1.3 %collective-permute-start.6 = (f32[128,264]{0,1:T(8,128)S(1)}, f32[128,264]{0,1:T(8,128)S(1)}, u32[]{:S(2)}, u32[]{:S(2)}) collective-permute-start(f32[128,264]{0,1:T(8,128)S(1)} %select_select_fusion.1), channel_id=1, source_target_pairs={{0,1},{4,5},{8,9},{12,13},{16,17},{20,21},{24,25},{28,29},{32,33},... | collective-permute-start | bytes 405512 | tf_op jit(solution)/shard_map/ppermute | solution.py:26
  24.2 1.3 %collective-permute-start.5 = (f32[128,264]{0,1:T(8,128)S(1)}, f32[128,264]{0,1:T(8,128)S(1)}, u32[]{:S(2)}, u32[]{:S(2)}) collective-permute-start(f32[128,264]{0,1:T(8,128)S(1)} %select_select_fusion.1), channel_id=1, source_target_pairs={{0,2},{4,6},{8,10},{12,14},{16,18},{20,22},{24,26},{28,30},{32,34}... | collective-permute-start | bytes 405512 | tf_op jit(solution)/shard_map/ppermute | solution.py:26
  25.5 1.3 %collective-permute-start.4 = (f32[128,264]{0,1:T(8,128)S(1)}, f32[128,264]{0,1:T(8,128)S(1)}, u32[]{:S(2)}, u32[]{:S(2)}) collective-permute-start(f32[128,264]{0,1:T(8,128)S(1)} %select_select_fusion.1), channel_id=1, source_target_pairs={{0,3},{4,7},{8,11},{12,15},{16,19},{20,23},{24,27},{28,31},{32,35}... | collective-permute-start | bytes 405512 | tf_op jit(solution)/shard_map/ppermute | solution.py:26
  26.8 0.7 collective-permute-start.7
  27.6 1.4 %collective-permute-done.4 = f32[128,264]{0,1:T(8,128)S(1)} collective-permute-done((f32[128,264]{0,1:T(8,128)S(1)}, f32[128,264]{0,1:T(8,128)S(1)}, u32[]{:S(2)}, u32[]{:S(2)}) %collective-permute-start.4) | collective-permute-done | bytes 135200 | tf_op jit(solution)/shard_map/ppermute | solution.py:26
  29.8 0.7 collective-permute-start.9
  31.2 0.7 collective-permute-start.11
  34.0 0.7 collective-permute-start.15
  34.9 1.3 %collective-permute-start.16 = (f32[128,128]{0,1:T(8,128)S(1)}, f32[128,128]{0,1:T(8,128)S(1)}, u32[]{:S(2)}, u32[]{:S(2)}) collective-permute-start(f32[128,128]{0,1:T(8,128)S(1)} %select_select_fusion.3), channel_id=1, source_target_pairs={{0,16},{32,48},{64,80},{96,112},{128,144},{160,176},{192,208},{224... | collective-permute-start | bytes 196616 | tf_op jit(solution)/shard_map/ppermute | solution.py:26
  36.2 1.3 %collective-permute-start.17 = (f32[512,128]{1,0:T(8,128)S(1)}, f32[512,128]{1,0:T(8,128)S(1)}, u32[]{:S(2)}, u32[]{:S(2)}) collective-permute-start(f32[512,128]{1,0:T(8,128)S(1)} %broadcast_select_fusion.4), channel_id=1, source_target_pairs={{0,16},{32,48},{64,80},{96,112},{128,144},{160,176},{192,208},{224... | collective-permute-start | bytes 786440 | tf_op jit(solution)/shard_map/ppermute | solution.py:26
  37.5 30.8 %collective-permute-done.16 = f32[128,128]{0,1:T(8,128)S(1)} collective-permute-done((f32[128,128]{0,1:T(8,128)S(1)}, f32[128,128]{0,1:T(8,128)S(1)}, u32[]{:S(2)}, u32[]{:S(2)}) %collective-permute-start.16) | collective-permute-done | bytes 65568 | tf_op jit(solution)/shard_map/ppermute | solution.py:26
  68.4 1.6 %collective-permute-done.17 = f32[512,128]{1,0:T(8,128)S(1)} collective-permute-done((f32[512,128]{1,0:T(8,128)S(1)}, f32[512,128]{1,0:T(8,128)S(1)}, u32[]{:S(2)}, u32[]{:S(2)}) %collective-permute-start.17) | collective-permute-done | bytes 262176 | tf_op jit(solution)/shard_map/ppermute | solution.py:26
  70.1 11.7 %cholesky.18 = f32[128,128]{1,0:T(8,128)S(1)} custom-call(f32[128,128]{1,0:T(8,128)S(1)} %fusion.7), custom_call_target="Cholesky" | custom-call | tf_op jit(solution)/shard_map/jit(cholesky)/cholesky | solution.py:91
  83.2 9.8 %custom-call.7 = f32[1,128,128]{1,2,0:T(8,128)S(1)} custom-call(f32[1,128,128]{2,1,0:T(8,128)S(1)} %get-tuple-element.22), custom_call_target="InvertDiagBlocksLowerTriangular" | custom-call | tf_op jit(solution)/shard_map/jit(_solve_triangular)/triangular_solve | solution.py:93
  93.0 0.8 fusion.1
  95.5 0.7 broadcast_select_fusion.8
  96.3 1.5 %broadcast_select_fusion = f32[4,1,128,2,1,128]{5,4,3,2,1,0:T(1,128)} fusion(pred[2]{0:T(512)(128)(4,1)S(1)} %get-tuple-element.25, f32[4,1,128,2,1,128]{5,4,3,2,1,0:T(1,128)S(1)} %bitcast.38, pred[4,2]{1,0:T(4,128)(4,1)S(1)} %broadcast_and_fusion, f32[4,128,128]{2,1,0:T(8,128)S(1)} %broadcast_select_fusion.2), kind=kLoop, calls=%fused_computation.3 | loop fusion | flops 262144 | bytes 1310730 | tf_op jit(solution)/shard_map/jit(_where)/select_n | solution.py:112
  (57 shorter events, 7.4 us)
Async XLA Ops:
  1.3 0.9 slice-start.2
  1.3 19.3 %copy-start.1 = (f32[4,1,128,2,1,128]{5,4,3,2,1,0:T(1,128)S(1)}, f32[4,1,128,2,1,128]{5,4,3,2,1,0:T(1,128)}, u32[]{:S(2)}) copy-start(f32[4,1,128,2,1,128]{5,4,3,2,1,0:T(1,128)} %param.2) | copy-start | bytes 1572868
  2.3 19.1 %collective-permute-start.2 = (f32[128,264]{0,1:T(8,128)S(1)}, f32[128,264]{0,1:T(8,128)S(1)}, u32[]{:S(2)}, u32[]{:S(2)}) collective-permute-start(f32[128,264]{0,1:T(8,128)S(1)} %pad_maximum_fusion), channel_id=1, source_target_pairs={{0,4},{16,20},{32,36},{48,52},{64,68},{80,84},{96,100},{112,116},{... | collective-permute-start | bytes 405512 | tf_op jit(solution)/shard_map/ppermute | solution.py:26
  12.0 9.5 %collective-permute-start.1 = (f32[128,264]{0,1:T(8,128)S(1)}, f32[128,264]{0,1:T(8,128)S(1)}, u32[]{:S(2)}, u32[]{:S(2)}) collective-permute-start(f32[128,264]{0,1:T(8,128)S(1)} %pad_maximum_fusion), channel_id=1, source_target_pairs={{0,8},{16,24},{32,40},{48,56},{64,72},{80,88},{96,104},{112,120},{... | collective-permute-start | bytes 405512 | tf_op jit(solution)/shard_map/ppermute | solution.py:26
  19.3 3.5 %collective-permute-start = (f32[128,264]{0,1:T(8,128)S(1)}, f32[128,264]{0,1:T(8,128)S(1)}, u32[]{:S(2)}, u32[]{:S(2)}) collective-permute-start(f32[128,264]{0,1:T(8,128)S(1)} %pad_maximum_fusion), channel_id=1, source_target_pairs={{0,12},{16,28},{32,44},{48,60},{64,76},{80,92},{96,108},{112,124},... | collective-permute-start | bytes 405512 | tf_op jit(solution)/shard_map/ppermute | solution.py:26
  20.7 2.2 %collective-permute-start.3 = (f32[512,128]{1,0:T(8,128)S(1)}, f32[512,128]{1,0:T(8,128)S(1)}, u32[]{:S(2)}, u32[]{:S(2)}) collective-permute-start(f32[512,128]{1,0:T(8,128)S(1)} %slice.44), channel_id=1, source_target_pairs={{0,256},{1,257},{2,258},{3,259},{4,260},{5,261},{6,262},{7,263},{8... | collective-permute-start | bytes 786440 | tf_op jit(solution)/shard_map/ppermute | solution.py:26
  22.9 4.6 %collective-permute-start.6 = (f32[128,264]{0,1:T(8,128)S(1)}, f32[128,264]{0,1:T(8,128)S(1)}, u32[]{:S(2)}, u32[]{:S(2)}) collective-permute-start(f32[128,264]{0,1:T(8,128)S(1)} %select_select_fusion.1), channel_id=1, source_target_pairs={{0,1},{4,5},{8,9},{12,13},{16,17},{20,21},{24,25},{28,29},{32,33},... | collective-permute-start | bytes 405512 | tf_op jit(solution)/shard_map/ppermute | solution.py:26
  24.2 3.4 %collective-permute-start.5 = (f32[128,264]{0,1:T(8,128)S(1)}, f32[128,264]{0,1:T(8,128)S(1)}, u32[]{:S(2)}, u32[]{:S(2)}) collective-permute-start(f32[128,264]{0,1:T(8,128)S(1)} %select_select_fusion.1), channel_id=1, source_target_pairs={{0,2},{4,6},{8,10},{12,14},{16,18},{20,22},{24,26},{28,30},{32,34}... | collective-permute-start | bytes 405512 | tf_op jit(solution)/shard_map/ppermute | solution.py:26
  25.5 3.5 %collective-permute-start.4 = (f32[128,264]{0,1:T(8,128)S(1)}, f32[128,264]{0,1:T(8,128)S(1)}, u32[]{:S(2)}, u32[]{:S(2)}) collective-permute-start(f32[128,264]{0,1:T(8,128)S(1)} %select_select_fusion.1), channel_id=1, source_target_pairs={{0,3},{4,7},{8,11},{12,15},{16,19},{20,23},{24,27},{28,31},{32,35}... | collective-permute-start | bytes 405512 | tf_op jit(solution)/shard_map/ppermute | solution.py:26
  26.8 2.3 %collective-permute-start.7 = (f32[512,128]{1,0:T(8,128)S(1)}, f32[512,128]{1,0:T(8,128)S(1)}, u32[]{:S(2)}, u32[]{:S(2)}) collective-permute-start(f32[512,128]{1,0:T(8,128)S(1)} %broadcast_select_fusion.7), channel_id=1, source_target_pairs={{0,128},{256,384},{1,129},{257,385},{2,130},{258,386},{3,131},{259... | collective-permute-start | bytes 786440 | tf_op jit(solution)/shard_map/ppermute | solution.py:26
  29.2 2.7 %collective-permute-start.10 = (f32[128,128]{0,1:T(8,128)S(1)}, f32[128,128]{0,1:T(8,128)S(1)}, u32[]{:S(2)}, u32[]{:S(2)}) collective-permute-start(f32[128,128]{0,1:T(8,128)S(1)} %slice.40), channel_id=1, source_target_pairs={{0,128},{1,129},{2,130},{3,131},{4,132},{5,133},{6,134},{7,135},{8... | collective-permute-start | bytes 196616 | tf_op jit(solution)/shard_map/ppermute | solution.py:26
  29.8 2.1 %collective-permute-start.9 = (f32[128,128]{0,1:T(8,128)S(1)}, f32[128,128]{0,1:T(8,128)S(1)}, u32[]{:S(2)}, u32[]{:S(2)}) collective-permute-start(f32[128,128]{0,1:T(8,128)S(1)} %slice.40), channel_id=1, source_target_pairs={{0,256},{1,257},{2,258},{3,259},{4,260},{5,261},{6,262},{7,263},{8... | collective-permute-start | bytes 196616 | tf_op jit(solution)/shard_map/ppermute | solution.py:26
  30.5 1.4 %collective-permute-start.8 = (f32[128,128]{0,1:T(8,128)S(1)}, f32[128,128]{0,1:T(8,128)S(1)}, u32[]{:S(2)}, u32[]{:S(2)}) collective-permute-start(f32[128,128]{0,1:T(8,128)S(1)} %slice.40), channel_id=1, source_target_pairs={{0,384},{1,385},{2,386},{3,387},{4,388},{5,389},{6,390},{7,391},{8... | collective-permute-start | bytes 196616 | tf_op jit(solution)/shard_map/ppermute | solution.py:26
  31.2 0.8 collective-permute-start.11
  32.0 2.7 %collective-permute-start.14 = (f32[128,128]{0,1:T(8,128)S(1)}, f32[128,128]{0,1:T(8,128)S(1)}, u32[]{:S(2)}, u32[]{:S(2)}) collective-permute-start(f32[128,128]{0,1:T(8,128)S(1)} %select_select_fusion.4), channel_id=1, source_target_pairs={{0,32},{128,160},{256,288},{384,416},{1,33},{129,161},{257,289},{3... | collective-permute-start | bytes 196616 | tf_op jit(solution)/shard_map/ppermute | solution.py:26
  32.7 2.1 %collective-permute-start.13 = (f32[128,128]{0,1:T(8,128)S(1)}, f32[128,128]{0,1:T(8,128)S(1)}, u32[]{:S(2)}, u32[]{:S(2)}) collective-permute-start(f32[128,128]{0,1:T(8,128)S(1)} %select_select_fusion.4), channel_id=1, source_target_pairs={{0,64},{128,192},{256,320},{384,448},{1,65},{129,193},{257,321},{3... | collective-permute-start | bytes 196616 | tf_op jit(solution)/shard_map/ppermute | solution.py:26
  33.4 1.4 %collective-permute-start.12 = (f32[128,128]{0,1:T(8,128)S(1)}, f32[128,128]{0,1:T(8,128)S(1)}, u32[]{:S(2)}, u32[]{:S(2)}) collective-permute-start(f32[128,128]{0,1:T(8,128)S(1)} %select_select_fusion.4), channel_id=1, source_target_pairs={{0,96},{128,224},{256,352},{384,480},{1,97},{129,225},{257,353},{3... | collective-permute-start | bytes 196616 | tf_op jit(solution)/shard_map/ppermute | solution.py:26
  34.0 0.8 collective-permute-start.15
  34.9 33.5 %collective-permute-start.16 = (f32[128,128]{0,1:T(8,128)S(1)}, f32[128,128]{0,1:T(8,128)S(1)}, u32[]{:S(2)}, u32[]{:S(2)}) collective-permute-start(f32[128,128]{0,1:T(8,128)S(1)} %select_select_fusion.3), channel_id=1, source_target_pairs={{0,16},{32,48},{64,80},{96,112},{128,144},{160,176},{192,208},{224... | collective-permute-start | bytes 196616 | tf_op jit(solution)/shard_map/ppermute | solution.py:26
  36.2 33.8 %collective-permute-start.17 = (f32[512,128]{1,0:T(8,128)S(1)}, f32[512,128]{1,0:T(8,128)S(1)}, u32[]{:S(2)}, u32[]{:S(2)}) collective-permute-start(f32[512,128]{1,0:T(8,128)S(1)} %broadcast_select_fusion.4), channel_id=1, source_target_pairs={{0,16},{32,48},{64,80},{96,112},{128,144},{160,176},{192,208},{224... | collective-permute-start | bytes 786440 | tf_op jit(solution)/shard_map/ppermute | solution.py:26
  93.8 0.8 copy-start
  93.8 0.7 copy-start.2
  94.8 0.7 slice-start
  94.8 1.4 %slice-start.1 = ((f32[776,128]{1,0:T(8,128)}), f32[512,128]{1,0:T(8,128)S(1)}, s32[]{:S(2)}) async-start(f32[776,128]{1,0:T(8,128)} %copy-done), calls=%async_computation.1 | async-start | bytes 524288 | tf_op jit(solution)/shard_map/slice | solution.py:94

commit v6 on v4

--- a/solution.py
+++ b/solution.py
@@ -48,18 +48,31 @@
     row_count = lax.axis_size("row")
     side_count = right_sides.shape[0]
     local = normal_matrix.reshape(row_blocks * block, col_blocks * block)
+    identity = jnp.eye(block, dtype=jnp.float32)
 
+    def factor(corner_raw):
+        corner = jnp.linalg.cholesky(corner_raw)
+        inverse = jax.scipy.linalg.solve_triangular(corner, identity, lower=True)
+        return corner, inverse
+
+    def skip(corner_raw):
+        return jnp.zeros_like(corner_raw), jnp.zeros_like(corner_raw)
+
+    holder = (row_id == 0) & (col_id == 0)
+    corner, inverse = lax.cond(holder, factor, skip, local[:block, :block])
+    inverse = spread_wide(spread_wide(inverse, "row"), "col")
     left = spread(local[:, :block], "col")
     top = jnp.concatenate([local[:block], right_sides[:, 0, 0, :].T], axis=1)
     top = spread_wide(top, "row")
-    corner_raw = spread_wide(top[:, :block], "col")
 
-    corner = jnp.linalg.cholesky(corner_raw)
-    rhs = jnp.concatenate([left.T, top], axis=1)
-    solved = jax.scipy.linalg.solve_triangular(corner, rhs, lower=True).T
-    rows_factor = solved[: row_blocks * block]
-    cols_factor = solved[row_blocks * block: (row_blocks + col_blocks) * block]
-    lead = solved[(row_blocks + col_blocks) * block:]
+    rows_factor = jnp.dot(
+        left, inverse.T, precision=lax.Precision.HIGHEST, preferred_element_type=jnp.float32
+    )
+    solved = jnp.dot(
+        inverse, top, precision=lax.Precision.HIGHEST, preferred_element_type=jnp.float32
+    ).T
+    cols_factor = solved[: col_blocks * block]
+    lead = solved[col_blocks * block:]
 
     change = jnp.dot(
         rows_factor,

time: 89.5 us -> 81.2 us (0.907)
  the two profiles are of different devices: /device:TPU:28 before, /device:TPU:1 now
where the time goes in v6:
time: 81.2 us; the launch traced here: 79.9 us
  starting transfers between devices  47.3 us (58%)
  waiting for transfers between devices  23.8 us (29%)
  local copies, waits for them, and re-layouts  3.11 us (4%)
  other arithmetic  2.65 us (3%)
  matrix products  1.74 us (2%)
  between operations  1.24 us (2%)
    ppermute x19, starting transfers between devices, spread_wide(): arrived = lax.ppermute(block, axis, pairs)  43.1 us
    ppermute x19, waiting for transfers between devices, spread_wide(): arrived = lax.ppermute(block, axis, pairs)  22.7 us
    ppermute x5, starting transfers between devices, spread(): arrived = lax.ppermute(block, axis, pairs)  4.17 us
  transfers between devices with their start and end apart: 24, of which 6 were waited for; matrix products, arithmetic and copies ran while one was open for 2% of the time, Pallas kernels for 0%

profile of v6, /device:TPU:1, one launch (start us, length us, event | category | flops | bytes accessed | tf_op | source)
XLA Modules:
  0.0 79.9 jit_solution(15428561797785449769)
XLA Ops:
  0.7 1.1 %copy.18 = f32[64,8,2,128]{3,1,2,0:T(8,128)S(1)} copy(f32[64,8,2,128]{3,2,1,0:T(2,128)} %bitcast.40) | data formatting | bytes 1048576
  1.8 13.4 %collective-permute-start.5 = (f32[128,128]{1,0:T(8,128)S(1)}, f32[128,128]{1,0:T(8,128)S(1)}, u32[]{:S(2)}, u32[]{:S(2)}) collective-permute-start(f32[128,128]{1,0:T(8,128)S(1)} %get-tuple-element.12), channel_id=1, source_target_pairs={{0,12},{16,28},{32,44},{48,60},{64,76},{80,92},{96,108},{112,124},... | collective-permute-start | bytes 196616 | tf_op jit(solution)/shard_map/ppermute | solution.py:36
  15.2 3.7 %collective-permute-start.6 = (f32[128,128]{1,0:T(8,128)S(1)}, f32[128,128]{1,0:T(8,128)S(1)}, u32[]{:S(2)}, u32[]{:S(2)}) collective-permute-start(f32[128,128]{1,0:T(8,128)S(1)} %get-tuple-element.12), channel_id=1, source_target_pairs={{0,8},{16,24},{32,40},{48,56},{64,72},{80,88},{96,104},{112,120},{... | collective-permute-start | bytes 196616 | tf_op jit(solution)/shard_map/ppermute | solution.py:36
  18.9 1.3 %collective-permute-start.7 = (f32[128,128]{1,0:T(8,128)S(1)}, f32[128,128]{1,0:T(8,128)S(1)}, u32[]{:S(2)}, u32[]{:S(2)}) collective-permute-start(f32[128,128]{1,0:T(8,128)S(1)} %get-tuple-element.12), channel_id=1, source_target_pairs={{0,4},{16,20},{32,36},{48,52},{64,68},{80,84},{96,100},{112,116},{... | collective-permute-start | bytes 196616 | tf_op jit(solution)/shard_map/ppermute | solution.py:36
  20.6 0.7 slice-done.1
  21.4 1.3 %collective-permute-start.18 = (f32[128,264]{1,0:T(8,128)S(1)}, f32[128,264]{1,0:T(8,128)S(1)}, u32[]{:S(2)}, u32[]{:S(2)}) collective-permute-start(f32[128,264]{1,0:T(8,128)S(1)} %pad_maximum_fusion), channel_id=1, source_target_pairs={{0,12},{16,28},{32,44},{48,60},{64,76},{80,92},{96,108},{112,124},... | collective-permute-start | bytes 405512 | tf_op jit(solution)/shard_map/ppermute | solution.py:36
  23.5 1.3 %collective-permute-start.10 = (f32[128,128]{1,0:T(8,128)S(1)}, f32[128,128]{1,0:T(8,128)S(1)}, u32[]{:S(2)}, u32[]{:S(2)}) collective-permute-start(f32[128,128]{1,0:T(8,128)S(1)} %select_select_fusion.5), channel_id=1, source_target_pairs={{0,1},{4,5},{8,9},{12,13},{16,17},{20,21},{24,25},{28,29},{32,33},... | collective-permute-start | bytes 196616 | tf_op jit(solution)/shard_map/ppermute | solution.py:36
  24.8 1.3 %collective-permute-start.8 = (f32[128,128]{1,0:T(8,128)S(1)}, f32[128,128]{1,0:T(8,128)S(1)}, u32[]{:S(2)}, u32[]{:S(2)}) collective-permute-start(f32[128,128]{1,0:T(8,128)S(1)} %select_select_fusion.5), channel_id=1, source_target_pairs={{0,3},{4,7},{8,11},{12,15},{16,19},{20,23},{24,27},{28,31},{32,35}... | collective-permute-start | bytes 196616 | tf_op jit(solution)/shard_map/ppermute | solution.py:36
  26.1 1.3 %collective-permute-start.9 = (f32[128,128]{1,0:T(8,128)S(1)}, f32[128,128]{1,0:T(8,128)S(1)}, u32[]{:S(2)}, u32[]{:S(2)}) collective-permute-start(f32[128,128]{1,0:T(8,128)S(1)} %select_select_fusion.5), channel_id=1, source_target_pairs={{0,2},{4,6},{8,10},{12,14},{16,18},{20,22},{24,26},{28,30},{32,34}... | collective-permute-start | bytes 196616 | tf_op jit(solution)/shard_map/ppermute | solution.py:36
  27.5 0.7 collective-permute-start.1
  30.8 0.7 collective-permute-start.2
  31.6 9.1 %collective-permute-start.19 = (f32[128,264]{1,0:T(8,128)S(1)}, f32[128,264]{1,0:T(8,128)S(1)}, u32[]{:S(2)}, u32[]{:S(2)}) collective-permute-start(f32[128,264]{1,0:T(8,128)S(1)} %pad_maximum_fusion), channel_id=1, source_target_pairs={{0,8},{16,24},{32,40},{48,56},{64,72},{80,88},{96,104},{112,120},{... | collective-permute-start | bytes 405512 | tf_op jit(solution)/shard_map/ppermute | solution.py:36
  40.7 1.3 %collective-permute-start.20 = (f32[128,264]{1,0:T(8,128)S(1)}, f32[128,264]{1,0:T(8,128)S(1)}, u32[]{:S(2)}, u32[]{:S(2)}) collective-permute-start(f32[128,264]{1,0:T(8,128)S(1)} %pad_maximum_fusion), channel_id=1, source_target_pairs={{0,4},{16,20},{32,36},{48,52},{64,68},{80,84},{96,100},{112,116},{... | collective-permute-start | bytes 405512 | tf_op jit(solution)/shard_map/ppermute | solution.py:36
  45.3 2.2 %collective-permute-done.20 = f32[128,264]{1,0:T(8,128)S(1)} collective-permute-done((f32[128,264]{1,0:T(8,128)S(1)}, f32[128,264]{1,0:T(8,128)S(1)}, u32[]{:S(2)}, u32[]{:S(2)}) %collective-permute-start.20) | collective-permute-done | bytes 135200 | tf_op jit(solution)/shard_map/ppermute | solution.py:36
  47.5 1.3 %collective-permute-start.21 = (f32[128,264]{1,0:T(8,128)S(1)}, f32[128,264]{1,0:T(8,128)S(1)}, u32[]{:S(2)}, u32[]{:S(2)}) collective-permute-start(f32[128,264]{1,0:T(8,128)S(1)} %select_select_fusion.1), channel_id=1, source_target_pairs={{0,3},{4,7},{8,11},{12,15},{16,19},{20,23},{24,27},{28,31},{32,35}... | collective-permute-start | bytes 405512 | tf_op jit(solution)/shard_map/ppermute | solution.py:36
  48.9 1.3 %collective-permute-start.22 = (f32[128,264]{1,0:T(8,128)S(1)}, f32[128,264]{1,0:T(8,128)S(1)}, u32[]{:S(2)}, u32[]{:S(2)}) collective-permute-start(f32[128,264]{1,0:T(8,128)S(1)} %select_select_fusion.1), channel_id=1, source_target_pairs={{0,2},{4,6},{8,10},{12,14},{16,18},{20,22},{24,26},{28,30},{32,34}... | collective-permute-start | bytes 405512 | tf_op jit(solution)/shard_map/ppermute | solution.py:36
  50.2 1.3 %collective-permute-start.23 = (f32[128,264]{1,0:T(8,128)S(1)}, f32[128,264]{1,0:T(8,128)S(1)}, u32[]{:S(2)}, u32[]{:S(2)}) collective-permute-start(f32[128,264]{1,0:T(8,128)S(1)} %select_select_fusion.1), channel_id=1, source_target_pairs={{0,1},{4,5},{8,9},{12,13},{16,17},{20,21},{24,25},{28,29},{32,33},... | collective-permute-start | bytes 405512 | tf_op jit(solution)/shard_map/ppermute | solution.py:36
  51.5 1.3 %collective-permute-start.17 = (f32[128,128]{1,0:T(8,128)S(1)}, f32[128,128]{1,0:T(8,128)S(1)}, u32[]{:S(2)}, u32[]{:S(2)}) collective-permute-start(f32[128,128]{1,0:T(8,128)S(1)} %select_select_fusion.2), channel_id=1, source_target_pairs={{0,16},{32,48},{64,80},{96,112},{128,144},{160,176},{192,208},{224... | collective-permute-start | bytes 196616 | tf_op jit(solution)/shard_map/ppermute | solution.py:36
  52.9 1.5 %collective-permute-start.4 = (f32[512,128]{1,0:T(8,128)S(1)}, f32[512,128]{1,0:T(8,128)S(1)}, u32[]{:S(2)}, u32[]{:S(2)}) collective-permute-start(f32[512,128]{1,0:T(8,128)S(1)} %broadcast_select_fusion.6), channel_id=1, source_target_pairs={{0,16},{32,48},{64,80},{96,112},{128,144},{160,176},{192,208},{224... | collective-permute-start | bytes 786440 | tf_op jit(solution)/shard_map/ppermute | solution.py:15
  54.4 1.2 %collective-permute-done.23 = f32[128,264]{1,0:T(8,128)S(1)} collective-permute-done((f32[128,264]{1,0:T(8,128)S(1)}, f32[128,264]{1,0:T(8,128)S(1)}, u32[]{:S(2)}, u32[]{:S(2)}) %collective-permute-start.23) | collective-permute-done | bytes 135200 | tf_op jit(solution)/shard_map/ppermute | solution.py:36
  55.6 18.2 %collective-permute-done.17 = f32[128,128]{1,0:T(8,128)S(1)} collective-permute-done((f32[128,128]{1,0:T(8,128)S(1)}, f32[128,128]{1,0:T(8,128)S(1)}, u32[]{:S(2)}, u32[]{:S(2)}) %collective-permute-start.17) | collective-permute-done | bytes 65568 | tf_op jit(solution)/shard_map/ppermute | solution.py:36
  74.4 1.1 %collective-permute-done.4 = f32[512,128]{1,0:T(8,128)S(1)} collective-permute-done((f32[512,128]{1,0:T(8,128)S(1)}, f32[512,128]{1,0:T(8,128)S(1)}, u32[]{:S(2)}, u32[]{:S(2)}) %collective-permute-start.4) | collective-permute-done | bytes 262176 | tf_op jit(solution)/shard_map/ppermute | solution.py:15
  77.6 0.7 broadcast_select_fusion.7
  78.4 1.5 %broadcast_select_fusion = f32[4,1,128,2,1,128]{5,4,3,2,1,0:T(1,128)} fusion(pred[2]{0:T(512)(128)(4,1)S(1)} %fusion.17, f32[4,1,128,2,1,128]{5,4,3,2,1,0:T(1,128)S(1)} %bitcast.42, pred[4,2]{1,0:T(4,128)(4,1)S(1)} %broadcast_and_fusion, f32[4,128,128]{2,1,0:T(8,128)S(1)} %broadcast_select_fusion.2), kind=kLoop, calls=%fused_computation.13 | loop fusion | flops 262144 | bytes 1310730 | tf_op jit(solution)/shard_map/jit(_where)/select_n | solution.py:91
  (65 shorter events, 9.9 us)
Async XLA Ops:
  1.8 21.7 %collective-permute-start.5 = (f32[128,128]{1,0:T(8,128)S(1)}, f32[128,128]{1,0:T(8,128)S(1)}, u32[]{:S(2)}, u32[]{:S(2)}) collective-permute-start(f32[128,128]{1,0:T(8,128)S(1)} %get-tuple-element.12), channel_id=1, source_target_pairs={{0,12},{16,28},{32,44},{48,60},{64,76},{80,92},{96,108},{112,124},... | collective-permute-start | bytes 196616 | tf_op jit(solution)/shard_map/ppermute | solution.py:36
  15.2 8.3 %collective-permute-start.6 = (f32[128,128]{1,0:T(8,128)S(1)}, f32[128,128]{1,0:T(8,128)S(1)}, u32[]{:S(2)}, u32[]{:S(2)}) collective-permute-start(f32[128,128]{1,0:T(8,128)S(1)} %get-tuple-element.12), channel_id=1, source_target_pairs={{0,8},{16,24},{32,40},{48,56},{64,72},{80,88},{96,104},{112,120},{... | collective-permute-start | bytes 196616 | tf_op jit(solution)/shard_map/ppermute | solution.py:36
  18.9 4.6 %collective-permute-start.7 = (f32[128,128]{1,0:T(8,128)S(1)}, f32[128,128]{1,0:T(8,128)S(1)}, u32[]{:S(2)}, u32[]{:S(2)}) collective-permute-start(f32[128,128]{1,0:T(8,128)S(1)} %get-tuple-element.12), channel_id=1, source_target_pairs={{0,4},{16,20},{32,36},{48,52},{64,68},{80,84},{96,100},{112,116},{... | collective-permute-start | bytes 196616 | tf_op jit(solution)/shard_map/ppermute | solution.py:36
  21.4 22.0 %collective-permute-start.18 = (f32[128,264]{1,0:T(8,128)S(1)}, f32[128,264]{1,0:T(8,128)S(1)}, u32[]{:S(2)}, u32[]{:S(2)}) collective-permute-start(f32[128,264]{1,0:T(8,128)S(1)} %pad_maximum_fusion), channel_id=1, source_target_pairs={{0,12},{16,28},{32,44},{48,60},{64,76},{80,92},{96,108},{112,124},... | collective-permute-start | bytes 405512 | tf_op jit(solution)/shard_map/ppermute | solution.py:36
  22.8 4.7 %collective-permute-start = (f32[512,128]{1,0:T(8,128)S(1)}, f32[512,128]{1,0:T(8,128)S(1)}, u32[]{:S(2)}, u32[]{:S(2)}) collective-permute-start(f32[512,128]{1,0:T(8,128)S(1)} %slice.41), channel_id=1, source_target_pairs={{0,256},{1,257},{2,258},{3,259},{4,260},{5,261},{6,262},{7,263},{8... | collective-permute-start | bytes 786440 | tf_op jit(solution)/shard_map/ppermute | solution.py:15
  23.5 4.7 %collective-permute-start.10 = (f32[128,128]{1,0:T(8,128)S(1)}, f32[128,128]{1,0:T(8,128)S(1)}, u32[]{:S(2)}, u32[]{:S(2)}) collective-permute-start(f32[128,128]{1,0:T(8,128)S(1)} %select_select_fusion.5), channel_id=1, source_target_pairs={{0,1},{4,5},{8,9},{12,13},{16,17},{20,21},{24,25},{28,29},{32,33},... | collective-permute-start | bytes 196616 | tf_op jit(solution)/shard_map/ppermute | solution.py:36
  24.8 3.4 %collective-permute-start.8 = (f32[128,128]{1,0:T(8,128)S(1)}, f32[128,128]{1,0:T(8,128)S(1)}, u32[]{:S(2)}, u32[]{:S(2)}) collective-permute-start(f32[128,128]{1,0:T(8,128)S(1)} %select_select_fusion.5), channel_id=1, source_target_pairs={{0,3},{4,7},{8,11},{12,15},{16,19},{20,23},{24,27},{28,31},{32,35}... | collective-permute-start | bytes 196616 | tf_op jit(solution)/shard_map/ppermute | solution.py:36
  26.1 2.6 %collective-permute-start.9 = (f32[128,128]{1,0:T(8,128)S(1)}, f32[128,128]{1,0:T(8,128)S(1)}, u32[]{:S(2)}, u32[]{:S(2)}) collective-permute-start(f32[128,128]{1,0:T(8,128)S(1)} %select_select_fusion.5), channel_id=1, source_target_pairs={{0,2},{4,6},{8,10},{12,14},{16,18},{20,22},{24,26},{28,30},{32,34}... | collective-permute-start | bytes 196616 | tf_op jit(solution)/shard_map/ppermute | solution.py:36
  27.5 3.3 %collective-permute-start.1 = (f32[512,128]{1,0:T(8,128)S(1)}, f32[512,128]{1,0:T(8,128)S(1)}, u32[]{:S(2)}, u32[]{:S(2)}) collective-permute-start(f32[512,128]{1,0:T(8,128)S(1)} %broadcast_select_fusion.3), channel_id=1, source_target_pairs={{0,128},{256,384},{1,129},{257,385},{2,130},{258,386},{3,131},{259... | collective-permute-start | bytes 786440 | tf_op jit(solution)/shard_map/ppermute | solution.py:15
  28.8 2.8 %collective-permute-start.11 = (f32[128,128]{1,0:T(8,128)S(1)}, f32[128,128]{1,0:T(8,128)S(1)}, u32[]{:S(2)}, u32[]{:S(2)}) collective-permute-start(f32[128,128]{1,0:T(8,128)S(1)} %select_select_fusion.4), channel_id=1, source_target_pairs={{0,384},{1,385},{2,386},{3,387},{4,388},{5,389},{6,390},{7,391},{8... | collective-permute-start | bytes 196616 | tf_op jit(solution)/shard_map/ppermute | solution.py:36
  29.4 11.3 %collective-permute-start.12 = (f32[128,128]{1,0:T(8,128)S(1)}, f32[128,128]{1,0:T(8,128)S(1)}, u32[]{:S(2)}, u32[]{:S(2)}) collective-permute-start(f32[128,128]{1,0:T(8,128)S(1)} %select_select_fusion.4), channel_id=1, source_target_pairs={{0,256},{1,257},{2,258},{3,259},{4,260},{5,261},{6,262},{7,263},{8... | collective-permute-start | bytes 196616 | tf_op jit(solution)/shard_map/ppermute | solution.py:36
  30.1 11.9 %collective-permute-start.13 = (f32[128,128]{1,0:T(8,128)S(1)}, f32[128,128]{1,0:T(8,128)S(1)}, u32[]{:S(2)}, u32[]{:S(2)}) collective-permute-start(f32[128,128]{1,0:T(8,128)S(1)} %select_select_fusion.4), channel_id=1, source_target_pairs={{0,128},{1,129},{2,130},{3,131},{4,132},{5,133},{6,134},{7,135},{8... | collective-permute-start | bytes 196616 | tf_op jit(solution)/shard_map/ppermute | solution.py:36
  30.8 11.9 %collective-permute-start.2 = (f32[512,128]{1,0:T(8,128)S(1)}, f32[512,128]{1,0:T(8,128)S(1)}, u32[]{:S(2)}, u32[]{:S(2)}) collective-permute-start(f32[512,128]{1,0:T(8,128)S(1)} %broadcast_select_fusion.4), channel_id=1, source_target_pairs={{0,64},{128,192},{256,320},{384,448},{1,65},{129,193},{257,321},{3... | collective-permute-start | bytes 786440 | tf_op jit(solution)/shard_map/ppermute | solution.py:15
  31.6 13.0 %collective-permute-start.19 = (f32[128,264]{1,0:T(8,128)S(1)}, f32[128,264]{1,0:T(8,128)S(1)}, u32[]{:S(2)}, u32[]{:S(2)}) collective-permute-start(f32[128,264]{1,0:T(8,128)S(1)} %pad_maximum_fusion), channel_id=1, source_target_pairs={{0,8},{16,24},{32,40},{48,56},{64,72},{80,88},{96,104},{112,120},{... | collective-permute-start | bytes 405512 | tf_op jit(solution)/shard_map/ppermute | solution.py:36
  40.7 6.8 %collective-permute-start.20 = (f32[128,264]{1,0:T(8,128)S(1)}, f32[128,264]{1,0:T(8,128)S(1)}, u32[]{:S(2)}, u32[]{:S(2)}) collective-permute-start(f32[128,264]{1,0:T(8,128)S(1)} %pad_maximum_fusion), channel_id=1, source_target_pairs={{0,4},{16,20},{32,36},{48,52},{64,68},{80,84},{96,100},{112,116},{... | collective-permute-start | bytes 405512 | tf_op jit(solution)/shard_map/ppermute | solution.py:36
  42.1 6.8 %collective-permute-start.14 = (f32[128,128]{1,0:T(8,128)S(1)}, f32[128,128]{1,0:T(8,128)S(1)}, u32[]{:S(2)}, u32[]{:S(2)}) collective-permute-start(f32[128,128]{1,0:T(8,128)S(1)} %select_select_fusion.3), channel_id=1, source_target_pairs={{0,96},{128,224},{256,352},{384,480},{1,97},{129,225},{257,353},{3... | collective-permute-start | bytes 196616 | tf_op jit(solution)/shard_map/ppermute | solution.py:36
  42.7 7.4 %collective-permute-start.15 = (f32[128,128]{1,0:T(8,128)S(1)}, f32[128,128]{1,0:T(8,128)S(1)}, u32[]{:S(2)}, u32[]{:S(2)}) collective-permute-start(f32[128,128]{1,0:T(8,128)S(1)} %select_select_fusion.3), channel_id=1, source_target_pairs={{0,64},{128,192},{256,320},{384,448},{1,65},{129,193},{257,321},{3... | collective-permute-start | bytes 196616 | tf_op jit(solution)/shard_map/ppermute | solution.py:36
  43.5 8.0 %collective-permute-start.16 = (f32[128,128]{1,0:T(8,128)S(1)}, f32[128,128]{1,0:T(8,128)S(1)}, u32[]{:S(2)}, u32[]{:S(2)}) collective-permute-start(f32[128,128]{1,0:T(8,128)S(1)} %select_select_fusion.3), channel_id=1, source_target_pairs={{0,32},{128,160},{256,288},{384,416},{1,33},{129,161},{257,289},{3... | collective-permute-start | bytes 196616 | tf_op jit(solution)/shard_map/ppermute | solution.py:36
  44.6 8.2 %collective-permute-start.3 = (f32[512,128]{1,0:T(8,128)S(1)}, f32[512,128]{1,0:T(8,128)S(1)}, u32[]{:S(2)}, u32[]{:S(2)}) collective-permute-start(f32[512,128]{1,0:T(8,128)S(1)} %broadcast_select_fusion.5), channel_id=1, source_target_pairs={{0,32},{64,96},{128,160},{192,224},{256,288},{320,352},{384,416},{... | collective-permute-start | bytes 786440 | tf_op jit(solution)/shard_map/ppermute | solution.py:15
  47.5 6.8 %collective-permute-start.21 = (f32[128,264]{1,0:T(8,128)S(1)}, f32[128,264]{1,0:T(8,128)S(1)}, u32[]{:S(2)}, u32[]{:S(2)}) collective-permute-start(f32[128,264]{1,0:T(8,128)S(1)} %select_select_fusion.1), channel_id=1, source_target_pairs={{0,3},{4,7},{8,11},{12,15},{16,19},{20,23},{24,27},{28,31},{32,35}... | collective-permute-start | bytes 405512 | tf_op jit(solution)/shard_map/ppermute | solution.py:36
  48.9 5.5 %collective-permute-start.22 = (f32[128,264]{1,0:T(8,128)S(1)}, f32[128,264]{1,0:T(8,128)S(1)}, u32[]{:S(2)}, u32[]{:S(2)}) collective-permute-start(f32[128,264]{1,0:T(8,128)S(1)} %select_select_fusion.1), channel_id=1, source_target_pairs={{0,2},{4,6},{8,10},{12,14},{16,18},{20,22},{24,26},{28,30},{32,34}... | collective-permute-start | bytes 405512 | tf_op jit(solution)/shard_map/ppermute | solution.py:36
  50.2 5.5 %collective-permute-start.23 = (f32[128,264]{1,0:T(8,128)S(1)}, f32[128,264]{1,0:T(8,128)S(1)}, u32[]{:S(2)}, u32[]{:S(2)}) collective-permute-start(f32[128,264]{1,0:T(8,128)S(1)} %select_select_fusion.1), channel_id=1, source_target_pairs={{0,1},{4,5},{8,9},{12,13},{16,17},{20,21},{24,25},{28,29},{32,33},... | collective-permute-start | bytes 405512 | tf_op jit(solution)/shard_map/ppermute | solution.py:36
  51.5 22.3 %collective-permute-start.17 = (f32[128,128]{1,0:T(8,128)S(1)}, f32[128,128]{1,0:T(8,128)S(1)}, u32[]{:S(2)}, u32[]{:S(2)}) collective-permute-start(f32[128,128]{1,0:T(8,128)S(1)} %select_select_fusion.2), channel_id=1, source_target_pairs={{0,16},{32,48},{64,80},{96,112},{128,144},{160,176},{192,208},{224... | collective-permute-start | bytes 196616 | tf_op jit(solution)/shard_map/ppermute | solution.py:36
  52.9 22.6 %collective-permute-start.4 = (f32[512,128]{1,0:T(8,128)S(1)}, f32[512,128]{1,0:T(8,128)S(1)}, u32[]{:S(2)}, u32[]{:S(2)}) collective-permute-start(f32[512,128]{1,0:T(8,128)S(1)} %broadcast_select_fusion.6), channel_id=1, source_target_pairs={{0,16},{32,48},{64,80},{96,112},{128,144},{160,176},{192,208},{224... | collective-permute-start | bytes 786440 | tf_op jit(solution)/shard_map/ppermute | solution.py:15
  (5 other events, 22.7 us)

commit v7 on v6

--- a/solution.py
+++ b/solution.py
@@ -18,9 +18,9 @@
     return block
 
 
-def spread_wide(block, axis):
+def spread_wide(block, axis, root=0):
     count = lax.axis_size(axis)
-    index = lax.axis_index(axis)
+    index = lax.axis_index(axis) ^ root
     radices = []
     rest = count
     while rest > 1:
@@ -32,7 +32,10 @@
         span //= radix
         got = block
         for digit in range(1, radix):
-            pairs = [(i, i + digit * span) for i in range(0, count, span * radix)]
+            pairs = [
+                (i ^ root, (i + digit * span) ^ root)
+                for i in range(0, count, span * radix)
+            ]
             arrived = lax.ppermute(block, axis, pairs)
             mine = (index % (span * radix)) == digit * span
             got = jnp.where(mine, arrived, got)
@@ -58,9 +61,11 @@
     def skip(corner_raw):
         return jnp.zeros_like(corner_raw), jnp.zeros_like(corner_raw)
 
-    holder = (row_id == 0) & (col_id == 0)
-    corner, inverse = lax.cond(holder, factor, skip, local[:block, :block])
-    inverse = spread_wide(spread_wide(inverse, "row"), "col")
+    corner_raw = lax.ppermute(local[:block, :block], "col", [(0, 1)])
+    holder = (row_id == 0) & (col_id == 1)
+    corner, inverse = lax.cond(holder, factor, skip, corner_raw)
+    corner = lax.ppermute(corner, "col", [(1, 0)])
+    inverse = spread_wide(spread_wide(inverse, "row"), "col", root=1)
     left = spread(local[:, :block], "col")
     top = jnp.concatenate([local[:block], right_sides[:, 0, 0, :].T], axis=1)
     top = spread_wide(top, "row")

time: 81.2 us -> 89.3 us (1.100)
  other arithmetic: 2.65 us -> 25.5 us
  waiting for transfers between devices: 23.8 us -> 1.82 us
  starting transfers between devices: 47.3 us -> 55.1 us
    another operation x0 -> x5, other arithmetic: none -> 22.9 us  [the longest x3 12.4 us: factor(): corner = jnp.linalg.cholesky(corner_raw)]
    ppermute x19, waiting for transfers between devices: 22.7 us -> 1.8 us  [spread_wide(): arrived = lax.ppermute(block, axis, pairs)]
    ppermute x0 -> x2, starting transfers between devices: none -> 4.52 us  [the longest x1 3.23 us: on_device(): corner = lax.ppermute(corner, 'col', [(1, 0)])]
    ppermute x19, starting transfers between devices: 43.1 us -> 46.4 us  [spread_wide(): arrived = lax.ppermute(block, axis, pairs)]
    ppermute x5, waiting for transfers between devices: 1.14 us -> 0.01 us  [spread(): arrived = lax.ppermute(block, axis, pairs)]
  transfers between devices with their start and end apart: 24 -> 26, of which waited for: 6 -> 2; matrix products, arithmetic and copies ran while one was open for 2% -> 30% of each run, Pallas kernels for 0% -> 0%
where the time goes in v7:
time: 89.3 us; the launch traced here: 88.6 us
  starting transfers between devices  55.1 us (62%)
  other arithmetic  25.5 us (29%)
  local copies, waits for them, and re-layouts  2.77 us (3%)
  matrix products  2.04 us (2%)
  waiting for transfers between devices  1.82 us (2%)
  between operations  1.32 us (1%)
    ppermute x19, starting transfers between devices, spread_wide(): arrived = lax.ppermute(block, axis, pairs)  46.4 us
    another operation x3, other arithmetic, factor(): corner = jnp.linalg.cholesky(corner_raw)  12.4 us
    another operation x2, other arithmetic, factor(): inverse = jax.scipy.linalg.solve_triangular(corner, identity, lower=True)  10.5 us
    ppermute x5, starting transfers between devices, spread(): arrived = lax.ppermute(block, axis, pairs)  4.13 us
    ppermute x1, starting transfers between devices, on_device(): corner = lax.ppermute(corner, 'col', [(1, 0)])  3.23 us
    ppermute x19, waiting for transfers between devices, spread_wide(): arrived = lax.ppermute(block, axis, pairs)  1.8 us
  transfers between devices with their start and end apart: 26, of which 2 were waited for; matrix products, arithmetic and copies ran while one was open for 30% of the time, Pallas kernels for 0%

profile of v7, /device:TPU:1, one launch (start us, length us, event | category | flops | bytes accessed | tf_op | source)
XLA Modules:
  0.0 88.6 jit_solution(11483762147798969154)
XLA Ops:
  5.1 13.3 %collective-permute-start.20 = (f32[128,264]{1,0:T(8,128)S(1)}, f32[128,264]{1,0:T(8,128)S(1)}, u32[]{:S(2)}, u32[]{:S(2)}) collective-permute-start(f32[128,264]{1,0:T(8,128)S(1)} %pad_maximum_fusion), channel_id=1, source_target_pairs={{0,12},{16,28},{32,44},{48,60},{64,76},{80,92},{96,108},{112,124},... | collective-permute-start | bytes 405512 | tf_op jit(solution)/shard_map/ppermute | solution.py:39
  18.4 23.3 %conditional.1 = (f32[128,128]{1,0:T(8,128)S(1)}, f32[128,128]{1,0:T(8,128)S(1)}) conditional(s32[]{:T(128)} %convert_element_type.6, () %tuple.16, (f32[128,128]{1,0:T(8,128)S(1)}, f32[128,128]{1,0:T(8,128)S(1)}) %tuple.17), branch_computations={%region_0.0_spmd, %region_1.0_spmd} | conditional | flops 25313408 | bytes 787474 | solution.py:66
  18.6 11.7 %cholesky.3 = f32[128,128]{1,0:T(8,128)S(1)} custom-call(f32[128,128]{1,0:T(8,128)S(1)} %fusion.2), custom_call_target="Cholesky" | custom-call | tf_op jit(solution)/shard_map/cond/branch_1_fun/jit(cholesky)/cholesky | solution.py:57
  31.6 9.8 %custom-call.6 = f32[1,128,128]{1,2,0:T(8,128)S(1)} custom-call(f32[1,128,128]{2,1,0:T(8,128)S(1)} %get-tuple-element.14), custom_call_target="InvertDiagBlocksLowerTriangular" | custom-call | tf_op jit(solution)/shard_map/cond/branch_1_fun/jit(_solve_triangular)/triangular_solve | solution.py:58
  41.7 1.3 %collective-permute-start.7 = (f32[128,128]{1,0:T(8,128)S(1)}, f32[128,128]{1,0:T(8,128)S(1)}, u32[]{:S(2)}, u32[]{:S(2)}) collective-permute-start(f32[128,128]{1,0:T(8,128)S(1)} %get-tuple-element.11), channel_id=1, source_target_pairs={{0,12},{16,28},{32,44},{48,60},{64,76},{80,92},{96,108},{112,124},... | collective-permute-start | bytes 196616 | tf_op jit(solution)/shard_map/ppermute | solution.py:39
  43.0 1.3 %collective-permute-start.8 = (f32[128,128]{1,0:T(8,128)S(1)}, f32[128,128]{1,0:T(8,128)S(1)}, u32[]{:S(2)}, u32[]{:S(2)}) collective-permute-start(f32[128,128]{1,0:T(8,128)S(1)} %get-tuple-element.11), channel_id=1, source_target_pairs={{0,8},{16,24},{32,40},{48,56},{64,72},{80,88},{96,104},{112,120},{... | collective-permute-start | bytes 196616 | tf_op jit(solution)/shard_map/ppermute | solution.py:39
  44.4 1.3 %collective-permute-start.9 = (f32[128,128]{1,0:T(8,128)S(1)}, f32[128,128]{1,0:T(8,128)S(1)}, u32[]{:S(2)}, u32[]{:S(2)}) collective-permute-start(f32[128,128]{1,0:T(8,128)S(1)} %get-tuple-element.11), channel_id=1, source_target_pairs={{0,4},{16,20},{32,36},{48,52},{64,68},{80,84},{96,100},{112,116},{... | collective-permute-start | bytes 196616 | tf_op jit(solution)/shard_map/ppermute | solution.py:39
  47.0 1.3 %collective-permute-start.10 = (f32[128,128]{1,0:T(8,128)S(1)}, f32[128,128]{1,0:T(8,128)S(1)}, u32[]{:S(2)}, u32[]{:S(2)}) collective-permute-start(f32[128,128]{1,0:T(8,128)S(1)} %select_select_fusion.5), channel_id=1, source_target_pairs={{0,3},{4,7},{8,11},{12,15},{16,19},{20,23},{24,27},{28,31},{32,35}... | collective-permute-start | bytes 196616 | tf_op jit(solution)/shard_map/ppermute | solution.py:39
  48.3 1.3 %collective-permute-start.11 = (f32[128,128]{1,0:T(8,128)S(1)}, f32[128,128]{1,0:T(8,128)S(1)}, u32[]{:S(2)}, u32[]{:S(2)}) collective-permute-start(f32[128,128]{1,0:T(8,128)S(1)} %select_select_fusion.5), channel_id=1, source_target_pairs={{0,2},{4,6},{8,10},{12,14},{16,18},{20,22},{24,26},{28,30},{32,34}... | collective-permute-start | bytes 196616 | tf_op jit(solution)/shard_map/ppermute | solution.py:39
  49.6 1.3 %collective-permute-start.12 = (f32[128,128]{1,0:T(8,128)S(1)}, f32[128,128]{1,0:T(8,128)S(1)}, u32[]{:S(2)}, u32[]{:S(2)}) collective-permute-start(f32[128,128]{1,0:T(8,128)S(1)} %select_select_fusion.5), channel_id=1, source_target_pairs={{0,1},{4,5},{8,9},{12,13},{16,17},{20,21},{24,25},{28,29},{32,33},... | collective-permute-start | bytes 196616 | tf_op jit(solution)/shard_map/ppermute | solution.py:39
  52.2 1.3 %collective-permute-start.13 = (f32[128,128]{1,0:T(8,128)S(1)}, f32[128,128]{1,0:T(8,128)S(1)}, u32[]{:S(2)}, u32[]{:S(2)}) collective-permute-start(f32[128,128]{1,0:T(8,128)S(1)} %select_select_fusion.4), channel_id=1, source_target_pairs={{16,400},{17,401},{18,402},{19,403},{20,404},{21,405},{22,406},{23... | collective-permute-start | bytes 196616 | tf_op jit(solution)/shard_map/ppermute | solution.py:39
  53.5 1.3 %collective-permute-start.14 = (f32[128,128]{1,0:T(8,128)S(1)}, f32[128,128]{1,0:T(8,128)S(1)}, u32[]{:S(2)}, u32[]{:S(2)}) collective-permute-start(f32[128,128]{1,0:T(8,128)S(1)} %select_select_fusion.4), channel_id=1, source_target_pairs={{16,272},{17,273},{18,274},{19,275},{20,276},{21,277},{22,278},{23... | collective-permute-start | bytes 196616 | tf_op jit(solution)/shard_map/ppermute | solution.py:39
  54.8 1.3 %collective-permute-start.15 = (f32[128,128]{1,0:T(8,128)S(1)}, f32[128,128]{1,0:T(8,128)S(1)}, u32[]{:S(2)}, u32[]{:S(2)}) collective-permute-start(f32[128,128]{1,0:T(8,128)S(1)} %select_select_fusion.4), channel_id=1, source_target_pairs={{16,144},{17,145},{18,146},{19,147},{20,148},{21,149},{22,150},{23... | collective-permute-start | bytes 196616 | tf_op jit(solution)/shard_map/ppermute | solution.py:39
  56.9 11.1 %collective-permute-start.21 = (f32[128,264]{1,0:T(8,128)S(1)}, f32[128,264]{1,0:T(8,128)S(1)}, u32[]{:S(2)}, u32[]{:S(2)}) collective-permute-start(f32[128,264]{1,0:T(8,128)S(1)} %pad_maximum_fusion), channel_id=1, source_target_pairs={{0,8},{16,24},{32,40},{48,56},{64,72},{80,88},{96,104},{112,120},{... | collective-permute-start | bytes 405512 | tf_op jit(solution)/shard_map/ppermute | solution.py:39
  68.1 1.3 %collective-permute-start.22 = (f32[128,264]{1,0:T(8,128)S(1)}, f32[128,264]{1,0:T(8,128)S(1)}, u32[]{:S(2)}, u32[]{:S(2)}) collective-permute-start(f32[128,264]{1,0:T(8,128)S(1)} %pad_maximum_fusion), channel_id=1, source_target_pairs={{0,4},{16,20},{32,36},{48,52},{64,68},{80,84},{96,100},{112,116},{... | collective-permute-start | bytes 405512 | tf_op jit(solution)/shard_map/ppermute | solution.py:39
  69.4 1.3 %collective-permute-start.16 = (f32[128,128]{1,0:T(8,128)S(1)}, f32[128,128]{1,0:T(8,128)S(1)}, u32[]{:S(2)}, u32[]{:S(2)}) collective-permute-start(f32[128,128]{1,0:T(8,128)S(1)} %select_select_fusion.3), channel_id=1, source_target_pairs={{16,112},{144,240},{272,368},{400,496},{17,113},{145,241},{273,369... | collective-permute-start | bytes 196616 | tf_op jit(solution)/shard_map/ppermute | solution.py:39
  70.7 1.3 %collective-permute-start.17 = (f32[128,128]{1,0:T(8,128)S(1)}, f32[128,128]{1,0:T(8,128)S(1)}, u32[]{:S(2)}, u32[]{:S(2)}) collective-permute-start(f32[128,128]{1,0:T(8,128)S(1)} %select_select_fusion.3), channel_id=1, source_target_pairs={{16,80},{144,208},{272,336},{400,464},{17,81},{145,209},{273,337},... | collective-permute-start | bytes 196616 | tf_op jit(solution)/shard_map/ppermute | solution.py:39
  72.1 1.3 %collective-permute-start.18 = (f32[128,128]{1,0:T(8,128)S(1)}, f32[128,128]{1,0:T(8,128)S(1)}, u32[]{:S(2)}, u32[]{:S(2)}) collective-permute-start(f32[128,128]{1,0:T(8,128)S(1)} %select_select_fusion.3), channel_id=1, source_target_pairs={{16,48},{144,176},{272,304},{400,432},{17,49},{145,177},{273,305},... | collective-permute-start | bytes 196616 | tf_op jit(solution)/shard_map/ppermute | solution.py:39
  74.1 1.3 %collective-permute-start.23 = (f32[128,264]{1,0:T(8,128)S(1)}, f32[128,264]{1,0:T(8,128)S(1)}, u32[]{:S(2)}, u32[]{:S(2)}) collective-permute-start(f32[128,264]{1,0:T(8,128)S(1)} %select_select_fusion.1), channel_id=1, source_target_pairs={{0,3},{4,7},{8,11},{12,15},{16,19},{20,23},{24,27},{28,31},{32,35}... | collective-permute-start | bytes 405512 | tf_op jit(solution)/shard_map/ppermute | solution.py:39
  75.5 1.3 %collective-permute-start.24 = (f32[128,264]{1,0:T(8,128)S(1)}, f32[128,264]{1,0:T(8,128)S(1)}, u32[]{:S(2)}, u32[]{:S(2)}) collective-permute-start(f32[128,264]{1,0:T(8,128)S(1)} %select_select_fusion.1), channel_id=1, source_target_pairs={{0,2},{4,6},{8,10},{12,14},{16,18},{20,22},{24,26},{28,30},{32,34}... | collective-permute-start | bytes 405512 | tf_op jit(solution)/shard_map/ppermute | solution.py:39
  76.8 1.3 %collective-permute-start.25 = (f32[128,264]{1,0:T(8,128)S(1)}, f32[128,264]{1,0:T(8,128)S(1)}, u32[]{:S(2)}, u32[]{:S(2)}) collective-permute-start(f32[128,264]{1,0:T(8,128)S(1)} %select_select_fusion.1), channel_id=1, source_target_pairs={{0,1},{4,5},{8,9},{12,13},{16,17},{20,21},{24,25},{28,29},{32,33},... | collective-permute-start | bytes 405512 | tf_op jit(solution)/shard_map/ppermute | solution.py:39
  78.1 1.3 %collective-permute-start.19 = (f32[128,128]{1,0:T(8,128)S(1)}, f32[128,128]{1,0:T(8,128)S(1)}, u32[]{:S(2)}, u32[]{:S(2)}) collective-permute-start(f32[128,128]{1,0:T(8,128)S(1)} %select_select_fusion.2), channel_id=1, source_target_pairs={{16,0},{48,32},{80,64},{112,96},{144,128},{176,160},{208,192},{240... | collective-permute-start | bytes 196616 | tf_op jit(solution)/shard_map/ppermute | solution.py:39
  80.8 3.2 %collective-permute-start.1 = (f32[128,128]{1,0:T(8,128)S(1)}, f32[128,128]{1,0:T(8,128)S(1)}, u32[]{:S(2)}, u32[]{:S(2)}) collective-permute-start(f32[128,128]{1,0:T(8,128)S(1)} %get-tuple-element.10), channel_id=1, source_target_pairs={{16,0},{17,1},{18,2},{19,3},{20,4},{21,5},{22,6},{23,7},{24,8},{25... | collective-permute-start | bytes 196616 | tf_op jit(solution)/shard_map/ppermute | solution.py:67
  87.1 1.5 %broadcast_select_fusion = f32[4,1,128,2,1,128]{5,4,3,2,1,0:T(1,128)} fusion(pred[2]{0:T(512)(128)(4,1)S(1)} %fusion.17, f32[4,1,128,2,1,128]{5,4,3,2,1,0:T(1,128)S(1)} %bitcast.42, pred[4,2]{1,0:T(4,128)(4,1)S(1)} %broadcast_and_fusion, f32[4,128,128]{2,1,0:T(8,128)S(1)} %broadcast_select_fusion.2), kind=kLoop, calls=%fused_computation.13 | loop fusion | flops 262144 | bytes 1310730 | tf_op jit(solution)/shard_map/jit(_where)/select_n | solution.py:96
  (73 shorter events, 14.6 us)
Async XLA Ops:
  1.7 49.1 %collective-permute-start.2 = (f32[512,128]{1,0:T(8,128)S(1)}, f32[512,128]{1,0:T(8,128)S(1)}, u32[]{:S(2)}, u32[]{:S(2)}) collective-permute-start(f32[512,128]{1,0:T(8,128)S(1)} %slice.41), channel_id=1, source_target_pairs={{0,256},{1,257},{2,258},{3,259},{4,260},{5,261},{6,262},{7,263},{8... | collective-permute-start | bytes 786440 | tf_op jit(solution)/shard_map/ppermute | solution.py:15
  2.6 15.9 %collective-permute-start = (f32[128,128]{1,0:T(8,128)S(1)}, f32[128,128]{1,0:T(8,128)S(1)}, u32[]{:S(2)}, u32[]{:S(2)}) collective-permute-start(f32[128,128]{1,0:T(8,128)S(1)} %slice.40), channel_id=1, source_target_pairs={{0,16},{1,17},{2,18},{3,19},{4,20},{5,21},{6,22},{7,23},{8,24},{9,... | collective-permute-start | bytes 196616 | tf_op jit(solution)/shard_map/ppermute | solution.py:64
  5.1 67.0 %collective-permute-start.20 = (f32[128,264]{1,0:T(8,128)S(1)}, f32[128,264]{1,0:T(8,128)S(1)}, u32[]{:S(2)}, u32[]{:S(2)}) collective-permute-start(f32[128,264]{1,0:T(8,128)S(1)} %pad_maximum_fusion), channel_id=1, source_target_pairs={{0,12},{16,28},{32,44},{48,60},{64,76},{80,92},{96,108},{112,124},... | collective-permute-start | bytes 405512 | tf_op jit(solution)/shard_map/ppermute | solution.py:39
  41.7 3.9 %collective-permute-start.7 = (f32[128,128]{1,0:T(8,128)S(1)}, f32[128,128]{1,0:T(8,128)S(1)}, u32[]{:S(2)}, u32[]{:S(2)}) collective-permute-start(f32[128,128]{1,0:T(8,128)S(1)} %get-tuple-element.11), channel_id=1, source_target_pairs={{0,12},{16,28},{32,44},{48,60},{64,76},{80,92},{96,108},{112,124},... | collective-permute-start | bytes 196616 | tf_op jit(solution)/shard_map/ppermute | solution.py:39
  43.0 2.7 %collective-permute-start.8 = (f32[128,128]{1,0:T(8,128)S(1)}, f32[128,128]{1,0:T(8,128)S(1)}, u32[]{:S(2)}, u32[]{:S(2)}) collective-permute-start(f32[128,128]{1,0:T(8,128)S(1)} %get-tuple-element.11), channel_id=1, source_target_pairs={{0,8},{16,24},{32,40},{48,56},{64,72},{80,88},{96,104},{112,120},{... | collective-permute-start | bytes 196616 | tf_op jit(solution)/shard_map/ppermute | solution.py:39
  47.0 4.7 %collective-permute-start.10 = (f32[128,128]{1,0:T(8,128)S(1)}, f32[128,128]{1,0:T(8,128)S(1)}, u32[]{:S(2)}, u32[]{:S(2)}) collective-permute-start(f32[128,128]{1,0:T(8,128)S(1)} %select_select_fusion.5), channel_id=1, source_target_pairs={{0,3},{4,7},{8,11},{12,15},{16,19},{20,23},{24,27},{28,31},{32,35}... | collective-permute-start | bytes 196616 | tf_op jit(solution)/shard_map/ppermute | solution.py:39
  48.3 3.4 %collective-permute-start.11 = (f32[128,128]{1,0:T(8,128)S(1)}, f32[128,128]{1,0:T(8,128)S(1)}, u32[]{:S(2)}, u32[]{:S(2)}) collective-permute-start(f32[128,128]{1,0:T(8,128)S(1)} %select_select_fusion.5), channel_id=1, source_target_pairs={{0,2},{4,6},{8,10},{12,14},{16,18},{20,22},{24,26},{28,30},{32,34}... | collective-permute-start | bytes 196616 | tf_op jit(solution)/shard_map/ppermute | solution.py:39
  50.9 5.2 %collective-permute-start.3 = (f32[512,128]{1,0:T(8,128)S(1)}, f32[512,128]{1,0:T(8,128)S(1)}, u32[]{:S(2)}, u32[]{:S(2)}) collective-permute-start(f32[512,128]{1,0:T(8,128)S(1)} %broadcast_select_fusion.3), channel_id=1, source_target_pairs={{0,128},{256,384},{1,129},{257,385},{2,130},{258,386},{3,131},{259... | collective-permute-start | bytes 786440 | tf_op jit(solution)/shard_map/ppermute | solution.py:15
  52.2 4.7 %collective-permute-start.13 = (f32[128,128]{1,0:T(8,128)S(1)}, f32[128,128]{1,0:T(8,128)S(1)}, u32[]{:S(2)}, u32[]{:S(2)}) collective-permute-start(f32[128,128]{1,0:T(8,128)S(1)} %select_select_fusion.4), channel_id=1, source_target_pairs={{16,400},{17,401},{18,402},{19,403},{20,404},{21,405},{22,406},{23... | collective-permute-start | bytes 196616 | tf_op jit(solution)/shard_map/ppermute | solution.py:39
  53.5 14.6 %collective-permute-start.14 = (f32[128,128]{1,0:T(8,128)S(1)}, f32[128,128]{1,0:T(8,128)S(1)}, u32[]{:S(2)}, u32[]{:S(2)}) collective-permute-start(f32[128,128]{1,0:T(8,128)S(1)} %select_select_fusion.4), channel_id=1, source_target_pairs={{16,272},{17,273},{18,274},{19,275},{20,276},{21,277},{22,278},{23... | collective-permute-start | bytes 196616 | tf_op jit(solution)/shard_map/ppermute | solution.py:39
  54.8 14.6 %collective-permute-start.15 = (f32[128,128]{1,0:T(8,128)S(1)}, f32[128,128]{1,0:T(8,128)S(1)}, u32[]{:S(2)}, u32[]{:S(2)}) collective-permute-start(f32[128,128]{1,0:T(8,128)S(1)} %select_select_fusion.4), channel_id=1, source_target_pairs={{16,144},{17,145},{18,146},{19,147},{20,148},{21,149},{22,150},{23... | collective-permute-start | bytes 196616 | tf_op jit(solution)/shard_map/ppermute | solution.py:39
  56.2 14.6 %collective-permute-start.4 = (f32[512,128]{1,0:T(8,128)S(1)}, f32[512,128]{1,0:T(8,128)S(1)}, u32[]{:S(2)}, u32[]{:S(2)}) collective-permute-start(f32[512,128]{1,0:T(8,128)S(1)} %broadcast_select_fusion.4), channel_id=1, source_target_pairs={{0,64},{128,192},{256,320},{384,448},{1,65},{129,193},{257,321},{3... | collective-permute-start | bytes 786440 | tf_op jit(solution)/shard_map/ppermute | solution.py:15
  56.9 16.4 %collective-permute-start.21 = (f32[128,264]{1,0:T(8,128)S(1)}, f32[128,264]{1,0:T(8,128)S(1)}, u32[]{:S(2)}, u32[]{:S(2)}) collective-permute-start(f32[128,264]{1,0:T(8,128)S(1)} %pad_maximum_fusion), channel_id=1, source_target_pairs={{0,8},{16,24},{32,40},{48,56},{64,72},{80,88},{96,104},{112,120},{... | collective-permute-start | bytes 405512 | tf_op jit(solution)/shard_map/ppermute | solution.py:39
  68.1 6.0 %collective-permute-start.22 = (f32[128,264]{1,0:T(8,128)S(1)}, f32[128,264]{1,0:T(8,128)S(1)}, u32[]{:S(2)}, u32[]{:S(2)}) collective-permute-start(f32[128,264]{1,0:T(8,128)S(1)} %pad_maximum_fusion), channel_id=1, source_target_pairs={{0,4},{16,20},{32,36},{48,52},{64,68},{80,84},{96,100},{112,116},{... | collective-permute-start | bytes 405512 | tf_op jit(solution)/shard_map/ppermute | solution.py:39
  69.4 6.0 %collective-permute-start.16 = (f32[128,128]{1,0:T(8,128)S(1)}, f32[128,128]{1,0:T(8,128)S(1)}, u32[]{:S(2)}, u32[]{:S(2)}) collective-permute-start(f32[128,128]{1,0:T(8,128)S(1)} %select_select_fusion.3), channel_id=1, source_target_pairs={{16,112},{144,240},{272,368},{400,496},{17,113},{145,241},{273,369... | collective-permute-start | bytes 196616 | tf_op jit(solution)/shard_map/ppermute | solution.py:39
  70.7 6.0 %collective-permute-start.17 = (f32[128,128]{1,0:T(8,128)S(1)}, f32[128,128]{1,0:T(8,128)S(1)}, u32[]{:S(2)}, u32[]{:S(2)}) collective-permute-start(f32[128,128]{1,0:T(8,128)S(1)} %select_select_fusion.3), channel_id=1, source_target_pairs={{16,80},{144,208},{272,336},{400,464},{17,81},{145,209},{273,337},... | collective-permute-start | bytes 196616 | tf_op jit(solution)/shard_map/ppermute | solution.py:39
  72.1 6.0 %collective-permute-start.18 = (f32[128,128]{1,0:T(8,128)S(1)}, f32[128,128]{1,0:T(8,128)S(1)}, u32[]{:S(2)}, u32[]{:S(2)}) collective-permute-start(f32[128,128]{1,0:T(8,128)S(1)} %select_select_fusion.3), channel_id=1, source_target_pairs={{16,48},{144,176},{272,304},{400,432},{17,49},{145,177},{273,305},... | collective-permute-start | bytes 196616 | tf_op jit(solution)/shard_map/ppermute | solution.py:39
  73.4 6.0 %collective-permute-start.5 = (f32[512,128]{1,0:T(8,128)S(1)}, f32[512,128]{1,0:T(8,128)S(1)}, u32[]{:S(2)}, u32[]{:S(2)}) collective-permute-start(f32[512,128]{1,0:T(8,128)S(1)} %broadcast_select_fusion.5), channel_id=1, source_target_pairs={{0,32},{64,96},{128,160},{192,224},{256,288},{320,352},{384,416},{... | collective-permute-start | bytes 786440 | tf_op jit(solution)/shard_map/ppermute | solution.py:15
  74.1 6.7 %collective-permute-start.23 = (f32[128,264]{1,0:T(8,128)S(1)}, f32[128,264]{1,0:T(8,128)S(1)}, u32[]{:S(2)}, u32[]{:S(2)}) collective-permute-start(f32[128,264]{1,0:T(8,128)S(1)} %select_select_fusion.1), channel_id=1, source_target_pairs={{0,3},{4,7},{8,11},{12,15},{16,19},{20,23},{24,27},{28,31},{32,35}... | collective-permute-start | bytes 405512 | tf_op jit(solution)/shard_map/ppermute | solution.py:39
  75.5 8.6 %collective-permute-start.24 = (f32[128,264]{1,0:T(8,128)S(1)}, f32[128,264]{1,0:T(8,128)S(1)}, u32[]{:S(2)}, u32[]{:S(2)}) collective-permute-start(f32[128,264]{1,0:T(8,128)S(1)} %select_select_fusion.1), channel_id=1, source_target_pairs={{0,2},{4,6},{8,10},{12,14},{16,18},{20,22},{24,26},{28,30},{32,34}... | collective-permute-start | bytes 405512 | tf_op jit(solution)/shard_map/ppermute | solution.py:39
  76.8 7.3 %collective-permute-start.25 = (f32[128,264]{1,0:T(8,128)S(1)}, f32[128,264]{1,0:T(8,128)S(1)}, u32[]{:S(2)}, u32[]{:S(2)}) collective-permute-start(f32[128,264]{1,0:T(8,128)S(1)} %select_select_fusion.1), channel_id=1, source_target_pairs={{0,1},{4,5},{8,9},{12,13},{16,17},{20,21},{24,25},{28,29},{32,33},... | collective-permute-start | bytes 405512 | tf_op jit(solution)/shard_map/ppermute | solution.py:39
  78.1 6.0 %collective-permute-start.19 = (f32[128,128]{1,0:T(8,128)S(1)}, f32[128,128]{1,0:T(8,128)S(1)}, u32[]{:S(2)}, u32[]{:S(2)}) collective-permute-start(f32[128,128]{1,0:T(8,128)S(1)} %select_select_fusion.2), channel_id=1, source_target_pairs={{16,0},{48,32},{80,64},{112,96},{144,128},{176,160},{208,192},{240... | collective-permute-start | bytes 196616 | tf_op jit(solution)/shard_map/ppermute | solution.py:39
  79.5 5.1 %collective-permute-start.6 = (f32[512,128]{1,0:T(8,128)S(1)}, f32[512,128]{1,0:T(8,128)S(1)}, u32[]{:S(2)}, u32[]{:S(2)}) collective-permute-start(f32[512,128]{1,0:T(8,128)S(1)} %broadcast_select_fusion.6), channel_id=1, source_target_pairs={{0,16},{32,48},{64,80},{96,112},{128,144},{160,176},{192,208},{224... | collective-permute-start | bytes 786440 | tf_op jit(solution)/shard_map/ppermute | solution.py:15
  80.8 6.2 %collective-permute-start.1 = (f32[128,128]{1,0:T(8,128)S(1)}, f32[128,128]{1,0:T(8,128)S(1)}, u32[]{:S(2)}, u32[]{:S(2)}) collective-permute-start(f32[128,128]{1,0:T(8,128)S(1)} %get-tuple-element.10), channel_id=1, source_target_pairs={{16,0},{17,1},{18,2},{19,3},{20,4},{21,5},{22,6},{23,7},{24,8},{25... | collective-permute-start | bytes 196616 | tf_op jit(solution)/shard_map/ppermute | solution.py:67
  (5 other events, 8.8 us)

commit v8 on v6

--- a/solution.py
+++ b/solution.py
@@ -60,10 +60,14 @@
 
     holder = (row_id == 0) & (col_id == 0)
     corner, inverse = lax.cond(holder, factor, skip, local[:block, :block])
-    inverse = spread_wide(spread_wide(inverse, "row"), "col")
-    left = spread(local[:, :block], "col")
-    top = jnp.concatenate([local[:block], right_sides[:, 0, 0, :].T], axis=1)
+    top = jnp.concatenate([local[:block], right_sides[:, 0, 0, :].T, inverse], axis=1)
     top = spread_wide(top, "row")
+    width = col_blocks * block + side_count
+    left = jnp.concatenate([local[:, :block], top[:, width:]], axis=0)
+    left = spread_wide(left, "col")
+    inverse = left[row_blocks * block:]
+    left = left[: row_blocks * block]
+    top = top[:, :width]
 
     rows_factor = jnp.dot(
         left, inverse.T, precision=lax.Precision.HIGHEST, preferred_element_type=jnp.float32

time: 81.2 us -> 84.7 us (1.043)
  the two profiles are of different devices: /device:TPU:1 before, /device:TPU:43 now
where the time goes in v8:
time: 84.7 us; the launch traced here: 84.1 us
  waiting for transfers between devices  64.1 us (76%)
  starting transfers between devices  10.1 us (12%)
  local copies, waits for them, and re-layouts  4.26 us (5%)
  other arithmetic  2.86 us (3%)
  matrix products  1.74 us (2%)
  between operations  1.08 us (1%)
    ppermute x13, waiting for transfers between devices, spread_wide(): arrived = lax.ppermute(block, axis, pairs)  64.1 us
    ppermute x13, starting transfers between devices, spread_wide(): arrived = lax.ppermute(block, axis, pairs)  10.1 us
  transfers between devices with their start and end apart: 13, of which 2 were waited for; matrix products, arithmetic and copies ran while one was open for 0% of the time, Pallas kernels for 0%

profile of v8, /device:TPU:43, one launch (start us, length us, event | category | flops | bytes accessed | tf_op | source)
XLA Modules:
  0.0 84.1 jit_solution(13660760393333951297)
XLA Ops:
  0.7 1.3 %slice_reduce_fusion = f32[128,2,128]{2,1,0:T(2,128)S(1)} fusion(f32[4,1,128,2,1,128]{5,4,3,2,1,0:T(1,128)} %param.4), kind=kLoop, calls=%fused_computation.29 | loop fusion | bytes 262144 | tf_op jit(solution)/shard_map/slice | solution.py:63
  2.0 1.1 %copy.19 = f32[64,8,2,128]{3,1,2,0:T(8,128)S(1)} copy(f32[64,8,2,128]{3,2,1,0:T(2,128)} %bitcast.39) | data formatting | bytes 1048576
  3.1 0.7 slice-done.1
  4.0 0.7 collective-permute-start
  4.7 0.7 collective-permute-start.1
  5.4 0.7 collective-permute-start.2
  6.2 0.7 collective-permute-start.3
  6.9 0.7 collective-permute-start.4
  7.6 1.3 %collective-permute-start.5 = (f32[128,392]{1,0:T(8,128)S(1)}, f32[128,392]{1,0:T(8,128)S(1)}, u32[]{:S(2)}, u32[]{:S(2)}) collective-permute-start(f32[128,392]{1,0:T(8,128)S(1)} %select_select_fusion.4), channel_id=1, source_target_pairs={{0,1},{4,5},{8,9},{12,13},{16,17},{20,21},{24,25},{28,29},{32,33},... | collective-permute-start | bytes 602120 | tf_op jit(solution)/shard_map/ppermute | solution.py:36
  9.0 39.3 %collective-permute-done.5 = f32[128,392]{1,0:T(8,128)S(1)} collective-permute-done((f32[128,392]{1,0:T(8,128)S(1)}, f32[128,392]{1,0:T(8,128)S(1)}, u32[]{:S(2)}, u32[]{:S(2)}) %collective-permute-start.5) | collective-permute-done | bytes 200736 | tf_op jit(solution)/shard_map/ppermute | solution.py:36
  48.4 0.7 collective-permute-start.6
  49.1 0.7 collective-permute-start.7
  49.8 0.7 collective-permute-start.8
  50.6 0.7 collective-permute-start.10
  51.3 0.7 collective-permute-start.11
  52.0 0.7 collective-permute-start.9
  52.8 1.3 %collective-permute-start.12 = (f32[640,128]{1,0:T(8,128)S(1)}, f32[640,128]{1,0:T(8,128)S(1)}, u32[]{:S(2)}, u32[]{:S(2)}) collective-permute-start(f32[640,128]{1,0:T(8,128)S(1)} %select_select_fusion.1), channel_id=1, source_target_pairs={{0,16},{32,48},{64,80},{96,112},{128,144},{160,176},{192,208},{224... | collective-permute-start | bytes 983048 | tf_op jit(solution)/shard_map/ppermute | solution.py:36
  54.2 24.8 %collective-permute-done.12 = f32[640,128]{1,0:T(8,128)S(1)} collective-permute-done((f32[640,128]{1,0:T(8,128)S(1)}, f32[640,128]{1,0:T(8,128)S(1)}, u32[]{:S(2)}, u32[]{:S(2)}) %collective-permute-start.12) | collective-permute-done | bytes 327712 | tf_op jit(solution)/shard_map/ppermute | solution.py:36
  79.1 0.5 fusion.6
  79.6 0.4 fusion.4
  80.1 0.6 convolution_subtract_fusion
  81.4 0.4 slice-done
  81.8 0.7 broadcast_select_fusion.4
  82.6 1.5 %broadcast_select_fusion = f32[4,1,128,2,1,128]{5,4,3,2,1,0:T(1,128)} fusion(pred[2]{0:T(512)(128)(4,1)S(1)} %get-tuple-element.18, f32[4,1,128,2,1,128]{5,4,3,2,1,0:T(1,128)S(1)} %bitcast.41, pred[4,2]{1,0:T(4,128)(4,1)S(1)} %broadcast_and_fusion, f32[4,128,128]{2,1,0:T(8,128)S(1)} %broadcast_select_fusion.3), kind=kLoop, calls=%fused_computation.13 | loop fusion | flops 262144 | bytes 1310730 | tf_op jit(solution)/shard_map/jit(_where)/select_n | solution.py:95
  (40 shorter events, 1.8 us)
Async XLA Ops:
  3.1 0.7 slice-start.1
  4.0 2.1 %collective-permute-start = (f32[128,392]{1,0:T(8,128)S(1)}, f32[128,392]{1,0:T(8,128)S(1)}, u32[]{:S(2)}, u32[]{:S(2)}) collective-permute-start(f32[128,392]{1,0:T(8,128)S(1)} %pad_maximum_fusion.1), channel_id=1, source_target_pairs={{0,12},{16,28},{32,44},{48,60},{64,76},{80,92},{96,108},{112,124},... | collective-permute-start | bytes 602120 | tf_op jit(solution)/shard_map/ppermute | solution.py:36
  4.7 1.4 %collective-permute-start.1 = (f32[128,392]{1,0:T(8,128)S(1)}, f32[128,392]{1,0:T(8,128)S(1)}, u32[]{:S(2)}, u32[]{:S(2)}) collective-permute-start(f32[128,392]{1,0:T(8,128)S(1)} %pad_maximum_fusion.1), channel_id=1, source_target_pairs={{0,8},{16,24},{32,40},{48,56},{64,72},{80,88},{96,104},{112,120},{... | collective-permute-start | bytes 602120 | tf_op jit(solution)/shard_map/ppermute | solution.py:36
  5.4 0.7 collective-permute-start.2
  6.2 2.7 %collective-permute-start.3 = (f32[128,392]{1,0:T(8,128)S(1)}, f32[128,392]{1,0:T(8,128)S(1)}, u32[]{:S(2)}, u32[]{:S(2)}) collective-permute-start(f32[128,392]{1,0:T(8,128)S(1)} %select_select_fusion.4), channel_id=1, source_target_pairs={{0,3},{4,7},{8,11},{12,15},{16,19},{20,23},{24,27},{28,31},{32,35}... | collective-permute-start | bytes 602120 | tf_op jit(solution)/shard_map/ppermute | solution.py:36
  6.9 2.0 %collective-permute-start.4 = (f32[128,392]{1,0:T(8,128)S(1)}, f32[128,392]{1,0:T(8,128)S(1)}, u32[]{:S(2)}, u32[]{:S(2)}) collective-permute-start(f32[128,392]{1,0:T(8,128)S(1)} %select_select_fusion.4), channel_id=1, source_target_pairs={{0,2},{4,6},{8,10},{12,14},{16,18},{20,22},{24,26},{28,30},{32,34}... | collective-permute-start | bytes 602120 | tf_op jit(solution)/shard_map/ppermute | solution.py:36
  7.6 40.6 %collective-permute-start.5 = (f32[128,392]{1,0:T(8,128)S(1)}, f32[128,392]{1,0:T(8,128)S(1)}, u32[]{:S(2)}, u32[]{:S(2)}) collective-permute-start(f32[128,392]{1,0:T(8,128)S(1)} %select_select_fusion.4), channel_id=1, source_target_pairs={{0,1},{4,5},{8,9},{12,13},{16,17},{20,21},{24,25},{28,29},{32,33},... | collective-permute-start | bytes 602120 | tf_op jit(solution)/shard_map/ppermute | solution.py:36
  48.4 2.1 %collective-permute-start.6 = (f32[640,128]{1,0:T(8,128)S(1)}, f32[640,128]{1,0:T(8,128)S(1)}, u32[]{:S(2)}, u32[]{:S(2)}) collective-permute-start(f32[640,128]{1,0:T(8,128)S(1)} %pad_maximum_fusion), channel_id=1, source_target_pairs={{0,384},{1,385},{2,386},{3,387},{4,388},{5,389},{6,390},{7,391},{8... | collective-permute-start | bytes 983048 | tf_op jit(solution)/shard_map/ppermute | solution.py:36
  49.1 1.4 %collective-permute-start.7 = (f32[640,128]{1,0:T(8,128)S(1)}, f32[640,128]{1,0:T(8,128)S(1)}, u32[]{:S(2)}, u32[]{:S(2)}) collective-permute-start(f32[640,128]{1,0:T(8,128)S(1)} %pad_maximum_fusion), channel_id=1, source_target_pairs={{0,256},{1,257},{2,258},{3,259},{4,260},{5,261},{6,262},{7,263},{8... | collective-permute-start | bytes 983048 | tf_op jit(solution)/shard_map/ppermute | solution.py:36
  49.8 0.7 collective-permute-start.8
  50.6 2.1 %collective-permute-start.10 = (f32[640,128]{1,0:T(8,128)S(1)}, f32[640,128]{1,0:T(8,128)S(1)}, u32[]{:S(2)}, u32[]{:S(2)}) collective-permute-start(f32[640,128]{1,0:T(8,128)S(1)} %select_select_fusion.2), channel_id=1, source_target_pairs={{0,64},{128,192},{256,320},{384,448},{1,65},{129,193},{257,321},{3... | collective-permute-start | bytes 983048 | tf_op jit(solution)/shard_map/ppermute | solution.py:36
  51.3 1.4 %collective-permute-start.11 = (f32[640,128]{1,0:T(8,128)S(1)}, f32[640,128]{1,0:T(8,128)S(1)}, u32[]{:S(2)}, u32[]{:S(2)}) collective-permute-start(f32[640,128]{1,0:T(8,128)S(1)} %select_select_fusion.2), channel_id=1, source_target_pairs={{0,32},{128,160},{256,288},{384,416},{1,33},{129,161},{257,289},{3... | collective-permute-start | bytes 983048 | tf_op jit(solution)/shard_map/ppermute | solution.py:36
  52.0 0.8 collective-permute-start.9
  52.8 26.2 %collective-permute-start.12 = (f32[640,128]{1,0:T(8,128)S(1)}, f32[640,128]{1,0:T(8,128)S(1)}, u32[]{:S(2)}, u32[]{:S(2)}) collective-permute-start(f32[640,128]{1,0:T(8,128)S(1)} %select_select_fusion.1), channel_id=1, source_target_pairs={{0,16},{32,48},{64,80},{96,112},{128,144},{160,176},{192,208},{224... | collective-permute-start | bytes 983048 | tf_op jit(solution)/shard_map/ppermute | solution.py:36
  79.0 1.0 %copy-start = (f32[4,1,128,2,1,128]{5,4,3,2,1,0:T(1,128)S(1)}, f32[4,1,128,2,1,128]{5,4,3,2,1,0:T(1,128)}, u32[]{:S(2)}) copy-start(f32[4,1,128,2,1,128]{5,4,3,2,1,0:T(1,128)} %param.4) | copy-start | bytes 1572868
  79.5 1.1 %copy-start.1 = (f32[264,128]{1,0:T(8,128)}, f32[264,128]{1,0:T(8,128)S(1)}, u32[]{:S(2)}) copy-start(f32[264,128]{1,0:T(8,128)S(1)} %fusion.6) | copy-start | bytes 405508
  80.1 0.7 copy-start.2
  81.1 0.7 slice-start

commit v9 on v6

--- a/solution.py
+++ b/solution.py
@@ -1,6 +1,7 @@
 import jax
 import jax.numpy as jnp
 from jax import lax
+from jax.experimental import pallas as pl
 from jax.sharding import PartitionSpec as P
 
 
@@ -40,6 +41,38 @@
     return block
 
 
+def _factor_kernel(block_ref, factor_ref, inverse_ref):
+    n = block_ref.shape[0]
+    rows = lax.broadcasted_iota(jnp.int32, (n, n), 0)
+    cols = lax.broadcasted_iota(jnp.int32, (n, n), 1)
+    upper = block_ref[...]
+    lower = jnp.where(rows == cols, jnp.float32(1.0), jnp.float32(0.0))
+    index = lax.broadcasted_iota(jnp.int32, (n, 1), 0)
+    for k in range(n):
+        pivot_upper = upper[k:k + 1, :]
+        pivot_lower = lower[k:k + 1, :]
+        scale = jnp.where(
+            index > k, upper[:, k:k + 1] / pivot_upper[:, k:k + 1], jnp.float32(0.0)
+        )
+        upper = upper - scale * pivot_upper
+        lower = lower - scale * pivot_lower
+    diagonal = jnp.sum(jnp.where(rows == cols, upper, 0.0), axis=1, keepdims=True)
+    root = jnp.sqrt(diagonal)
+    factor_ref[...] = jnp.where(rows <= cols, upper, 0.0) / root
+    inverse_ref[...] = lower / root
+
+
+def factor_and_invert(block):
+    n = block.shape[0]
+    return pl.pallas_call(
+        _factor_kernel,
+        out_shape=(
+            jax.ShapeDtypeStruct((n, n), jnp.float32),
+            jax.ShapeDtypeStruct((n, n), jnp.float32),
+        ),
+    )(block)
+
+
 def on_device(normal_matrix, right_sides):
     row_blocks, _, block, col_blocks, _, _ = normal_matrix.shape
     col_id = lax.axis_index("col")
@@ -48,12 +81,10 @@
     row_count = lax.axis_size("row")
     side_count = right_sides.shape[0]
     local = normal_matrix.reshape(row_blocks * block, col_blocks * block)
-    identity = jnp.eye(block, dtype=jnp.float32)
 
     def factor(corner_raw):
-        corner = jnp.linalg.cholesky(corner_raw)
-        inverse = jax.scipy.linalg.solve_triangular(corner, identity, lower=True)
-        return corner, inverse
+        corner_t, inverse = factor_and_invert(corner_raw)
+        return corner_t.T, inverse
 
     def skip(corner_raw):
         return jnp.zeros_like(corner_raw), jnp.zeros_like(corner_raw)

time: 81.2 us -> 72.6 us (0.89)
  the two profiles are of different devices: /device:TPU:1 before, /device:TPU:40 now
where the time goes in v9:
time: 72.6 us; the launch traced here: 71.9 us
  waiting for transfers between devices  33.1 us (46%)
  starting transfers between devices  29.4 us (40%)
  local copies, waits for them, and re-layouts  3.68 us (5%)
  other arithmetic  2.65 us (4%)
  matrix products  1.76 us (2%)
  between operations  1.27 us (2%)
    ppermute x19, waiting for transfers between devices, spread_wide(): arrived = lax.ppermute(block, axis, pairs)  33.1 us
    ppermute x19, starting transfers between devices, spread_wide(): arrived = lax.ppermute(block, axis, pairs)  20.5 us
    ppermute x5, starting transfers between devices, spread(): arrived = lax.ppermute(block, axis, pairs)  8.9 us
    unnamed x8, local copies, waits for them, and re-layouts  1.52 us
    select_n x1, other arithmetic, on_device(): jnp.where((global_cols == 0)[None, None, :, None], column[:, :, None, :],...  1.52 us
  transfers between devices with their start and end apart: 24, of which 3 were waited for; matrix products, arithmetic and copies ran while one was open for 2% of the time, Pallas kernels for 0%

profile of v9, /device:TPU:40, one launch (start us, length us, event | category | flops | bytes accessed | tf_op | source)
XLA Modules:
  0.0 71.9 jit_solution(14103628420583571189)
XLA Ops:
  0.6 1.1 %copy.18 = f32[64,8,2,128]{3,1,2,0:T(8,128)S(1)} copy(f32[64,8,2,128]{3,2,1,0:T(2,128)} %bitcast.28) | data formatting | bytes 1048576
  1.8 0.8 %collective-permute-start.5 = (f32[128,128]{1,0:T(8,128)S(1)}, f32[128,128]{1,0:T(8,128)S(1)}, u32[]{:S(2)}, u32[]{:S(2)}) collective-permute-start(f32[128,128]{1,0:T(8,128)S(1)} %get-tuple-element.9), channel_id=1, source_target_pairs={{0,12},{16,28},{32,44},{48,60},{64,76},{80,92},{96,108},{112,124},... | collective-permute-start | bytes 196616 | tf_op jit(solution)/shard_map/ppermute | solution.py:37
  4.0 0.7 collective-permute-start
  5.1 0.7 slice-done.1
  5.9 0.7 collective-permute-start.18
  8.0 1.3 %collective-permute-start.10 = (f32[128,128]{1,0:T(8,128)S(1)}, f32[128,128]{1,0:T(8,128)S(1)}, u32[]{:S(2)}, u32[]{:S(2)}) collective-permute-start(f32[128,128]{1,0:T(8,128)S(1)} %select_select_fusion.4), channel_id=1, source_target_pairs={{0,1},{4,5},{8,9},{12,13},{16,17},{20,21},{24,25},{28,29},{32,33},... | collective-permute-start | bytes 196616 | tf_op jit(solution)/shard_map/ppermute | solution.py:37
  9.4 1.3 %collective-permute-start.1 = (f32[512,128]{1,0:T(8,128)S(1)}, f32[512,128]{1,0:T(8,128)S(1)}, u32[]{:S(2)}, u32[]{:S(2)}) collective-permute-start(f32[512,128]{1,0:T(8,128)S(1)} %broadcast_select_fusion.3), channel_id=1, source_target_pairs={{0,128},{256,384},{1,129},{257,385},{2,130},{258,386},{3,131},{259... | collective-permute-start | bytes 786440 | tf_op jit(solution)/shard_map/ppermute | solution.py:16
  10.7 18.7 %collective-permute-done.10 = f32[128,128]{1,0:T(8,128)S(1)} collective-permute-done((f32[128,128]{1,0:T(8,128)S(1)}, f32[128,128]{1,0:T(8,128)S(1)}, u32[]{:S(2)}, u32[]{:S(2)}) %collective-permute-start.10) | collective-permute-done | bytes 65568 | tf_op jit(solution)/shard_map/ppermute | solution.py:37
  30.8 1.3 %collective-permute-start.13 = (f32[128,128]{1,0:T(8,128)S(1)}, f32[128,128]{1,0:T(8,128)S(1)}, u32[]{:S(2)}, u32[]{:S(2)}) collective-permute-start(f32[128,128]{1,0:T(8,128)S(1)} %select_select_fusion.3), channel_id=1, source_target_pairs={{0,128},{1,129},{2,130},{3,131},{4,132},{5,133},{6,134},{7,135},{8... | collective-permute-start | bytes 196616 | tf_op jit(solution)/shard_map/ppermute | solution.py:37
  32.1 4.3 %collective-permute-start.2 = (f32[512,128]{1,0:T(8,128)S(1)}, f32[512,128]{1,0:T(8,128)S(1)}, u32[]{:S(2)}, u32[]{:S(2)}) collective-permute-start(f32[512,128]{1,0:T(8,128)S(1)} %broadcast_select_fusion.4), channel_id=1, source_target_pairs={{0,64},{128,192},{256,320},{384,448},{1,65},{129,193},{257,321},{3... | collective-permute-start | bytes 786440 | tf_op jit(solution)/shard_map/ppermute | solution.py:16
  37.2 0.7 collective-permute-start.20
  37.9 2.3 %collective-permute-done.13 = f32[128,128]{1,0:T(8,128)S(1)} collective-permute-done((f32[128,128]{1,0:T(8,128)S(1)}, f32[128,128]{1,0:T(8,128)S(1)}, u32[]{:S(2)}, u32[]{:S(2)}) %collective-permute-start.13) | collective-permute-done | bytes 65568 | tf_op jit(solution)/shard_map/ppermute | solution.py:37
  40.2 1.3 %collective-permute-start.14 = (f32[128,128]{1,0:T(8,128)S(1)}, f32[128,128]{1,0:T(8,128)S(1)}, u32[]{:S(2)}, u32[]{:S(2)}) collective-permute-start(f32[128,128]{1,0:T(8,128)S(1)} %select_select_fusion.2), channel_id=1, source_target_pairs={{0,96},{128,224},{256,352},{384,480},{1,97},{129,225},{257,353},{3... | collective-permute-start | bytes 196616 | tf_op jit(solution)/shard_map/ppermute | solution.py:37
  41.6 4.6 %collective-permute-start.15 = (f32[128,128]{1,0:T(8,128)S(1)}, f32[128,128]{1,0:T(8,128)S(1)}, u32[]{:S(2)}, u32[]{:S(2)}) collective-permute-start(f32[128,128]{1,0:T(8,128)S(1)} %select_select_fusion.2), channel_id=1, source_target_pairs={{0,64},{128,192},{256,320},{384,448},{1,65},{129,193},{257,321},{3... | collective-permute-start | bytes 196616 | tf_op jit(solution)/shard_map/ppermute | solution.py:37
  46.2 1.3 %collective-permute-start.16 = (f32[128,128]{1,0:T(8,128)S(1)}, f32[128,128]{1,0:T(8,128)S(1)}, u32[]{:S(2)}, u32[]{:S(2)}) collective-permute-start(f32[128,128]{1,0:T(8,128)S(1)} %select_select_fusion.2), channel_id=1, source_target_pairs={{0,32},{128,160},{256,288},{384,416},{1,33},{129,161},{257,289},{3... | collective-permute-start | bytes 196616 | tf_op jit(solution)/shard_map/ppermute | solution.py:37
  47.6 1.3 %collective-permute-start.3 = (f32[512,128]{1,0:T(8,128)S(1)}, f32[512,128]{1,0:T(8,128)S(1)}, u32[]{:S(2)}, u32[]{:S(2)}) collective-permute-start(f32[512,128]{1,0:T(8,128)S(1)} %broadcast_select_fusion.5), channel_id=1, source_target_pairs={{0,32},{64,96},{128,160},{192,224},{256,288},{320,352},{384,416},{... | collective-permute-start | bytes 786440 | tf_op jit(solution)/shard_map/ppermute | solution.py:16
  48.9 0.7 collective-permute-start.21
  49.6 0.7 collective-permute-start.22
  50.3 1.3 %collective-permute-start.23 = (f32[128,264]{1,0:T(8,128)S(1)}, f32[128,264]{1,0:T(8,128)S(1)}, u32[]{:S(2)}, u32[]{:S(2)}) collective-permute-start(f32[128,264]{1,0:T(8,128)S(1)} %select_select_fusion), channel_id=1, source_target_pairs={{0,1},{4,5},{8,9},{12,13},{16,17},{20,21},{24,25},{28,29},{32,33},... | collective-permute-start | bytes 405512 | tf_op jit(solution)/shard_map/ppermute | solution.py:37
  51.6 1.3 %collective-permute-start.17 = (f32[128,128]{1,0:T(8,128)S(1)}, f32[128,128]{1,0:T(8,128)S(1)}, u32[]{:S(2)}, u32[]{:S(2)}) collective-permute-start(f32[128,128]{1,0:T(8,128)S(1)} %select_select_fusion.1), channel_id=1, source_target_pairs={{0,16},{32,48},{64,80},{96,112},{128,144},{160,176},{192,208},{224... | collective-permute-start | bytes 196616 | tf_op jit(solution)/shard_map/ppermute | solution.py:37
  53.0 1.3 %collective-permute-start.4 = (f32[512,128]{1,0:T(8,128)S(1)}, f32[512,128]{1,0:T(8,128)S(1)}, u32[]{:S(2)}, u32[]{:S(2)}) collective-permute-start(f32[512,128]{1,0:T(8,128)S(1)} %broadcast_select_fusion.6), channel_id=1, source_target_pairs={{0,16},{32,48},{64,80},{96,112},{128,144},{160,176},{192,208},{224... | collective-permute-start | bytes 786440 | tf_op jit(solution)/shard_map/ppermute | solution.py:16
  54.5 12.0 %collective-permute-done.23 = f32[128,264]{1,0:T(8,128)S(1)} collective-permute-done((f32[128,264]{1,0:T(8,128)S(1)}, f32[128,264]{1,0:T(8,128)S(1)}, u32[]{:S(2)}, u32[]{:S(2)}) %collective-permute-start.23) | collective-permute-done | bytes 135200 | tf_op jit(solution)/shard_map/ppermute | solution.py:37
  69.7 0.7 broadcast_select_fusion.7
  70.4 1.5 %broadcast_select_fusion = f32[4,1,128,2,1,128]{5,4,3,2,1,0:T(1,128)} fusion(pred[2]{0:T(512)(128)(4,1)S(1)} %fusion.13, f32[4,1,128,2,1,128]{5,4,3,2,1,0:T(1,128)S(1)} %bitcast.33, pred[4,2]{1,0:T(4,128)(4,1)S(1)} %broadcast_and_fusion, f32[4,128,128]{2,1,0:T(8,128)S(1)} %broadcast_select_fusion.2), kind=kLoop, calls=%fused_computation.3 | loop fusion | flops 262144 | bytes 1310730 | tf_op jit(solution)/shard_map/jit(_where)/select_n | solution.py:122
  (65 shorter events, 8.9 us)
Async XLA Ops:
  1.8 4.8 %collective-permute-start.5 = (f32[128,128]{1,0:T(8,128)S(1)}, f32[128,128]{1,0:T(8,128)S(1)}, u32[]{:S(2)}, u32[]{:S(2)}) collective-permute-start(f32[128,128]{1,0:T(8,128)S(1)} %get-tuple-element.9), channel_id=1, source_target_pairs={{0,12},{16,28},{32,44},{48,60},{64,76},{80,92},{96,108},{112,124},... | collective-permute-start | bytes 196616 | tf_op jit(solution)/shard_map/ppermute | solution.py:37
  2.6 4.0 %collective-permute-start.6 = (f32[128,128]{1,0:T(8,128)S(1)}, f32[128,128]{1,0:T(8,128)S(1)}, u32[]{:S(2)}, u32[]{:S(2)}) collective-permute-start(f32[128,128]{1,0:T(8,128)S(1)} %get-tuple-element.9), channel_id=1, source_target_pairs={{0,8},{16,24},{32,40},{48,56},{64,72},{80,88},{96,104},{112,120},{... | collective-permute-start | bytes 196616 | tf_op jit(solution)/shard_map/ppermute | solution.py:37
  3.3 3.4 %collective-permute-start.7 = (f32[128,128]{1,0:T(8,128)S(1)}, f32[128,128]{1,0:T(8,128)S(1)}, u32[]{:S(2)}, u32[]{:S(2)}) collective-permute-start(f32[128,128]{1,0:T(8,128)S(1)} %get-tuple-element.9), channel_id=1, source_target_pairs={{0,4},{16,20},{32,36},{48,52},{64,68},{80,84},{96,100},{112,116},{... | collective-permute-start | bytes 196616 | tf_op jit(solution)/shard_map/ppermute | solution.py:37
  4.0 5.3 %collective-permute-start = (f32[512,128]{1,0:T(8,128)S(1)}, f32[512,128]{1,0:T(8,128)S(1)}, u32[]{:S(2)}, u32[]{:S(2)}) collective-permute-start(f32[512,128]{1,0:T(8,128)S(1)} %slice.30), channel_id=1, source_target_pairs={{0,256},{1,257},{2,258},{3,259},{4,260},{5,261},{6,262},{7,263},{8... | collective-permute-start | bytes 786440 | tf_op jit(solution)/shard_map/ppermute | solution.py:16
  5.9 40.4 %collective-permute-start.18 = (f32[128,264]{1,0:T(8,128)S(1)}, f32[128,264]{1,0:T(8,128)S(1)}, u32[]{:S(2)}, u32[]{:S(2)}) collective-permute-start(f32[128,264]{1,0:T(8,128)S(1)} %pad_maximum_fusion), channel_id=1, source_target_pairs={{0,12},{16,28},{32,44},{48,60},{64,76},{80,92},{96,108},{112,124},... | collective-permute-start | bytes 405512 | tf_op jit(solution)/shard_map/ppermute | solution.py:37
  6.7 4.0 %collective-permute-start.8 = (f32[128,128]{1,0:T(8,128)S(1)}, f32[128,128]{1,0:T(8,128)S(1)}, u32[]{:S(2)}, u32[]{:S(2)}) collective-permute-start(f32[128,128]{1,0:T(8,128)S(1)} %select_select_fusion.4), channel_id=1, source_target_pairs={{0,3},{4,7},{8,11},{12,15},{16,19},{20,23},{24,27},{28,31},{32,35}... | collective-permute-start | bytes 196616 | tf_op jit(solution)/shard_map/ppermute | solution.py:37
  7.3 3.4 %collective-permute-start.9 = (f32[128,128]{1,0:T(8,128)S(1)}, f32[128,128]{1,0:T(8,128)S(1)}, u32[]{:S(2)}, u32[]{:S(2)}) collective-permute-start(f32[128,128]{1,0:T(8,128)S(1)} %select_select_fusion.4), channel_id=1, source_target_pairs={{0,2},{4,6},{8,10},{12,14},{16,18},{20,22},{24,26},{28,30},{32,34}... | collective-permute-start | bytes 196616 | tf_op jit(solution)/shard_map/ppermute | solution.py:37
  8.0 21.4 %collective-permute-start.10 = (f32[128,128]{1,0:T(8,128)S(1)}, f32[128,128]{1,0:T(8,128)S(1)}, u32[]{:S(2)}, u32[]{:S(2)}) collective-permute-start(f32[128,128]{1,0:T(8,128)S(1)} %select_select_fusion.4), channel_id=1, source_target_pairs={{0,1},{4,5},{8,9},{12,13},{16,17},{20,21},{24,25},{28,29},{32,33},... | collective-permute-start | bytes 196616 | tf_op jit(solution)/shard_map/ppermute | solution.py:37
  9.4 22.7 %collective-permute-start.1 = (f32[512,128]{1,0:T(8,128)S(1)}, f32[512,128]{1,0:T(8,128)S(1)}, u32[]{:S(2)}, u32[]{:S(2)}) collective-permute-start(f32[512,128]{1,0:T(8,128)S(1)} %broadcast_select_fusion.3), channel_id=1, source_target_pairs={{0,128},{256,384},{1,129},{257,385},{2,130},{258,386},{3,131},{259... | collective-permute-start | bytes 786440 | tf_op jit(solution)/shard_map/ppermute | solution.py:16
  29.4 7.1 %collective-permute-start.11 = (f32[128,128]{1,0:T(8,128)S(1)}, f32[128,128]{1,0:T(8,128)S(1)}, u32[]{:S(2)}, u32[]{:S(2)}) collective-permute-start(f32[128,128]{1,0:T(8,128)S(1)} %select_select_fusion.3), channel_id=1, source_target_pairs={{0,384},{1,385},{2,386},{3,387},{4,388},{5,389},{6,390},{7,391},{8... | collective-permute-start | bytes 196616 | tf_op jit(solution)/shard_map/ppermute | solution.py:37
  30.1 7.1 %collective-permute-start.12 = (f32[128,128]{1,0:T(8,128)S(1)}, f32[128,128]{1,0:T(8,128)S(1)}, u32[]{:S(2)}, u32[]{:S(2)}) collective-permute-start(f32[128,128]{1,0:T(8,128)S(1)} %select_select_fusion.3), channel_id=1, source_target_pairs={{0,256},{1,257},{2,258},{3,259},{4,260},{5,261},{6,262},{7,263},{8... | collective-permute-start | bytes 196616 | tf_op jit(solution)/shard_map/ppermute | solution.py:37
  30.8 9.5 %collective-permute-start.13 = (f32[128,128]{1,0:T(8,128)S(1)}, f32[128,128]{1,0:T(8,128)S(1)}, u32[]{:S(2)}, u32[]{:S(2)}) collective-permute-start(f32[128,128]{1,0:T(8,128)S(1)} %select_select_fusion.3), channel_id=1, source_target_pairs={{0,128},{1,129},{2,130},{3,131},{4,132},{5,133},{6,134},{7,135},{8... | collective-permute-start | bytes 196616 | tf_op jit(solution)/shard_map/ppermute | solution.py:37
  32.1 9.4 %collective-permute-start.2 = (f32[512,128]{1,0:T(8,128)S(1)}, f32[512,128]{1,0:T(8,128)S(1)}, u32[]{:S(2)}, u32[]{:S(2)}) collective-permute-start(f32[512,128]{1,0:T(8,128)S(1)} %broadcast_select_fusion.4), channel_id=1, source_target_pairs={{0,64},{128,192},{256,320},{384,448},{1,65},{129,193},{257,321},{3... | collective-permute-start | bytes 786440 | tf_op jit(solution)/shard_map/ppermute | solution.py:16
  36.5 11.0 %collective-permute-start.19 = (f32[128,264]{1,0:T(8,128)S(1)}, f32[128,264]{1,0:T(8,128)S(1)}, u32[]{:S(2)}, u32[]{:S(2)}) collective-permute-start(f32[128,264]{1,0:T(8,128)S(1)} %pad_maximum_fusion), channel_id=1, source_target_pairs={{0,8},{16,24},{32,40},{48,56},{64,72},{80,88},{96,104},{112,120},{... | collective-permute-start | bytes 405512 | tf_op jit(solution)/shard_map/ppermute | solution.py:37
  37.2 11.7 %collective-permute-start.20 = (f32[128,264]{1,0:T(8,128)S(1)}, f32[128,264]{1,0:T(8,128)S(1)}, u32[]{:S(2)}, u32[]{:S(2)}) collective-permute-start(f32[128,264]{1,0:T(8,128)S(1)} %pad_maximum_fusion), channel_id=1, source_target_pairs={{0,4},{16,20},{32,36},{48,52},{64,68},{80,84},{96,100},{112,116},{... | collective-permute-start | bytes 405512 | tf_op jit(solution)/shard_map/ppermute | solution.py:37
  40.2 9.4 %collective-permute-start.14 = (f32[128,128]{1,0:T(8,128)S(1)}, f32[128,128]{1,0:T(8,128)S(1)}, u32[]{:S(2)}, u32[]{:S(2)}) collective-permute-start(f32[128,128]{1,0:T(8,128)S(1)} %select_select_fusion.2), channel_id=1, source_target_pairs={{0,96},{128,224},{256,352},{384,480},{1,97},{129,225},{257,353},{3... | collective-permute-start | bytes 196616 | tf_op jit(solution)/shard_map/ppermute | solution.py:37
  41.6 8.7 %collective-permute-start.15 = (f32[128,128]{1,0:T(8,128)S(1)}, f32[128,128]{1,0:T(8,128)S(1)}, u32[]{:S(2)}, u32[]{:S(2)}) collective-permute-start(f32[128,128]{1,0:T(8,128)S(1)} %select_select_fusion.2), channel_id=1, source_target_pairs={{0,64},{128,192},{256,320},{384,448},{1,65},{129,193},{257,321},{3... | collective-permute-start | bytes 196616 | tf_op jit(solution)/shard_map/ppermute | solution.py:37
  46.2 5.4 %collective-permute-start.16 = (f32[128,128]{1,0:T(8,128)S(1)}, f32[128,128]{1,0:T(8,128)S(1)}, u32[]{:S(2)}, u32[]{:S(2)}) collective-permute-start(f32[128,128]{1,0:T(8,128)S(1)} %select_select_fusion.2), channel_id=1, source_target_pairs={{0,32},{128,160},{256,288},{384,416},{1,33},{129,161},{257,289},{3... | collective-permute-start | bytes 196616 | tf_op jit(solution)/shard_map/ppermute | solution.py:37
  47.6 5.4 %collective-permute-start.3 = (f32[512,128]{1,0:T(8,128)S(1)}, f32[512,128]{1,0:T(8,128)S(1)}, u32[]{:S(2)}, u32[]{:S(2)}) collective-permute-start(f32[512,128]{1,0:T(8,128)S(1)} %broadcast_select_fusion.5), channel_id=1, source_target_pairs={{0,32},{64,96},{128,160},{192,224},{256,288},{320,352},{384,416},{... | collective-permute-start | bytes 786440 | tf_op jit(solution)/shard_map/ppermute | solution.py:16
  48.9 5.5 %collective-permute-start.21 = (f32[128,264]{1,0:T(8,128)S(1)}, f32[128,264]{1,0:T(8,128)S(1)}, u32[]{:S(2)}, u32[]{:S(2)}) collective-permute-start(f32[128,264]{1,0:T(8,128)S(1)} %select_select_fusion), channel_id=1, source_target_pairs={{0,3},{4,7},{8,11},{12,15},{16,19},{20,23},{24,27},{28,31},{32,35}... | collective-permute-start | bytes 405512 | tf_op jit(solution)/shard_map/ppermute | solution.py:37
  49.6 4.8 %collective-permute-start.22 = (f32[128,264]{1,0:T(8,128)S(1)}, f32[128,264]{1,0:T(8,128)S(1)}, u32[]{:S(2)}, u32[]{:S(2)}) collective-permute-start(f32[128,264]{1,0:T(8,128)S(1)} %select_select_fusion), channel_id=1, source_target_pairs={{0,2},{4,6},{8,10},{12,14},{16,18},{20,22},{24,26},{28,30},{32,34}... | collective-permute-start | bytes 405512 | tf_op jit(solution)/shard_map/ppermute | solution.py:37
  50.3 16.2 %collective-permute-start.23 = (f32[128,264]{1,0:T(8,128)S(1)}, f32[128,264]{1,0:T(8,128)S(1)}, u32[]{:S(2)}, u32[]{:S(2)}) collective-permute-start(f32[128,264]{1,0:T(8,128)S(1)} %select_select_fusion), channel_id=1, source_target_pairs={{0,1},{4,5},{8,9},{12,13},{16,17},{20,21},{24,25},{28,29},{32,33},... | collective-permute-start | bytes 405512 | tf_op jit(solution)/shard_map/ppermute | solution.py:37
  51.6 14.8 %collective-permute-start.17 = (f32[128,128]{1,0:T(8,128)S(1)}, f32[128,128]{1,0:T(8,128)S(1)}, u32[]{:S(2)}, u32[]{:S(2)}) collective-permute-start(f32[128,128]{1,0:T(8,128)S(1)} %select_select_fusion.1), channel_id=1, source_target_pairs={{0,16},{32,48},{64,80},{96,112},{128,144},{160,176},{192,208},{224... | collective-permute-start | bytes 196616 | tf_op jit(solution)/shard_map/ppermute | solution.py:37
  53.0 14.0 %collective-permute-start.4 = (f32[512,128]{1,0:T(8,128)S(1)}, f32[512,128]{1,0:T(8,128)S(1)}, u32[]{:S(2)}, u32[]{:S(2)}) collective-permute-start(f32[512,128]{1,0:T(8,128)S(1)} %broadcast_select_fusion.6), channel_id=1, source_target_pairs={{0,16},{32,48},{64,80},{96,112},{128,144},{160,176},{192,208},{224... | collective-permute-start | bytes 786440 | tf_op jit(solution)/shard_map/ppermute | solution.py:16
  (5 other events, 6.4 us)

commit v10 on v9

--- a/solution.py
+++ b/solution.py
@@ -43,19 +43,30 @@
 
 def _factor_kernel(block_ref, factor_ref, inverse_ref):
     n = block_ref.shape[0]
+    tile = 8
+    upper = [block_ref[t * tile:(t + 1) * tile, :] for t in range(n // tile)]
+    tile_rows = lax.broadcasted_iota(jnp.int32, (tile, n), 0)
+    tile_cols = lax.broadcasted_iota(jnp.int32, (tile, n), 1)
+    lower = [
+        jnp.where(tile_rows + t * tile == tile_cols, jnp.float32(1.0), jnp.float32(0.0))
+        for t in range(n // tile)
+    ]
+    index = lax.broadcasted_iota(jnp.int32, (tile, 1), 0)
+    for k in range(n):
+        first = k // tile
+        pivot_upper = upper[first][k % tile:k % tile + 1, :]
+        pivot_lower = lower[first][k % tile:k % tile + 1, :]
+        reciprocal = 1.0 / pivot_upper[:, k:k + 1]
+        for t in range(first, n // tile):
+            scale = upper[t][:, k:k + 1] * reciprocal
+            if t == first:
+                scale = jnp.where(index + t * tile > k, scale, jnp.float32(0.0))
+            upper[t] = upper[t] - scale * pivot_upper
+            lower[t] = lower[t] - scale * pivot_lower
+    upper = jnp.concatenate(upper, axis=0)
+    lower = jnp.concatenate(lower, axis=0)
     rows = lax.broadcasted_iota(jnp.int32, (n, n), 0)
     cols = lax.broadcasted_iota(jnp.int32, (n, n), 1)
-    upper = block_ref[...]
-    lower = jnp.where(rows == cols, jnp.float32(1.0), jnp.float32(0.0))
-    index = lax.broadcasted_iota(jnp.int32, (n, 1), 0)
-    for k in range(n):
-        pivot_upper = upper[k:k + 1, :]
-        pivot_lower = lower[k:k + 1, :]
-        scale = jnp.where(
-            index > k, upper[:, k:k + 1] / pivot_upper[:, k:k + 1], jnp.float32(0.0)
-        )
-        upper = upper - scale * pivot_upper
-        lower = lower - scale * pivot_lower
     diagonal = jnp.sum(jnp.where(rows == cols, upper, 0.0), axis=1, keepdims=True)
     root = jnp.sqrt(diagonal)
     factor_ref[...] = jnp.where(rows <= cols, upper, 0.0) / root

time: 72.6 us -> 72.6 us (level)
  no operation moved by 1% of the time
where the time goes in v10:
time: 72.6 us; the launch traced here: 71.9 us
  waiting for transfers between devices  33.1 us (46%)
  starting transfers between devices  29.4 us (40%)
  local copies, waits for them, and re-layouts  3.68 us (5%)
  other arithmetic  2.65 us (4%)
  matrix products  1.76 us (2%)
  between operations  1.27 us (2%)
    ppermute x19, waiting for transfers between devices, spread_wide(): arrived = lax.ppermute(block, axis, pairs)  33.1 us
    ppermute x19, starting transfers between devices, spread_wide(): arrived = lax.ppermute(block, axis, pairs)  20.5 us
    ppermute x5, starting transfers between devices, spread(): arrived = lax.ppermute(block, axis, pairs)  8.9 us
    unnamed x8, local copies, waits for them, and re-layouts  1.52 us
    select_n x1, other arithmetic, on_device(): jnp.where((global_cols == 0)[None, None, :, None], column[:, :, None, :],...  1.52 us
  transfers between devices with their start and end apart: 24, of which 3 were waited for; matrix products, arithmetic and copies ran while one was open for 2% of the time, Pallas kernels for 0%

profile of v10, /device:TPU:40, one launch (start us, length us, event | category | flops | bytes accessed | tf_op | source)
XLA Modules:
  0.0 71.9 jit_solution(2032116719225906920)
XLA Ops:
  0.6 1.1 %copy.18 = f32[64,8,2,128]{3,1,2,0:T(8,128)S(1)} copy(f32[64,8,2,128]{3,2,1,0:T(2,128)} %bitcast.28) | data formatting | bytes 1048576
  1.8 0.8 %collective-permute-start.5 = (f32[128,128]{1,0:T(8,128)S(1)}, f32[128,128]{1,0:T(8,128)S(1)}, u32[]{:S(2)}, u32[]{:S(2)}) collective-permute-start(f32[128,128]{1,0:T(8,128)S(1)} %get-tuple-element.9), channel_id=1, source_target_pairs={{0,12},{16,28},{32,44},{48,60},{64,76},{80,92},{96,108},{112,124},... | collective-permute-start | bytes 196616 | tf_op jit(solution)/shard_map/ppermute | solution.py:37
  4.0 0.7 collective-permute-start
  5.1 0.7 slice-done.1
  5.9 0.7 collective-permute-start.18
  8.0 1.3 %collective-permute-start.10 = (f32[128,128]{1,0:T(8,128)S(1)}, f32[128,128]{1,0:T(8,128)S(1)}, u32[]{:S(2)}, u32[]{:S(2)}) collective-permute-start(f32[128,128]{1,0:T(8,128)S(1)} %select_select_fusion.4), channel_id=1, source_target_pairs={{0,1},{4,5},{8,9},{12,13},{16,17},{20,21},{24,25},{28,29},{32,33},... | collective-permute-start | bytes 196616 | tf_op jit(solution)/shard_map/ppermute | solution.py:37
  9.4 1.3 %collective-permute-start.1 = (f32[512,128]{1,0:T(8,128)S(1)}, f32[512,128]{1,0:T(8,128)S(1)}, u32[]{:S(2)}, u32[]{:S(2)}) collective-permute-start(f32[512,128]{1,0:T(8,128)S(1)} %broadcast_select_fusion.3), channel_id=1, source_target_pairs={{0,128},{256,384},{1,129},{257,385},{2,130},{258,386},{3,131},{259... | collective-permute-start | bytes 786440 | tf_op jit(solution)/shard_map/ppermute | solution.py:16
  10.7 18.7 %collective-permute-done.10 = f32[128,128]{1,0:T(8,128)S(1)} collective-permute-done((f32[128,128]{1,0:T(8,128)S(1)}, f32[128,128]{1,0:T(8,128)S(1)}, u32[]{:S(2)}, u32[]{:S(2)}) %collective-permute-start.10) | collective-permute-done | bytes 65568 | tf_op jit(solution)/shard_map/ppermute | solution.py:37
  30.8 1.3 %collective-permute-start.13 = (f32[128,128]{1,0:T(8,128)S(1)}, f32[128,128]{1,0:T(8,128)S(1)}, u32[]{:S(2)}, u32[]{:S(2)}) collective-permute-start(f32[128,128]{1,0:T(8,128)S(1)} %select_select_fusion.3), channel_id=1, source_target_pairs={{0,128},{1,129},{2,130},{3,131},{4,132},{5,133},{6,134},{7,135},{8... | collective-permute-start | bytes 196616 | tf_op jit(solution)/shard_map/ppermute | solution.py:37
  32.1 4.3 %collective-permute-start.2 = (f32[512,128]{1,0:T(8,128)S(1)}, f32[512,128]{1,0:T(8,128)S(1)}, u32[]{:S(2)}, u32[]{:S(2)}) collective-permute-start(f32[512,128]{1,0:T(8,128)S(1)} %broadcast_select_fusion.4), channel_id=1, source_target_pairs={{0,64},{128,192},{256,320},{384,448},{1,65},{129,193},{257,321},{3... | collective-permute-start | bytes 786440 | tf_op jit(solution)/shard_map/ppermute | solution.py:16
  37.2 0.7 collective-permute-start.20
  37.9 2.3 %collective-permute-done.13 = f32[128,128]{1,0:T(8,128)S(1)} collective-permute-done((f32[128,128]{1,0:T(8,128)S(1)}, f32[128,128]{1,0:T(8,128)S(1)}, u32[]{:S(2)}, u32[]{:S(2)}) %collective-permute-start.13) | collective-permute-done | bytes 65568 | tf_op jit(solution)/shard_map/ppermute | solution.py:37
  40.2 1.3 %collective-permute-start.14 = (f32[128,128]{1,0:T(8,128)S(1)}, f32[128,128]{1,0:T(8,128)S(1)}, u32[]{:S(2)}, u32[]{:S(2)}) collective-permute-start(f32[128,128]{1,0:T(8,128)S(1)} %select_select_fusion.2), channel_id=1, source_target_pairs={{0,96},{128,224},{256,352},{384,480},{1,97},{129,225},{257,353},{3... | collective-permute-start | bytes 196616 | tf_op jit(solution)/shard_map/ppermute | solution.py:37
  41.6 4.6 %collective-permute-start.15 = (f32[128,128]{1,0:T(8,128)S(1)}, f32[128,128]{1,0:T(8,128)S(1)}, u32[]{:S(2)}, u32[]{:S(2)}) collective-permute-start(f32[128,128]{1,0:T(8,128)S(1)} %select_select_fusion.2), channel_id=1, source_target_pairs={{0,64},{128,192},{256,320},{384,448},{1,65},{129,193},{257,321},{3... | collective-permute-start | bytes 196616 | tf_op jit(solution)/shard_map/ppermute | solution.py:37
  46.2 1.3 %collective-permute-start.16 = (f32[128,128]{1,0:T(8,128)S(1)}, f32[128,128]{1,0:T(8,128)S(1)}, u32[]{:S(2)}, u32[]{:S(2)}) collective-permute-start(f32[128,128]{1,0:T(8,128)S(1)} %select_select_fusion.2), channel_id=1, source_target_pairs={{0,32},{128,160},{256,288},{384,416},{1,33},{129,161},{257,289},{3... | collective-permute-start | bytes 196616 | tf_op jit(solution)/shard_map/ppermute | solution.py:37
  47.6 1.3 %collective-permute-start.3 = (f32[512,128]{1,0:T(8,128)S(1)}, f32[512,128]{1,0:T(8,128)S(1)}, u32[]{:S(2)}, u32[]{:S(2)}) collective-permute-start(f32[512,128]{1,0:T(8,128)S(1)} %broadcast_select_fusion.5), channel_id=1, source_target_pairs={{0,32},{64,96},{128,160},{192,224},{256,288},{320,352},{384,416},{... | collective-permute-start | bytes 786440 | tf_op jit(solution)/shard_map/ppermute | solution.py:16
  48.9 0.7 collective-permute-start.21
  49.6 0.7 collective-permute-start.22
  50.3 1.3 %collective-permute-start.23 = (f32[128,264]{1,0:T(8,128)S(1)}, f32[128,264]{1,0:T(8,128)S(1)}, u32[]{:S(2)}, u32[]{:S(2)}) collective-permute-start(f32[128,264]{1,0:T(8,128)S(1)} %select_select_fusion), channel_id=1, source_target_pairs={{0,1},{4,5},{8,9},{12,13},{16,17},{20,21},{24,25},{28,29},{32,33},... | collective-permute-start | bytes 405512 | tf_op jit(solution)/shard_map/ppermute | solution.py:37
  51.6 1.3 %collective-permute-start.17 = (f32[128,128]{1,0:T(8,128)S(1)}, f32[128,128]{1,0:T(8,128)S(1)}, u32[]{:S(2)}, u32[]{:S(2)}) collective-permute-start(f32[128,128]{1,0:T(8,128)S(1)} %select_select_fusion.1), channel_id=1, source_target_pairs={{0,16},{32,48},{64,80},{96,112},{128,144},{160,176},{192,208},{224... | collective-permute-start | bytes 196616 | tf_op jit(solution)/shard_map/ppermute | solution.py:37
  53.0 1.3 %collective-permute-start.4 = (f32[512,128]{1,0:T(8,128)S(1)}, f32[512,128]{1,0:T(8,128)S(1)}, u32[]{:S(2)}, u32[]{:S(2)}) collective-permute-start(f32[512,128]{1,0:T(8,128)S(1)} %broadcast_select_fusion.6), channel_id=1, source_target_pairs={{0,16},{32,48},{64,80},{96,112},{128,144},{160,176},{192,208},{224... | collective-permute-start | bytes 786440 | tf_op jit(solution)/shard_map/ppermute | solution.py:16
  54.5 12.0 %collective-permute-done.23 = f32[128,264]{1,0:T(8,128)S(1)} collective-permute-done((f32[128,264]{1,0:T(8,128)S(1)}, f32[128,264]{1,0:T(8,128)S(1)}, u32[]{:S(2)}, u32[]{:S(2)}) %collective-permute-start.23) | collective-permute-done | bytes 135200 | tf_op jit(solution)/shard_map/ppermute | solution.py:37
  69.7 0.7 broadcast_select_fusion.7
  70.4 1.5 %broadcast_select_fusion = f32[4,1,128,2,1,128]{5,4,3,2,1,0:T(1,128)} fusion(pred[2]{0:T(512)(128)(4,1)S(1)} %fusion.13, f32[4,1,128,2,1,128]{5,4,3,2,1,0:T(1,128)S(1)} %bitcast.33, pred[4,2]{1,0:T(4,128)(4,1)S(1)} %broadcast_and_fusion, f32[4,128,128]{2,1,0:T(8,128)S(1)} %broadcast_select_fusion.2), kind=kLoop, calls=%fused_computation.3 | loop fusion | flops 262144 | bytes 1310730 | tf_op jit(solution)/shard_map/jit(_where)/select_n | solution.py:133
  (65 shorter events, 8.9 us)
Async XLA Ops:
  1.8 4.8 %collective-permute-start.5 = (f32[128,128]{1,0:T(8,128)S(1)}, f32[128,128]{1,0:T(8,128)S(1)}, u32[]{:S(2)}, u32[]{:S(2)}) collective-permute-start(f32[128,128]{1,0:T(8,128)S(1)} %get-tuple-element.9), channel_id=1, source_target_pairs={{0,12},{16,28},{32,44},{48,60},{64,76},{80,92},{96,108},{112,124},... | collective-permute-start | bytes 196616 | tf_op jit(solution)/shard_map/ppermute | solution.py:37
  2.6 4.0 %collective-permute-start.6 = (f32[128,128]{1,0:T(8,128)S(1)}, f32[128,128]{1,0:T(8,128)S(1)}, u32[]{:S(2)}, u32[]{:S(2)}) collective-permute-start(f32[128,128]{1,0:T(8,128)S(1)} %get-tuple-element.9), channel_id=1, source_target_pairs={{0,8},{16,24},{32,40},{48,56},{64,72},{80,88},{96,104},{112,120},{... | collective-permute-start | bytes 196616 | tf_op jit(solution)/shard_map/ppermute | solution.py:37
  3.3 3.4 %collective-permute-start.7 = (f32[128,128]{1,0:T(8,128)S(1)}, f32[128,128]{1,0:T(8,128)S(1)}, u32[]{:S(2)}, u32[]{:S(2)}) collective-permute-start(f32[128,128]{1,0:T(8,128)S(1)} %get-tuple-element.9), channel_id=1, source_target_pairs={{0,4},{16,20},{32,36},{48,52},{64,68},{80,84},{96,100},{112,116},{... | collective-permute-start | bytes 196616 | tf_op jit(solution)/shard_map/ppermute | solution.py:37
  4.0 5.3 %collective-permute-start = (f32[512,128]{1,0:T(8,128)S(1)}, f32[512,128]{1,0:T(8,128)S(1)}, u32[]{:S(2)}, u32[]{:S(2)}) collective-permute-start(f32[512,128]{1,0:T(8,128)S(1)} %slice.30), channel_id=1, source_target_pairs={{0,256},{1,257},{2,258},{3,259},{4,260},{5,261},{6,262},{7,263},{8... | collective-permute-start | bytes 786440 | tf_op jit(solution)/shard_map/ppermute | solution.py:16
  5.9 40.4 %collective-permute-start.18 = (f32[128,264]{1,0:T(8,128)S(1)}, f32[128,264]{1,0:T(8,128)S(1)}, u32[]{:S(2)}, u32[]{:S(2)}) collective-permute-start(f32[128,264]{1,0:T(8,128)S(1)} %pad_maximum_fusion), channel_id=1, source_target_pairs={{0,12},{16,28},{32,44},{48,60},{64,76},{80,92},{96,108},{112,124},... | collective-permute-start | bytes 405512 | tf_op jit(solution)/shard_map/ppermute | solution.py:37
  6.7 4.0 %collective-permute-start.8 = (f32[128,128]{1,0:T(8,128)S(1)}, f32[128,128]{1,0:T(8,128)S(1)}, u32[]{:S(2)}, u32[]{:S(2)}) collective-permute-start(f32[128,128]{1,0:T(8,128)S(1)} %select_select_fusion.4), channel_id=1, source_target_pairs={{0,3},{4,7},{8,11},{12,15},{16,19},{20,23},{24,27},{28,31},{32,35}... | collective-permute-start | bytes 196616 | tf_op jit(solution)/shard_map/ppermute | solution.py:37
  7.3 3.4 %collective-permute-start.9 = (f32[128,128]{1,0:T(8,128)S(1)}, f32[128,128]{1,0:T(8,128)S(1)}, u32[]{:S(2)}, u32[]{:S(2)}) collective-permute-start(f32[128,128]{1,0:T(8,128)S(1)} %select_select_fusion.4), channel_id=1, source_target_pairs={{0,2},{4,6},{8,10},{12,14},{16,18},{20,22},{24,26},{28,30},{32,34}... | collective-permute-start | bytes 196616 | tf_op jit(solution)/shard_map/ppermute | solution.py:37
  8.0 21.4 %collective-permute-start.10 = (f32[128,128]{1,0:T(8,128)S(1)}, f32[128,128]{1,0:T(8,128)S(1)}, u32[]{:S(2)}, u32[]{:S(2)}) collective-permute-start(f32[128,128]{1,0:T(8,128)S(1)} %select_select_fusion.4), channel_id=1, source_target_pairs={{0,1},{4,5},{8,9},{12,13},{16,17},{20,21},{24,25},{28,29},{32,33},... | collective-permute-start | bytes 196616 | tf_op jit(solution)/shard_map/ppermute | solution.py:37
  9.4 22.7 %collective-permute-start.1 = (f32[512,128]{1,0:T(8,128)S(1)}, f32[512,128]{1,0:T(8,128)S(1)}, u32[]{:S(2)}, u32[]{:S(2)}) collective-permute-start(f32[512,128]{1,0:T(8,128)S(1)} %broadcast_select_fusion.3), channel_id=1, source_target_pairs={{0,128},{256,384},{1,129},{257,385},{2,130},{258,386},{3,131},{259... | collective-permute-start | bytes 786440 | tf_op jit(solution)/shard_map/ppermute | solution.py:16
  29.4 7.1 %collective-permute-start.11 = (f32[128,128]{1,0:T(8,128)S(1)}, f32[128,128]{1,0:T(8,128)S(1)}, u32[]{:S(2)}, u32[]{:S(2)}) collective-permute-start(f32[128,128]{1,0:T(8,128)S(1)} %select_select_fusion.3), channel_id=1, source_target_pairs={{0,384},{1,385},{2,386},{3,387},{4,388},{5,389},{6,390},{7,391},{8... | collective-permute-start | bytes 196616 | tf_op jit(solution)/shard_map/ppermute | solution.py:37
  30.1 7.1 %collective-permute-start.12 = (f32[128,128]{1,0:T(8,128)S(1)}, f32[128,128]{1,0:T(8,128)S(1)}, u32[]{:S(2)}, u32[]{:S(2)}) collective-permute-start(f32[128,128]{1,0:T(8,128)S(1)} %select_select_fusion.3), channel_id=1, source_target_pairs={{0,256},{1,257},{2,258},{3,259},{4,260},{5,261},{6,262},{7,263},{8... | collective-permute-start | bytes 196616 | tf_op jit(solution)/shard_map/ppermute | solution.py:37
  30.8 9.5 %collective-permute-start.13 = (f32[128,128]{1,0:T(8,128)S(1)}, f32[128,128]{1,0:T(8,128)S(1)}, u32[]{:S(2)}, u32[]{:S(2)}) collective-permute-start(f32[128,128]{1,0:T(8,128)S(1)} %select_select_fusion.3), channel_id=1, source_target_pairs={{0,128},{1,129},{2,130},{3,131},{4,132},{5,133},{6,134},{7,135},{8... | collective-permute-start | bytes 196616 | tf_op jit(solution)/shard_map/ppermute | solution.py:37
  32.1 9.4 %collective-permute-start.2 = (f32[512,128]{1,0:T(8,128)S(1)}, f32[512,128]{1,0:T(8,128)S(1)}, u32[]{:S(2)}, u32[]{:S(2)}) collective-permute-start(f32[512,128]{1,0:T(8,128)S(1)} %broadcast_select_fusion.4), channel_id=1, source_target_pairs={{0,64},{128,192},{256,320},{384,448},{1,65},{129,193},{257,321},{3... | collective-permute-start | bytes 786440 | tf_op jit(solution)/shard_map/ppermute | solution.py:16
  36.5 11.0 %collective-permute-start.19 = (f32[128,264]{1,0:T(8,128)S(1)}, f32[128,264]{1,0:T(8,128)S(1)}, u32[]{:S(2)}, u32[]{:S(2)}) collective-permute-start(f32[128,264]{1,0:T(8,128)S(1)} %pad_maximum_fusion), channel_id=1, source_target_pairs={{0,8},{16,24},{32,40},{48,56},{64,72},{80,88},{96,104},{112,120},{... | collective-permute-start | bytes 405512 | tf_op jit(solution)/shard_map/ppermute | solution.py:37
  37.2 11.7 %collective-permute-start.20 = (f32[128,264]{1,0:T(8,128)S(1)}, f32[128,264]{1,0:T(8,128)S(1)}, u32[]{:S(2)}, u32[]{:S(2)}) collective-permute-start(f32[128,264]{1,0:T(8,128)S(1)} %pad_maximum_fusion), channel_id=1, source_target_pairs={{0,4},{16,20},{32,36},{48,52},{64,68},{80,84},{96,100},{112,116},{... | collective-permute-start | bytes 405512 | tf_op jit(solution)/shard_map/ppermute | solution.py:37
  40.2 9.4 %collective-permute-start.14 = (f32[128,128]{1,0:T(8,128)S(1)}, f32[128,128]{1,0:T(8,128)S(1)}, u32[]{:S(2)}, u32[]{:S(2)}) collective-permute-start(f32[128,128]{1,0:T(8,128)S(1)} %select_select_fusion.2), channel_id=1, source_target_pairs={{0,96},{128,224},{256,352},{384,480},{1,97},{129,225},{257,353},{3... | collective-permute-start | bytes 196616 | tf_op jit(solution)/shard_map/ppermute | solution.py:37
  41.6 8.7 %collective-permute-start.15 = (f32[128,128]{1,0:T(8,128)S(1)}, f32[128,128]{1,0:T(8,128)S(1)}, u32[]{:S(2)}, u32[]{:S(2)}) collective-permute-start(f32[128,128]{1,0:T(8,128)S(1)} %select_select_fusion.2), channel_id=1, source_target_pairs={{0,64},{128,192},{256,320},{384,448},{1,65},{129,193},{257,321},{3... | collective-permute-start | bytes 196616 | tf_op jit(solution)/shard_map/ppermute | solution.py:37
  46.2 5.4 %collective-permute-start.16 = (f32[128,128]{1,0:T(8,128)S(1)}, f32[128,128]{1,0:T(8,128)S(1)}, u32[]{:S(2)}, u32[]{:S(2)}) collective-permute-start(f32[128,128]{1,0:T(8,128)S(1)} %select_select_fusion.2), channel_id=1, source_target_pairs={{0,32},{128,160},{256,288},{384,416},{1,33},{129,161},{257,289},{3... | collective-permute-start | bytes 196616 | tf_op jit(solution)/shard_map/ppermute | solution.py:37
  47.6 5.4 %collective-permute-start.3 = (f32[512,128]{1,0:T(8,128)S(1)}, f32[512,128]{1,0:T(8,128)S(1)}, u32[]{:S(2)}, u32[]{:S(2)}) collective-permute-start(f32[512,128]{1,0:T(8,128)S(1)} %broadcast_select_fusion.5), channel_id=1, source_target_pairs={{0,32},{64,96},{128,160},{192,224},{256,288},{320,352},{384,416},{... | collective-permute-start | bytes 786440 | tf_op jit(solution)/shard_map/ppermute | solution.py:16
  48.9 5.5 %collective-permute-start.21 = (f32[128,264]{1,0:T(8,128)S(1)}, f32[128,264]{1,0:T(8,128)S(1)}, u32[]{:S(2)}, u32[]{:S(2)}) collective-permute-start(f32[128,264]{1,0:T(8,128)S(1)} %select_select_fusion), channel_id=1, source_target_pairs={{0,3},{4,7},{8,11},{12,15},{16,19},{20,23},{24,27},{28,31},{32,35}... | collective-permute-start | bytes 405512 | tf_op jit(solution)/shard_map/ppermute | solution.py:37
  49.6 4.8 %collective-permute-start.22 = (f32[128,264]{1,0:T(8,128)S(1)}, f32[128,264]{1,0:T(8,128)S(1)}, u32[]{:S(2)}, u32[]{:S(2)}) collective-permute-start(f32[128,264]{1,0:T(8,128)S(1)} %select_select_fusion), channel_id=1, source_target_pairs={{0,2},{4,6},{8,10},{12,14},{16,18},{20,22},{24,26},{28,30},{32,34}... | collective-permute-start | bytes 405512 | tf_op jit(solution)/shard_map/ppermute | solution.py:37
  50.3 16.2 %collective-permute-start.23 = (f32[128,264]{1,0:T(8,128)S(1)}, f32[128,264]{1,0:T(8,128)S(1)}, u32[]{:S(2)}, u32[]{:S(2)}) collective-permute-start(f32[128,264]{1,0:T(8,128)S(1)} %select_select_fusion), channel_id=1, source_target_pairs={{0,1},{4,5},{8,9},{12,13},{16,17},{20,21},{24,25},{28,29},{32,33},... | collective-permute-start | bytes 405512 | tf_op jit(solution)/shard_map/ppermute | solution.py:37
  51.6 14.8 %collective-permute-start.17 = (f32[128,128]{1,0:T(8,128)S(1)}, f32[128,128]{1,0:T(8,128)S(1)}, u32[]{:S(2)}, u32[]{:S(2)}) collective-permute-start(f32[128,128]{1,0:T(8,128)S(1)} %select_select_fusion.1), channel_id=1, source_target_pairs={{0,16},{32,48},{64,80},{96,112},{128,144},{160,176},{192,208},{224... | collective-permute-start | bytes 196616 | tf_op jit(solution)/shard_map/ppermute | solution.py:37
  53.0 14.0 %collective-permute-start.4 = (f32[512,128]{1,0:T(8,128)S(1)}, f32[512,128]{1,0:T(8,128)S(1)}, u32[]{:S(2)}, u32[]{:S(2)}) collective-permute-start(f32[512,128]{1,0:T(8,128)S(1)} %broadcast_select_fusion.6), channel_id=1, source_target_pairs={{0,16},{32,48},{64,80},{96,112},{128,144},{160,176},{192,208},{224... | collective-permute-start | bytes 786440 | tf_op jit(solution)/shard_map/ppermute | solution.py:16
  (5 other events, 6.4 us)

commit v11 on v10

--- a/solution.py
+++ b/solution.py
@@ -102,10 +102,12 @@
 
     holder = (row_id == 0) & (col_id == 0)
     corner, inverse = lax.cond(holder, factor, skip, local[:block, :block])
-    inverse = spread_wide(spread_wide(inverse, "row"), "col")
     left = spread(local[:, :block], "col")
-    top = jnp.concatenate([local[:block], right_sides[:, 0, 0, :].T], axis=1)
+    width = col_blocks * block + side_count
+    top = jnp.concatenate([local[:block], right_sides[:, 0, 0, :].T, inverse], axis=1)
     top = spread_wide(top, "row")
+    inverse = spread_wide(top[:, width:], "col")
+    top = top[:, :width]
 
     rows_factor = jnp.dot(
         left, inverse.T, precision=lax.Precision.HIGHEST, preferred_element_type=jnp.float32

time: 72.6 us -> 78 us (1.074)
  the two profiles are of different devices: /device:TPU:40 before, /device:TPU:75 now
where the time goes in v11:
time: 78 us; the launch traced here: 77.3 us
  waiting for transfers between devices  53.3 us (68%)
  starting transfers between devices  14 us (18%)
  local copies, waits for them, and re-layouts  4.2 us (5%)
  other arithmetic  2.89 us (4%)
  matrix products  1.74 us (2%)
  between operations  1.2 us (2%)
    ppermute x13, waiting for transfers between devices, spread_wide(): arrived = lax.ppermute(block, axis, pairs)  50 us
    ppermute x13, starting transfers between devices, spread_wide(): arrived = lax.ppermute(block, axis, pairs)  9.95 us
    ppermute x5, starting transfers between devices, spread(): arrived = lax.ppermute(block, axis, pairs)  4 us
    ppermute x5, waiting for transfers between devices, spread(): arrived = lax.ppermute(block, axis, pairs)  3.25 us
  transfers between devices with their start and end apart: 18, of which 3 were waited for; matrix products, arithmetic and copies ran while one was open for 2% of the time, Pallas kernels for 0%

profile of v11, /device:TPU:75, one launch (start us, length us, event | category | flops | bytes accessed | tf_op | source)
XLA Modules:
  0.0 77.3 jit_solution(7109562733376859453)
XLA Ops:
  0.6 1.3 %slice_reduce_fusion = f32[128,2,128]{2,1,0:T(2,128)S(1)} fusion(f32[4,1,128,2,1,128]{5,4,3,2,1,0:T(1,128)} %param.4), kind=kLoop, calls=%fused_computation.15 | loop fusion | bytes 262144 | tf_op jit(solution)/shard_map/slice | solution.py:107
  2.0 1.1 %copy.18 = f32[64,8,2,128]{3,1,2,0:T(8,128)S(1)} copy(f32[64,8,2,128]{3,2,1,0:T(2,128)} %bitcast.28) | data formatting | bytes 1048576
  3.1 0.7 slice-done.1
  4.0 0.7 collective-permute-start.5
  4.7 0.7 collective-permute-start.6
  5.4 0.7 collective-permute-start.7
  6.1 0.7 collective-permute-start
  6.9 0.7 collective-permute-start.10
  7.6 0.7 collective-permute-start.8
  8.3 1.3 %collective-permute-start.9 = (f32[128,392]{1,0:T(8,128)S(1)}, f32[128,392]{1,0:T(8,128)S(1)}, u32[]{:S(2)}, u32[]{:S(2)}) collective-permute-start(f32[128,392]{1,0:T(8,128)S(1)} %select_select_fusion.1), channel_id=1, source_target_pairs={{0,2},{4,6},{8,10},{12,14},{16,18},{20,22},{24,26},{28,30},{32,34}... | collective-permute-start | bytes 602120 | tf_op jit(solution)/shard_map/ppermute | solution.py:37
  9.6 0.7 collective-permute-start.1
  10.4 37.4 %collective-permute-done.9 = f32[128,392]{1,0:T(8,128)S(1)} collective-permute-done((f32[128,392]{1,0:T(8,128)S(1)}, f32[128,392]{1,0:T(8,128)S(1)}, u32[]{:S(2)}, u32[]{:S(2)}) %collective-permute-start.9) | collective-permute-done | bytes 200736 | tf_op jit(solution)/shard_map/ppermute | solution.py:37
  48.6 0.7 collective-permute-start.12
  49.3 0.7 collective-permute-start.13
  50.0 0.7 collective-permute-start.2
  51.5 0.7 collective-permute-start.15
  52.2 0.7 collective-permute-start.16
  52.9 0.7 collective-permute-start.3
  53.7 1.3 %collective-permute-start.17 = (f32[128,128]{1,0:T(8,128)S(1)}, f32[128,128]{1,0:T(8,128)S(1)}, u32[]{:S(2)}, u32[]{:S(2)}) collective-permute-start(f32[128,128]{1,0:T(8,128)S(1)} %select_select_fusion.2), channel_id=1, source_target_pairs={{0,16},{32,48},{64,80},{96,112},{128,144},{160,176},{192,208},{224... | collective-permute-start | bytes 196616 | tf_op jit(solution)/shard_map/ppermute | solution.py:37
  55.0 1.3 %collective-permute-start.4 = (f32[512,128]{1,0:T(8,128)S(1)}, f32[512,128]{1,0:T(8,128)S(1)}, u32[]{:S(2)}, u32[]{:S(2)}) collective-permute-start(f32[512,128]{1,0:T(8,128)S(1)} %broadcast_select_fusion.6), channel_id=1, source_target_pairs={{0,16},{32,48},{64,80},{96,112},{128,144},{160,176},{192,208},{224... | collective-permute-start | bytes 786440 | tf_op jit(solution)/shard_map/ppermute | solution.py:16
  56.5 12.6 %collective-permute-done.17 = f32[128,128]{1,0:T(8,128)S(1)} collective-permute-done((f32[128,128]{1,0:T(8,128)S(1)}, f32[128,128]{1,0:T(8,128)S(1)}, u32[]{:S(2)}, u32[]{:S(2)}) %collective-permute-start.17) | collective-permute-done | bytes 65568 | tf_op jit(solution)/shard_map/ppermute | solution.py:37
  69.6 3.2 %collective-permute-done.4 = f32[512,128]{1,0:T(8,128)S(1)} collective-permute-done((f32[512,128]{1,0:T(8,128)S(1)}, f32[512,128]{1,0:T(8,128)S(1)}, u32[]{:S(2)}, u32[]{:S(2)}) %collective-permute-start.4) | collective-permute-done | bytes 262176 | tf_op jit(solution)/shard_map/ppermute | solution.py:16
  75.0 0.7 broadcast_select_fusion.7
  75.8 1.5 %broadcast_select_fusion = f32[4,1,128,2,1,128]{5,4,3,2,1,0:T(1,128)} fusion(pred[2]{0:T(512)(128)(4,1)S(1)} %get-tuple-element.13, f32[4,1,128,2,1,128]{5,4,3,2,1,0:T(1,128)S(1)} %bitcast.33, pred[4,2]{1,0:T(4,128)(4,1)S(1)} %broadcast_and_fusion, f32[4,128,128]{2,1,0:T(8,128)S(1)} %broadcast_select_fusion.2), kind=kLoop, calls=%fused_computation.3 | loop fusion | flops 262144 | bytes 1310730 | tf_op jit(solution)/shard_map/jit(_where)/select_n | solution.py:135
  (52 shorter events, 5.0 us)
Async XLA Ops:
  3.1 0.7 slice-start.1
  4.0 2.8 %collective-permute-start.5 = (f32[128,392]{1,0:T(8,128)S(1)}, f32[128,392]{1,0:T(8,128)S(1)}, u32[]{:S(2)}, u32[]{:S(2)}) collective-permute-start(f32[128,392]{1,0:T(8,128)S(1)} %pad_maximum_fusion), channel_id=1, source_target_pairs={{0,12},{16,28},{32,44},{48,60},{64,76},{80,92},{96,108},{112,124},... | collective-permute-start | bytes 602120 | tf_op jit(solution)/shard_map/ppermute | solution.py:37
  4.7 2.1 %collective-permute-start.6 = (f32[128,392]{1,0:T(8,128)S(1)}, f32[128,392]{1,0:T(8,128)S(1)}, u32[]{:S(2)}, u32[]{:S(2)}) collective-permute-start(f32[128,392]{1,0:T(8,128)S(1)} %pad_maximum_fusion), channel_id=1, source_target_pairs={{0,8},{16,24},{32,40},{48,56},{64,72},{80,88},{96,104},{112,120},{... | collective-permute-start | bytes 602120 | tf_op jit(solution)/shard_map/ppermute | solution.py:37
  5.4 1.4 %collective-permute-start.7 = (f32[128,392]{1,0:T(8,128)S(1)}, f32[128,392]{1,0:T(8,128)S(1)}, u32[]{:S(2)}, u32[]{:S(2)}) collective-permute-start(f32[128,392]{1,0:T(8,128)S(1)} %pad_maximum_fusion), channel_id=1, source_target_pairs={{0,4},{16,20},{32,36},{48,52},{64,68},{80,84},{96,100},{112,116},{... | collective-permute-start | bytes 602120 | tf_op jit(solution)/shard_map/ppermute | solution.py:37
  6.1 3.5 %collective-permute-start = (f32[512,128]{1,0:T(8,128)S(1)}, f32[512,128]{1,0:T(8,128)S(1)}, u32[]{:S(2)}, u32[]{:S(2)}) collective-permute-start(f32[512,128]{1,0:T(8,128)S(1)} %slice.38), channel_id=1, source_target_pairs={{0,256},{1,257},{2,258},{3,259},{4,260},{5,261},{6,262},{7,263},{8... | collective-permute-start | bytes 786440 | tf_op jit(solution)/shard_map/ppermute | solution.py:16
  6.9 3.4 %collective-permute-start.10 = (f32[128,392]{1,0:T(8,128)S(1)}, f32[128,392]{1,0:T(8,128)S(1)}, u32[]{:S(2)}, u32[]{:S(2)}) collective-permute-start(f32[128,392]{1,0:T(8,128)S(1)} %select_select_fusion.1), channel_id=1, source_target_pairs={{0,1},{4,5},{8,9},{12,13},{16,17},{20,21},{24,25},{28,29},{32,33},... | collective-permute-start | bytes 602120 | tf_op jit(solution)/shard_map/ppermute | solution.py:37
  7.6 2.8 %collective-permute-start.8 = (f32[128,392]{1,0:T(8,128)S(1)}, f32[128,392]{1,0:T(8,128)S(1)}, u32[]{:S(2)}, u32[]{:S(2)}) collective-permute-start(f32[128,392]{1,0:T(8,128)S(1)} %select_select_fusion.1), channel_id=1, source_target_pairs={{0,3},{4,7},{8,11},{12,15},{16,19},{20,23},{24,27},{28,31},{32,35}... | collective-permute-start | bytes 602120 | tf_op jit(solution)/shard_map/ppermute | solution.py:37
  8.3 39.5 %collective-permute-start.9 = (f32[128,392]{1,0:T(8,128)S(1)}, f32[128,392]{1,0:T(8,128)S(1)}, u32[]{:S(2)}, u32[]{:S(2)}) collective-permute-start(f32[128,392]{1,0:T(8,128)S(1)} %select_select_fusion.1), channel_id=1, source_target_pairs={{0,2},{4,6},{8,10},{12,14},{16,18},{20,22},{24,26},{28,30},{32,34}... | collective-permute-start | bytes 602120 | tf_op jit(solution)/shard_map/ppermute | solution.py:37
  9.6 40.3 %collective-permute-start.1 = (f32[512,128]{1,0:T(8,128)S(1)}, f32[512,128]{1,0:T(8,128)S(1)}, u32[]{:S(2)}, u32[]{:S(2)}) collective-permute-start(f32[512,128]{1,0:T(8,128)S(1)} %broadcast_select_fusion.3), channel_id=1, source_target_pairs={{0,128},{256,384},{1,129},{257,385},{2,130},{258,386},{3,131},{259... | collective-permute-start | bytes 786440 | tf_op jit(solution)/shard_map/ppermute | solution.py:16
  47.9 2.8 %collective-permute-start.11 = (f32[128,128]{1,0:T(8,128)S(1)}, f32[128,128]{1,0:T(8,128)S(1)}, u32[]{:S(2)}, u32[]{:S(2)}) collective-permute-start(f32[128,128]{1,0:T(8,128)S(1)} %slice.39), channel_id=1, source_target_pairs={{0,384},{1,385},{2,386},{3,387},{4,388},{5,389},{6,390},{7,391},{8... | collective-permute-start | bytes 196616 | tf_op jit(solution)/shard_map/ppermute | solution.py:37
  48.6 2.1 %collective-permute-start.12 = (f32[128,128]{1,0:T(8,128)S(1)}, f32[128,128]{1,0:T(8,128)S(1)}, u32[]{:S(2)}, u32[]{:S(2)}) collective-permute-start(f32[128,128]{1,0:T(8,128)S(1)} %slice.39), channel_id=1, source_target_pairs={{0,256},{1,257},{2,258},{3,259},{4,260},{5,261},{6,262},{7,263},{8... | collective-permute-start | bytes 196616 | tf_op jit(solution)/shard_map/ppermute | solution.py:37
  49.3 1.5 %collective-permute-start.13 = (f32[128,128]{1,0:T(8,128)S(1)}, f32[128,128]{1,0:T(8,128)S(1)}, u32[]{:S(2)}, u32[]{:S(2)}) collective-permute-start(f32[128,128]{1,0:T(8,128)S(1)} %slice.39), channel_id=1, source_target_pairs={{0,128},{1,129},{2,130},{3,131},{4,132},{5,133},{6,134},{7,135},{8... | collective-permute-start | bytes 196616 | tf_op jit(solution)/shard_map/ppermute | solution.py:37
  50.0 2.9 %collective-permute-start.2 = (f32[512,128]{1,0:T(8,128)S(1)}, f32[512,128]{1,0:T(8,128)S(1)}, u32[]{:S(2)}, u32[]{:S(2)}) collective-permute-start(f32[512,128]{1,0:T(8,128)S(1)} %broadcast_select_fusion.4), channel_id=1, source_target_pairs={{0,64},{128,192},{256,320},{384,448},{1,65},{129,193},{257,321},{3... | collective-permute-start | bytes 786440 | tf_op jit(solution)/shard_map/ppermute | solution.py:16
  50.8 2.8 %collective-permute-start.14 = (f32[128,128]{1,0:T(8,128)S(1)}, f32[128,128]{1,0:T(8,128)S(1)}, u32[]{:S(2)}, u32[]{:S(2)}) collective-permute-start(f32[128,128]{1,0:T(8,128)S(1)} %select_select_fusion.3), channel_id=1, source_target_pairs={{0,96},{128,224},{256,352},{384,480},{1,97},{129,225},{257,353},{3... | collective-permute-start | bytes 196616 | tf_op jit(solution)/shard_map/ppermute | solution.py:37
  51.5 2.1 %collective-permute-start.15 = (f32[128,128]{1,0:T(8,128)S(1)}, f32[128,128]{1,0:T(8,128)S(1)}, u32[]{:S(2)}, u32[]{:S(2)}) collective-permute-start(f32[128,128]{1,0:T(8,128)S(1)} %select_select_fusion.3), channel_id=1, source_target_pairs={{0,64},{128,192},{256,320},{384,448},{1,65},{129,193},{257,321},{3... | collective-permute-start | bytes 196616 | tf_op jit(solution)/shard_map/ppermute | solution.py:37
  52.2 1.5 %collective-permute-start.16 = (f32[128,128]{1,0:T(8,128)S(1)}, f32[128,128]{1,0:T(8,128)S(1)}, u32[]{:S(2)}, u32[]{:S(2)}) collective-permute-start(f32[128,128]{1,0:T(8,128)S(1)} %select_select_fusion.3), channel_id=1, source_target_pairs={{0,32},{128,160},{256,288},{384,416},{1,33},{129,161},{257,289},{3... | collective-permute-start | bytes 196616 | tf_op jit(solution)/shard_map/ppermute | solution.py:37
  52.9 2.1 %collective-permute-start.3 = (f32[512,128]{1,0:T(8,128)S(1)}, f32[512,128]{1,0:T(8,128)S(1)}, u32[]{:S(2)}, u32[]{:S(2)}) collective-permute-start(f32[512,128]{1,0:T(8,128)S(1)} %broadcast_select_fusion.5), channel_id=1, source_target_pairs={{0,32},{64,96},{128,160},{192,224},{256,288},{320,352},{384,416},{... | collective-permute-start | bytes 786440 | tf_op jit(solution)/shard_map/ppermute | solution.py:16
  53.7 15.4 %collective-permute-start.17 = (f32[128,128]{1,0:T(8,128)S(1)}, f32[128,128]{1,0:T(8,128)S(1)}, u32[]{:S(2)}, u32[]{:S(2)}) collective-permute-start(f32[128,128]{1,0:T(8,128)S(1)} %select_select_fusion.2), channel_id=1, source_target_pairs={{0,16},{32,48},{64,80},{96,112},{128,144},{160,176},{192,208},{224... | collective-permute-start | bytes 196616 | tf_op jit(solution)/shard_map/ppermute | solution.py:37
  55.0 17.8 %collective-permute-start.4 = (f32[512,128]{1,0:T(8,128)S(1)}, f32[512,128]{1,0:T(8,128)S(1)}, u32[]{:S(2)}, u32[]{:S(2)}) collective-permute-start(f32[512,128]{1,0:T(8,128)S(1)} %broadcast_select_fusion.6), channel_id=1, source_target_pairs={{0,16},{32,48},{64,80},{96,112},{128,144},{160,176},{192,208},{224... | collective-permute-start | bytes 786440 | tf_op jit(solution)/shard_map/ppermute | solution.py:16
  69.6 4.3 %copy-start.1 = (f32[264,128]{1,0:T(8,128)}, f32[264,128]{1,0:T(8,128)S(1)}, u32[]{:S(2)}) copy-start(f32[264,128]{1,0:T(8,128)S(1)} %fusion.3) | copy-start | bytes 405508
  69.6 3.6 %copy-start = (f32[4,1,128,2,1,128]{5,4,3,2,1,0:T(1,128)S(1)}, f32[4,1,128,2,1,128]{5,4,3,2,1,0:T(1,128)}, u32[]{:S(2)}) copy-start(f32[4,1,128,2,1,128]{5,4,3,2,1,0:T(1,128)} %param.4) | copy-start | bytes 1572868
  73.3 0.7 copy-start.2
  74.3 0.7 slice-start

commit v12 on v10

--- a/solution.py
+++ b/solution.py
@@ -102,10 +102,12 @@
 
     holder = (row_id == 0) & (col_id == 0)
     corner, inverse = lax.cond(holder, factor, skip, local[:block, :block])
-    inverse = spread_wide(spread_wide(inverse, "row"), "col")
     left = spread(local[:, :block], "col")
     top = jnp.concatenate([local[:block], right_sides[:, 0, 0, :].T], axis=1)
     top = spread_wide(top, "row")
+    inverse = spread_wide(inverse, "row")
+    inverse, top = lax.optimization_barrier((inverse, top))
+    inverse = spread_wide(inverse, "col")
 
     rows_factor = jnp.dot(
         left, inverse.T, precision=lax.Precision.HIGHEST, preferred_element_type=jnp.float32

time: 72.6 us -> 77.7 us (1.070)
  the two profiles are of different devices: /device:TPU:40 before, /device:TPU:43 now
where the time goes in v12:
time: 77.7 us; the launch traced here: 77 us
  waiting for transfers between devices  49.4 us (64%)
  starting transfers between devices  18.5 us (24%)
  local copies, waits for them, and re-layouts  3.26 us (4%)
  other arithmetic  2.72 us (4%)
  matrix products  1.75 us (2%)
  between operations  1.29 us (2%)
    ppermute x19, waiting for transfers between devices, spread_wide(): arrived = lax.ppermute(block, axis, pairs)  46.1 us
    ppermute x19, starting transfers between devices, spread_wide(): arrived = lax.ppermute(block, axis, pairs)  14.5 us
    ppermute x5, starting transfers between devices, spread(): arrived = lax.ppermute(block, axis, pairs)  4 us
    ppermute x5, waiting for transfers between devices, spread(): arrived = lax.ppermute(block, axis, pairs)  3.26 us
  transfers between devices with their start and end apart: 24, of which 4 were waited for; matrix products, arithmetic and copies ran while one was open for 2% of the time, Pallas kernels for 0%

profile of v12, /device:TPU:43, one launch (start us, length us, event | category | flops | bytes accessed | tf_op | source)
XLA Modules:
  0.0 77.0 jit_solution(13293348435443322657)
XLA Ops:
  0.7 1.1 %copy.18 = f32[64,8,2,128]{3,1,2,0:T(8,128)S(1)} copy(f32[64,8,2,128]{3,2,1,0:T(2,128)} %bitcast.29) | data formatting | bytes 1048576
  1.8 0.7 collective-permute-start.5
  3.2 0.7 collective-permute-start.7
  4.3 0.7 slice-done.1
  5.1 0.7 collective-permute-start.11
  5.8 0.7 collective-permute-start.12
  6.6 0.7 collective-permute-start.13
  7.3 0.7 collective-permute-start
  8.0 1.3 %collective-permute-start.10 = (f32[128,128]{1,0:T(8,128)S(1)}, f32[128,128]{1,0:T(8,128)S(1)}, u32[]{:S(2)}, u32[]{:S(2)}) collective-permute-start(f32[128,128]{1,0:T(8,128)S(1)} %select_select_fusion.5), channel_id=1, source_target_pairs={{0,1},{4,5},{8,9},{12,13},{16,17},{20,21},{24,25},{28,29},{32,33},... | collective-permute-start | bytes 196616 | tf_op jit(solution)/shard_map/ppermute | solution.py:37
  9.3 0.7 collective-permute-start.8
  10.7 0.7 collective-permute-start.14
  11.4 0.7 collective-permute-start.15
  12.1 20.4 %collective-permute-done.10 = f32[128,128]{1,0:T(8,128)S(1)} collective-permute-done((f32[128,128]{1,0:T(8,128)S(1)}, f32[128,128]{1,0:T(8,128)S(1)}, u32[]{:S(2)}, u32[]{:S(2)}) %collective-permute-start.10) | collective-permute-done | bytes 65568 | tf_op jit(solution)/shard_map/ppermute | solution.py:37
  32.5 1.3 %collective-permute-start.16 = (f32[128,264]{1,0:T(8,128)S(1)}, f32[128,264]{1,0:T(8,128)S(1)}, u32[]{:S(2)}, u32[]{:S(2)}) collective-permute-start(f32[128,264]{1,0:T(8,128)S(1)} %select_select_fusion.1), channel_id=1, source_target_pairs={{0,1},{4,5},{8,9},{12,13},{16,17},{20,21},{24,25},{28,29},{32,33},... | collective-permute-start | bytes 405512 | tf_op jit(solution)/shard_map/ppermute | solution.py:37
  33.8 0.7 collective-permute-start.1
  34.6 13.7 %collective-permute-done.16 = f32[128,264]{1,0:T(8,128)S(1)} collective-permute-done((f32[128,264]{1,0:T(8,128)S(1)}, f32[128,264]{1,0:T(8,128)S(1)}, u32[]{:S(2)}, u32[]{:S(2)}) %collective-permute-start.16) | collective-permute-done | bytes 135200 | tf_op jit(solution)/shard_map/ppermute | solution.py:37
  50.4 0.7 collective-permute-start.2
  53.2 0.7 collective-permute-start.3
  54.0 1.3 %collective-permute-start.23 = (f32[128,128]{1,0:T(8,128)S(1)}, f32[128,128]{1,0:T(8,128)S(1)}, u32[]{:S(2)}, u32[]{:S(2)}) collective-permute-start(f32[128,128]{1,0:T(8,128)S(1)} %select_select_fusion.2), channel_id=1, source_target_pairs={{0,16},{32,48},{64,80},{96,112},{128,144},{160,176},{192,208},{224... | collective-permute-start | bytes 196616 | tf_op jit(solution)/shard_map/ppermute | solution.py:37
  55.4 1.3 %collective-permute-start.4 = (f32[512,128]{1,0:T(8,128)S(1)}, f32[512,128]{1,0:T(8,128)S(1)}, u32[]{:S(2)}, u32[]{:S(2)}) collective-permute-start(f32[512,128]{1,0:T(8,128)S(1)} %broadcast_select_fusion.6), channel_id=1, source_target_pairs={{0,16},{32,48},{64,80},{96,112},{128,144},{160,176},{192,208},{224... | collective-permute-start | bytes 786440 | tf_op jit(solution)/shard_map/ppermute | solution.py:16
  56.8 12.0 %collective-permute-done.23 = f32[128,128]{1,0:T(8,128)S(1)} collective-permute-done((f32[128,128]{1,0:T(8,128)S(1)}, f32[128,128]{1,0:T(8,128)S(1)}, u32[]{:S(2)}, u32[]{:S(2)}) %collective-permute-start.23) | collective-permute-done | bytes 65568 | tf_op jit(solution)/shard_map/ppermute | solution.py:37
  69.3 3.2 %collective-permute-done.4 = f32[512,128]{1,0:T(8,128)S(1)} collective-permute-done((f32[512,128]{1,0:T(8,128)S(1)}, f32[512,128]{1,0:T(8,128)S(1)}, u32[]{:S(2)}, u32[]{:S(2)}) %collective-permute-start.4) | collective-permute-done | bytes 262176 | tf_op jit(solution)/shard_map/ppermute | solution.py:16
  74.7 0.7 broadcast_select_fusion.7
  75.4 1.5 %broadcast_select_fusion = f32[4,1,128,2,1,128]{5,4,3,2,1,0:T(1,128)} fusion(pred[2]{0:T(512)(128)(4,1)S(1)} %get-tuple-element.17, f32[4,1,128,2,1,128]{5,4,3,2,1,0:T(1,128)S(1)} %bitcast.34, pred[4,2]{1,0:T(4,128)(4,1)S(1)} %broadcast_and_fusion, f32[4,128,128]{2,1,0:T(8,128)S(1)} %broadcast_select_fusion.2), kind=kLoop, calls=%fused_computation.3 | loop fusion | flops 262144 | bytes 1310730 | tf_op jit(solution)/shard_map/jit(_where)/select_n | solution.py:135
  (65 shorter events, 9.1 us)
Async XLA Ops:
  1.8 4.7 %collective-permute-start.5 = (f32[128,128]{1,0:T(8,128)S(1)}, f32[128,128]{1,0:T(8,128)S(1)}, u32[]{:S(2)}, u32[]{:S(2)}) collective-permute-start(f32[128,128]{1,0:T(8,128)S(1)} %get-tuple-element.11), channel_id=1, source_target_pairs={{0,12},{16,28},{32,44},{48,60},{64,76},{80,92},{96,108},{112,124},... | collective-permute-start | bytes 196616 | tf_op jit(solution)/shard_map/ppermute | solution.py:37
  2.5 4.7 %collective-permute-start.6 = (f32[128,128]{1,0:T(8,128)S(1)}, f32[128,128]{1,0:T(8,128)S(1)}, u32[]{:S(2)}, u32[]{:S(2)}) collective-permute-start(f32[128,128]{1,0:T(8,128)S(1)} %get-tuple-element.11), channel_id=1, source_target_pairs={{0,8},{16,24},{32,40},{48,56},{64,72},{80,88},{96,104},{112,120},{... | collective-permute-start | bytes 196616 | tf_op jit(solution)/shard_map/ppermute | solution.py:37
  3.2 4.8 %collective-permute-start.7 = (f32[128,128]{1,0:T(8,128)S(1)}, f32[128,128]{1,0:T(8,128)S(1)}, u32[]{:S(2)}, u32[]{:S(2)}) collective-permute-start(f32[128,128]{1,0:T(8,128)S(1)} %get-tuple-element.11), channel_id=1, source_target_pairs={{0,4},{16,20},{32,36},{48,52},{64,68},{80,84},{96,100},{112,116},{... | collective-permute-start | bytes 196616 | tf_op jit(solution)/shard_map/ppermute | solution.py:37
  5.1 4.2 %collective-permute-start.11 = (f32[128,264]{1,0:T(8,128)S(1)}, f32[128,264]{1,0:T(8,128)S(1)}, u32[]{:S(2)}, u32[]{:S(2)}) collective-permute-start(f32[128,264]{1,0:T(8,128)S(1)} %pad_maximum_fusion), channel_id=1, source_target_pairs={{0,12},{16,28},{32,44},{48,60},{64,76},{80,92},{96,108},{112,124},... | collective-permute-start | bytes 405512 | tf_op jit(solution)/shard_map/ppermute | solution.py:37
  5.8 4.2 %collective-permute-start.12 = (f32[128,264]{1,0:T(8,128)S(1)}, f32[128,264]{1,0:T(8,128)S(1)}, u32[]{:S(2)}, u32[]{:S(2)}) collective-permute-start(f32[128,264]{1,0:T(8,128)S(1)} %pad_maximum_fusion), channel_id=1, source_target_pairs={{0,8},{16,24},{32,40},{48,56},{64,72},{80,88},{96,104},{112,120},{... | collective-permute-start | bytes 405512 | tf_op jit(solution)/shard_map/ppermute | solution.py:37
  6.6 4.1 %collective-permute-start.13 = (f32[128,264]{1,0:T(8,128)S(1)}, f32[128,264]{1,0:T(8,128)S(1)}, u32[]{:S(2)}, u32[]{:S(2)}) collective-permute-start(f32[128,264]{1,0:T(8,128)S(1)} %pad_maximum_fusion), channel_id=1, source_target_pairs={{0,4},{16,20},{32,36},{48,52},{64,68},{80,84},{96,100},{112,116},{... | collective-permute-start | bytes 405512 | tf_op jit(solution)/shard_map/ppermute | solution.py:37
  7.3 4.1 %collective-permute-start = (f32[512,128]{1,0:T(8,128)S(1)}, f32[512,128]{1,0:T(8,128)S(1)}, u32[]{:S(2)}, u32[]{:S(2)}) collective-permute-start(f32[512,128]{1,0:T(8,128)S(1)} %slice.30), channel_id=1, source_target_pairs={{0,256},{1,257},{2,258},{3,259},{4,260},{5,261},{6,262},{7,263},{8... | collective-permute-start | bytes 786440 | tf_op jit(solution)/shard_map/ppermute | solution.py:16
  8.0 24.6 %collective-permute-start.10 = (f32[128,128]{1,0:T(8,128)S(1)}, f32[128,128]{1,0:T(8,128)S(1)}, u32[]{:S(2)}, u32[]{:S(2)}) collective-permute-start(f32[128,128]{1,0:T(8,128)S(1)} %select_select_fusion.5), channel_id=1, source_target_pairs={{0,1},{4,5},{8,9},{12,13},{16,17},{20,21},{24,25},{28,29},{32,33},... | collective-permute-start | bytes 196616 | tf_op jit(solution)/shard_map/ppermute | solution.py:37
  9.3 24.5 %collective-permute-start.8 = (f32[128,128]{1,0:T(8,128)S(1)}, f32[128,128]{1,0:T(8,128)S(1)}, u32[]{:S(2)}, u32[]{:S(2)}) collective-permute-start(f32[128,128]{1,0:T(8,128)S(1)} %select_select_fusion.5), channel_id=1, source_target_pairs={{0,3},{4,7},{8,11},{12,15},{16,19},{20,23},{24,27},{28,31},{32,35}... | collective-permute-start | bytes 196616 | tf_op jit(solution)/shard_map/ppermute | solution.py:37
  10.0 24.6 %collective-permute-start.9 = (f32[128,128]{1,0:T(8,128)S(1)}, f32[128,128]{1,0:T(8,128)S(1)}, u32[]{:S(2)}, u32[]{:S(2)}) collective-permute-start(f32[128,128]{1,0:T(8,128)S(1)} %select_select_fusion.5), channel_id=1, source_target_pairs={{0,2},{4,6},{8,10},{12,14},{16,18},{20,22},{24,26},{28,30},{32,34}... | collective-permute-start | bytes 196616 | tf_op jit(solution)/shard_map/ppermute | solution.py:37
  10.7 23.8 %collective-permute-start.14 = (f32[128,264]{1,0:T(8,128)S(1)}, f32[128,264]{1,0:T(8,128)S(1)}, u32[]{:S(2)}, u32[]{:S(2)}) collective-permute-start(f32[128,264]{1,0:T(8,128)S(1)} %select_select_fusion.1), channel_id=1, source_target_pairs={{0,3},{4,7},{8,11},{12,15},{16,19},{20,23},{24,27},{28,31},{32,35}... | collective-permute-start | bytes 405512 | tf_op jit(solution)/shard_map/ppermute | solution.py:37
  11.4 23.2 %collective-permute-start.15 = (f32[128,264]{1,0:T(8,128)S(1)}, f32[128,264]{1,0:T(8,128)S(1)}, u32[]{:S(2)}, u32[]{:S(2)}) collective-permute-start(f32[128,264]{1,0:T(8,128)S(1)} %select_select_fusion.1), channel_id=1, source_target_pairs={{0,2},{4,6},{8,10},{12,14},{16,18},{20,22},{24,26},{28,30},{32,34}... | collective-permute-start | bytes 405512 | tf_op jit(solution)/shard_map/ppermute | solution.py:37
  32.5 15.7 %collective-permute-start.16 = (f32[128,264]{1,0:T(8,128)S(1)}, f32[128,264]{1,0:T(8,128)S(1)}, u32[]{:S(2)}, u32[]{:S(2)}) collective-permute-start(f32[128,264]{1,0:T(8,128)S(1)} %select_select_fusion.1), channel_id=1, source_target_pairs={{0,1},{4,5},{8,9},{12,13},{16,17},{20,21},{24,25},{28,29},{32,33},... | collective-permute-start | bytes 405512 | tf_op jit(solution)/shard_map/ppermute | solution.py:37
  33.8 16.5 %collective-permute-start.1 = (f32[512,128]{1,0:T(8,128)S(1)}, f32[512,128]{1,0:T(8,128)S(1)}, u32[]{:S(2)}, u32[]{:S(2)}) collective-permute-start(f32[512,128]{1,0:T(8,128)S(1)} %broadcast_select_fusion.3), channel_id=1, source_target_pairs={{0,128},{256,384},{1,129},{257,385},{2,130},{258,386},{3,131},{259... | collective-permute-start | bytes 786440 | tf_op jit(solution)/shard_map/ppermute | solution.py:16
  48.3 2.8 %collective-permute-start.17 = (f32[128,128]{1,0:T(8,128)S(1)}, f32[128,128]{1,0:T(8,128)S(1)}, u32[]{:S(2)}, u32[]{:S(2)}) collective-permute-start(f32[128,128]{1,0:T(8,128)S(1)} %select_select_fusion.4), channel_id=1, source_target_pairs={{0,384},{1,385},{2,386},{3,387},{4,388},{5,389},{6,390},{7,391},{8... | collective-permute-start | bytes 196616 | tf_op jit(solution)/shard_map/ppermute | solution.py:37
  49.0 2.1 %collective-permute-start.18 = (f32[128,128]{1,0:T(8,128)S(1)}, f32[128,128]{1,0:T(8,128)S(1)}, u32[]{:S(2)}, u32[]{:S(2)}) collective-permute-start(f32[128,128]{1,0:T(8,128)S(1)} %select_select_fusion.4), channel_id=1, source_target_pairs={{0,256},{1,257},{2,258},{3,259},{4,260},{5,261},{6,262},{7,263},{8... | collective-permute-start | bytes 196616 | tf_op jit(solution)/shard_map/ppermute | solution.py:37
  49.7 1.5 %collective-permute-start.19 = (f32[128,128]{1,0:T(8,128)S(1)}, f32[128,128]{1,0:T(8,128)S(1)}, u32[]{:S(2)}, u32[]{:S(2)}) collective-permute-start(f32[128,128]{1,0:T(8,128)S(1)} %select_select_fusion.4), channel_id=1, source_target_pairs={{0,128},{1,129},{2,130},{3,131},{4,132},{5,133},{6,134},{7,135},{8... | collective-permute-start | bytes 196616 | tf_op jit(solution)/shard_map/ppermute | solution.py:37
  50.4 2.8 %collective-permute-start.2 = (f32[512,128]{1,0:T(8,128)S(1)}, f32[512,128]{1,0:T(8,128)S(1)}, u32[]{:S(2)}, u32[]{:S(2)}) collective-permute-start(f32[512,128]{1,0:T(8,128)S(1)} %broadcast_select_fusion.4), channel_id=1, source_target_pairs={{0,64},{128,192},{256,320},{384,448},{1,65},{129,193},{257,321},{3... | collective-permute-start | bytes 786440 | tf_op jit(solution)/shard_map/ppermute | solution.py:16
  51.2 2.8 %collective-permute-start.20 = (f32[128,128]{1,0:T(8,128)S(1)}, f32[128,128]{1,0:T(8,128)S(1)}, u32[]{:S(2)}, u32[]{:S(2)}) collective-permute-start(f32[128,128]{1,0:T(8,128)S(1)} %select_select_fusion.3), channel_id=1, source_target_pairs={{0,96},{128,224},{256,352},{384,480},{1,97},{129,225},{257,353},{3... | collective-permute-start | bytes 196616 | tf_op jit(solution)/shard_map/ppermute | solution.py:37
  51.8 2.1 %collective-permute-start.21 = (f32[128,128]{1,0:T(8,128)S(1)}, f32[128,128]{1,0:T(8,128)S(1)}, u32[]{:S(2)}, u32[]{:S(2)}) collective-permute-start(f32[128,128]{1,0:T(8,128)S(1)} %select_select_fusion.3), channel_id=1, source_target_pairs={{0,64},{128,192},{256,320},{384,448},{1,65},{129,193},{257,321},{3... | collective-permute-start | bytes 196616 | tf_op jit(solution)/shard_map/ppermute | solution.py:37
  52.5 1.5 %collective-permute-start.22 = (f32[128,128]{1,0:T(8,128)S(1)}, f32[128,128]{1,0:T(8,128)S(1)}, u32[]{:S(2)}, u32[]{:S(2)}) collective-permute-start(f32[128,128]{1,0:T(8,128)S(1)} %select_select_fusion.3), channel_id=1, source_target_pairs={{0,32},{128,160},{256,288},{384,416},{1,33},{129,161},{257,289},{3... | collective-permute-start | bytes 196616 | tf_op jit(solution)/shard_map/ppermute | solution.py:37
  53.2 2.1 %collective-permute-start.3 = (f32[512,128]{1,0:T(8,128)S(1)}, f32[512,128]{1,0:T(8,128)S(1)}, u32[]{:S(2)}, u32[]{:S(2)}) collective-permute-start(f32[512,128]{1,0:T(8,128)S(1)} %broadcast_select_fusion.5), channel_id=1, source_target_pairs={{0,32},{64,96},{128,160},{192,224},{256,288},{320,352},{384,416},{... | collective-permute-start | bytes 786440 | tf_op jit(solution)/shard_map/ppermute | solution.py:16
  54.0 14.8 %collective-permute-start.23 = (f32[128,128]{1,0:T(8,128)S(1)}, f32[128,128]{1,0:T(8,128)S(1)}, u32[]{:S(2)}, u32[]{:S(2)}) collective-permute-start(f32[128,128]{1,0:T(8,128)S(1)} %select_select_fusion.2), channel_id=1, source_target_pairs={{0,16},{32,48},{64,80},{96,112},{128,144},{160,176},{192,208},{224... | collective-permute-start | bytes 196616 | tf_op jit(solution)/shard_map/ppermute | solution.py:37
  55.4 17.2 %collective-permute-start.4 = (f32[512,128]{1,0:T(8,128)S(1)}, f32[512,128]{1,0:T(8,128)S(1)}, u32[]{:S(2)}, u32[]{:S(2)}) collective-permute-start(f32[512,128]{1,0:T(8,128)S(1)} %broadcast_select_fusion.6), channel_id=1, source_target_pairs={{0,16},{32,48},{64,80},{96,112},{128,144},{160,176},{192,208},{224... | collective-permute-start | bytes 786440 | tf_op jit(solution)/shard_map/ppermute | solution.py:16
  (5 other events, 9.6 us)

commit v13 on v9

--- a/solution.py
+++ b/solution.py
@@ -94,7 +94,7 @@
     inverse = spread_wide(spread_wide(inverse, "row"), "col")
     left = spread(local[:, :block], "col")
     top = jnp.concatenate([local[:block], right_sides[:, 0, 0, :].T], axis=1)
-    top = spread_wide(top, "row")
+    top = spread(top, "row")
 
     rows_factor = jnp.dot(
         left, inverse.T, precision=lax.Precision.HIGHEST, preferred_element_type=jnp.float32

time: 72.6 us -> 66.3 us (0.913)
  the two profiles are of different devices: /device:TPU:40 before, /device:TPU:1 now
where the time goes in v13:
time: 66.3 us; the launch traced here: 65.5 us
  starting transfers between devices  41 us (62%)
  waiting for transfers between devices  15.6 us (24%)
  local copies, waits for them, and re-layouts  3.26 us (5%)
  other arithmetic  2.69 us (4%)
  matrix products  1.74 us (3%)
  between operations  1.21 us (2%)
    ppermute x13, starting transfers between devices, spread_wide(): arrived = lax.ppermute(block, axis, pairs)  27.4 us
    ppermute x9, starting transfers between devices, spread(): arrived = lax.ppermute(block, axis, pairs)  13.6 us
    ppermute x13, waiting for transfers between devices, spread_wide(): arrived = lax.ppermute(block, axis, pairs)  11.4 us
    ppermute x9, waiting for transfers between devices, spread(): arrived = lax.ppermute(block, axis, pairs)  4.12 us
    select_n x1, other arithmetic, on_device(): jnp.where((global_cols == 0)[None, None, :, None], column[:, :, None, :],...  1.52 us
  transfers between devices with their start and end apart: 22, of which 4 were waited for; matrix products, arithmetic and copies ran while one was open for 2% of the time, Pallas kernels for 0%

profile of v13, /device:TPU:1, one launch (start us, length us, event | category | flops | bytes accessed | tf_op | source)
XLA Modules:
  0.0 65.5 jit_solution(14482198585987169373)
XLA Ops:
  0.7 1.1 %copy.18 = f32[64,8,2,128]{3,1,2,0:T(8,128)S(1)} copy(f32[64,8,2,128]{3,2,1,0:T(2,128)} %bitcast.28) | data formatting | bytes 1048576
  1.8 13.3 %collective-permute-start.5 = (f32[128,128]{1,0:T(8,128)S(1)}, f32[128,128]{1,0:T(8,128)S(1)}, u32[]{:S(2)}, u32[]{:S(2)}) collective-permute-start(f32[128,128]{1,0:T(8,128)S(1)} %get-tuple-element.9), channel_id=1, source_target_pairs={{0,12},{16,28},{32,44},{48,60},{64,76},{80,92},{96,108},{112,124},... | collective-permute-start | bytes 196616 | tf_op jit(solution)/shard_map/ppermute | solution.py:37
  15.1 3.7 %collective-permute-start.6 = (f32[128,128]{1,0:T(8,128)S(1)}, f32[128,128]{1,0:T(8,128)S(1)}, u32[]{:S(2)}, u32[]{:S(2)}) collective-permute-start(f32[128,128]{1,0:T(8,128)S(1)} %get-tuple-element.9), channel_id=1, source_target_pairs={{0,8},{16,24},{32,40},{48,56},{64,72},{80,88},{96,104},{112,120},{... | collective-permute-start | bytes 196616 | tf_op jit(solution)/shard_map/ppermute | solution.py:37
  18.8 1.3 %collective-permute-start.7 = (f32[128,128]{1,0:T(8,128)S(1)}, f32[128,128]{1,0:T(8,128)S(1)}, u32[]{:S(2)}, u32[]{:S(2)}) collective-permute-start(f32[128,128]{1,0:T(8,128)S(1)} %get-tuple-element.9), channel_id=1, source_target_pairs={{0,4},{16,20},{32,36},{48,52},{64,68},{80,84},{96,100},{112,116},{... | collective-permute-start | bytes 196616 | tf_op jit(solution)/shard_map/ppermute | solution.py:37
  20.5 0.7 %slice-done.1 = f32[8,1,1,128]{3,2,1,0:T(1,128)S(1)} async-done(((f32[8,4,1,128]{3,2,1,0:T(1,128)}), f32[8,1,1,128]{3,2,1,0:T(1,128)S(1)}, s32[]{:S(2)}) %slice-start.1) | async-done | bytes 4120 | tf_op jit(solution)/shard_map/slice | solution.py:96
  21.3 1.3 %collective-permute-start.18 = (f32[128,264]{1,0:T(8,128)S(1)}, f32[128,264]{1,0:T(8,128)S(1)}, u32[]{:S(2)}, u32[]{:S(2)}) collective-permute-start(f32[128,264]{1,0:T(8,128)S(1)} %pad_maximum_fusion), channel_id=1, source_target_pairs={{0,8},{16,24},{32,40},{48,56},{64,72},{80,88},{96,104},{112,120},{... | collective-permute-start | bytes 405512 | tf_op jit(solution)/shard_map/ppermute | solution.py:16
  22.7 0.7 %collective-permute-start = (f32[512,128]{1,0:T(8,128)S(1)}, f32[512,128]{1,0:T(8,128)S(1)}, u32[]{:S(2)}, u32[]{:S(2)}) collective-permute-start(f32[512,128]{1,0:T(8,128)S(1)} %slice.30), channel_id=1, source_target_pairs={{0,256},{1,257},{2,258},{3,259},{4,260},{5,261},{6,262},{7,263},{8... | collective-permute-start | bytes 786440 | tf_op jit(solution)/shard_map/ppermute | solution.py:16
  23.5 1.3 %collective-permute-start.10 = (f32[128,128]{1,0:T(8,128)S(1)}, f32[128,128]{1,0:T(8,128)S(1)}, u32[]{:S(2)}, u32[]{:S(2)}) collective-permute-start(f32[128,128]{1,0:T(8,128)S(1)} %select_select_fusion.3), channel_id=1, source_target_pairs={{0,1},{4,5},{8,9},{12,13},{16,17},{20,21},{24,25},{28,29},{32,33},... | collective-permute-start | bytes 196616 | tf_op jit(solution)/shard_map/ppermute | solution.py:37
  24.8 1.3 %collective-permute-start.8 = (f32[128,128]{1,0:T(8,128)S(1)}, f32[128,128]{1,0:T(8,128)S(1)}, u32[]{:S(2)}, u32[]{:S(2)}) collective-permute-start(f32[128,128]{1,0:T(8,128)S(1)} %select_select_fusion.3), channel_id=1, source_target_pairs={{0,3},{4,7},{8,11},{12,15},{16,19},{20,23},{24,27},{28,31},{32,35}... | collective-permute-start | bytes 196616 | tf_op jit(solution)/shard_map/ppermute | solution.py:37
  26.1 1.3 %collective-permute-start.9 = (f32[128,128]{1,0:T(8,128)S(1)}, f32[128,128]{1,0:T(8,128)S(1)}, u32[]{:S(2)}, u32[]{:S(2)}) collective-permute-start(f32[128,128]{1,0:T(8,128)S(1)} %select_select_fusion.3), channel_id=1, source_target_pairs={{0,2},{4,6},{8,10},{12,14},{16,18},{20,22},{24,26},{28,30},{32,34}... | collective-permute-start | bytes 196616 | tf_op jit(solution)/shard_map/ppermute | solution.py:37
  27.5 0.7 %collective-permute-start.1 = (f32[512,128]{1,0:T(8,128)S(1)}, f32[512,128]{1,0:T(8,128)S(1)}, u32[]{:S(2)}, u32[]{:S(2)}) collective-permute-start(f32[512,128]{1,0:T(8,128)S(1)} %broadcast_select_fusion.3), channel_id=1, source_target_pairs={{0,128},{256,384},{1,129},{257,385},{2,130},{258,386},{3,131},{259... | collective-permute-start | bytes 786440 | tf_op jit(solution)/shard_map/ppermute | solution.py:16
  28.2 1.2 %collective-permute-done.9 = f32[128,128]{1,0:T(8,128)S(1)} collective-permute-done((f32[128,128]{1,0:T(8,128)S(1)}, f32[128,128]{1,0:T(8,128)S(1)}, u32[]{:S(2)}, u32[]{:S(2)}) %collective-permute-start.9) | collective-permute-done | bytes 65568 | tf_op jit(solution)/shard_map/ppermute | solution.py:37
  30.0 0.7 %collective-permute-start.12 = (f32[128,128]{1,0:T(8,128)S(1)}, f32[128,128]{1,0:T(8,128)S(1)}, u32[]{:S(2)}, u32[]{:S(2)}) collective-permute-start(f32[128,128]{1,0:T(8,128)S(1)} %select_select_fusion.2), channel_id=1, source_target_pairs={{0,256},{1,257},{2,258},{3,259},{4,260},{5,261},{6,262},{7,263},{8... | collective-permute-start | bytes 196616 | tf_op jit(solution)/shard_map/ppermute | solution.py:37
  31.4 5.7 %collective-permute-start.19 = (f32[128,264]{1,0:T(8,128)S(1)}, f32[128,264]{1,0:T(8,128)S(1)}, u32[]{:S(2)}, u32[]{:S(2)}) collective-permute-start(f32[128,264]{1,0:T(8,128)S(1)} %broadcast_select_fusion.7), channel_id=1, source_target_pairs={{0,4},{8,12},{16,20},{24,28},{32,36},{40,44},{48,52},{56,60},{64,6... | collective-permute-start | bytes 405512 | tf_op jit(solution)/shard_map/ppermute | solution.py:16
  37.2 0.7 %collective-permute-start.2 = (f32[512,128]{1,0:T(8,128)S(1)}, f32[512,128]{1,0:T(8,128)S(1)}, u32[]{:S(2)}, u32[]{:S(2)}) collective-permute-start(f32[512,128]{1,0:T(8,128)S(1)} %broadcast_select_fusion.4), channel_id=1, source_target_pairs={{0,64},{128,192},{256,320},{384,448},{1,65},{129,193},{257,321},{3... | collective-permute-start | bytes 786440 | tf_op jit(solution)/shard_map/ppermute | solution.py:16
  40.0 1.3 %collective-permute-start.20 = (f32[128,264]{1,0:T(8,128)S(1)}, f32[128,264]{1,0:T(8,128)S(1)}, u32[]{:S(2)}, u32[]{:S(2)}) collective-permute-start(f32[128,264]{1,0:T(8,128)S(1)} %broadcast_select_fusion.8), channel_id=1, source_target_pairs={{0,2},{4,6},{8,10},{12,14},{16,18},{20,22},{24,26},{28,30},{32,34}... | collective-permute-start | bytes 405512 | tf_op jit(solution)/shard_map/ppermute | solution.py:16
  41.3 0.7 %collective-permute-start.3 = (f32[512,128]{1,0:T(8,128)S(1)}, f32[512,128]{1,0:T(8,128)S(1)}, u32[]{:S(2)}, u32[]{:S(2)}) collective-permute-start(f32[512,128]{1,0:T(8,128)S(1)} %broadcast_select_fusion.5), channel_id=1, source_target_pairs={{0,32},{64,96},{128,160},{192,224},{256,288},{320,352},{384,416},{... | collective-permute-start | bytes 786440 | tf_op jit(solution)/shard_map/ppermute | solution.py:16
  42.1 1.3 %collective-permute-start.17 = (f32[128,128]{1,0:T(8,128)S(1)}, f32[128,128]{1,0:T(8,128)S(1)}, u32[]{:S(2)}, u32[]{:S(2)}) collective-permute-start(f32[128,128]{1,0:T(8,128)S(1)} %select_select_fusion), channel_id=1, source_target_pairs={{0,16},{32,48},{64,80},{96,112},{128,144},{160,176},{192,208},{224... | collective-permute-start | bytes 196616 | tf_op jit(solution)/shard_map/ppermute | solution.py:37
  43.9 1.3 %collective-permute-start.21 = (f32[128,264]{1,0:T(8,128)S(1)}, f32[128,264]{1,0:T(8,128)S(1)}, u32[]{:S(2)}, u32[]{:S(2)}) collective-permute-start(f32[128,264]{1,0:T(8,128)S(1)} %broadcast_select_fusion.9), channel_id=1, source_target_pairs={{0,1},{2,3},{4,5},{6,7},{8,9},{10,11},{12,13},{14,15},{16,17},{18,... | collective-permute-start | bytes 405512 | tf_op jit(solution)/shard_map/ppermute | solution.py:16
  45.3 1.3 %collective-permute-start.4 = (f32[512,128]{1,0:T(8,128)S(1)}, f32[512,128]{1,0:T(8,128)S(1)}, u32[]{:S(2)}, u32[]{:S(2)}) collective-permute-start(f32[512,128]{1,0:T(8,128)S(1)} %broadcast_select_fusion.6), channel_id=1, source_target_pairs={{0,16},{32,48},{64,80},{96,112},{128,144},{160,176},{192,208},{224... | collective-permute-start | bytes 786440 | tf_op jit(solution)/shard_map/ppermute | solution.py:16
  46.7 10.3 %collective-permute-done.17 = f32[128,128]{1,0:T(8,128)S(1)} collective-permute-done((f32[128,128]{1,0:T(8,128)S(1)}, f32[128,128]{1,0:T(8,128)S(1)}, u32[]{:S(2)}, u32[]{:S(2)}) %collective-permute-start.17) | collective-permute-done | bytes 65568 | tf_op jit(solution)/shard_map/ppermute | solution.py:37
  57.4 3.6 %collective-permute-done.4 = f32[512,128]{1,0:T(8,128)S(1)} collective-permute-done((f32[512,128]{1,0:T(8,128)S(1)}, f32[512,128]{1,0:T(8,128)S(1)}, u32[]{:S(2)}, u32[]{:S(2)}) %collective-permute-start.4) | collective-permute-done | bytes 262176 | tf_op jit(solution)/shard_map/ppermute | solution.py:16
  63.2 0.7 %broadcast_select_fusion.10 = f32[8,4,1,128]{3,2,1,0:T(1,128)} fusion(pred[4]{0:T(512)(128)(4,1)S(1)} %get-tuple-element.13, f32[8,4,1,128]{3,0,1,2:T(8,128)S(1)} %fusion, f32[8,128]{1,0:T(8,128)S(1)} %slice-done), kind=kLoop, calls=%fused_computation.28 | loop fusion | flops 4096 | bytes 36868 | tf_op jit(solution)/shard_map/jit(_where)/select_n | solution.py:130
  63.9 1.5 %broadcast_select_fusion = f32[4,1,128,2,1,128]{5,4,3,2,1,0:T(1,128)} fusion(pred[2]{0:T(512)(128)(4,1)S(1)} %fusion.9, f32[4,1,128,2,1,128]{5,4,3,2,1,0:T(1,128)S(1)} %bitcast.33, pred[4,2]{1,0:T(4,128)(4,1)S(1)} %broadcast_and_fusion, f32[4,128,128]{2,1,0:T(8,128)S(1)} %broadcast_select_fusion.2), kind=kLoop, calls=%fused_computation.3 | loop fusion | flops 262144 | bytes 1310730 | tf_op jit(solution)/shard_map/jit(_where)/select_n | solution.py:122
  (63 shorter events, 7.6 us)
Async XLA Ops:
  0.6 19.5 %copy-start = (f32[4,1,128,2,1,128]{5,4,3,2,1,0:T(1,128)S(1)}, f32[4,1,128,2,1,128]{5,4,3,2,1,0:T(1,128)}, u32[]{:S(2)}) copy-start(f32[4,1,128,2,1,128]{5,4,3,2,1,0:T(1,128)} %param.4) | copy-start | bytes 1572868
  1.8 21.6 %collective-permute-start.5 = (f32[128,128]{1,0:T(8,128)S(1)}, f32[128,128]{1,0:T(8,128)S(1)}, u32[]{:S(2)}, u32[]{:S(2)}) collective-permute-start(f32[128,128]{1,0:T(8,128)S(1)} %get-tuple-element.9), channel_id=1, source_target_pairs={{0,12},{16,28},{32,44},{48,60},{64,76},{80,92},{96,108},{112,124},... | collective-permute-start | bytes 196616 | tf_op jit(solution)/shard_map/ppermute | solution.py:37
  15.1 8.4 %collective-permute-start.6 = (f32[128,128]{1,0:T(8,128)S(1)}, f32[128,128]{1,0:T(8,128)S(1)}, u32[]{:S(2)}, u32[]{:S(2)}) collective-permute-start(f32[128,128]{1,0:T(8,128)S(1)} %get-tuple-element.9), channel_id=1, source_target_pairs={{0,8},{16,24},{32,40},{48,56},{64,72},{80,88},{96,104},{112,120},{... | collective-permute-start | bytes 196616 | tf_op jit(solution)/shard_map/ppermute | solution.py:37
  18.8 4.7 %collective-permute-start.7 = (f32[128,128]{1,0:T(8,128)S(1)}, f32[128,128]{1,0:T(8,128)S(1)}, u32[]{:S(2)}, u32[]{:S(2)}) collective-permute-start(f32[128,128]{1,0:T(8,128)S(1)} %get-tuple-element.9), channel_id=1, source_target_pairs={{0,4},{16,20},{32,36},{48,52},{64,68},{80,84},{96,100},{112,116},{... | collective-permute-start | bytes 196616 | tf_op jit(solution)/shard_map/ppermute | solution.py:37
  21.3 10.1 %collective-permute-start.18 = (f32[128,264]{1,0:T(8,128)S(1)}, f32[128,264]{1,0:T(8,128)S(1)}, u32[]{:S(2)}, u32[]{:S(2)}) collective-permute-start(f32[128,264]{1,0:T(8,128)S(1)} %pad_maximum_fusion), channel_id=1, source_target_pairs={{0,8},{16,24},{32,40},{48,56},{64,72},{80,88},{96,104},{112,120},{... | collective-permute-start | bytes 405512 | tf_op jit(solution)/shard_map/ppermute | solution.py:16
  22.7 4.8 %collective-permute-start = (f32[512,128]{1,0:T(8,128)S(1)}, f32[512,128]{1,0:T(8,128)S(1)}, u32[]{:S(2)}, u32[]{:S(2)}) collective-permute-start(f32[512,128]{1,0:T(8,128)S(1)} %slice.30), channel_id=1, source_target_pairs={{0,256},{1,257},{2,258},{3,259},{4,260},{5,261},{6,262},{7,263},{8... | collective-permute-start | bytes 786440 | tf_op jit(solution)/shard_map/ppermute | solution.py:16
  23.5 4.6 %collective-permute-start.10 = (f32[128,128]{1,0:T(8,128)S(1)}, f32[128,128]{1,0:T(8,128)S(1)}, u32[]{:S(2)}, u32[]{:S(2)}) collective-permute-start(f32[128,128]{1,0:T(8,128)S(1)} %select_select_fusion.3), channel_id=1, source_target_pairs={{0,1},{4,5},{8,9},{12,13},{16,17},{20,21},{24,25},{28,29},{32,33},... | collective-permute-start | bytes 196616 | tf_op jit(solution)/shard_map/ppermute | solution.py:37
  24.8 3.3 %collective-permute-start.8 = (f32[128,128]{1,0:T(8,128)S(1)}, f32[128,128]{1,0:T(8,128)S(1)}, u32[]{:S(2)}, u32[]{:S(2)}) collective-permute-start(f32[128,128]{1,0:T(8,128)S(1)} %select_select_fusion.3), channel_id=1, source_target_pairs={{0,3},{4,7},{8,11},{12,15},{16,19},{20,23},{24,27},{28,31},{32,35}... | collective-permute-start | bytes 196616 | tf_op jit(solution)/shard_map/ppermute | solution.py:37
  26.1 3.2 %collective-permute-start.9 = (f32[128,128]{1,0:T(8,128)S(1)}, f32[128,128]{1,0:T(8,128)S(1)}, u32[]{:S(2)}, u32[]{:S(2)}) collective-permute-start(f32[128,128]{1,0:T(8,128)S(1)} %select_select_fusion.3), channel_id=1, source_target_pairs={{0,2},{4,6},{8,10},{12,14},{16,18},{20,22},{24,26},{28,30},{32,34}... | collective-permute-start | bytes 196616 | tf_op jit(solution)/shard_map/ppermute | solution.py:37
  27.5 9.6 %collective-permute-start.1 = (f32[512,128]{1,0:T(8,128)S(1)}, f32[512,128]{1,0:T(8,128)S(1)}, u32[]{:S(2)}, u32[]{:S(2)}) collective-permute-start(f32[512,128]{1,0:T(8,128)S(1)} %broadcast_select_fusion.3), channel_id=1, source_target_pairs={{0,128},{256,384},{1,129},{257,385},{2,130},{258,386},{3,131},{259... | collective-permute-start | bytes 786440 | tf_op jit(solution)/shard_map/ppermute | solution.py:16
  29.4 8.5 %collective-permute-start.11 = (f32[128,128]{1,0:T(8,128)S(1)}, f32[128,128]{1,0:T(8,128)S(1)}, u32[]{:S(2)}, u32[]{:S(2)}) collective-permute-start(f32[128,128]{1,0:T(8,128)S(1)} %select_select_fusion.2), channel_id=1, source_target_pairs={{0,384},{1,385},{2,386},{3,387},{4,388},{5,389},{6,390},{7,391},{8... | collective-permute-start | bytes 196616 | tf_op jit(solution)/shard_map/ppermute | solution.py:37
  30.0 7.8 %collective-permute-start.12 = (f32[128,128]{1,0:T(8,128)S(1)}, f32[128,128]{1,0:T(8,128)S(1)}, u32[]{:S(2)}, u32[]{:S(2)}) collective-permute-start(f32[128,128]{1,0:T(8,128)S(1)} %select_select_fusion.2), channel_id=1, source_target_pairs={{0,256},{1,257},{2,258},{3,259},{4,260},{5,261},{6,262},{7,263},{8... | collective-permute-start | bytes 196616 | tf_op jit(solution)/shard_map/ppermute | solution.py:37
  30.7 7.2 %collective-permute-start.13 = (f32[128,128]{1,0:T(8,128)S(1)}, f32[128,128]{1,0:T(8,128)S(1)}, u32[]{:S(2)}, u32[]{:S(2)}) collective-permute-start(f32[128,128]{1,0:T(8,128)S(1)} %select_select_fusion.2), channel_id=1, source_target_pairs={{0,128},{1,129},{2,130},{3,131},{4,132},{5,133},{6,134},{7,135},{8... | collective-permute-start | bytes 196616 | tf_op jit(solution)/shard_map/ppermute | solution.py:37
  31.4 8.5 %collective-permute-start.19 = (f32[128,264]{1,0:T(8,128)S(1)}, f32[128,264]{1,0:T(8,128)S(1)}, u32[]{:S(2)}, u32[]{:S(2)}) collective-permute-start(f32[128,264]{1,0:T(8,128)S(1)} %broadcast_select_fusion.7), channel_id=1, source_target_pairs={{0,4},{8,12},{16,20},{24,28},{32,36},{40,44},{48,52},{56,60},{64,6... | collective-permute-start | bytes 405512 | tf_op jit(solution)/shard_map/ppermute | solution.py:16
  37.2 4.1 %collective-permute-start.2 = (f32[512,128]{1,0:T(8,128)S(1)}, f32[512,128]{1,0:T(8,128)S(1)}, u32[]{:S(2)}, u32[]{:S(2)}) collective-permute-start(f32[512,128]{1,0:T(8,128)S(1)} %broadcast_select_fusion.4), channel_id=1, source_target_pairs={{0,64},{128,192},{256,320},{384,448},{1,65},{129,193},{257,321},{3... | collective-permute-start | bytes 786440 | tf_op jit(solution)/shard_map/ppermute | solution.py:16
  37.9 4.1 %collective-permute-start.14 = (f32[128,128]{1,0:T(8,128)S(1)}, f32[128,128]{1,0:T(8,128)S(1)}, u32[]{:S(2)}, u32[]{:S(2)}) collective-permute-start(f32[128,128]{1,0:T(8,128)S(1)} %select_select_fusion.1), channel_id=1, source_target_pairs={{0,96},{128,224},{256,352},{384,480},{1,97},{129,225},{257,353},{3... | collective-permute-start | bytes 196616 | tf_op jit(solution)/shard_map/ppermute | solution.py:37
  38.6 3.4 %collective-permute-start.15 = (f32[128,128]{1,0:T(8,128)S(1)}, f32[128,128]{1,0:T(8,128)S(1)}, u32[]{:S(2)}, u32[]{:S(2)}) collective-permute-start(f32[128,128]{1,0:T(8,128)S(1)} %select_select_fusion.1), channel_id=1, source_target_pairs={{0,64},{128,192},{256,320},{384,448},{1,65},{129,193},{257,321},{3... | collective-permute-start | bytes 196616 | tf_op jit(solution)/shard_map/ppermute | solution.py:37
  39.3 2.8 %collective-permute-start.16 = (f32[128,128]{1,0:T(8,128)S(1)}, f32[128,128]{1,0:T(8,128)S(1)}, u32[]{:S(2)}, u32[]{:S(2)}) collective-permute-start(f32[128,128]{1,0:T(8,128)S(1)} %select_select_fusion.1), channel_id=1, source_target_pairs={{0,32},{128,160},{256,288},{384,416},{1,33},{129,161},{257,289},{3... | collective-permute-start | bytes 196616 | tf_op jit(solution)/shard_map/ppermute | solution.py:37
  40.0 3.9 %collective-permute-start.20 = (f32[128,264]{1,0:T(8,128)S(1)}, f32[128,264]{1,0:T(8,128)S(1)}, u32[]{:S(2)}, u32[]{:S(2)}) collective-permute-start(f32[128,264]{1,0:T(8,128)S(1)} %broadcast_select_fusion.8), channel_id=1, source_target_pairs={{0,2},{4,6},{8,10},{12,14},{16,18},{20,22},{24,26},{28,30},{32,34}... | collective-permute-start | bytes 405512 | tf_op jit(solution)/shard_map/ppermute | solution.py:16
  41.3 3.9 %collective-permute-start.3 = (f32[512,128]{1,0:T(8,128)S(1)}, f32[512,128]{1,0:T(8,128)S(1)}, u32[]{:S(2)}, u32[]{:S(2)}) collective-permute-start(f32[512,128]{1,0:T(8,128)S(1)} %broadcast_select_fusion.5), channel_id=1, source_target_pairs={{0,32},{64,96},{128,160},{192,224},{256,288},{320,352},{384,416},{... | collective-permute-start | bytes 786440 | tf_op jit(solution)/shard_map/ppermute | solution.py:16
  42.1 14.9 %collective-permute-start.17 = (f32[128,128]{1,0:T(8,128)S(1)}, f32[128,128]{1,0:T(8,128)S(1)}, u32[]{:S(2)}, u32[]{:S(2)}) collective-permute-start(f32[128,128]{1,0:T(8,128)S(1)} %select_select_fusion), channel_id=1, source_target_pairs={{0,16},{32,48},{64,80},{96,112},{128,144},{160,176},{192,208},{224... | collective-permute-start | bytes 196616 | tf_op jit(solution)/shard_map/ppermute | solution.py:37
  43.9 13.0 %collective-permute-start.21 = (f32[128,264]{1,0:T(8,128)S(1)}, f32[128,264]{1,0:T(8,128)S(1)}, u32[]{:S(2)}, u32[]{:S(2)}) collective-permute-start(f32[128,264]{1,0:T(8,128)S(1)} %broadcast_select_fusion.9), channel_id=1, source_target_pairs={{0,1},{2,3},{4,5},{6,7},{8,9},{10,11},{12,13},{14,15},{16,17},{18,... | collective-permute-start | bytes 405512 | tf_op jit(solution)/shard_map/ppermute | solution.py:16
  45.3 15.8 %collective-permute-start.4 = (f32[512,128]{1,0:T(8,128)S(1)}, f32[512,128]{1,0:T(8,128)S(1)}, u32[]{:S(2)}, u32[]{:S(2)}) collective-permute-start(f32[512,128]{1,0:T(8,128)S(1)} %broadcast_select_fusion.6), channel_id=1, source_target_pairs={{0,16},{32,48},{64,80},{96,112},{128,144},{160,176},{192,208},{224... | collective-permute-start | bytes 786440 | tf_op jit(solution)/shard_map/ppermute | solution.py:16
  57.4 4.6 %copy-start.1 = (f32[264,128]{1,0:T(8,128)}, f32[264,128]{1,0:T(8,128)S(1)}, u32[]{:S(2)}) copy-start(f32[264,128]{1,0:T(8,128)S(1)} %fusion.3) | copy-start | bytes 405508
  (3 other events, 2.1 us)

commit v14 on v13

--- a/solution.py
+++ b/solution.py
@@ -91,7 +91,7 @@
 
     holder = (row_id == 0) & (col_id == 0)
     corner, inverse = lax.cond(holder, factor, skip, local[:block, :block])
-    inverse = spread_wide(spread_wide(inverse, "row"), "col")
+    inverse = spread(spread(inverse, "row"), "col")
     left = spread(local[:, :block], "col")
     top = jnp.concatenate([local[:block], right_sides[:, 0, 0, :].T], axis=1)
     top = spread(top, "row")

time: 66.3 us -> 71.5 us (1.078)
  the two profiles are of different devices: /device:TPU:1 before, /device:TPU:23 now
where the time goes in v14:
time: 71.5 us; the launch traced here: 70.9 us
  starting transfers between devices  38.9 us (54%)
  waiting for transfers between devices  23.1 us (32%)
  local copies, waits for them, and re-layouts  3.26 us (5%)
  other arithmetic  2.7 us (4%)
  matrix products  1.75 us (2%)
  between operations  1.13 us (2%)
    ppermute x18, starting transfers between devices, spread(): arrived = lax.ppermute(block, axis, pairs)  38.9 us
    ppermute x18, waiting for transfers between devices, spread(): arrived = lax.ppermute(block, axis, pairs)  23.1 us
    select_n x1, other arithmetic, on_device(): jnp.where((global_cols == 0)[None, None, :, None], column[:, :, None, :],...  1.52 us
  transfers between devices with their start and end apart: 18, of which 8 were waited for; matrix products, arithmetic and copies ran while one was open for 2% of the time, Pallas kernels for 0%

profile of v14, /device:TPU:23, one launch (start us, length us, event | category | flops | bytes accessed | tf_op | source)
XLA Modules:
  0.0 70.9 jit_solution(7950343739637649841)
XLA Ops:
  0.7 1.1 %copy.18 = f32[64,8,2,128]{3,1,2,0:T(8,128)S(1)} copy(f32[64,8,2,128]{3,2,1,0:T(2,128)} %bitcast.28) | data formatting | bytes 1048576
  1.8 15.4 %collective-permute-start.5 = (f32[128,128]{1,0:T(8,128)S(1)}, f32[128,128]{1,0:T(8,128)S(1)}, u32[]{:S(2)}, u32[]{:S(2)}) collective-permute-start(f32[128,128]{1,0:T(8,128)S(1)} %get-tuple-element.9), channel_id=1, source_target_pairs={{0,8},{16,24},{32,40},{48,56},{64,72},{80,88},{96,104},{112,120},{... | collective-permute-start | bytes 196616 | tf_op jit(solution)/shard_map/ppermute | solution.py:16
  17.7 0.7 slice-done.1
  18.5 1.3 %collective-permute-start.14 = (f32[128,264]{1,0:T(8,128)S(1)}, f32[128,264]{1,0:T(8,128)S(1)}, u32[]{:S(2)}, u32[]{:S(2)}) collective-permute-start(f32[128,264]{1,0:T(8,128)S(1)} %pad_maximum_fusion), channel_id=1, source_target_pairs={{0,8},{16,24},{32,40},{48,56},{64,72},{80,88},{96,104},{112,120},{... | collective-permute-start | bytes 405512 | tf_op jit(solution)/shard_map/ppermute | solution.py:16
  19.9 0.7 collective-permute-start
  20.6 1.3 %collective-permute-start.6 = (f32[128,128]{1,0:T(8,128)S(1)}, f32[128,128]{1,0:T(8,128)S(1)}, u32[]{:S(2)}, u32[]{:S(2)}) collective-permute-start(f32[128,128]{1,0:T(8,128)S(1)} %broadcast_select_fusion.11), channel_id=1, source_target_pairs={{0,4},{8,12},{16,20},{24,28},{32,36},{40,44},{48,52},{56,60},{64,6... | collective-permute-start | bytes 196616 | tf_op jit(solution)/shard_map/ppermute | solution.py:16
  21.9 2.9 %collective-permute-done.6 = f32[128,128]{1,0:T(8,128)S(1)} collective-permute-done((f32[128,128]{1,0:T(8,128)S(1)}, f32[128,128]{1,0:T(8,128)S(1)}, u32[]{:S(2)}, u32[]{:S(2)}) %collective-permute-start.6) | collective-permute-done | bytes 65568 | tf_op jit(solution)/shard_map/ppermute | solution.py:16
  24.8 1.3 %collective-permute-start.7 = (f32[128,128]{1,0:T(8,128)S(1)}, f32[128,128]{1,0:T(8,128)S(1)}, u32[]{:S(2)}, u32[]{:S(2)}) collective-permute-start(f32[128,128]{1,0:T(8,128)S(1)} %broadcast_select_fusion.12), channel_id=1, source_target_pairs={{0,2},{4,6},{8,10},{12,14},{16,18},{20,22},{24,26},{28,30},{32,34}... | collective-permute-start | bytes 196616 | tf_op jit(solution)/shard_map/ppermute | solution.py:16
  26.1 1.3 %collective-permute-done.7 = f32[128,128]{1,0:T(8,128)S(1)} collective-permute-done((f32[128,128]{1,0:T(8,128)S(1)}, f32[128,128]{1,0:T(8,128)S(1)}, u32[]{:S(2)}, u32[]{:S(2)}) %collective-permute-start.7) | collective-permute-done | bytes 65568 | tf_op jit(solution)/shard_map/ppermute | solution.py:16
  27.4 1.3 %collective-permute-start.8 = (f32[128,128]{1,0:T(8,128)S(1)}, f32[128,128]{1,0:T(8,128)S(1)}, u32[]{:S(2)}, u32[]{:S(2)}) collective-permute-start(f32[128,128]{1,0:T(8,128)S(1)} %broadcast_select_fusion.13), channel_id=1, source_target_pairs={{0,1},{2,3},{4,5},{6,7},{8,9},{10,11},{12,13},{14,15},{16,17},{18,... | collective-permute-start | bytes 196616 | tf_op jit(solution)/shard_map/ppermute | solution.py:16
  28.8 1.2 %collective-permute-done.8 = f32[128,128]{1,0:T(8,128)S(1)} collective-permute-done((f32[128,128]{1,0:T(8,128)S(1)}, f32[128,128]{1,0:T(8,128)S(1)}, u32[]{:S(2)}, u32[]{:S(2)}) %collective-permute-start.8) | collective-permute-done | bytes 65568 | tf_op jit(solution)/shard_map/ppermute | solution.py:16
  30.8 0.7 collective-permute-start.1
  32.2 7.7 %collective-permute-start.15 = (f32[128,264]{1,0:T(8,128)S(1)}, f32[128,264]{1,0:T(8,128)S(1)}, u32[]{:S(2)}, u32[]{:S(2)}) collective-permute-start(f32[128,264]{1,0:T(8,128)S(1)} %broadcast_select_fusion.7), channel_id=1, source_target_pairs={{0,4},{8,12},{16,20},{24,28},{32,36},{40,44},{48,52},{56,60},{64,6... | collective-permute-start | bytes 405512 | tf_op jit(solution)/shard_map/ppermute | solution.py:16
  41.4 1.1 %collective-permute-done.15 = f32[128,264]{1,0:T(8,128)S(1)} collective-permute-done((f32[128,264]{1,0:T(8,128)S(1)}, f32[128,264]{1,0:T(8,128)S(1)}, u32[]{:S(2)}, u32[]{:S(2)}) %collective-permute-start.15) | collective-permute-done | bytes 135200 | tf_op jit(solution)/shard_map/ppermute | solution.py:16
  42.5 1.3 %collective-permute-start.16 = (f32[128,264]{1,0:T(8,128)S(1)}, f32[128,264]{1,0:T(8,128)S(1)}, u32[]{:S(2)}, u32[]{:S(2)}) collective-permute-start(f32[128,264]{1,0:T(8,128)S(1)} %broadcast_select_fusion.8), channel_id=1, source_target_pairs={{0,2},{4,6},{8,10},{12,14},{16,18},{20,22},{24,26},{28,30},{32,34}... | collective-permute-start | bytes 405512 | tf_op jit(solution)/shard_map/ppermute | solution.py:16
  45.3 2.8 %collective-permute-done.16 = f32[128,264]{1,0:T(8,128)S(1)} collective-permute-done((f32[128,264]{1,0:T(8,128)S(1)}, f32[128,264]{1,0:T(8,128)S(1)}, u32[]{:S(2)}, u32[]{:S(2)}) %collective-permute-start.16) | collective-permute-done | bytes 135200 | tf_op jit(solution)/shard_map/ppermute | solution.py:16
  48.1 1.3 %collective-permute-start.17 = (f32[128,264]{1,0:T(8,128)S(1)}, f32[128,264]{1,0:T(8,128)S(1)}, u32[]{:S(2)}, u32[]{:S(2)}) collective-permute-start(f32[128,264]{1,0:T(8,128)S(1)} %broadcast_select_fusion.9), channel_id=1, source_target_pairs={{0,1},{2,3},{4,5},{6,7},{8,9},{10,11},{12,13},{14,15},{16,17},{18,... | collective-permute-start | bytes 405512 | tf_op jit(solution)/shard_map/ppermute | solution.py:16
  49.5 1.3 %collective-permute-start.13 = (f32[128,128]{1,0:T(8,128)S(1)}, f32[128,128]{1,0:T(8,128)S(1)}, u32[]{:S(2)}, u32[]{:S(2)}) collective-permute-start(f32[128,128]{1,0:T(8,128)S(1)} %broadcast_select_fusion.18), channel_id=1, source_target_pairs={{0,16},{32,48},{64,80},{96,112},{128,144},{160,176},{192,208},{224... | collective-permute-start | bytes 196616 | tf_op jit(solution)/shard_map/ppermute | solution.py:16
  50.8 1.3 %collective-permute-start.4 = (f32[512,128]{1,0:T(8,128)S(1)}, f32[512,128]{1,0:T(8,128)S(1)}, u32[]{:S(2)}, u32[]{:S(2)}) collective-permute-start(f32[512,128]{1,0:T(8,128)S(1)} %broadcast_select_fusion.6), channel_id=1, source_target_pairs={{0,16},{32,48},{64,80},{96,112},{128,144},{160,176},{192,208},{224... | collective-permute-start | bytes 786440 | tf_op jit(solution)/shard_map/ppermute | solution.py:16
  52.2 1.7 %collective-permute-done.17 = f32[128,264]{1,0:T(8,128)S(1)} collective-permute-done((f32[128,264]{1,0:T(8,128)S(1)}, f32[128,264]{1,0:T(8,128)S(1)}, u32[]{:S(2)}, u32[]{:S(2)}) %collective-permute-start.17) | collective-permute-done | bytes 135200 | tf_op jit(solution)/shard_map/ppermute | solution.py:16
  53.9 6.6 %collective-permute-done.13 = f32[128,128]{1,0:T(8,128)S(1)} collective-permute-done((f32[128,128]{1,0:T(8,128)S(1)}, f32[128,128]{1,0:T(8,128)S(1)}, u32[]{:S(2)}, u32[]{:S(2)}) %collective-permute-start.13) | collective-permute-done | bytes 65568 | tf_op jit(solution)/shard_map/ppermute | solution.py:16
  61.0 5.4 %collective-permute-done.4 = f32[512,128]{1,0:T(8,128)S(1)} collective-permute-done((f32[512,128]{1,0:T(8,128)S(1)}, f32[512,128]{1,0:T(8,128)S(1)}, u32[]{:S(2)}, u32[]{:S(2)}) %collective-permute-start.4) | collective-permute-done | bytes 262176 | tf_op jit(solution)/shard_map/ppermute | solution.py:16
  68.6 0.7 broadcast_select_fusion.10
  69.3 1.5 %broadcast_select_fusion = f32[4,1,128,2,1,128]{5,4,3,2,1,0:T(1,128)} fusion(pred[2]{0:T(512)(128)(4,1)S(1)} %fusion.9, f32[4,1,128,2,1,128]{5,4,3,2,1,0:T(1,128)S(1)} %bitcast.33, pred[4,2]{1,0:T(4,128)(4,1)S(1)} %broadcast_and_fusion, f32[4,128,128]{2,1,0:T(8,128)S(1)} %broadcast_select_fusion.2), kind=kLoop, calls=%fused_computation.3 | loop fusion | flops 262144 | bytes 1310730 | tf_op jit(solution)/shard_map/jit(_where)/select_n | solution.py:122
  (59 shorter events, 7.8 us)
Async XLA Ops:
  0.6 16.7 %copy-start = (f32[4,1,128,2,1,128]{5,4,3,2,1,0:T(1,128)S(1)}, f32[4,1,128,2,1,128]{5,4,3,2,1,0:T(1,128)}, u32[]{:S(2)}) copy-start(f32[4,1,128,2,1,128]{5,4,3,2,1,0:T(1,128)} %param.4) | copy-start | bytes 1572868
  1.8 18.7 %collective-permute-start.5 = (f32[128,128]{1,0:T(8,128)S(1)}, f32[128,128]{1,0:T(8,128)S(1)}, u32[]{:S(2)}, u32[]{:S(2)}) collective-permute-start(f32[128,128]{1,0:T(8,128)S(1)} %get-tuple-element.9), channel_id=1, source_target_pairs={{0,8},{16,24},{32,40},{48,56},{64,72},{80,88},{96,104},{112,120},{... | collective-permute-start | bytes 196616 | tf_op jit(solution)/shard_map/ppermute | solution.py:16
  17.7 0.7 slice-start.1
  18.5 13.6 %collective-permute-start.14 = (f32[128,264]{1,0:T(8,128)S(1)}, f32[128,264]{1,0:T(8,128)S(1)}, u32[]{:S(2)}, u32[]{:S(2)}) collective-permute-start(f32[128,264]{1,0:T(8,128)S(1)} %pad_maximum_fusion), channel_id=1, source_target_pairs={{0,8},{16,24},{32,40},{48,56},{64,72},{80,88},{96,104},{112,120},{... | collective-permute-start | bytes 405512 | tf_op jit(solution)/shard_map/ppermute | solution.py:16
  19.9 10.9 %collective-permute-start = (f32[512,128]{1,0:T(8,128)S(1)}, f32[512,128]{1,0:T(8,128)S(1)}, u32[]{:S(2)}, u32[]{:S(2)}) collective-permute-start(f32[512,128]{1,0:T(8,128)S(1)} %slice.30), channel_id=1, source_target_pairs={{0,256},{1,257},{2,258},{3,259},{4,260},{5,261},{6,262},{7,263},{8... | collective-permute-start | bytes 786440 | tf_op jit(solution)/shard_map/ppermute | solution.py:16
  20.6 4.2 %collective-permute-start.6 = (f32[128,128]{1,0:T(8,128)S(1)}, f32[128,128]{1,0:T(8,128)S(1)}, u32[]{:S(2)}, u32[]{:S(2)}) collective-permute-start(f32[128,128]{1,0:T(8,128)S(1)} %broadcast_select_fusion.11), channel_id=1, source_target_pairs={{0,4},{8,12},{16,20},{24,28},{32,36},{40,44},{48,52},{56,60},{64,6... | collective-permute-start | bytes 196616 | tf_op jit(solution)/shard_map/ppermute | solution.py:16
  24.8 2.6 %collective-permute-start.7 = (f32[128,128]{1,0:T(8,128)S(1)}, f32[128,128]{1,0:T(8,128)S(1)}, u32[]{:S(2)}, u32[]{:S(2)}) collective-permute-start(f32[128,128]{1,0:T(8,128)S(1)} %broadcast_select_fusion.12), channel_id=1, source_target_pairs={{0,2},{4,6},{8,10},{12,14},{16,18},{20,22},{24,26},{28,30},{32,34}... | collective-permute-start | bytes 196616 | tf_op jit(solution)/shard_map/ppermute | solution.py:16
  27.4 2.6 %collective-permute-start.8 = (f32[128,128]{1,0:T(8,128)S(1)}, f32[128,128]{1,0:T(8,128)S(1)}, u32[]{:S(2)}, u32[]{:S(2)}) collective-permute-start(f32[128,128]{1,0:T(8,128)S(1)} %broadcast_select_fusion.13), channel_id=1, source_target_pairs={{0,1},{2,3},{4,5},{6,7},{8,9},{10,11},{12,13},{14,15},{16,17},{18,... | collective-permute-start | bytes 196616 | tf_op jit(solution)/shard_map/ppermute | solution.py:16
  30.0 1.4 %collective-permute-start.9 = (f32[128,128]{1,0:T(8,128)S(1)}, f32[128,128]{1,0:T(8,128)S(1)}, u32[]{:S(2)}, u32[]{:S(2)}) collective-permute-start(f32[128,128]{1,0:T(8,128)S(1)} %broadcast_select_fusion.14), channel_id=1, source_target_pairs={{0,256},{1,257},{2,258},{3,259},{4,260},{5,261},{6,262},{7,263},{8... | collective-permute-start | bytes 196616 | tf_op jit(solution)/shard_map/ppermute | solution.py:16
  30.8 9.9 %collective-permute-start.1 = (f32[512,128]{1,0:T(8,128)S(1)}, f32[512,128]{1,0:T(8,128)S(1)}, u32[]{:S(2)}, u32[]{:S(2)}) collective-permute-start(f32[512,128]{1,0:T(8,128)S(1)} %broadcast_select_fusion.3), channel_id=1, source_target_pairs={{0,128},{256,384},{1,129},{257,385},{2,130},{258,386},{3,131},{259... | collective-permute-start | bytes 786440 | tf_op jit(solution)/shard_map/ppermute | solution.py:16
  31.5 8.5 %collective-permute-start.10 = (f32[128,128]{1,0:T(8,128)S(1)}, f32[128,128]{1,0:T(8,128)S(1)}, u32[]{:S(2)}, u32[]{:S(2)}) collective-permute-start(f32[128,128]{1,0:T(8,128)S(1)} %broadcast_select_fusion.15), channel_id=1, source_target_pairs={{0,128},{256,384},{1,129},{257,385},{2,130},{258,386},{3,131},{259... | collective-permute-start | bytes 196616 | tf_op jit(solution)/shard_map/ppermute | solution.py:16
  32.2 10.3 %collective-permute-start.15 = (f32[128,264]{1,0:T(8,128)S(1)}, f32[128,264]{1,0:T(8,128)S(1)}, u32[]{:S(2)}, u32[]{:S(2)}) collective-permute-start(f32[128,264]{1,0:T(8,128)S(1)} %broadcast_select_fusion.7), channel_id=1, source_target_pairs={{0,4},{8,12},{16,20},{24,28},{32,36},{40,44},{48,52},{56,60},{64,6... | collective-permute-start | bytes 405512 | tf_op jit(solution)/shard_map/ppermute | solution.py:16
  39.9 3.9 %collective-permute-start.11 = (f32[128,128]{1,0:T(8,128)S(1)}, f32[128,128]{1,0:T(8,128)S(1)}, u32[]{:S(2)}, u32[]{:S(2)}) collective-permute-start(f32[128,128]{1,0:T(8,128)S(1)} %broadcast_select_fusion.16), channel_id=1, source_target_pairs={{0,64},{128,192},{256,320},{384,448},{1,65},{129,193},{257,321},{3... | collective-permute-start | bytes 196616 | tf_op jit(solution)/shard_map/ppermute | solution.py:16
  40.7 3.9 %collective-permute-start.2 = (f32[512,128]{1,0:T(8,128)S(1)}, f32[512,128]{1,0:T(8,128)S(1)}, u32[]{:S(2)}, u32[]{:S(2)}) collective-permute-start(f32[512,128]{1,0:T(8,128)S(1)} %broadcast_select_fusion.4), channel_id=1, source_target_pairs={{0,64},{128,192},{256,320},{384,448},{1,65},{129,193},{257,321},{3... | collective-permute-start | bytes 786440 | tf_op jit(solution)/shard_map/ppermute | solution.py:16
  42.5 5.6 %collective-permute-start.16 = (f32[128,264]{1,0:T(8,128)S(1)}, f32[128,264]{1,0:T(8,128)S(1)}, u32[]{:S(2)}, u32[]{:S(2)}) collective-permute-start(f32[128,264]{1,0:T(8,128)S(1)} %broadcast_select_fusion.8), channel_id=1, source_target_pairs={{0,2},{4,6},{8,10},{12,14},{16,18},{20,22},{24,26},{28,30},{32,34}... | collective-permute-start | bytes 405512 | tf_op jit(solution)/shard_map/ppermute | solution.py:16
  43.9 5.6 %collective-permute-start.12 = (f32[128,128]{1,0:T(8,128)S(1)}, f32[128,128]{1,0:T(8,128)S(1)}, u32[]{:S(2)}, u32[]{:S(2)}) collective-permute-start(f32[128,128]{1,0:T(8,128)S(1)} %broadcast_select_fusion.17), channel_id=1, source_target_pairs={{0,32},{64,96},{128,160},{192,224},{256,288},{320,352},{384,416},{... | collective-permute-start | bytes 196616 | tf_op jit(solution)/shard_map/ppermute | solution.py:16
  44.6 6.2 %collective-permute-start.3 = (f32[512,128]{1,0:T(8,128)S(1)}, f32[512,128]{1,0:T(8,128)S(1)}, u32[]{:S(2)}, u32[]{:S(2)}) collective-permute-start(f32[512,128]{1,0:T(8,128)S(1)} %broadcast_select_fusion.5), channel_id=1, source_target_pairs={{0,32},{64,96},{128,160},{192,224},{256,288},{320,352},{384,416},{... | collective-permute-start | bytes 786440 | tf_op jit(solution)/shard_map/ppermute | solution.py:16
  48.1 5.8 %collective-permute-start.17 = (f32[128,264]{1,0:T(8,128)S(1)}, f32[128,264]{1,0:T(8,128)S(1)}, u32[]{:S(2)}, u32[]{:S(2)}) collective-permute-start(f32[128,264]{1,0:T(8,128)S(1)} %broadcast_select_fusion.9), channel_id=1, source_target_pairs={{0,1},{2,3},{4,5},{6,7},{8,9},{10,11},{12,13},{14,15},{16,17},{18,... | collective-permute-start | bytes 405512 | tf_op jit(solution)/shard_map/ppermute | solution.py:16
  49.5 11.1 %collective-permute-start.13 = (f32[128,128]{1,0:T(8,128)S(1)}, f32[128,128]{1,0:T(8,128)S(1)}, u32[]{:S(2)}, u32[]{:S(2)}) collective-permute-start(f32[128,128]{1,0:T(8,128)S(1)} %broadcast_select_fusion.18), channel_id=1, source_target_pairs={{0,16},{32,48},{64,80},{96,112},{128,144},{160,176},{192,208},{224... | collective-permute-start | bytes 196616 | tf_op jit(solution)/shard_map/ppermute | solution.py:16
  50.8 15.6 %collective-permute-start.4 = (f32[512,128]{1,0:T(8,128)S(1)}, f32[512,128]{1,0:T(8,128)S(1)}, u32[]{:S(2)}, u32[]{:S(2)}) collective-permute-start(f32[512,128]{1,0:T(8,128)S(1)} %broadcast_select_fusion.6), channel_id=1, source_target_pairs={{0,16},{32,48},{64,80},{96,112},{128,144},{160,176},{192,208},{224... | collective-permute-start | bytes 786440 | tf_op jit(solution)/shard_map/ppermute | solution.py:16
  61.0 6.4 %copy-start.1 = (f32[264,128]{1,0:T(8,128)}, f32[264,128]{1,0:T(8,128)S(1)}, u32[]{:S(2)}) copy-start(f32[264,128]{1,0:T(8,128)S(1)} %fusion.3) | copy-start | bytes 405508
  66.8 0.7 %copy-start.2 = (f32[8,4,1,128]{3,2,1,0:T(1,128)S(1)}, f32[8,4,1,128]{3,2,1,0:T(1,128)}, u32[]{:S(2)}) copy-start(f32[8,4,1,128]{3,2,1,0:T(1,128)} %param.5) | copy-start | bytes 49156
  67.9 0.7 slice-start

commit v15 on v14

--- a/solution.py
+++ b/solution.py
@@ -91,7 +91,7 @@
 
     holder = (row_id == 0) & (col_id == 0)
     corner, inverse = lax.cond(holder, factor, skip, local[:block, :block])
-    inverse = spread(spread(inverse, "row"), "col")
+    inverse = spread(spread_wide(inverse, "row"), "col")
     left = spread(local[:, :block], "col")
     top = jnp.concatenate([local[:block], right_sides[:, 0, 0, :].T], axis=1)
     top = spread(top, "row")

time: 71.5 us -> 70.2 us (0.982)
  waiting for transfers between devices: 23.1 us -> 19.5 us
  starting transfers between devices: 38.9 us -> 41.2 us
    ppermute x0 -> x6, starting transfers between devices: none -> 21.3 us  [spread_wide(): arrived = lax.ppermute(block, axis, pairs)]
    ppermute x18 -> x14, starting transfers between devices: 38.9 us -> 19.9 us  [spread(): arrived = lax.ppermute(block, axis, pairs)]
    ppermute x18 -> x14, waiting for transfers between devices: 23.1 us -> 16.4 us  [spread(): arrived = lax.ppermute(block, axis, pairs)]
    ppermute x0 -> x6, waiting for transfers between devices: none -> 3.03 us  [spread_wide(): arrived = lax.ppermute(block, axis, pairs)]
  transfers between devices with their start and end apart: 18 -> 20, of which waited for: 8 -> 7; matrix products, arithmetic and copies ran while one was open for 2% -> 2% of each run, Pallas kernels for 0% -> 0%
where the time goes in v15:
time: 70.2 us; the launch traced here: 69.6 us
  starting transfers between devices  41.2 us (59%)
  waiting for transfers between devices  19.5 us (28%)
  local copies, waits for them, and re-layouts  3.26 us (5%)
  other arithmetic  2.7 us (4%)
  matrix products  1.74 us (2%)
  between operations  1.15 us (2%)
    ppermute x6, starting transfers between devices, spread_wide(): arrived = lax.ppermute(block, axis, pairs)  21.3 us
    ppermute x14, starting transfers between devices, spread(): arrived = lax.ppermute(block, axis, pairs)  19.9 us
    ppermute x14, waiting for transfers between devices, spread(): arrived = lax.ppermute(block, axis, pairs)  16.4 us
    ppermute x6, waiting for transfers between devices, spread_wide(): arrived = lax.ppermute(block, axis, pairs)  3.03 us
    select_n x1, other arithmetic, on_device(): jnp.where((global_cols == 0)[None, None, :, None], column[:, :, None, :],...  1.52 us
  transfers between devices with their start and end apart: 20, of which 7 were waited for; matrix products, arithmetic and copies ran while one was open for 2% of the time, Pallas kernels for 0%

profile of v15, /device:TPU:23, one launch (start us, length us, event | category | flops | bytes accessed | tf_op | source)
XLA Modules:
  0.0 69.6 jit_solution(5775634133506658942)
XLA Ops:
  0.7 1.1 %copy.18 = f32[64,8,2,128]{3,1,2,0:T(8,128)S(1)} copy(f32[64,8,2,128]{3,2,1,0:T(2,128)} %bitcast.28) | data formatting | bytes 1048576
  1.8 12.5 %collective-permute-start.5 = (f32[128,128]{1,0:T(8,128)S(1)}, f32[128,128]{1,0:T(8,128)S(1)}, u32[]{:S(2)}, u32[]{:S(2)}) collective-permute-start(f32[128,128]{1,0:T(8,128)S(1)} %get-tuple-element.9), channel_id=1, source_target_pairs={{0,12},{16,28},{32,44},{48,60},{64,76},{80,92},{96,108},{112,124},... | collective-permute-start | bytes 196616 | tf_op jit(solution)/shard_map/ppermute | solution.py:37
  14.3 3.7 %collective-permute-start.6 = (f32[128,128]{1,0:T(8,128)S(1)}, f32[128,128]{1,0:T(8,128)S(1)}, u32[]{:S(2)}, u32[]{:S(2)}) collective-permute-start(f32[128,128]{1,0:T(8,128)S(1)} %get-tuple-element.9), channel_id=1, source_target_pairs={{0,8},{16,24},{32,40},{48,56},{64,72},{80,88},{96,104},{112,120},{... | collective-permute-start | bytes 196616 | tf_op jit(solution)/shard_map/ppermute | solution.py:37
  18.0 1.3 %collective-permute-start.7 = (f32[128,128]{1,0:T(8,128)S(1)}, f32[128,128]{1,0:T(8,128)S(1)}, u32[]{:S(2)}, u32[]{:S(2)}) collective-permute-start(f32[128,128]{1,0:T(8,128)S(1)} %get-tuple-element.9), channel_id=1, source_target_pairs={{0,4},{16,20},{32,36},{48,52},{64,68},{80,84},{96,100},{112,116},{... | collective-permute-start | bytes 196616 | tf_op jit(solution)/shard_map/ppermute | solution.py:37
  19.7 0.7 slice-done.1
  20.5 1.3 %collective-permute-start.16 = (f32[128,264]{1,0:T(8,128)S(1)}, f32[128,264]{1,0:T(8,128)S(1)}, u32[]{:S(2)}, u32[]{:S(2)}) collective-permute-start(f32[128,264]{1,0:T(8,128)S(1)} %pad_maximum_fusion), channel_id=1, source_target_pairs={{0,8},{16,24},{32,40},{48,56},{64,72},{80,88},{96,104},{112,120},{... | collective-permute-start | bytes 405512 | tf_op jit(solution)/shard_map/ppermute | solution.py:16
  21.8 0.7 collective-permute-start
  22.6 1.3 %collective-permute-start.10 = (f32[128,128]{1,0:T(8,128)S(1)}, f32[128,128]{1,0:T(8,128)S(1)}, u32[]{:S(2)}, u32[]{:S(2)}) collective-permute-start(f32[128,128]{1,0:T(8,128)S(1)} %select_select_fusion.1), channel_id=1, source_target_pairs={{0,1},{4,5},{8,9},{12,13},{16,17},{20,21},{24,25},{28,29},{32,33},... | collective-permute-start | bytes 196616 | tf_op jit(solution)/shard_map/ppermute | solution.py:37
  23.9 1.3 %collective-permute-start.8 = (f32[128,128]{1,0:T(8,128)S(1)}, f32[128,128]{1,0:T(8,128)S(1)}, u32[]{:S(2)}, u32[]{:S(2)}) collective-permute-start(f32[128,128]{1,0:T(8,128)S(1)} %select_select_fusion.1), channel_id=1, source_target_pairs={{0,3},{4,7},{8,11},{12,15},{16,19},{20,23},{24,27},{28,31},{32,35}... | collective-permute-start | bytes 196616 | tf_op jit(solution)/shard_map/ppermute | solution.py:37
  25.2 1.3 %collective-permute-start.9 = (f32[128,128]{1,0:T(8,128)S(1)}, f32[128,128]{1,0:T(8,128)S(1)}, u32[]{:S(2)}, u32[]{:S(2)}) collective-permute-start(f32[128,128]{1,0:T(8,128)S(1)} %select_select_fusion.1), channel_id=1, source_target_pairs={{0,2},{4,6},{8,10},{12,14},{16,18},{20,22},{24,26},{28,30},{32,34}... | collective-permute-start | bytes 196616 | tf_op jit(solution)/shard_map/ppermute | solution.py:37
  26.7 1.4 %collective-permute-done.8 = f32[128,128]{1,0:T(8,128)S(1)} collective-permute-done((f32[128,128]{1,0:T(8,128)S(1)}, f32[128,128]{1,0:T(8,128)S(1)}, u32[]{:S(2)}, u32[]{:S(2)}) %collective-permute-start.8) | collective-permute-done | bytes 65568 | tf_op jit(solution)/shard_map/ppermute | solution.py:37
  28.2 1.4 %collective-permute-done.9 = f32[128,128]{1,0:T(8,128)S(1)} collective-permute-done((f32[128,128]{1,0:T(8,128)S(1)}, f32[128,128]{1,0:T(8,128)S(1)}, u32[]{:S(2)}, u32[]{:S(2)}) %collective-permute-start.9) | collective-permute-done | bytes 65568 | tf_op jit(solution)/shard_map/ppermute | solution.py:37
  31.1 0.7 collective-permute-start.1
  31.8 8.1 %collective-permute-start.17 = (f32[128,264]{1,0:T(8,128)S(1)}, f32[128,264]{1,0:T(8,128)S(1)}, u32[]{:S(2)}, u32[]{:S(2)}) collective-permute-start(f32[128,264]{1,0:T(8,128)S(1)} %broadcast_select_fusion.7), channel_id=1, source_target_pairs={{0,4},{8,12},{16,20},{24,28},{32,36},{40,44},{48,52},{56,60},{64,6... | collective-permute-start | bytes 405512 | tf_op jit(solution)/shard_map/ppermute | solution.py:16
  40.6 0.7 collective-permute-start.2
  41.3 2.3 %collective-permute-done.17 = f32[128,264]{1,0:T(8,128)S(1)} collective-permute-done((f32[128,264]{1,0:T(8,128)S(1)}, f32[128,264]{1,0:T(8,128)S(1)}, u32[]{:S(2)}, u32[]{:S(2)}) %collective-permute-start.17) | collective-permute-done | bytes 135200 | tf_op jit(solution)/shard_map/ppermute | solution.py:16
  43.6 1.3 %collective-permute-start.18 = (f32[128,264]{1,0:T(8,128)S(1)}, f32[128,264]{1,0:T(8,128)S(1)}, u32[]{:S(2)}, u32[]{:S(2)}) collective-permute-start(f32[128,264]{1,0:T(8,128)S(1)} %broadcast_select_fusion.8), channel_id=1, source_target_pairs={{0,2},{4,6},{8,10},{12,14},{16,18},{20,22},{24,26},{28,30},{32,34}... | collective-permute-start | bytes 405512 | tf_op jit(solution)/shard_map/ppermute | solution.py:16
  46.4 1.3 %collective-permute-start.15 = (f32[128,128]{1,0:T(8,128)S(1)}, f32[128,128]{1,0:T(8,128)S(1)}, u32[]{:S(2)}, u32[]{:S(2)}) collective-permute-start(f32[128,128]{1,0:T(8,128)S(1)} %broadcast_select_fusion.14), channel_id=1, source_target_pairs={{0,16},{32,48},{64,80},{96,112},{128,144},{160,176},{192,208},{224... | collective-permute-start | bytes 196616 | tf_op jit(solution)/shard_map/ppermute | solution.py:16
  48.1 1.3 %collective-permute-start.19 = (f32[128,264]{1,0:T(8,128)S(1)}, f32[128,264]{1,0:T(8,128)S(1)}, u32[]{:S(2)}, u32[]{:S(2)}) collective-permute-start(f32[128,264]{1,0:T(8,128)S(1)} %broadcast_select_fusion.9), channel_id=1, source_target_pairs={{0,1},{2,3},{4,5},{6,7},{8,9},{10,11},{12,13},{14,15},{16,17},{18,... | collective-permute-start | bytes 405512 | tf_op jit(solution)/shard_map/ppermute | solution.py:16
  49.4 1.3 %collective-permute-start.4 = (f32[512,128]{1,0:T(8,128)S(1)}, f32[512,128]{1,0:T(8,128)S(1)}, u32[]{:S(2)}, u32[]{:S(2)}) collective-permute-start(f32[512,128]{1,0:T(8,128)S(1)} %broadcast_select_fusion.6), channel_id=1, source_target_pairs={{0,16},{32,48},{64,80},{96,112},{128,144},{160,176},{192,208},{224... | collective-permute-start | bytes 786440 | tf_op jit(solution)/shard_map/ppermute | solution.py:16
  50.9 8.4 %collective-permute-done.15 = f32[128,128]{1,0:T(8,128)S(1)} collective-permute-done((f32[128,128]{1,0:T(8,128)S(1)}, f32[128,128]{1,0:T(8,128)S(1)}, u32[]{:S(2)}, u32[]{:S(2)}) %collective-permute-start.15) | collective-permute-done | bytes 65568 | tf_op jit(solution)/shard_map/ppermute | solution.py:16
  59.8 5.4 %collective-permute-done.4 = f32[512,128]{1,0:T(8,128)S(1)} collective-permute-done((f32[512,128]{1,0:T(8,128)S(1)}, f32[512,128]{1,0:T(8,128)S(1)}, u32[]{:S(2)}, u32[]{:S(2)}) %collective-permute-start.4) | collective-permute-done | bytes 262176 | tf_op jit(solution)/shard_map/ppermute | solution.py:16
  67.3 0.7 broadcast_select_fusion.10
  68.0 1.5 %broadcast_select_fusion = f32[4,1,128,2,1,128]{5,4,3,2,1,0:T(1,128)} fusion(pred[2]{0:T(512)(128)(4,1)S(1)} %fusion.9, f32[4,1,128,2,1,128]{5,4,3,2,1,0:T(1,128)S(1)} %bitcast.33, pred[4,2]{1,0:T(4,128)(4,1)S(1)} %broadcast_and_fusion, f32[4,128,128]{2,1,0:T(8,128)S(1)} %broadcast_select_fusion.2), kind=kLoop, calls=%fused_computation.3 | loop fusion | flops 262144 | bytes 1310730 | tf_op jit(solution)/shard_map/jit(_where)/select_n | solution.py:122
  (61 shorter events, 7.6 us)
Async XLA Ops:
  0.6 18.6 %copy-start = (f32[4,1,128,2,1,128]{5,4,3,2,1,0:T(1,128)S(1)}, f32[4,1,128,2,1,128]{5,4,3,2,1,0:T(1,128)}, u32[]{:S(2)}) copy-start(f32[4,1,128,2,1,128]{5,4,3,2,1,0:T(1,128)} %param.4) | copy-start | bytes 1572868
  1.8 20.7 %collective-permute-start.5 = (f32[128,128]{1,0:T(8,128)S(1)}, f32[128,128]{1,0:T(8,128)S(1)}, u32[]{:S(2)}, u32[]{:S(2)}) collective-permute-start(f32[128,128]{1,0:T(8,128)S(1)} %get-tuple-element.9), channel_id=1, source_target_pairs={{0,12},{16,28},{32,44},{48,60},{64,76},{80,92},{96,108},{112,124},... | collective-permute-start | bytes 196616 | tf_op jit(solution)/shard_map/ppermute | solution.py:37
  14.3 8.3 %collective-permute-start.6 = (f32[128,128]{1,0:T(8,128)S(1)}, f32[128,128]{1,0:T(8,128)S(1)}, u32[]{:S(2)}, u32[]{:S(2)}) collective-permute-start(f32[128,128]{1,0:T(8,128)S(1)} %get-tuple-element.9), channel_id=1, source_target_pairs={{0,8},{16,24},{32,40},{48,56},{64,72},{80,88},{96,104},{112,120},{... | collective-permute-start | bytes 196616 | tf_op jit(solution)/shard_map/ppermute | solution.py:37
  18.0 4.6 %collective-permute-start.7 = (f32[128,128]{1,0:T(8,128)S(1)}, f32[128,128]{1,0:T(8,128)S(1)}, u32[]{:S(2)}, u32[]{:S(2)}) collective-permute-start(f32[128,128]{1,0:T(8,128)S(1)} %get-tuple-element.9), channel_id=1, source_target_pairs={{0,4},{16,20},{32,36},{48,52},{64,68},{80,84},{96,100},{112,116},{... | collective-permute-start | bytes 196616 | tf_op jit(solution)/shard_map/ppermute | solution.py:37
  20.5 11.3 %collective-permute-start.16 = (f32[128,264]{1,0:T(8,128)S(1)}, f32[128,264]{1,0:T(8,128)S(1)}, u32[]{:S(2)}, u32[]{:S(2)}) collective-permute-start(f32[128,264]{1,0:T(8,128)S(1)} %pad_maximum_fusion), channel_id=1, source_target_pairs={{0,8},{16,24},{32,40},{48,56},{64,72},{80,88},{96,104},{112,120},{... | collective-permute-start | bytes 405512 | tf_op jit(solution)/shard_map/ppermute | solution.py:16
  21.8 9.2 %collective-permute-start = (f32[512,128]{1,0:T(8,128)S(1)}, f32[512,128]{1,0:T(8,128)S(1)}, u32[]{:S(2)}, u32[]{:S(2)}) collective-permute-start(f32[512,128]{1,0:T(8,128)S(1)} %slice.30), channel_id=1, source_target_pairs={{0,256},{1,257},{2,258},{3,259},{4,260},{5,261},{6,262},{7,263},{8... | collective-permute-start | bytes 786440 | tf_op jit(solution)/shard_map/ppermute | solution.py:16
  22.6 4.1 %collective-permute-start.10 = (f32[128,128]{1,0:T(8,128)S(1)}, f32[128,128]{1,0:T(8,128)S(1)}, u32[]{:S(2)}, u32[]{:S(2)}) collective-permute-start(f32[128,128]{1,0:T(8,128)S(1)} %select_select_fusion.1), channel_id=1, source_target_pairs={{0,1},{4,5},{8,9},{12,13},{16,17},{20,21},{24,25},{28,29},{32,33},... | collective-permute-start | bytes 196616 | tf_op jit(solution)/shard_map/ppermute | solution.py:37
  23.9 4.2 %collective-permute-start.8 = (f32[128,128]{1,0:T(8,128)S(1)}, f32[128,128]{1,0:T(8,128)S(1)}, u32[]{:S(2)}, u32[]{:S(2)}) collective-permute-start(f32[128,128]{1,0:T(8,128)S(1)} %select_select_fusion.1), channel_id=1, source_target_pairs={{0,3},{4,7},{8,11},{12,15},{16,19},{20,23},{24,27},{28,31},{32,35}... | collective-permute-start | bytes 196616 | tf_op jit(solution)/shard_map/ppermute | solution.py:37
  25.2 4.3 %collective-permute-start.9 = (f32[128,128]{1,0:T(8,128)S(1)}, f32[128,128]{1,0:T(8,128)S(1)}, u32[]{:S(2)}, u32[]{:S(2)}) collective-permute-start(f32[128,128]{1,0:T(8,128)S(1)} %select_select_fusion.1), channel_id=1, source_target_pairs={{0,2},{4,6},{8,10},{12,14},{16,18},{20,22},{24,26},{28,30},{32,34}... | collective-permute-start | bytes 196616 | tf_op jit(solution)/shard_map/ppermute | solution.py:37
  29.6 0.7 %collective-permute-start.11 = (f32[128,128]{1,0:T(8,128)S(1)}, f32[128,128]{1,0:T(8,128)S(1)}, u32[]{:S(2)}, u32[]{:S(2)}) collective-permute-start(f32[128,128]{1,0:T(8,128)S(1)} %select_select_fusion), channel_id=1, source_target_pairs={{0,256},{1,257},{2,258},{3,259},{4,260},{5,261},{6,262},{7,263},{8... | collective-permute-start | bytes 196616 | tf_op jit(solution)/shard_map/ppermute | solution.py:16
  30.3 9.5 %collective-permute-start.12 = (f32[128,128]{1,0:T(8,128)S(1)}, f32[128,128]{1,0:T(8,128)S(1)}, u32[]{:S(2)}, u32[]{:S(2)}) collective-permute-start(f32[128,128]{1,0:T(8,128)S(1)} %broadcast_select_fusion.11), channel_id=1, source_target_pairs={{0,128},{256,384},{1,129},{257,385},{2,130},{258,386},{3,131},{259... | collective-permute-start | bytes 196616 | tf_op jit(solution)/shard_map/ppermute | solution.py:16
  31.1 9.5 %collective-permute-start.1 = (f32[512,128]{1,0:T(8,128)S(1)}, f32[512,128]{1,0:T(8,128)S(1)}, u32[]{:S(2)}, u32[]{:S(2)}) collective-permute-start(f32[512,128]{1,0:T(8,128)S(1)} %broadcast_select_fusion.3), channel_id=1, source_target_pairs={{0,128},{256,384},{1,129},{257,385},{2,130},{258,386},{3,131},{259... | collective-permute-start | bytes 786440 | tf_op jit(solution)/shard_map/ppermute | solution.py:16
  31.8 11.8 %collective-permute-start.17 = (f32[128,264]{1,0:T(8,128)S(1)}, f32[128,264]{1,0:T(8,128)S(1)}, u32[]{:S(2)}, u32[]{:S(2)}) collective-permute-start(f32[128,264]{1,0:T(8,128)S(1)} %broadcast_select_fusion.7), channel_id=1, source_target_pairs={{0,4},{8,12},{16,20},{24,28},{32,36},{40,44},{48,52},{56,60},{64,6... | collective-permute-start | bytes 405512 | tf_op jit(solution)/shard_map/ppermute | solution.py:16
  39.9 5.1 %collective-permute-start.13 = (f32[128,128]{1,0:T(8,128)S(1)}, f32[128,128]{1,0:T(8,128)S(1)}, u32[]{:S(2)}, u32[]{:S(2)}) collective-permute-start(f32[128,128]{1,0:T(8,128)S(1)} %broadcast_select_fusion.12), channel_id=1, source_target_pairs={{0,64},{128,192},{256,320},{384,448},{1,65},{129,193},{257,321},{3... | collective-permute-start | bytes 196616 | tf_op jit(solution)/shard_map/ppermute | solution.py:16
  40.6 5.0 %collective-permute-start.2 = (f32[512,128]{1,0:T(8,128)S(1)}, f32[512,128]{1,0:T(8,128)S(1)}, u32[]{:S(2)}, u32[]{:S(2)}) collective-permute-start(f32[512,128]{1,0:T(8,128)S(1)} %broadcast_select_fusion.4), channel_id=1, source_target_pairs={{0,64},{128,192},{256,320},{384,448},{1,65},{129,193},{257,321},{3... | collective-permute-start | bytes 786440 | tf_op jit(solution)/shard_map/ppermute | solution.py:16
  43.6 4.4 %collective-permute-start.18 = (f32[128,264]{1,0:T(8,128)S(1)}, f32[128,264]{1,0:T(8,128)S(1)}, u32[]{:S(2)}, u32[]{:S(2)}) collective-permute-start(f32[128,264]{1,0:T(8,128)S(1)} %broadcast_select_fusion.8), channel_id=1, source_target_pairs={{0,2},{4,6},{8,10},{12,14},{16,18},{20,22},{24,26},{28,30},{32,34}... | collective-permute-start | bytes 405512 | tf_op jit(solution)/shard_map/ppermute | solution.py:16
  45.0 1.4 %collective-permute-start.14 = (f32[128,128]{1,0:T(8,128)S(1)}, f32[128,128]{1,0:T(8,128)S(1)}, u32[]{:S(2)}, u32[]{:S(2)}) collective-permute-start(f32[128,128]{1,0:T(8,128)S(1)} %broadcast_select_fusion.13), channel_id=1, source_target_pairs={{0,32},{64,96},{128,160},{192,224},{256,288},{320,352},{384,416},{... | collective-permute-start | bytes 196616 | tf_op jit(solution)/shard_map/ppermute | solution.py:16
  45.7 3.7 %collective-permute-start.3 = (f32[512,128]{1,0:T(8,128)S(1)}, f32[512,128]{1,0:T(8,128)S(1)}, u32[]{:S(2)}, u32[]{:S(2)}) collective-permute-start(f32[512,128]{1,0:T(8,128)S(1)} %broadcast_select_fusion.5), channel_id=1, source_target_pairs={{0,32},{64,96},{128,160},{192,224},{256,288},{320,352},{384,416},{... | collective-permute-start | bytes 786440 | tf_op jit(solution)/shard_map/ppermute | solution.py:16
  46.4 12.8 %collective-permute-start.15 = (f32[128,128]{1,0:T(8,128)S(1)}, f32[128,128]{1,0:T(8,128)S(1)}, u32[]{:S(2)}, u32[]{:S(2)}) collective-permute-start(f32[128,128]{1,0:T(8,128)S(1)} %broadcast_select_fusion.14), channel_id=1, source_target_pairs={{0,16},{32,48},{64,80},{96,112},{128,144},{160,176},{192,208},{224... | collective-permute-start | bytes 196616 | tf_op jit(solution)/shard_map/ppermute | solution.py:16
  48.1 11.2 %collective-permute-start.19 = (f32[128,264]{1,0:T(8,128)S(1)}, f32[128,264]{1,0:T(8,128)S(1)}, u32[]{:S(2)}, u32[]{:S(2)}) collective-permute-start(f32[128,264]{1,0:T(8,128)S(1)} %broadcast_select_fusion.9), channel_id=1, source_target_pairs={{0,1},{2,3},{4,5},{6,7},{8,9},{10,11},{12,13},{14,15},{16,17},{18,... | collective-permute-start | bytes 405512 | tf_op jit(solution)/shard_map/ppermute | solution.py:16
  49.4 15.7 %collective-permute-start.4 = (f32[512,128]{1,0:T(8,128)S(1)}, f32[512,128]{1,0:T(8,128)S(1)}, u32[]{:S(2)}, u32[]{:S(2)}) collective-permute-start(f32[512,128]{1,0:T(8,128)S(1)} %broadcast_select_fusion.6), channel_id=1, source_target_pairs={{0,16},{32,48},{64,80},{96,112},{128,144},{160,176},{192,208},{224... | collective-permute-start | bytes 786440 | tf_op jit(solution)/shard_map/ppermute | solution.py:16
  59.7 6.4 %copy-start.1 = (f32[264,128]{1,0:T(8,128)}, f32[264,128]{1,0:T(8,128)S(1)}, u32[]{:S(2)}) copy-start(f32[264,128]{1,0:T(8,128)S(1)} %fusion.3) | copy-start | bytes 405508
  65.5 0.7 %copy-start.2 = (f32[8,4,1,128]{3,2,1,0:T(1,128)S(1)}, f32[8,4,1,128]{3,2,1,0:T(1,128)}, u32[]{:S(2)}) copy-start(f32[8,4,1,128]{3,2,1,0:T(1,128)} %param.5) | copy-start | bytes 49156
  66.6 0.7 %slice-start = ((f32[264,128]{1,0:T(8,128)}), f32[8,128]{1,0:T(8,128)S(1)}, s32[]{:S(2)}) async-start(f32[264,128]{1,0:T(8,128)} %copy-done.1), calls=%async_computation | async-start | bytes 8192 | tf_op jit(solution)/shard_map/slice | solution.py:106
  (1 other events, 0.7 us)

commit v16 on v15

--- a/solution.py
+++ b/solution.py
@@ -91,7 +91,7 @@
 
     holder = (row_id == 0) & (col_id == 0)
     corner, inverse = lax.cond(holder, factor, skip, local[:block, :block])
-    inverse = spread(spread_wide(inverse, "row"), "col")
+    inverse = spread_wide(spread_wide(inverse, "col"), "row")
     left = spread(local[:, :block], "col")
     top = jnp.concatenate([local[:block], right_sides[:, 0, 0, :].T], axis=1)
     top = spread(top, "row")

time: 70.2 us -> 66 us (0.940)
  the two profiles are of different devices: /device:TPU:23 before, /device:TPU:1 now
where the time goes in v16:
time: 66 us; the launch traced here: 65 us
  starting transfers between devices  37.2 us (56%)
  waiting for transfers between devices  18.8 us (28%)
  local copies, waits for them, and re-layouts  3.26 us (5%)
  other arithmetic  2.69 us (4%)
  matrix products  1.75 us (3%)
  between operations  1.23 us (2%)
    ppermute x9, starting transfers between devices, spread(): arrived = lax.ppermute(block, axis, pairs)  24.2 us
    ppermute x13, starting transfers between devices, spread_wide(): arrived = lax.ppermute(block, axis, pairs)  13 us
    ppermute x9, waiting for transfers between devices, spread(): arrived = lax.ppermute(block, axis, pairs)  10.5 us
    ppermute x13, waiting for transfers between devices, spread_wide(): arrived = lax.ppermute(block, axis, pairs)  8.32 us
    select_n x1, other arithmetic, on_device(): jnp.where((global_cols == 0)[None, None, :, None], column[:, :, None, :],...  1.52 us
  transfers between devices with their start and end apart: 22, of which 3 were waited for; matrix products, arithmetic and copies ran while one was open for 2% of the time, Pallas kernels for 0%

profile of v16, /device:TPU:1, one launch (start us, length us, event | category | flops | bytes accessed | tf_op | source)
XLA Modules:
  0.0 65.0 jit_solution(16731212291693739066)
XLA Ops:
  0.7 1.1 %copy.18 = f32[64,8,2,128]{3,1,2,0:T(8,128)S(1)} copy(f32[64,8,2,128]{3,2,1,0:T(2,128)} %bitcast.30) | data formatting | bytes 1048576
  1.8 0.7 %collective-permute-start.7 = (f32[128,128]{1,0:T(8,128)S(1)}, f32[128,128]{1,0:T(8,128)S(1)}, u32[]{:S(2)}, u32[]{:S(2)}) collective-permute-start(f32[128,128]{1,0:T(8,128)S(1)} %get-tuple-element.9), channel_id=1, source_target_pairs={{0,128},{1,129},{2,130},{3,131},{4,132},{5,133},{6,134},{7,135},{8... | collective-permute-start | bytes 196616 | tf_op jit(solution)/shard_map/ppermute | solution.py:37
  4.3 0.7 %slice-done.1 = f32[8,1,1,128]{3,2,1,0:T(1,128)S(1)} async-done(((f32[8,4,1,128]{3,2,1,0:T(1,128)}), f32[8,1,1,128]{3,2,1,0:T(1,128)S(1)}, s32[]{:S(2)}) %slice-start.1) | async-done | bytes 4120 | tf_op jit(solution)/shard_map/slice | solution.py:96
  5.1 16.3 %collective-permute-start.18 = (f32[128,264]{1,0:T(8,128)S(1)}, f32[128,264]{1,0:T(8,128)S(1)}, u32[]{:S(2)}, u32[]{:S(2)}) collective-permute-start(f32[128,264]{1,0:T(8,128)S(1)} %pad_maximum_fusion), channel_id=1, source_target_pairs={{0,8},{16,24},{32,40},{48,56},{64,72},{80,88},{96,104},{112,120},{... | collective-permute-start | bytes 405512 | tf_op jit(solution)/shard_map/ppermute | solution.py:16
  21.4 0.7 %collective-permute-start = (f32[512,128]{1,0:T(8,128)S(1)}, f32[512,128]{1,0:T(8,128)S(1)}, u32[]{:S(2)}, u32[]{:S(2)}) collective-permute-start(f32[512,128]{1,0:T(8,128)S(1)} %slice.30), channel_id=1, source_target_pairs={{0,256},{1,257},{2,258},{3,259},{4,260},{5,261},{6,262},{7,263},{8... | collective-permute-start | bytes 786440 | tf_op jit(solution)/shard_map/ppermute | solution.py:16
  24.5 0.7 %collective-permute-start.1 = (f32[512,128]{1,0:T(8,128)S(1)}, f32[512,128]{1,0:T(8,128)S(1)}, u32[]{:S(2)}, u32[]{:S(2)}) collective-permute-start(f32[512,128]{1,0:T(8,128)S(1)} %broadcast_select_fusion.3), channel_id=1, source_target_pairs={{0,128},{256,384},{1,129},{257,385},{2,130},{258,386},{3,131},{259... | collective-permute-start | bytes 786440 | tf_op jit(solution)/shard_map/ppermute | solution.py:16
  25.2 1.3 %collective-permute-start.11 = (f32[128,128]{1,0:T(8,128)S(1)}, f32[128,128]{1,0:T(8,128)S(1)}, u32[]{:S(2)}, u32[]{:S(2)}) collective-permute-start(f32[128,128]{1,0:T(8,128)S(1)} %select_select_fusion.2), channel_id=1, source_target_pairs={{0,16},{32,48},{64,80},{96,112},{128,144},{160,176},{192,208},{224... | collective-permute-start | bytes 196616 | tf_op jit(solution)/shard_map/ppermute | solution.py:37
  26.6 1.3 %collective-permute-start.19 = (f32[128,264]{1,0:T(8,128)S(1)}, f32[128,264]{1,0:T(8,128)S(1)}, u32[]{:S(2)}, u32[]{:S(2)}) collective-permute-start(f32[128,264]{1,0:T(8,128)S(1)} %broadcast_select_fusion.7), channel_id=1, source_target_pairs={{0,4},{8,12},{16,20},{24,28},{32,36},{40,44},{48,52},{56,60},{64,6... | collective-permute-start | bytes 405512 | tf_op jit(solution)/shard_map/ppermute | solution.py:16
  27.9 0.7 %collective-permute-start.2 = (f32[512,128]{1,0:T(8,128)S(1)}, f32[512,128]{1,0:T(8,128)S(1)}, u32[]{:S(2)}, u32[]{:S(2)}) collective-permute-start(f32[512,128]{1,0:T(8,128)S(1)} %broadcast_select_fusion.4), channel_id=1, source_target_pairs={{0,64},{128,192},{256,320},{384,448},{1,65},{129,193},{257,321},{3... | collective-permute-start | bytes 786440 | tf_op jit(solution)/shard_map/ppermute | solution.py:16
  28.6 8.3 %collective-permute-done.11 = f32[128,128]{1,0:T(8,128)S(1)} collective-permute-done((f32[128,128]{1,0:T(8,128)S(1)}, f32[128,128]{1,0:T(8,128)S(1)}, u32[]{:S(2)}, u32[]{:S(2)}) %collective-permute-start.11) | collective-permute-done | bytes 65568 | tf_op jit(solution)/shard_map/ppermute | solution.py:37
  36.9 1.3 %collective-permute-start.14 = (f32[128,128]{1,0:T(8,128)S(1)}, f32[128,128]{1,0:T(8,128)S(1)}, u32[]{:S(2)}, u32[]{:S(2)}) collective-permute-start(f32[128,128]{1,0:T(8,128)S(1)} %broadcast_select_fusion.11), channel_id=1, source_target_pairs={{0,4},{16,20},{32,36},{48,52},{64,68},{80,84},{96,100},{112,116},{... | collective-permute-start | bytes 196616 | tf_op jit(solution)/shard_map/ppermute | solution.py:37
  38.2 1.3 %collective-permute-start.13 = (f32[128,128]{1,0:T(8,128)S(1)}, f32[128,128]{1,0:T(8,128)S(1)}, u32[]{:S(2)}, u32[]{:S(2)}) collective-permute-start(f32[128,128]{1,0:T(8,128)S(1)} %broadcast_select_fusion.11), channel_id=1, source_target_pairs={{0,8},{16,24},{32,40},{48,56},{64,72},{80,88},{96,104},{112,120},{... | collective-permute-start | bytes 196616 | tf_op jit(solution)/shard_map/ppermute | solution.py:37
  39.5 1.3 %collective-permute-start.12 = (f32[128,128]{1,0:T(8,128)S(1)}, f32[128,128]{1,0:T(8,128)S(1)}, u32[]{:S(2)}, u32[]{:S(2)}) collective-permute-start(f32[128,128]{1,0:T(8,128)S(1)} %broadcast_select_fusion.11), channel_id=1, source_target_pairs={{0,12},{16,28},{32,44},{48,60},{64,76},{80,92},{96,108},{112,124},... | collective-permute-start | bytes 196616 | tf_op jit(solution)/shard_map/ppermute | solution.py:37
  40.8 1.3 %collective-permute-start.20 = (f32[128,264]{1,0:T(8,128)S(1)}, f32[128,264]{1,0:T(8,128)S(1)}, u32[]{:S(2)}, u32[]{:S(2)}) collective-permute-start(f32[128,264]{1,0:T(8,128)S(1)} %broadcast_select_fusion.8), channel_id=1, source_target_pairs={{0,2},{4,6},{8,10},{12,14},{16,18},{20,22},{24,26},{28,30},{32,34}... | collective-permute-start | bytes 405512 | tf_op jit(solution)/shard_map/ppermute | solution.py:16
  42.2 0.7 %collective-permute-start.3 = (f32[512,128]{1,0:T(8,128)S(1)}, f32[512,128]{1,0:T(8,128)S(1)}, u32[]{:S(2)}, u32[]{:S(2)}) collective-permute-start(f32[512,128]{1,0:T(8,128)S(1)} %broadcast_select_fusion.5), channel_id=1, source_target_pairs={{0,32},{64,96},{128,160},{192,224},{256,288},{320,352},{384,416},{... | collective-permute-start | bytes 786440 | tf_op jit(solution)/shard_map/ppermute | solution.py:16
  42.9 1.3 %collective-permute-start.17 = (f32[128,128]{1,0:T(8,128)S(1)}, f32[128,128]{1,0:T(8,128)S(1)}, u32[]{:S(2)}, u32[]{:S(2)}) collective-permute-start(f32[128,128]{1,0:T(8,128)S(1)} %select_select_fusion.1), channel_id=1, source_target_pairs={{0,1},{4,5},{8,9},{12,13},{16,17},{20,21},{24,25},{28,29},{32,33},... | collective-permute-start | bytes 196616 | tf_op jit(solution)/shard_map/ppermute | solution.py:37
  44.2 1.3 %collective-permute-start.16 = (f32[128,128]{1,0:T(8,128)S(1)}, f32[128,128]{1,0:T(8,128)S(1)}, u32[]{:S(2)}, u32[]{:S(2)}) collective-permute-start(f32[128,128]{1,0:T(8,128)S(1)} %select_select_fusion.1), channel_id=1, source_target_pairs={{0,2},{4,6},{8,10},{12,14},{16,18},{20,22},{24,26},{28,30},{32,34}... | collective-permute-start | bytes 196616 | tf_op jit(solution)/shard_map/ppermute | solution.py:37
  45.6 1.3 %collective-permute-start.15 = (f32[128,128]{1,0:T(8,128)S(1)}, f32[128,128]{1,0:T(8,128)S(1)}, u32[]{:S(2)}, u32[]{:S(2)}) collective-permute-start(f32[128,128]{1,0:T(8,128)S(1)} %select_select_fusion.1), channel_id=1, source_target_pairs={{0,3},{4,7},{8,11},{12,15},{16,19},{20,23},{24,27},{28,31},{32,35}... | collective-permute-start | bytes 196616 | tf_op jit(solution)/shard_map/ppermute | solution.py:37
  46.9 1.3 %collective-permute-start.21 = (f32[128,264]{1,0:T(8,128)S(1)}, f32[128,264]{1,0:T(8,128)S(1)}, u32[]{:S(2)}, u32[]{:S(2)}) collective-permute-start(f32[128,264]{1,0:T(8,128)S(1)} %broadcast_select_fusion.9), channel_id=1, source_target_pairs={{0,1},{2,3},{4,5},{6,7},{8,9},{10,11},{12,13},{14,15},{16,17},{18,... | collective-permute-start | bytes 405512 | tf_op jit(solution)/shard_map/ppermute | solution.py:16
  48.3 1.3 %collective-permute-start.4 = (f32[512,128]{1,0:T(8,128)S(1)}, f32[512,128]{1,0:T(8,128)S(1)}, u32[]{:S(2)}, u32[]{:S(2)}) collective-permute-start(f32[512,128]{1,0:T(8,128)S(1)} %broadcast_select_fusion.6), channel_id=1, source_target_pairs={{0,16},{32,48},{64,80},{96,112},{128,144},{160,176},{192,208},{224... | collective-permute-start | bytes 786440 | tf_op jit(solution)/shard_map/ppermute | solution.py:16
  49.6 1.9 %collective-permute-done.21 = f32[128,264]{1,0:T(8,128)S(1)} collective-permute-done((f32[128,264]{1,0:T(8,128)S(1)}, f32[128,264]{1,0:T(8,128)S(1)}, u32[]{:S(2)}, u32[]{:S(2)}) %collective-permute-start.21) | collective-permute-done | bytes 135200 | tf_op jit(solution)/shard_map/ppermute | solution.py:16
  52.0 8.6 %collective-permute-done.4 = f32[512,128]{1,0:T(8,128)S(1)} collective-permute-done((f32[512,128]{1,0:T(8,128)S(1)}, f32[512,128]{1,0:T(8,128)S(1)}, u32[]{:S(2)}, u32[]{:S(2)}) %collective-permute-start.4) | collective-permute-done | bytes 262176 | tf_op jit(solution)/shard_map/ppermute | solution.py:16
  62.7 0.7 %broadcast_select_fusion.10 = f32[8,4,1,128]{3,2,1,0:T(1,128)} fusion(pred[4]{0:T(512)(128)(4,1)S(1)} %get-tuple-element.13, f32[8,4,1,128]{3,0,1,2:T(8,128)S(1)} %fusion, f32[8,128]{1,0:T(8,128)S(1)} %slice-done), kind=kLoop, calls=%fused_computation.28 | loop fusion | flops 4096 | bytes 36868 | tf_op jit(solution)/shard_map/jit(_where)/select_n | solution.py:130
  63.4 1.5 %broadcast_select_fusion = f32[4,1,128,2,1,128]{5,4,3,2,1,0:T(1,128)} fusion(pred[2]{0:T(512)(128)(4,1)S(1)} %fusion.9, f32[4,1,128,2,1,128]{5,4,3,2,1,0:T(1,128)S(1)} %bitcast.35, pred[4,2]{1,0:T(4,128)(4,1)S(1)} %broadcast_and_fusion, f32[4,128,128]{2,1,0:T(8,128)S(1)} %broadcast_select_fusion.2), kind=kLoop, calls=%fused_computation.3 | loop fusion | flops 262144 | bytes 1310730 | tf_op jit(solution)/shard_map/jit(_where)/select_n | solution.py:122
  (64 shorter events, 7.1 us)
Async XLA Ops:
  0.6 3.2 %copy-start = (f32[4,1,128,2,1,128]{5,4,3,2,1,0:T(1,128)S(1)}, f32[4,1,128,2,1,128]{5,4,3,2,1,0:T(1,128)}, u32[]{:S(2)}) copy-start(f32[4,1,128,2,1,128]{5,4,3,2,1,0:T(1,128)} %param.4) | copy-start | bytes 1572868
  1.8 20.5 %collective-permute-start.7 = (f32[128,128]{1,0:T(8,128)S(1)}, f32[128,128]{1,0:T(8,128)S(1)}, u32[]{:S(2)}, u32[]{:S(2)}) collective-permute-start(f32[128,128]{1,0:T(8,128)S(1)} %get-tuple-element.9), channel_id=1, source_target_pairs={{0,128},{1,129},{2,130},{3,131},{4,132},{5,133},{6,134},{7,135},{8... | collective-permute-start | bytes 196616 | tf_op jit(solution)/shard_map/ppermute | solution.py:37
  2.5 19.8 %collective-permute-start.6 = (f32[128,128]{1,0:T(8,128)S(1)}, f32[128,128]{1,0:T(8,128)S(1)}, u32[]{:S(2)}, u32[]{:S(2)}) collective-permute-start(f32[128,128]{1,0:T(8,128)S(1)} %get-tuple-element.9), channel_id=1, source_target_pairs={{0,256},{1,257},{2,258},{3,259},{4,260},{5,261},{6,262},{7,263},{8... | collective-permute-start | bytes 196616 | tf_op jit(solution)/shard_map/ppermute | solution.py:37
  3.2 19.2 %collective-permute-start.5 = (f32[128,128]{1,0:T(8,128)S(1)}, f32[128,128]{1,0:T(8,128)S(1)}, u32[]{:S(2)}, u32[]{:S(2)}) collective-permute-start(f32[128,128]{1,0:T(8,128)S(1)} %get-tuple-element.9), channel_id=1, source_target_pairs={{0,384},{1,385},{2,386},{3,387},{4,388},{5,389},{6,390},{7,391},{8... | collective-permute-start | bytes 196616 | tf_op jit(solution)/shard_map/ppermute | solution.py:37
  5.1 21.4 %collective-permute-start.18 = (f32[128,264]{1,0:T(8,128)S(1)}, f32[128,264]{1,0:T(8,128)S(1)}, u32[]{:S(2)}, u32[]{:S(2)}) collective-permute-start(f32[128,264]{1,0:T(8,128)S(1)} %pad_maximum_fusion), channel_id=1, source_target_pairs={{0,8},{16,24},{32,40},{48,56},{64,72},{80,88},{96,104},{112,120},{... | collective-permute-start | bytes 405512 | tf_op jit(solution)/shard_map/ppermute | solution.py:16
  21.4 3.0 %collective-permute-start = (f32[512,128]{1,0:T(8,128)S(1)}, f32[512,128]{1,0:T(8,128)S(1)}, u32[]{:S(2)}, u32[]{:S(2)}) collective-permute-start(f32[512,128]{1,0:T(8,128)S(1)} %slice.30), channel_id=1, source_target_pairs={{0,256},{1,257},{2,258},{3,259},{4,260},{5,261},{6,262},{7,263},{8... | collective-permute-start | bytes 786440 | tf_op jit(solution)/shard_map/ppermute | solution.py:16
  22.4 2.8 %collective-permute-start.10 = (f32[128,128]{1,0:T(8,128)S(1)}, f32[128,128]{1,0:T(8,128)S(1)}, u32[]{:S(2)}, u32[]{:S(2)}) collective-permute-start(f32[128,128]{1,0:T(8,128)S(1)} %select_select_fusion.3), channel_id=1, source_target_pairs={{0,32},{128,160},{256,288},{384,416},{1,33},{129,161},{257,289},{3... | collective-permute-start | bytes 196616 | tf_op jit(solution)/shard_map/ppermute | solution.py:37
  23.1 2.1 %collective-permute-start.9 = (f32[128,128]{1,0:T(8,128)S(1)}, f32[128,128]{1,0:T(8,128)S(1)}, u32[]{:S(2)}, u32[]{:S(2)}) collective-permute-start(f32[128,128]{1,0:T(8,128)S(1)} %select_select_fusion.3), channel_id=1, source_target_pairs={{0,64},{128,192},{256,320},{384,448},{1,65},{129,193},{257,321},{3... | collective-permute-start | bytes 196616 | tf_op jit(solution)/shard_map/ppermute | solution.py:37
  23.8 1.4 %collective-permute-start.8 = (f32[128,128]{1,0:T(8,128)S(1)}, f32[128,128]{1,0:T(8,128)S(1)}, u32[]{:S(2)}, u32[]{:S(2)}) collective-permute-start(f32[128,128]{1,0:T(8,128)S(1)} %select_select_fusion.3), channel_id=1, source_target_pairs={{0,96},{128,224},{256,352},{384,480},{1,97},{129,225},{257,353},{3... | collective-permute-start | bytes 196616 | tf_op jit(solution)/shard_map/ppermute | solution.py:37
  24.5 3.4 %collective-permute-start.1 = (f32[512,128]{1,0:T(8,128)S(1)}, f32[512,128]{1,0:T(8,128)S(1)}, u32[]{:S(2)}, u32[]{:S(2)}) collective-permute-start(f32[512,128]{1,0:T(8,128)S(1)} %broadcast_select_fusion.3), channel_id=1, source_target_pairs={{0,128},{256,384},{1,129},{257,385},{2,130},{258,386},{3,131},{259... | collective-permute-start | bytes 786440 | tf_op jit(solution)/shard_map/ppermute | solution.py:16
  25.2 11.7 %collective-permute-start.11 = (f32[128,128]{1,0:T(8,128)S(1)}, f32[128,128]{1,0:T(8,128)S(1)}, u32[]{:S(2)}, u32[]{:S(2)}) collective-permute-start(f32[128,128]{1,0:T(8,128)S(1)} %select_select_fusion.2), channel_id=1, source_target_pairs={{0,16},{32,48},{64,80},{96,112},{128,144},{160,176},{192,208},{224... | collective-permute-start | bytes 196616 | tf_op jit(solution)/shard_map/ppermute | solution.py:37
  26.6 14.2 %collective-permute-start.19 = (f32[128,264]{1,0:T(8,128)S(1)}, f32[128,264]{1,0:T(8,128)S(1)}, u32[]{:S(2)}, u32[]{:S(2)}) collective-permute-start(f32[128,264]{1,0:T(8,128)S(1)} %broadcast_select_fusion.7), channel_id=1, source_target_pairs={{0,4},{8,12},{16,20},{24,28},{32,36},{40,44},{48,52},{56,60},{64,6... | collective-permute-start | bytes 405512 | tf_op jit(solution)/shard_map/ppermute | solution.py:16
  27.9 14.2 %collective-permute-start.2 = (f32[512,128]{1,0:T(8,128)S(1)}, f32[512,128]{1,0:T(8,128)S(1)}, u32[]{:S(2)}, u32[]{:S(2)}) collective-permute-start(f32[512,128]{1,0:T(8,128)S(1)} %broadcast_select_fusion.4), channel_id=1, source_target_pairs={{0,64},{128,192},{256,320},{384,448},{1,65},{129,193},{257,321},{3... | collective-permute-start | bytes 786440 | tf_op jit(solution)/shard_map/ppermute | solution.py:16
  36.9 6.0 %collective-permute-start.14 = (f32[128,128]{1,0:T(8,128)S(1)}, f32[128,128]{1,0:T(8,128)S(1)}, u32[]{:S(2)}, u32[]{:S(2)}) collective-permute-start(f32[128,128]{1,0:T(8,128)S(1)} %broadcast_select_fusion.11), channel_id=1, source_target_pairs={{0,4},{16,20},{32,36},{48,52},{64,68},{80,84},{96,100},{112,116},{... | collective-permute-start | bytes 196616 | tf_op jit(solution)/shard_map/ppermute | solution.py:37
  38.2 4.7 %collective-permute-start.13 = (f32[128,128]{1,0:T(8,128)S(1)}, f32[128,128]{1,0:T(8,128)S(1)}, u32[]{:S(2)}, u32[]{:S(2)}) collective-permute-start(f32[128,128]{1,0:T(8,128)S(1)} %broadcast_select_fusion.11), channel_id=1, source_target_pairs={{0,8},{16,24},{32,40},{48,56},{64,72},{80,88},{96,104},{112,120},{... | collective-permute-start | bytes 196616 | tf_op jit(solution)/shard_map/ppermute | solution.py:37
  39.5 3.4 %collective-permute-start.12 = (f32[128,128]{1,0:T(8,128)S(1)}, f32[128,128]{1,0:T(8,128)S(1)}, u32[]{:S(2)}, u32[]{:S(2)}) collective-permute-start(f32[128,128]{1,0:T(8,128)S(1)} %broadcast_select_fusion.11), channel_id=1, source_target_pairs={{0,12},{16,28},{32,44},{48,60},{64,76},{80,92},{96,108},{112,124},... | collective-permute-start | bytes 196616 | tf_op jit(solution)/shard_map/ppermute | solution.py:37
  40.8 6.0 %collective-permute-start.20 = (f32[128,264]{1,0:T(8,128)S(1)}, f32[128,264]{1,0:T(8,128)S(1)}, u32[]{:S(2)}, u32[]{:S(2)}) collective-permute-start(f32[128,264]{1,0:T(8,128)S(1)} %broadcast_select_fusion.8), channel_id=1, source_target_pairs={{0,2},{4,6},{8,10},{12,14},{16,18},{20,22},{24,26},{28,30},{32,34}... | collective-permute-start | bytes 405512 | tf_op jit(solution)/shard_map/ppermute | solution.py:16
  42.2 6.0 %collective-permute-start.3 = (f32[512,128]{1,0:T(8,128)S(1)}, f32[512,128]{1,0:T(8,128)S(1)}, u32[]{:S(2)}, u32[]{:S(2)}) collective-permute-start(f32[512,128]{1,0:T(8,128)S(1)} %broadcast_select_fusion.5), channel_id=1, source_target_pairs={{0,32},{64,96},{128,160},{192,224},{256,288},{320,352},{384,416},{... | collective-permute-start | bytes 786440 | tf_op jit(solution)/shard_map/ppermute | solution.py:16
  42.9 6.6 %collective-permute-start.17 = (f32[128,128]{1,0:T(8,128)S(1)}, f32[128,128]{1,0:T(8,128)S(1)}, u32[]{:S(2)}, u32[]{:S(2)}) collective-permute-start(f32[128,128]{1,0:T(8,128)S(1)} %select_select_fusion.1), channel_id=1, source_target_pairs={{0,1},{4,5},{8,9},{12,13},{16,17},{20,21},{24,25},{28,29},{32,33},... | collective-permute-start | bytes 196616 | tf_op jit(solution)/shard_map/ppermute | solution.py:37
  44.2 5.3 %collective-permute-start.16 = (f32[128,128]{1,0:T(8,128)S(1)}, f32[128,128]{1,0:T(8,128)S(1)}, u32[]{:S(2)}, u32[]{:S(2)}) collective-permute-start(f32[128,128]{1,0:T(8,128)S(1)} %select_select_fusion.1), channel_id=1, source_target_pairs={{0,2},{4,6},{8,10},{12,14},{16,18},{20,22},{24,26},{28,30},{32,34}... | collective-permute-start | bytes 196616 | tf_op jit(solution)/shard_map/ppermute | solution.py:37
  45.6 4.0 %collective-permute-start.15 = (f32[128,128]{1,0:T(8,128)S(1)}, f32[128,128]{1,0:T(8,128)S(1)}, u32[]{:S(2)}, u32[]{:S(2)}) collective-permute-start(f32[128,128]{1,0:T(8,128)S(1)} %select_select_fusion.1), channel_id=1, source_target_pairs={{0,3},{4,7},{8,11},{12,15},{16,19},{20,23},{24,27},{28,31},{32,35}... | collective-permute-start | bytes 196616 | tf_op jit(solution)/shard_map/ppermute | solution.py:37
  46.9 4.6 %collective-permute-start.21 = (f32[128,264]{1,0:T(8,128)S(1)}, f32[128,264]{1,0:T(8,128)S(1)}, u32[]{:S(2)}, u32[]{:S(2)}) collective-permute-start(f32[128,264]{1,0:T(8,128)S(1)} %broadcast_select_fusion.9), channel_id=1, source_target_pairs={{0,1},{2,3},{4,5},{6,7},{8,9},{10,11},{12,13},{14,15},{16,17},{18,... | collective-permute-start | bytes 405512 | tf_op jit(solution)/shard_map/ppermute | solution.py:16
  48.3 12.3 %collective-permute-start.4 = (f32[512,128]{1,0:T(8,128)S(1)}, f32[512,128]{1,0:T(8,128)S(1)}, u32[]{:S(2)}, u32[]{:S(2)}) collective-permute-start(f32[512,128]{1,0:T(8,128)S(1)} %broadcast_select_fusion.6), channel_id=1, source_target_pairs={{0,16},{32,48},{64,80},{96,112},{128,144},{160,176},{192,208},{224... | collective-permute-start | bytes 786440 | tf_op jit(solution)/shard_map/ppermute | solution.py:16
  52.0 9.6 %copy-start.1 = (f32[264,128]{1,0:T(8,128)}, f32[264,128]{1,0:T(8,128)S(1)}, u32[]{:S(2)}) copy-start(f32[264,128]{1,0:T(8,128)S(1)} %fusion.3) | copy-start | bytes 405508
  (3 other events, 2.1 us)

commit v17 on v16

--- a/solution.py
+++ b/solution.py
@@ -92,7 +92,7 @@
     holder = (row_id == 0) & (col_id == 0)
     corner, inverse = lax.cond(holder, factor, skip, local[:block, :block])
     inverse = spread_wide(spread_wide(inverse, "col"), "row")
-    left = spread(local[:, :block], "col")
+    left = spread_wide(local[:, :block], "col")
     top = jnp.concatenate([local[:block], right_sides[:, 0, 0, :].T], axis=1)
     top = spread(top, "row")
 

time: 66 us -> 83.9 us (1.27)
  waiting for transfers between devices: 18.8 us -> 29.6 us
  starting transfers between devices: 37.2 us -> 43.8 us
    ppermute x13 -> x20, waiting for transfers between devices: 8.32 us -> 25.8 us  [spread_wide(): arrived = lax.ppermute(block, axis, pairs)]
    ppermute x13 -> x20, starting transfers between devices: 13 us -> 23.6 us  [spread_wide(): arrived = lax.ppermute(block, axis, pairs)]
    ppermute x9 -> x4, waiting for transfers between devices: 10.5 us -> 3.82 us  [spread(): arrived = lax.ppermute(block, axis, pairs)]
    ppermute x9 -> x4, starting transfers between devices: 24.2 us -> 20.2 us  [spread(): arrived = lax.ppermute(block, axis, pairs)]
  transfers between devices with their start and end apart: 22 -> 24, of which waited for: 3 -> 5; matrix products, arithmetic and copies ran while one was open for 2% -> 2% of each run, Pallas kernels for 0% -> 0%
where the time goes in v17:
time: 83.9 us; the launch traced here: 82.8 us
  starting transfers between devices  43.8 us (52%)
  waiting for transfers between devices  29.6 us (35%)
  local copies, waits for them, and re-layouts  3.68 us (4%)
  other arithmetic  2.69 us (3%)
  matrix products  1.75 us (2%)
  between operations  1.31 us (2%)
    ppermute x20, waiting for transfers between devices, spread_wide(): arrived = lax.ppermute(block, axis, pairs)  25.8 us
    ppermute x20, starting transfers between devices, spread_wide(): arrived = lax.ppermute(block, axis, pairs)  23.6 us
    ppermute x4, starting transfers between devices, spread(): arrived = lax.ppermute(block, axis, pairs)  20.2 us
    ppermute x4, waiting for transfers between devices, spread(): arrived = lax.ppermute(block, axis, pairs)  3.82 us
  transfers between devices with their start and end apart: 24, of which 5 were waited for; matrix products, arithmetic and copies ran while one was open for 2% of the time, Pallas kernels for 0%

profile of v17, /device:TPU:1, one launch (start us, length us, event | category | flops | bytes accessed | tf_op | source)
XLA Modules:
  0.0 82.8 jit_solution(2738177059443642505)
XLA Ops:
  0.6 1.1 %copy.18 = f32[64,8,2,128]{3,1,2,0:T(8,128)S(1)} copy(f32[64,8,2,128]{3,2,1,0:T(2,128)} %bitcast.30) | data formatting | bytes 1048576
  1.8 0.8 collective-permute-start.7
  4.0 0.7 collective-permute-start
  5.9 0.7 slice-done.1
  9.7 16.3 %collective-permute-start.20 = (f32[128,264]{1,0:T(8,128)S(1)}, f32[128,264]{1,0:T(8,128)S(1)}, u32[]{:S(2)}, u32[]{:S(2)}) collective-permute-start(f32[128,264]{1,0:T(8,128)S(1)} %pad_maximum_fusion), channel_id=1, source_target_pairs={{0,8},{16,24},{32,40},{48,56},{64,72},{80,88},{96,104},{112,120},{... | collective-permute-start | bytes 405512 | tf_op jit(solution)/shard_map/ppermute | solution.py:16
  26.0 1.3 %collective-permute-start.13 = (f32[128,128]{1,0:T(8,128)S(1)}, f32[128,128]{1,0:T(8,128)S(1)}, u32[]{:S(2)}, u32[]{:S(2)}) collective-permute-start(f32[128,128]{1,0:T(8,128)S(1)} %select_select_fusion.4), channel_id=1, source_target_pairs={{0,16},{32,48},{64,80},{96,112},{128,144},{160,176},{192,208},{224... | collective-permute-start | bytes 196616 | tf_op jit(solution)/shard_map/ppermute | solution.py:37
  27.3 1.2 %collective-permute-done.20 = f32[128,264]{1,0:T(8,128)S(1)} collective-permute-done((f32[128,264]{1,0:T(8,128)S(1)}, f32[128,264]{1,0:T(8,128)S(1)}, u32[]{:S(2)}, u32[]{:S(2)}) %collective-permute-start.20) | collective-permute-done | bytes 135200 | tf_op jit(solution)/shard_map/ppermute | solution.py:16
  28.6 1.3 %collective-permute-start.21 = (f32[128,264]{1,0:T(8,128)S(1)}, f32[128,264]{1,0:T(8,128)S(1)}, u32[]{:S(2)}, u32[]{:S(2)}) collective-permute-start(f32[128,264]{1,0:T(8,128)S(1)} %broadcast_select_fusion.3), channel_id=1, source_target_pairs={{0,4},{8,12},{16,20},{24,28},{32,36},{40,44},{48,52},{56,60},{64,6... | collective-permute-start | bytes 405512 | tf_op jit(solution)/shard_map/ppermute | solution.py:16
  29.9 9.0 %collective-permute-done.13 = f32[128,128]{1,0:T(8,128)S(1)} collective-permute-done((f32[128,128]{1,0:T(8,128)S(1)}, f32[128,128]{1,0:T(8,128)S(1)}, u32[]{:S(2)}, u32[]{:S(2)}) %collective-permute-start.13) | collective-permute-done | bytes 65568 | tf_op jit(solution)/shard_map/ppermute | solution.py:37
  38.9 1.3 %collective-permute-start.14 = (f32[128,128]{1,0:T(8,128)S(1)}, f32[128,128]{1,0:T(8,128)S(1)}, u32[]{:S(2)}, u32[]{:S(2)}) collective-permute-start(f32[128,128]{1,0:T(8,128)S(1)} %broadcast_select_fusion.7), channel_id=1, source_target_pairs={{0,12},{16,28},{32,44},{48,60},{64,76},{80,92},{96,108},{112,124},... | collective-permute-start | bytes 196616 | tf_op jit(solution)/shard_map/ppermute | solution.py:37
  40.2 2.9 %collective-permute-start.15 = (f32[128,128]{1,0:T(8,128)S(1)}, f32[128,128]{1,0:T(8,128)S(1)}, u32[]{:S(2)}, u32[]{:S(2)}) collective-permute-start(f32[128,128]{1,0:T(8,128)S(1)} %broadcast_select_fusion.7), channel_id=1, source_target_pairs={{0,8},{16,24},{32,40},{48,56},{64,72},{80,88},{96,104},{112,120},{... | collective-permute-start | bytes 196616 | tf_op jit(solution)/shard_map/ppermute | solution.py:37
  43.2 1.3 %collective-permute-start.16 = (f32[128,128]{1,0:T(8,128)S(1)}, f32[128,128]{1,0:T(8,128)S(1)}, u32[]{:S(2)}, u32[]{:S(2)}) collective-permute-start(f32[128,128]{1,0:T(8,128)S(1)} %broadcast_select_fusion.7), channel_id=1, source_target_pairs={{0,4},{16,20},{32,36},{48,52},{64,68},{80,84},{96,100},{112,116},{... | collective-permute-start | bytes 196616 | tf_op jit(solution)/shard_map/ppermute | solution.py:37
  45.2 0.7 collective-permute-start.4
  46.6 1.3 %collective-permute-start.22 = (f32[128,264]{1,0:T(8,128)S(1)}, f32[128,264]{1,0:T(8,128)S(1)}, u32[]{:S(2)}, u32[]{:S(2)}) collective-permute-start(f32[128,264]{1,0:T(8,128)S(1)} %broadcast_select_fusion.4), channel_id=1, source_target_pairs={{0,2},{4,6},{8,10},{12,14},{16,18},{20,22},{24,26},{28,30},{32,34}... | collective-permute-start | bytes 405512 | tf_op jit(solution)/shard_map/ppermute | solution.py:16
  48.0 1.3 %collective-permute-start.17 = (f32[128,128]{1,0:T(8,128)S(1)}, f32[128,128]{1,0:T(8,128)S(1)}, u32[]{:S(2)}, u32[]{:S(2)}) collective-permute-start(f32[128,128]{1,0:T(8,128)S(1)} %select_select_fusion.3), channel_id=1, source_target_pairs={{0,3},{4,7},{8,11},{12,15},{16,19},{20,23},{24,27},{28,31},{32,35}... | collective-permute-start | bytes 196616 | tf_op jit(solution)/shard_map/ppermute | solution.py:37
  49.3 1.2 %collective-permute-done.22 = f32[128,264]{1,0:T(8,128)S(1)} collective-permute-done((f32[128,264]{1,0:T(8,128)S(1)}, f32[128,264]{1,0:T(8,128)S(1)}, u32[]{:S(2)}, u32[]{:S(2)}) %collective-permute-start.22) | collective-permute-done | bytes 135200 | tf_op jit(solution)/shard_map/ppermute | solution.py:16
  50.5 4.7 %collective-permute-start.18 = (f32[128,128]{1,0:T(8,128)S(1)}, f32[128,128]{1,0:T(8,128)S(1)}, u32[]{:S(2)}, u32[]{:S(2)}) collective-permute-start(f32[128,128]{1,0:T(8,128)S(1)} %select_select_fusion.3), channel_id=1, source_target_pairs={{0,2},{4,6},{8,10},{12,14},{16,18},{20,22},{24,26},{28,30},{32,34}... | collective-permute-start | bytes 196616 | tf_op jit(solution)/shard_map/ppermute | solution.py:37
  55.3 1.3 %collective-permute-start.19 = (f32[128,128]{1,0:T(8,128)S(1)}, f32[128,128]{1,0:T(8,128)S(1)}, u32[]{:S(2)}, u32[]{:S(2)}) collective-permute-start(f32[128,128]{1,0:T(8,128)S(1)} %select_select_fusion.3), channel_id=1, source_target_pairs={{0,1},{4,5},{8,9},{12,13},{16,17},{20,21},{24,25},{28,29},{32,33},... | collective-permute-start | bytes 196616 | tf_op jit(solution)/shard_map/ppermute | solution.py:37
  56.6 1.3 %collective-permute-start.23 = (f32[128,264]{1,0:T(8,128)S(1)}, f32[128,264]{1,0:T(8,128)S(1)}, u32[]{:S(2)}, u32[]{:S(2)}) collective-permute-start(f32[128,264]{1,0:T(8,128)S(1)} %broadcast_select_fusion.5), channel_id=1, source_target_pairs={{0,1},{2,3},{4,5},{6,7},{8,9},{10,11},{12,13},{14,15},{16,17},{18,... | collective-permute-start | bytes 405512 | tf_op jit(solution)/shard_map/ppermute | solution.py:16
  58.0 1.3 %collective-permute-start.6 = (f32[512,128]{1,0:T(8,128)S(1)}, f32[512,128]{1,0:T(8,128)S(1)}, u32[]{:S(2)}, u32[]{:S(2)}) collective-permute-start(f32[512,128]{1,0:T(8,128)S(1)} %select_select_fusion), channel_id=1, source_target_pairs={{0,16},{32,48},{64,80},{96,112},{128,144},{160,176},{192,208},{224... | collective-permute-start | bytes 786440 | tf_op jit(solution)/shard_map/ppermute | solution.py:37
  59.3 1.3 %collective-permute-done.23 = f32[128,264]{1,0:T(8,128)S(1)} collective-permute-done((f32[128,264]{1,0:T(8,128)S(1)}, f32[128,264]{1,0:T(8,128)S(1)}, u32[]{:S(2)}, u32[]{:S(2)}) %collective-permute-start.23) | collective-permute-done | bytes 135200 | tf_op jit(solution)/shard_map/ppermute | solution.py:16
  61.2 16.7 %collective-permute-done.6 = f32[512,128]{1,0:T(8,128)S(1)} collective-permute-done((f32[512,128]{1,0:T(8,128)S(1)}, f32[512,128]{1,0:T(8,128)S(1)}, u32[]{:S(2)}, u32[]{:S(2)}) %collective-permute-start.6) | collective-permute-done | bytes 262176 | tf_op jit(solution)/shard_map/ppermute | solution.py:37
  80.6 0.7 broadcast_select_fusion.6
  81.3 1.5 %broadcast_select_fusion = f32[4,1,128,2,1,128]{5,4,3,2,1,0:T(1,128)} fusion(pred[2]{0:T(512)(128)(4,1)S(1)} %fusion.9, f32[4,1,128,2,1,128]{5,4,3,2,1,0:T(1,128)S(1)} %bitcast.35, pred[4,2]{1,0:T(4,128)(4,1)S(1)} %broadcast_and_fusion, f32[4,128,128]{2,1,0:T(8,128)S(1)} %broadcast_select_fusion.2), kind=kLoop, calls=%fused_computation.3 | loop fusion | flops 262144 | bytes 1310730 | tf_op jit(solution)/shard_map/jit(_where)/select_n | solution.py:122
  (66 shorter events, 10.3 us)
Async XLA Ops:
  1.8 5.1 %collective-permute-start.7 = (f32[128,128]{1,0:T(8,128)S(1)}, f32[128,128]{1,0:T(8,128)S(1)}, u32[]{:S(2)}, u32[]{:S(2)}) collective-permute-start(f32[128,128]{1,0:T(8,128)S(1)} %get-tuple-element.9), channel_id=1, source_target_pairs={{0,384},{1,385},{2,386},{3,387},{4,388},{5,389},{6,390},{7,391},{8... | collective-permute-start | bytes 196616 | tf_op jit(solution)/shard_map/ppermute | solution.py:37
  2.6 4.3 %collective-permute-start.8 = (f32[128,128]{1,0:T(8,128)S(1)}, f32[128,128]{1,0:T(8,128)S(1)}, u32[]{:S(2)}, u32[]{:S(2)}) collective-permute-start(f32[128,128]{1,0:T(8,128)S(1)} %get-tuple-element.9), channel_id=1, source_target_pairs={{0,256},{1,257},{2,258},{3,259},{4,260},{5,261},{6,262},{7,263},{8... | collective-permute-start | bytes 196616 | tf_op jit(solution)/shard_map/ppermute | solution.py:37
  3.3 3.7 %collective-permute-start.9 = (f32[128,128]{1,0:T(8,128)S(1)}, f32[128,128]{1,0:T(8,128)S(1)}, u32[]{:S(2)}, u32[]{:S(2)}) collective-permute-start(f32[128,128]{1,0:T(8,128)S(1)} %get-tuple-element.9), channel_id=1, source_target_pairs={{0,128},{1,129},{2,130},{3,131},{4,132},{5,133},{6,134},{7,135},{8... | collective-permute-start | bytes 196616 | tf_op jit(solution)/shard_map/ppermute | solution.py:37
  4.0 36.2 %collective-permute-start = (f32[512,128]{1,0:T(8,128)S(1)}, f32[512,128]{1,0:T(8,128)S(1)}, u32[]{:S(2)}, u32[]{:S(2)}) collective-permute-start(f32[512,128]{1,0:T(8,128)S(1)} %slice.30), channel_id=1, source_target_pairs={{0,384},{1,385},{2,386},{3,387},{4,388},{5,389},{6,390},{7,391},{8... | collective-permute-start | bytes 786440 | tf_op jit(solution)/shard_map/ppermute | solution.py:37
  4.7 38.5 %collective-permute-start.1 = (f32[512,128]{1,0:T(8,128)S(1)}, f32[512,128]{1,0:T(8,128)S(1)}, u32[]{:S(2)}, u32[]{:S(2)}) collective-permute-start(f32[512,128]{1,0:T(8,128)S(1)} %slice.30), channel_id=1, source_target_pairs={{0,256},{1,257},{2,258},{3,259},{4,260},{5,261},{6,262},{7,263},{8... | collective-permute-start | bytes 786440 | tf_op jit(solution)/shard_map/ppermute | solution.py:37
  6.9 2.0 %collective-permute-start.10 = (f32[128,128]{1,0:T(8,128)S(1)}, f32[128,128]{1,0:T(8,128)S(1)}, u32[]{:S(2)}, u32[]{:S(2)}) collective-permute-start(f32[128,128]{1,0:T(8,128)S(1)} %select_select_fusion.5), channel_id=1, source_target_pairs={{0,96},{128,224},{256,352},{384,480},{1,97},{129,225},{257,353},{3... | collective-permute-start | bytes 196616 | tf_op jit(solution)/shard_map/ppermute | solution.py:37
  7.6 2.1 %collective-permute-start.11 = (f32[128,128]{1,0:T(8,128)S(1)}, f32[128,128]{1,0:T(8,128)S(1)}, u32[]{:S(2)}, u32[]{:S(2)}) collective-permute-start(f32[128,128]{1,0:T(8,128)S(1)} %select_select_fusion.5), channel_id=1, source_target_pairs={{0,64},{128,192},{256,320},{384,448},{1,65},{129,193},{257,321},{3... | collective-permute-start | bytes 196616 | tf_op jit(solution)/shard_map/ppermute | solution.py:37
  8.3 17.7 %collective-permute-start.12 = (f32[128,128]{1,0:T(8,128)S(1)}, f32[128,128]{1,0:T(8,128)S(1)}, u32[]{:S(2)}, u32[]{:S(2)}) collective-permute-start(f32[128,128]{1,0:T(8,128)S(1)} %select_select_fusion.5), channel_id=1, source_target_pairs={{0,32},{128,160},{256,288},{384,416},{1,33},{129,161},{257,289},{3... | collective-permute-start | bytes 196616 | tf_op jit(solution)/shard_map/ppermute | solution.py:37
  9.0 35.5 %collective-permute-start.2 = (f32[512,128]{1,0:T(8,128)S(1)}, f32[512,128]{1,0:T(8,128)S(1)}, u32[]{:S(2)}, u32[]{:S(2)}) collective-permute-start(f32[512,128]{1,0:T(8,128)S(1)} %slice.30), channel_id=1, source_target_pairs={{0,128},{1,129},{2,130},{3,131},{4,132},{5,133},{6,134},{7,135},{8... | collective-permute-start | bytes 786440 | tf_op jit(solution)/shard_map/ppermute | solution.py:37
  9.7 18.9 %collective-permute-start.20 = (f32[128,264]{1,0:T(8,128)S(1)}, f32[128,264]{1,0:T(8,128)S(1)}, u32[]{:S(2)}, u32[]{:S(2)}) collective-permute-start(f32[128,264]{1,0:T(8,128)S(1)} %pad_maximum_fusion), channel_id=1, source_target_pairs={{0,8},{16,24},{32,40},{48,56},{64,72},{80,88},{96,104},{112,120},{... | collective-permute-start | bytes 405512 | tf_op jit(solution)/shard_map/ppermute | solution.py:16
  26.0 12.9 %collective-permute-start.13 = (f32[128,128]{1,0:T(8,128)S(1)}, f32[128,128]{1,0:T(8,128)S(1)}, u32[]{:S(2)}, u32[]{:S(2)}) collective-permute-start(f32[128,128]{1,0:T(8,128)S(1)} %select_select_fusion.4), channel_id=1, source_target_pairs={{0,16},{32,48},{64,80},{96,112},{128,144},{160,176},{192,208},{224... | collective-permute-start | bytes 196616 | tf_op jit(solution)/shard_map/ppermute | solution.py:37
  28.6 16.6 %collective-permute-start.21 = (f32[128,264]{1,0:T(8,128)S(1)}, f32[128,264]{1,0:T(8,128)S(1)}, u32[]{:S(2)}, u32[]{:S(2)}) collective-permute-start(f32[128,264]{1,0:T(8,128)S(1)} %broadcast_select_fusion.3), channel_id=1, source_target_pairs={{0,4},{8,12},{16,20},{24,28},{32,36},{40,44},{48,52},{56,60},{64,6... | collective-permute-start | bytes 405512 | tf_op jit(solution)/shard_map/ppermute | solution.py:16
  38.9 7.0 %collective-permute-start.14 = (f32[128,128]{1,0:T(8,128)S(1)}, f32[128,128]{1,0:T(8,128)S(1)}, u32[]{:S(2)}, u32[]{:S(2)}) collective-permute-start(f32[128,128]{1,0:T(8,128)S(1)} %broadcast_select_fusion.7), channel_id=1, source_target_pairs={{0,12},{16,28},{32,44},{48,60},{64,76},{80,92},{96,108},{112,124},... | collective-permute-start | bytes 196616 | tf_op jit(solution)/shard_map/ppermute | solution.py:37
  40.2 6.4 %collective-permute-start.15 = (f32[128,128]{1,0:T(8,128)S(1)}, f32[128,128]{1,0:T(8,128)S(1)}, u32[]{:S(2)}, u32[]{:S(2)}) collective-permute-start(f32[128,128]{1,0:T(8,128)S(1)} %broadcast_select_fusion.7), channel_id=1, source_target_pairs={{0,8},{16,24},{32,40},{48,56},{64,72},{80,88},{96,104},{112,120},{... | collective-permute-start | bytes 196616 | tf_op jit(solution)/shard_map/ppermute | solution.py:37
  43.2 4.8 %collective-permute-start.16 = (f32[128,128]{1,0:T(8,128)S(1)}, f32[128,128]{1,0:T(8,128)S(1)}, u32[]{:S(2)}, u32[]{:S(2)}) collective-permute-start(f32[128,128]{1,0:T(8,128)S(1)} %broadcast_select_fusion.7), channel_id=1, source_target_pairs={{0,4},{16,20},{32,36},{48,52},{64,68},{80,84},{96,100},{112,116},{... | collective-permute-start | bytes 196616 | tf_op jit(solution)/shard_map/ppermute | solution.py:37
  44.5 10.8 %collective-permute-start.3 = (f32[512,128]{1,0:T(8,128)S(1)}, f32[512,128]{1,0:T(8,128)S(1)}, u32[]{:S(2)}, u32[]{:S(2)}) collective-permute-start(f32[512,128]{1,0:T(8,128)S(1)} %select_select_fusion.1), channel_id=1, source_target_pairs={{0,96},{128,224},{256,352},{384,480},{1,97},{129,225},{257,353},{3... | collective-permute-start | bytes 786440 | tf_op jit(solution)/shard_map/ppermute | solution.py:37
  45.2 11.4 %collective-permute-start.4 = (f32[512,128]{1,0:T(8,128)S(1)}, f32[512,128]{1,0:T(8,128)S(1)}, u32[]{:S(2)}, u32[]{:S(2)}) collective-permute-start(f32[512,128]{1,0:T(8,128)S(1)} %select_select_fusion.1), channel_id=1, source_target_pairs={{0,64},{128,192},{256,320},{384,448},{1,65},{129,193},{257,321},{3... | collective-permute-start | bytes 786440 | tf_op jit(solution)/shard_map/ppermute | solution.py:37
  46.0 12.0 %collective-permute-start.5 = (f32[512,128]{1,0:T(8,128)S(1)}, f32[512,128]{1,0:T(8,128)S(1)}, u32[]{:S(2)}, u32[]{:S(2)}) collective-permute-start(f32[512,128]{1,0:T(8,128)S(1)} %select_select_fusion.1), channel_id=1, source_target_pairs={{0,32},{128,160},{256,288},{384,416},{1,33},{129,161},{257,289},{3... | collective-permute-start | bytes 786440 | tf_op jit(solution)/shard_map/ppermute | solution.py:37
  46.6 3.9 %collective-permute-start.22 = (f32[128,264]{1,0:T(8,128)S(1)}, f32[128,264]{1,0:T(8,128)S(1)}, u32[]{:S(2)}, u32[]{:S(2)}) collective-permute-start(f32[128,264]{1,0:T(8,128)S(1)} %broadcast_select_fusion.4), channel_id=1, source_target_pairs={{0,2},{4,6},{8,10},{12,14},{16,18},{20,22},{24,26},{28,30},{32,34}... | collective-permute-start | bytes 405512 | tf_op jit(solution)/shard_map/ppermute | solution.py:16
  48.0 11.3 %collective-permute-start.17 = (f32[128,128]{1,0:T(8,128)S(1)}, f32[128,128]{1,0:T(8,128)S(1)}, u32[]{:S(2)}, u32[]{:S(2)}) collective-permute-start(f32[128,128]{1,0:T(8,128)S(1)} %select_select_fusion.3), channel_id=1, source_target_pairs={{0,3},{4,7},{8,11},{12,15},{16,19},{20,23},{24,27},{28,31},{32,35}... | collective-permute-start | bytes 196616 | tf_op jit(solution)/shard_map/ppermute | solution.py:37
  50.5 8.8 %collective-permute-start.18 = (f32[128,128]{1,0:T(8,128)S(1)}, f32[128,128]{1,0:T(8,128)S(1)}, u32[]{:S(2)}, u32[]{:S(2)}) collective-permute-start(f32[128,128]{1,0:T(8,128)S(1)} %select_select_fusion.3), channel_id=1, source_target_pairs={{0,2},{4,6},{8,10},{12,14},{16,18},{20,22},{24,26},{28,30},{32,34}... | collective-permute-start | bytes 196616 | tf_op jit(solution)/shard_map/ppermute | solution.py:37
  55.3 4.0 %collective-permute-start.19 = (f32[128,128]{1,0:T(8,128)S(1)}, f32[128,128]{1,0:T(8,128)S(1)}, u32[]{:S(2)}, u32[]{:S(2)}) collective-permute-start(f32[128,128]{1,0:T(8,128)S(1)} %select_select_fusion.3), channel_id=1, source_target_pairs={{0,1},{4,5},{8,9},{12,13},{16,17},{20,21},{24,25},{28,29},{32,33},... | collective-permute-start | bytes 196616 | tf_op jit(solution)/shard_map/ppermute | solution.py:37
  56.6 4.0 %collective-permute-start.23 = (f32[128,264]{1,0:T(8,128)S(1)}, f32[128,264]{1,0:T(8,128)S(1)}, u32[]{:S(2)}, u32[]{:S(2)}) collective-permute-start(f32[128,264]{1,0:T(8,128)S(1)} %broadcast_select_fusion.5), channel_id=1, source_target_pairs={{0,1},{2,3},{4,5},{6,7},{8,9},{10,11},{12,13},{14,15},{16,17},{18,... | collective-permute-start | bytes 405512 | tf_op jit(solution)/shard_map/ppermute | solution.py:16
  58.0 19.9 %collective-permute-start.6 = (f32[512,128]{1,0:T(8,128)S(1)}, f32[512,128]{1,0:T(8,128)S(1)}, u32[]{:S(2)}, u32[]{:S(2)}) collective-permute-start(f32[512,128]{1,0:T(8,128)S(1)} %select_select_fusion), channel_id=1, source_target_pairs={{0,16},{32,48},{64,80},{96,112},{128,144},{160,176},{192,208},{224... | collective-permute-start | bytes 786440 | tf_op jit(solution)/shard_map/ppermute | solution.py:37
  (5 other events, 23.8 us)

commit v18 on v16

--- a/solution.py
+++ b/solution.py
@@ -32,7 +32,7 @@
     for radix in radices:
         span //= radix
         got = block
-        for digit in range(1, radix):
+        for digit in range(radix - 1, 0, -1):
             pairs = [(i, i + digit * span) for i in range(0, count, span * radix)]
             arrived = lax.ppermute(block, axis, pairs)
             mine = (index % (span * radix)) == digit * span

time: 66 us -> 66.6 us (level)
  no operation moved by 1% of the time
where the time goes in v18:
time: 66.6 us; the launch traced here: 65.6 us
  starting transfers between devices  37.2 us (56%)
  waiting for transfers between devices  19.4 us (29%)
  local copies, waits for them, and re-layouts  3.25 us (5%)
  other arithmetic  2.69 us (4%)
  matrix products  1.75 us (3%)
  between operations  1.23 us (2%)
    ppermute x9, starting transfers between devices, spread(): arrived = lax.ppermute(block, axis, pairs)  24.2 us
    ppermute x13, starting transfers between devices, spread_wide(): arrived = lax.ppermute(block, axis, pairs)  13 us
    ppermute x9, waiting for transfers between devices, spread(): arrived = lax.ppermute(block, axis, pairs)  10.6 us
    ppermute x13, waiting for transfers between devices, spread_wide(): arrived = lax.ppermute(block, axis, pairs)  8.77 us
    select_n x1, other arithmetic, on_device(): jnp.where((global_cols == 0)[None, None, :, None], column[:, :, None, :],...  1.52 us
  transfers between devices with their start and end apart: 22, of which 3 were waited for; matrix products, arithmetic and copies ran while one was open for 2% of the time, Pallas kernels for 0%

profile of v18, /device:TPU:1, one launch (start us, length us, event | category | flops | bytes accessed | tf_op | source)
XLA Modules:
  0.0 65.6 jit_solution(4701582796388416645)
XLA Ops:
  0.7 1.1 %copy.18 = f32[64,8,2,128]{3,1,2,0:T(8,128)S(1)} copy(f32[64,8,2,128]{3,2,1,0:T(2,128)} %bitcast.30) | data formatting | bytes 1048576
  1.8 0.7 %collective-permute-start.7 = (f32[128,128]{1,0:T(8,128)S(1)}, f32[128,128]{1,0:T(8,128)S(1)}, u32[]{:S(2)}, u32[]{:S(2)}) collective-permute-start(f32[128,128]{1,0:T(8,128)S(1)} %get-tuple-element.9), channel_id=1, source_target_pairs={{0,384},{1,385},{2,386},{3,387},{4,388},{5,389},{6,390},{7,391},{8... | collective-permute-start | bytes 196616 | tf_op jit(solution)/shard_map/ppermute | solution.py:37
  4.3 0.7 %slice-done.1 = f32[8,1,1,128]{3,2,1,0:T(1,128)S(1)} async-done(((f32[8,4,1,128]{3,2,1,0:T(1,128)}), f32[8,1,1,128]{3,2,1,0:T(1,128)S(1)}, s32[]{:S(2)}) %slice-start.1) | async-done | bytes 4120 | tf_op jit(solution)/shard_map/slice | solution.py:96
  5.1 16.3 %collective-permute-start.18 = (f32[128,264]{1,0:T(8,128)S(1)}, f32[128,264]{1,0:T(8,128)S(1)}, u32[]{:S(2)}, u32[]{:S(2)}) collective-permute-start(f32[128,264]{1,0:T(8,128)S(1)} %pad_maximum_fusion), channel_id=1, source_target_pairs={{0,8},{16,24},{32,40},{48,56},{64,72},{80,88},{96,104},{112,120},{... | collective-permute-start | bytes 405512 | tf_op jit(solution)/shard_map/ppermute | solution.py:16
  21.4 0.7 %collective-permute-start = (f32[512,128]{1,0:T(8,128)S(1)}, f32[512,128]{1,0:T(8,128)S(1)}, u32[]{:S(2)}, u32[]{:S(2)}) collective-permute-start(f32[512,128]{1,0:T(8,128)S(1)} %slice.30), channel_id=1, source_target_pairs={{0,256},{1,257},{2,258},{3,259},{4,260},{5,261},{6,262},{7,263},{8... | collective-permute-start | bytes 786440 | tf_op jit(solution)/shard_map/ppermute | solution.py:16
  24.5 0.7 %collective-permute-start.1 = (f32[512,128]{1,0:T(8,128)S(1)}, f32[512,128]{1,0:T(8,128)S(1)}, u32[]{:S(2)}, u32[]{:S(2)}) collective-permute-start(f32[512,128]{1,0:T(8,128)S(1)} %broadcast_select_fusion.3), channel_id=1, source_target_pairs={{0,128},{256,384},{1,129},{257,385},{2,130},{258,386},{3,131},{259... | collective-permute-start | bytes 786440 | tf_op jit(solution)/shard_map/ppermute | solution.py:16
  25.2 1.3 %collective-permute-start.11 = (f32[128,128]{1,0:T(8,128)S(1)}, f32[128,128]{1,0:T(8,128)S(1)}, u32[]{:S(2)}, u32[]{:S(2)}) collective-permute-start(f32[128,128]{1,0:T(8,128)S(1)} %select_select_fusion.2), channel_id=1, source_target_pairs={{0,16},{32,48},{64,80},{96,112},{128,144},{160,176},{192,208},{224... | collective-permute-start | bytes 196616 | tf_op jit(solution)/shard_map/ppermute | solution.py:37
  26.6 1.3 %collective-permute-start.19 = (f32[128,264]{1,0:T(8,128)S(1)}, f32[128,264]{1,0:T(8,128)S(1)}, u32[]{:S(2)}, u32[]{:S(2)}) collective-permute-start(f32[128,264]{1,0:T(8,128)S(1)} %broadcast_select_fusion.7), channel_id=1, source_target_pairs={{0,4},{8,12},{16,20},{24,28},{32,36},{40,44},{48,52},{56,60},{64,6... | collective-permute-start | bytes 405512 | tf_op jit(solution)/shard_map/ppermute | solution.py:16
  27.9 0.7 %collective-permute-start.2 = (f32[512,128]{1,0:T(8,128)S(1)}, f32[512,128]{1,0:T(8,128)S(1)}, u32[]{:S(2)}, u32[]{:S(2)}) collective-permute-start(f32[512,128]{1,0:T(8,128)S(1)} %broadcast_select_fusion.4), channel_id=1, source_target_pairs={{0,64},{128,192},{256,320},{384,448},{1,65},{129,193},{257,321},{3... | collective-permute-start | bytes 786440 | tf_op jit(solution)/shard_map/ppermute | solution.py:16
  28.6 8.7 %collective-permute-done.11 = f32[128,128]{1,0:T(8,128)S(1)} collective-permute-done((f32[128,128]{1,0:T(8,128)S(1)}, f32[128,128]{1,0:T(8,128)S(1)}, u32[]{:S(2)}, u32[]{:S(2)}) %collective-permute-start.11) | collective-permute-done | bytes 65568 | tf_op jit(solution)/shard_map/ppermute | solution.py:37
  37.4 1.3 %collective-permute-start.14 = (f32[128,128]{1,0:T(8,128)S(1)}, f32[128,128]{1,0:T(8,128)S(1)}, u32[]{:S(2)}, u32[]{:S(2)}) collective-permute-start(f32[128,128]{1,0:T(8,128)S(1)} %broadcast_select_fusion.11), channel_id=1, source_target_pairs={{0,12},{16,28},{32,44},{48,60},{64,76},{80,92},{96,108},{112,124},... | collective-permute-start | bytes 196616 | tf_op jit(solution)/shard_map/ppermute | solution.py:37
  38.7 1.3 %collective-permute-start.13 = (f32[128,128]{1,0:T(8,128)S(1)}, f32[128,128]{1,0:T(8,128)S(1)}, u32[]{:S(2)}, u32[]{:S(2)}) collective-permute-start(f32[128,128]{1,0:T(8,128)S(1)} %broadcast_select_fusion.11), channel_id=1, source_target_pairs={{0,8},{16,24},{32,40},{48,56},{64,72},{80,88},{96,104},{112,120},{... | collective-permute-start | bytes 196616 | tf_op jit(solution)/shard_map/ppermute | solution.py:37
  40.0 1.3 %collective-permute-start.12 = (f32[128,128]{1,0:T(8,128)S(1)}, f32[128,128]{1,0:T(8,128)S(1)}, u32[]{:S(2)}, u32[]{:S(2)}) collective-permute-start(f32[128,128]{1,0:T(8,128)S(1)} %broadcast_select_fusion.11), channel_id=1, source_target_pairs={{0,4},{16,20},{32,36},{48,52},{64,68},{80,84},{96,100},{112,116},{... | collective-permute-start | bytes 196616 | tf_op jit(solution)/shard_map/ppermute | solution.py:37
  41.3 1.3 %collective-permute-start.20 = (f32[128,264]{1,0:T(8,128)S(1)}, f32[128,264]{1,0:T(8,128)S(1)}, u32[]{:S(2)}, u32[]{:S(2)}) collective-permute-start(f32[128,264]{1,0:T(8,128)S(1)} %broadcast_select_fusion.8), channel_id=1, source_target_pairs={{0,2},{4,6},{8,10},{12,14},{16,18},{20,22},{24,26},{28,30},{32,34}... | collective-permute-start | bytes 405512 | tf_op jit(solution)/shard_map/ppermute | solution.py:16
  42.7 0.7 %collective-permute-start.3 = (f32[512,128]{1,0:T(8,128)S(1)}, f32[512,128]{1,0:T(8,128)S(1)}, u32[]{:S(2)}, u32[]{:S(2)}) collective-permute-start(f32[512,128]{1,0:T(8,128)S(1)} %broadcast_select_fusion.5), channel_id=1, source_target_pairs={{0,32},{64,96},{128,160},{192,224},{256,288},{320,352},{384,416},{... | collective-permute-start | bytes 786440 | tf_op jit(solution)/shard_map/ppermute | solution.py:16
  43.4 1.3 %collective-permute-start.17 = (f32[128,128]{1,0:T(8,128)S(1)}, f32[128,128]{1,0:T(8,128)S(1)}, u32[]{:S(2)}, u32[]{:S(2)}) collective-permute-start(f32[128,128]{1,0:T(8,128)S(1)} %select_select_fusion.1), channel_id=1, source_target_pairs={{0,3},{4,7},{8,11},{12,15},{16,19},{20,23},{24,27},{28,31},{32,35}... | collective-permute-start | bytes 196616 | tf_op jit(solution)/shard_map/ppermute | solution.py:37
  44.7 1.3 %collective-permute-start.16 = (f32[128,128]{1,0:T(8,128)S(1)}, f32[128,128]{1,0:T(8,128)S(1)}, u32[]{:S(2)}, u32[]{:S(2)}) collective-permute-start(f32[128,128]{1,0:T(8,128)S(1)} %select_select_fusion.1), channel_id=1, source_target_pairs={{0,2},{4,6},{8,10},{12,14},{16,18},{20,22},{24,26},{28,30},{32,34}... | collective-permute-start | bytes 196616 | tf_op jit(solution)/shard_map/ppermute | solution.py:37
  46.0 1.3 %collective-permute-start.15 = (f32[128,128]{1,0:T(8,128)S(1)}, f32[128,128]{1,0:T(8,128)S(1)}, u32[]{:S(2)}, u32[]{:S(2)}) collective-permute-start(f32[128,128]{1,0:T(8,128)S(1)} %select_select_fusion.1), channel_id=1, source_target_pairs={{0,1},{4,5},{8,9},{12,13},{16,17},{20,21},{24,25},{28,29},{32,33},... | collective-permute-start | bytes 196616 | tf_op jit(solution)/shard_map/ppermute | solution.py:37
  47.3 1.3 %collective-permute-start.21 = (f32[128,264]{1,0:T(8,128)S(1)}, f32[128,264]{1,0:T(8,128)S(1)}, u32[]{:S(2)}, u32[]{:S(2)}) collective-permute-start(f32[128,264]{1,0:T(8,128)S(1)} %broadcast_select_fusion.9), channel_id=1, source_target_pairs={{0,1},{2,3},{4,5},{6,7},{8,9},{10,11},{12,13},{14,15},{16,17},{18,... | collective-permute-start | bytes 405512 | tf_op jit(solution)/shard_map/ppermute | solution.py:16
  48.7 1.3 %collective-permute-start.4 = (f32[512,128]{1,0:T(8,128)S(1)}, f32[512,128]{1,0:T(8,128)S(1)}, u32[]{:S(2)}, u32[]{:S(2)}) collective-permute-start(f32[512,128]{1,0:T(8,128)S(1)} %broadcast_select_fusion.6), channel_id=1, source_target_pairs={{0,16},{32,48},{64,80},{96,112},{128,144},{160,176},{192,208},{224... | collective-permute-start | bytes 786440 | tf_op jit(solution)/shard_map/ppermute | solution.py:16
  50.1 2.3 %collective-permute-done.21 = f32[128,264]{1,0:T(8,128)S(1)} collective-permute-done((f32[128,264]{1,0:T(8,128)S(1)}, f32[128,264]{1,0:T(8,128)S(1)}, u32[]{:S(2)}, u32[]{:S(2)}) %collective-permute-start.21) | collective-permute-done | bytes 135200 | tf_op jit(solution)/shard_map/ppermute | solution.py:16
  52.8 8.3 %collective-permute-done.4 = f32[512,128]{1,0:T(8,128)S(1)} collective-permute-done((f32[512,128]{1,0:T(8,128)S(1)}, f32[512,128]{1,0:T(8,128)S(1)}, u32[]{:S(2)}, u32[]{:S(2)}) %collective-permute-start.4) | collective-permute-done | bytes 262176 | tf_op jit(solution)/shard_map/ppermute | solution.py:16
  63.3 0.7 %broadcast_select_fusion.10 = f32[8,4,1,128]{3,2,1,0:T(1,128)} fusion(pred[4]{0:T(512)(128)(4,1)S(1)} %get-tuple-element.13, f32[8,4,1,128]{3,0,1,2:T(8,128)S(1)} %fusion, f32[8,128]{1,0:T(8,128)S(1)} %slice-done), kind=kLoop, calls=%fused_computation.28 | loop fusion | flops 4096 | bytes 36868 | tf_op jit(solution)/shard_map/jit(_where)/select_n | solution.py:130
  64.0 1.5 %broadcast_select_fusion = f32[4,1,128,2,1,128]{5,4,3,2,1,0:T(1,128)} fusion(pred[2]{0:T(512)(128)(4,1)S(1)} %fusion.9, f32[4,1,128,2,1,128]{5,4,3,2,1,0:T(1,128)S(1)} %bitcast.35, pred[4,2]{1,0:T(4,128)(4,1)S(1)} %broadcast_and_fusion, f32[4,128,128]{2,1,0:T(8,128)S(1)} %broadcast_select_fusion.2), kind=kLoop, calls=%fused_computation.3 | loop fusion | flops 262144 | bytes 1310730 | tf_op jit(solution)/shard_map/jit(_where)/select_n | solution.py:122
  (64 shorter events, 7.1 us)
Async XLA Ops:
  0.6 3.2 %copy-start = (f32[4,1,128,2,1,128]{5,4,3,2,1,0:T(1,128)S(1)}, f32[4,1,128,2,1,128]{5,4,3,2,1,0:T(1,128)}, u32[]{:S(2)}) copy-start(f32[4,1,128,2,1,128]{5,4,3,2,1,0:T(1,128)} %param.4) | copy-start | bytes 1572868
  1.8 20.5 %collective-permute-start.7 = (f32[128,128]{1,0:T(8,128)S(1)}, f32[128,128]{1,0:T(8,128)S(1)}, u32[]{:S(2)}, u32[]{:S(2)}) collective-permute-start(f32[128,128]{1,0:T(8,128)S(1)} %get-tuple-element.9), channel_id=1, source_target_pairs={{0,384},{1,385},{2,386},{3,387},{4,388},{5,389},{6,390},{7,391},{8... | collective-permute-start | bytes 196616 | tf_op jit(solution)/shard_map/ppermute | solution.py:37
  2.5 19.8 %collective-permute-start.6 = (f32[128,128]{1,0:T(8,128)S(1)}, f32[128,128]{1,0:T(8,128)S(1)}, u32[]{:S(2)}, u32[]{:S(2)}) collective-permute-start(f32[128,128]{1,0:T(8,128)S(1)} %get-tuple-element.9), channel_id=1, source_target_pairs={{0,256},{1,257},{2,258},{3,259},{4,260},{5,261},{6,262},{7,263},{8... | collective-permute-start | bytes 196616 | tf_op jit(solution)/shard_map/ppermute | solution.py:37
  3.2 19.2 %collective-permute-start.5 = (f32[128,128]{1,0:T(8,128)S(1)}, f32[128,128]{1,0:T(8,128)S(1)}, u32[]{:S(2)}, u32[]{:S(2)}) collective-permute-start(f32[128,128]{1,0:T(8,128)S(1)} %get-tuple-element.9), channel_id=1, source_target_pairs={{0,128},{1,129},{2,130},{3,131},{4,132},{5,133},{6,134},{7,135},{8... | collective-permute-start | bytes 196616 | tf_op jit(solution)/shard_map/ppermute | solution.py:37
  5.1 21.4 %collective-permute-start.18 = (f32[128,264]{1,0:T(8,128)S(1)}, f32[128,264]{1,0:T(8,128)S(1)}, u32[]{:S(2)}, u32[]{:S(2)}) collective-permute-start(f32[128,264]{1,0:T(8,128)S(1)} %pad_maximum_fusion), channel_id=1, source_target_pairs={{0,8},{16,24},{32,40},{48,56},{64,72},{80,88},{96,104},{112,120},{... | collective-permute-start | bytes 405512 | tf_op jit(solution)/shard_map/ppermute | solution.py:16
  21.4 3.0 %collective-permute-start = (f32[512,128]{1,0:T(8,128)S(1)}, f32[512,128]{1,0:T(8,128)S(1)}, u32[]{:S(2)}, u32[]{:S(2)}) collective-permute-start(f32[512,128]{1,0:T(8,128)S(1)} %slice.30), channel_id=1, source_target_pairs={{0,256},{1,257},{2,258},{3,259},{4,260},{5,261},{6,262},{7,263},{8... | collective-permute-start | bytes 786440 | tf_op jit(solution)/shard_map/ppermute | solution.py:16
  22.4 2.8 %collective-permute-start.10 = (f32[128,128]{1,0:T(8,128)S(1)}, f32[128,128]{1,0:T(8,128)S(1)}, u32[]{:S(2)}, u32[]{:S(2)}) collective-permute-start(f32[128,128]{1,0:T(8,128)S(1)} %select_select_fusion.3), channel_id=1, source_target_pairs={{0,96},{128,224},{256,352},{384,480},{1,97},{129,225},{257,353},{3... | collective-permute-start | bytes 196616 | tf_op jit(solution)/shard_map/ppermute | solution.py:37
  23.1 2.1 %collective-permute-start.9 = (f32[128,128]{1,0:T(8,128)S(1)}, f32[128,128]{1,0:T(8,128)S(1)}, u32[]{:S(2)}, u32[]{:S(2)}) collective-permute-start(f32[128,128]{1,0:T(8,128)S(1)} %select_select_fusion.3), channel_id=1, source_target_pairs={{0,64},{128,192},{256,320},{384,448},{1,65},{129,193},{257,321},{3... | collective-permute-start | bytes 196616 | tf_op jit(solution)/shard_map/ppermute | solution.py:37
  23.8 1.4 %collective-permute-start.8 = (f32[128,128]{1,0:T(8,128)S(1)}, f32[128,128]{1,0:T(8,128)S(1)}, u32[]{:S(2)}, u32[]{:S(2)}) collective-permute-start(f32[128,128]{1,0:T(8,128)S(1)} %select_select_fusion.3), channel_id=1, source_target_pairs={{0,32},{128,160},{256,288},{384,416},{1,33},{129,161},{257,289},{3... | collective-permute-start | bytes 196616 | tf_op jit(solution)/shard_map/ppermute | solution.py:37
  24.5 3.4 %collective-permute-start.1 = (f32[512,128]{1,0:T(8,128)S(1)}, f32[512,128]{1,0:T(8,128)S(1)}, u32[]{:S(2)}, u32[]{:S(2)}) collective-permute-start(f32[512,128]{1,0:T(8,128)S(1)} %broadcast_select_fusion.3), channel_id=1, source_target_pairs={{0,128},{256,384},{1,129},{257,385},{2,130},{258,386},{3,131},{259... | collective-permute-start | bytes 786440 | tf_op jit(solution)/shard_map/ppermute | solution.py:16
  25.2 12.1 %collective-permute-start.11 = (f32[128,128]{1,0:T(8,128)S(1)}, f32[128,128]{1,0:T(8,128)S(1)}, u32[]{:S(2)}, u32[]{:S(2)}) collective-permute-start(f32[128,128]{1,0:T(8,128)S(1)} %select_select_fusion.2), channel_id=1, source_target_pairs={{0,16},{32,48},{64,80},{96,112},{128,144},{160,176},{192,208},{224... | collective-permute-start | bytes 196616 | tf_op jit(solution)/shard_map/ppermute | solution.py:37
  26.6 14.7 %collective-permute-start.19 = (f32[128,264]{1,0:T(8,128)S(1)}, f32[128,264]{1,0:T(8,128)S(1)}, u32[]{:S(2)}, u32[]{:S(2)}) collective-permute-start(f32[128,264]{1,0:T(8,128)S(1)} %broadcast_select_fusion.7), channel_id=1, source_target_pairs={{0,4},{8,12},{16,20},{24,28},{32,36},{40,44},{48,52},{56,60},{64,6... | collective-permute-start | bytes 405512 | tf_op jit(solution)/shard_map/ppermute | solution.py:16
  27.9 14.7 %collective-permute-start.2 = (f32[512,128]{1,0:T(8,128)S(1)}, f32[512,128]{1,0:T(8,128)S(1)}, u32[]{:S(2)}, u32[]{:S(2)}) collective-permute-start(f32[512,128]{1,0:T(8,128)S(1)} %broadcast_select_fusion.4), channel_id=1, source_target_pairs={{0,64},{128,192},{256,320},{384,448},{1,65},{129,193},{257,321},{3... | collective-permute-start | bytes 786440 | tf_op jit(solution)/shard_map/ppermute | solution.py:16
  37.4 6.0 %collective-permute-start.14 = (f32[128,128]{1,0:T(8,128)S(1)}, f32[128,128]{1,0:T(8,128)S(1)}, u32[]{:S(2)}, u32[]{:S(2)}) collective-permute-start(f32[128,128]{1,0:T(8,128)S(1)} %broadcast_select_fusion.11), channel_id=1, source_target_pairs={{0,12},{16,28},{32,44},{48,60},{64,76},{80,92},{96,108},{112,124},... | collective-permute-start | bytes 196616 | tf_op jit(solution)/shard_map/ppermute | solution.py:37
  38.7 4.7 %collective-permute-start.13 = (f32[128,128]{1,0:T(8,128)S(1)}, f32[128,128]{1,0:T(8,128)S(1)}, u32[]{:S(2)}, u32[]{:S(2)}) collective-permute-start(f32[128,128]{1,0:T(8,128)S(1)} %broadcast_select_fusion.11), channel_id=1, source_target_pairs={{0,8},{16,24},{32,40},{48,56},{64,72},{80,88},{96,104},{112,120},{... | collective-permute-start | bytes 196616 | tf_op jit(solution)/shard_map/ppermute | solution.py:37
  40.0 3.4 %collective-permute-start.12 = (f32[128,128]{1,0:T(8,128)S(1)}, f32[128,128]{1,0:T(8,128)S(1)}, u32[]{:S(2)}, u32[]{:S(2)}) collective-permute-start(f32[128,128]{1,0:T(8,128)S(1)} %broadcast_select_fusion.11), channel_id=1, source_target_pairs={{0,4},{16,20},{32,36},{48,52},{64,68},{80,84},{96,100},{112,116},{... | collective-permute-start | bytes 196616 | tf_op jit(solution)/shard_map/ppermute | solution.py:37
  41.3 6.0 %collective-permute-start.20 = (f32[128,264]{1,0:T(8,128)S(1)}, f32[128,264]{1,0:T(8,128)S(1)}, u32[]{:S(2)}, u32[]{:S(2)}) collective-permute-start(f32[128,264]{1,0:T(8,128)S(1)} %broadcast_select_fusion.8), channel_id=1, source_target_pairs={{0,2},{4,6},{8,10},{12,14},{16,18},{20,22},{24,26},{28,30},{32,34}... | collective-permute-start | bytes 405512 | tf_op jit(solution)/shard_map/ppermute | solution.py:16
  42.7 6.0 %collective-permute-start.3 = (f32[512,128]{1,0:T(8,128)S(1)}, f32[512,128]{1,0:T(8,128)S(1)}, u32[]{:S(2)}, u32[]{:S(2)}) collective-permute-start(f32[512,128]{1,0:T(8,128)S(1)} %broadcast_select_fusion.5), channel_id=1, source_target_pairs={{0,32},{64,96},{128,160},{192,224},{256,288},{320,352},{384,416},{... | collective-permute-start | bytes 786440 | tf_op jit(solution)/shard_map/ppermute | solution.py:16
  43.4 6.6 %collective-permute-start.17 = (f32[128,128]{1,0:T(8,128)S(1)}, f32[128,128]{1,0:T(8,128)S(1)}, u32[]{:S(2)}, u32[]{:S(2)}) collective-permute-start(f32[128,128]{1,0:T(8,128)S(1)} %select_select_fusion.1), channel_id=1, source_target_pairs={{0,3},{4,7},{8,11},{12,15},{16,19},{20,23},{24,27},{28,31},{32,35}... | collective-permute-start | bytes 196616 | tf_op jit(solution)/shard_map/ppermute | solution.py:37
  44.7 5.3 %collective-permute-start.16 = (f32[128,128]{1,0:T(8,128)S(1)}, f32[128,128]{1,0:T(8,128)S(1)}, u32[]{:S(2)}, u32[]{:S(2)}) collective-permute-start(f32[128,128]{1,0:T(8,128)S(1)} %select_select_fusion.1), channel_id=1, source_target_pairs={{0,2},{4,6},{8,10},{12,14},{16,18},{20,22},{24,26},{28,30},{32,34}... | collective-permute-start | bytes 196616 | tf_op jit(solution)/shard_map/ppermute | solution.py:37
  46.0 4.0 %collective-permute-start.15 = (f32[128,128]{1,0:T(8,128)S(1)}, f32[128,128]{1,0:T(8,128)S(1)}, u32[]{:S(2)}, u32[]{:S(2)}) collective-permute-start(f32[128,128]{1,0:T(8,128)S(1)} %select_select_fusion.1), channel_id=1, source_target_pairs={{0,1},{4,5},{8,9},{12,13},{16,17},{20,21},{24,25},{28,29},{32,33},... | collective-permute-start | bytes 196616 | tf_op jit(solution)/shard_map/ppermute | solution.py:37
  47.3 5.0 %collective-permute-start.21 = (f32[128,264]{1,0:T(8,128)S(1)}, f32[128,264]{1,0:T(8,128)S(1)}, u32[]{:S(2)}, u32[]{:S(2)}) collective-permute-start(f32[128,264]{1,0:T(8,128)S(1)} %broadcast_select_fusion.9), channel_id=1, source_target_pairs={{0,1},{2,3},{4,5},{6,7},{8,9},{10,11},{12,13},{14,15},{16,17},{18,... | collective-permute-start | bytes 405512 | tf_op jit(solution)/shard_map/ppermute | solution.py:16
  48.7 12.4 %collective-permute-start.4 = (f32[512,128]{1,0:T(8,128)S(1)}, f32[512,128]{1,0:T(8,128)S(1)}, u32[]{:S(2)}, u32[]{:S(2)}) collective-permute-start(f32[512,128]{1,0:T(8,128)S(1)} %broadcast_select_fusion.6), channel_id=1, source_target_pairs={{0,16},{32,48},{64,80},{96,112},{128,144},{160,176},{192,208},{224... | collective-permute-start | bytes 786440 | tf_op jit(solution)/shard_map/ppermute | solution.py:16
  52.8 9.3 %copy-start.1 = (f32[264,128]{1,0:T(8,128)}, f32[264,128]{1,0:T(8,128)S(1)}, u32[]{:S(2)}) copy-start(f32[264,128]{1,0:T(8,128)S(1)} %fusion.3) | copy-start | bytes 405508
  (3 other events, 2.1 us)

commit v19 on v16

--- a/solution.py
+++ b/solution.py
@@ -94,7 +94,7 @@
     inverse = spread_wide(spread_wide(inverse, "col"), "row")
     left = spread(local[:, :block], "col")
     top = jnp.concatenate([local[:block], right_sides[:, 0, 0, :].T], axis=1)
-    top = spread(top, "row")
+    top = spread_wide(top, "row")
 
     rows_factor = jnp.dot(
         left, inverse.T, precision=lax.Precision.HIGHEST, preferred_element_type=jnp.float32

time: 66 us -> 71.6 us (1.085)
  waiting for transfers between devices: 18.8 us -> 21.7 us
  starting transfers between devices: 37.2 us -> 39.3 us
    ppermute x13 -> x19, starting transfers between devices: 13 us -> 35.3 us  [spread_wide(): arrived = lax.ppermute(block, axis, pairs)]
    ppermute x9 -> x5, starting transfers between devices: 24.2 us -> 3.99 us  [spread(): arrived = lax.ppermute(block, axis, pairs)]
    ppermute x13 -> x19, waiting for transfers between devices: 8.32 us -> 18.4 us  [spread_wide(): arrived = lax.ppermute(block, axis, pairs)]
    ppermute x9 -> x5, waiting for transfers between devices: 10.5 us -> 3.37 us  [spread(): arrived = lax.ppermute(block, axis, pairs)]
  transfers between devices with their start and end apart: 22 -> 24, of which waited for: 3 -> 6; matrix products, arithmetic and copies ran while one was open for 2% -> 2% of each run, Pallas kernels for 0% -> 0%
where the time goes in v19:
time: 71.6 us; the launch traced here: 70.4 us
  starting transfers between devices  39.3 us (55%)
  waiting for transfers between devices  21.7 us (30%)
  local copies, waits for them, and re-layouts  3.68 us (5%)
  other arithmetic  2.66 us (4%)
  matrix products  1.76 us (2%)
  between operations  1.25 us (2%)
    ppermute x19, starting transfers between devices, spread_wide(): arrived = lax.ppermute(block, axis, pairs)  35.3 us
    ppermute x19, waiting for transfers between devices, spread_wide(): arrived = lax.ppermute(block, axis, pairs)  18.4 us
    ppermute x5, starting transfers between devices, spread(): arrived = lax.ppermute(block, axis, pairs)  3.99 us
    ppermute x5, waiting for transfers between devices, spread(): arrived = lax.ppermute(block, axis, pairs)  3.37 us
    unnamed x8, local copies, waits for them, and re-layouts  1.52 us
    select_n x1, other arithmetic, on_device(): jnp.where((global_cols == 0)[None, None, :, None], column[:, :, None, :],...  1.52 us
  transfers between devices with their start and end apart: 24, of which 6 were waited for; matrix products, arithmetic and copies ran while one was open for 2% of the time, Pallas kernels for 0%

profile of v19, /device:TPU:1, one launch (start us, length us, event | category | flops | bytes accessed | tf_op | source)
XLA Modules:
  0.0 70.4 jit_solution(16506870389749496522)
XLA Ops:
  0.6 1.1 %copy.18 = f32[64,8,2,128]{3,1,2,0:T(8,128)S(1)} copy(f32[64,8,2,128]{3,2,1,0:T(2,128)} %bitcast.30) | data formatting | bytes 1048576
  1.8 0.8 %collective-permute-start.5 = (f32[128,128]{1,0:T(8,128)S(1)}, f32[128,128]{1,0:T(8,128)S(1)}, u32[]{:S(2)}, u32[]{:S(2)}) collective-permute-start(f32[128,128]{1,0:T(8,128)S(1)} %get-tuple-element.9), channel_id=1, source_target_pairs={{0,384},{1,385},{2,386},{3,387},{4,388},{5,389},{6,390},{7,391},{8... | collective-permute-start | bytes 196616 | tf_op jit(solution)/shard_map/ppermute | solution.py:37
  5.1 0.7 slice-done.1
  5.9 13.3 %collective-permute-start.18 = (f32[128,264]{1,0:T(8,128)S(1)}, f32[128,264]{1,0:T(8,128)S(1)}, u32[]{:S(2)}, u32[]{:S(2)}) collective-permute-start(f32[128,264]{1,0:T(8,128)S(1)} %pad_maximum_fusion), channel_id=1, source_target_pairs={{0,12},{16,28},{32,44},{48,60},{64,76},{80,92},{96,108},{112,124},... | collective-permute-start | bytes 405512 | tf_op jit(solution)/shard_map/ppermute | solution.py:37
  22.1 3.6 %collective-permute-start.19 = (f32[128,264]{1,0:T(8,128)S(1)}, f32[128,264]{1,0:T(8,128)S(1)}, u32[]{:S(2)}, u32[]{:S(2)}) collective-permute-start(f32[128,264]{1,0:T(8,128)S(1)} %pad_maximum_fusion), channel_id=1, source_target_pairs={{0,8},{16,24},{32,40},{48,56},{64,72},{80,88},{96,104},{112,120},{... | collective-permute-start | bytes 405512 | tf_op jit(solution)/shard_map/ppermute | solution.py:37
  25.8 1.3 %collective-permute-start.20 = (f32[128,264]{1,0:T(8,128)S(1)}, f32[128,264]{1,0:T(8,128)S(1)}, u32[]{:S(2)}, u32[]{:S(2)}) collective-permute-start(f32[128,264]{1,0:T(8,128)S(1)} %pad_maximum_fusion), channel_id=1, source_target_pairs={{0,4},{16,20},{32,36},{48,52},{64,68},{80,84},{96,100},{112,116},{... | collective-permute-start | bytes 405512 | tf_op jit(solution)/shard_map/ppermute | solution.py:37
  27.1 1.3 %collective-permute-start.11 = (f32[128,128]{1,0:T(8,128)S(1)}, f32[128,128]{1,0:T(8,128)S(1)}, u32[]{:S(2)}, u32[]{:S(2)}) collective-permute-start(f32[128,128]{1,0:T(8,128)S(1)} %select_select_fusion.3), channel_id=1, source_target_pairs={{0,16},{32,48},{64,80},{96,112},{128,144},{160,176},{192,208},{224... | collective-permute-start | bytes 196616 | tf_op jit(solution)/shard_map/ppermute | solution.py:37
  28.5 0.7 collective-permute-start.2
  29.3 11.0 %collective-permute-done.11 = f32[128,128]{1,0:T(8,128)S(1)} collective-permute-done((f32[128,128]{1,0:T(8,128)S(1)}, f32[128,128]{1,0:T(8,128)S(1)}, u32[]{:S(2)}, u32[]{:S(2)}) %collective-permute-start.11) | collective-permute-done | bytes 65568 | tf_op jit(solution)/shard_map/ppermute | solution.py:37
  40.3 1.3 %collective-permute-start.12 = (f32[128,128]{1,0:T(8,128)S(1)}, f32[128,128]{1,0:T(8,128)S(1)}, u32[]{:S(2)}, u32[]{:S(2)}) collective-permute-start(f32[128,128]{1,0:T(8,128)S(1)} %broadcast_select_fusion.8), channel_id=1, source_target_pairs={{0,12},{16,28},{32,44},{48,60},{64,76},{80,92},{96,108},{112,124},... | collective-permute-start | bytes 196616 | tf_op jit(solution)/shard_map/ppermute | solution.py:37
  41.6 1.3 %collective-permute-start.13 = (f32[128,128]{1,0:T(8,128)S(1)}, f32[128,128]{1,0:T(8,128)S(1)}, u32[]{:S(2)}, u32[]{:S(2)}) collective-permute-start(f32[128,128]{1,0:T(8,128)S(1)} %broadcast_select_fusion.8), channel_id=1, source_target_pairs={{0,8},{16,24},{32,40},{48,56},{64,72},{80,88},{96,104},{112,120},{... | collective-permute-start | bytes 196616 | tf_op jit(solution)/shard_map/ppermute | solution.py:37
  43.0 1.3 %collective-permute-start.14 = (f32[128,128]{1,0:T(8,128)S(1)}, f32[128,128]{1,0:T(8,128)S(1)}, u32[]{:S(2)}, u32[]{:S(2)}) collective-permute-start(f32[128,128]{1,0:T(8,128)S(1)} %broadcast_select_fusion.8), channel_id=1, source_target_pairs={{0,4},{16,20},{32,36},{48,52},{64,68},{80,84},{96,100},{112,116},{... | collective-permute-start | bytes 196616 | tf_op jit(solution)/shard_map/ppermute | solution.py:37
  45.0 1.3 %collective-permute-start.21 = (f32[128,264]{1,0:T(8,128)S(1)}, f32[128,264]{1,0:T(8,128)S(1)}, u32[]{:S(2)}, u32[]{:S(2)}) collective-permute-start(f32[128,264]{1,0:T(8,128)S(1)} %select_select_fusion), channel_id=1, source_target_pairs={{0,3},{4,7},{8,11},{12,15},{16,19},{20,23},{24,27},{28,31},{32,35}... | collective-permute-start | bytes 405512 | tf_op jit(solution)/shard_map/ppermute | solution.py:37
  46.3 1.3 %collective-permute-start.22 = (f32[128,264]{1,0:T(8,128)S(1)}, f32[128,264]{1,0:T(8,128)S(1)}, u32[]{:S(2)}, u32[]{:S(2)}) collective-permute-start(f32[128,264]{1,0:T(8,128)S(1)} %select_select_fusion), channel_id=1, source_target_pairs={{0,2},{4,6},{8,10},{12,14},{16,18},{20,22},{24,26},{28,30},{32,34}... | collective-permute-start | bytes 405512 | tf_op jit(solution)/shard_map/ppermute | solution.py:37
  47.7 1.3 %collective-permute-start.15 = (f32[128,128]{1,0:T(8,128)S(1)}, f32[128,128]{1,0:T(8,128)S(1)}, u32[]{:S(2)}, u32[]{:S(2)}) collective-permute-start(f32[128,128]{1,0:T(8,128)S(1)} %select_select_fusion.2), channel_id=1, source_target_pairs={{0,3},{4,7},{8,11},{12,15},{16,19},{20,23},{24,27},{28,31},{32,35}... | collective-permute-start | bytes 196616 | tf_op jit(solution)/shard_map/ppermute | solution.py:37
  49.0 1.3 %collective-permute-start.16 = (f32[128,128]{1,0:T(8,128)S(1)}, f32[128,128]{1,0:T(8,128)S(1)}, u32[]{:S(2)}, u32[]{:S(2)}) collective-permute-start(f32[128,128]{1,0:T(8,128)S(1)} %select_select_fusion.2), channel_id=1, source_target_pairs={{0,2},{4,6},{8,10},{12,14},{16,18},{20,22},{24,26},{28,30},{32,34}... | collective-permute-start | bytes 196616 | tf_op jit(solution)/shard_map/ppermute | solution.py:37
  50.3 1.3 %collective-permute-start.17 = (f32[128,128]{1,0:T(8,128)S(1)}, f32[128,128]{1,0:T(8,128)S(1)}, u32[]{:S(2)}, u32[]{:S(2)}) collective-permute-start(f32[128,128]{1,0:T(8,128)S(1)} %select_select_fusion.2), channel_id=1, source_target_pairs={{0,1},{4,5},{8,9},{12,13},{16,17},{20,21},{24,25},{28,29},{32,33},... | collective-permute-start | bytes 196616 | tf_op jit(solution)/shard_map/ppermute | solution.py:37
  51.6 3.0 %collective-permute-done.15 = f32[128,128]{1,0:T(8,128)S(1)} collective-permute-done((f32[128,128]{1,0:T(8,128)S(1)}, f32[128,128]{1,0:T(8,128)S(1)}, u32[]{:S(2)}, u32[]{:S(2)}) %collective-permute-start.15) | collective-permute-done | bytes 65568 | tf_op jit(solution)/shard_map/ppermute | solution.py:37
  54.6 1.3 %collective-permute-start.23 = (f32[128,264]{1,0:T(8,128)S(1)}, f32[128,264]{1,0:T(8,128)S(1)}, u32[]{:S(2)}, u32[]{:S(2)}) collective-permute-start(f32[128,264]{1,0:T(8,128)S(1)} %select_select_fusion), channel_id=1, source_target_pairs={{0,1},{4,5},{8,9},{12,13},{16,17},{20,21},{24,25},{28,29},{32,33},... | collective-permute-start | bytes 405512 | tf_op jit(solution)/shard_map/ppermute | solution.py:37
  56.0 1.3 %collective-permute-start.4 = (f32[512,128]{1,0:T(8,128)S(1)}, f32[512,128]{1,0:T(8,128)S(1)}, u32[]{:S(2)}, u32[]{:S(2)}) collective-permute-start(f32[512,128]{1,0:T(8,128)S(1)} %broadcast_select_fusion.6), channel_id=1, source_target_pairs={{0,16},{32,48},{64,80},{96,112},{128,144},{160,176},{192,208},{224... | collective-permute-start | bytes 786440 | tf_op jit(solution)/shard_map/ppermute | solution.py:16
  57.4 4.2 %collective-permute-done.23 = f32[128,264]{1,0:T(8,128)S(1)} collective-permute-done((f32[128,264]{1,0:T(8,128)S(1)}, f32[128,264]{1,0:T(8,128)S(1)}, u32[]{:S(2)}, u32[]{:S(2)}) %collective-permute-start.23) | collective-permute-done | bytes 135200 | tf_op jit(solution)/shard_map/ppermute | solution.py:37
  62.1 3.4 %collective-permute-done.4 = f32[512,128]{1,0:T(8,128)S(1)} collective-permute-done((f32[512,128]{1,0:T(8,128)S(1)}, f32[512,128]{1,0:T(8,128)S(1)}, u32[]{:S(2)}, u32[]{:S(2)}) %collective-permute-start.4) | collective-permute-done | bytes 262176 | tf_op jit(solution)/shard_map/ppermute | solution.py:16
  68.2 0.7 broadcast_select_fusion.7
  68.9 1.5 %broadcast_select_fusion = f32[4,1,128,2,1,128]{5,4,3,2,1,0:T(1,128)} fusion(pred[2]{0:T(512)(128)(4,1)S(1)} %fusion.13, f32[4,1,128,2,1,128]{5,4,3,2,1,0:T(1,128)S(1)} %bitcast.35, pred[4,2]{1,0:T(4,128)(4,1)S(1)} %broadcast_and_fusion, f32[4,128,128]{2,1,0:T(8,128)S(1)} %broadcast_select_fusion.2), kind=kLoop, calls=%fused_computation.3 | loop fusion | flops 262144 | bytes 1310730 | tf_op jit(solution)/shard_map/jit(_where)/select_n | solution.py:122
  (66 shorter events, 9.8 us)
Async XLA Ops:
  1.8 17.4 %collective-permute-start.5 = (f32[128,128]{1,0:T(8,128)S(1)}, f32[128,128]{1,0:T(8,128)S(1)}, u32[]{:S(2)}, u32[]{:S(2)}) collective-permute-start(f32[128,128]{1,0:T(8,128)S(1)} %get-tuple-element.9), channel_id=1, source_target_pairs={{0,384},{1,385},{2,386},{3,387},{4,388},{5,389},{6,390},{7,391},{8... | collective-permute-start | bytes 196616 | tf_op jit(solution)/shard_map/ppermute | solution.py:37
  2.6 16.6 %collective-permute-start.6 = (f32[128,128]{1,0:T(8,128)S(1)}, f32[128,128]{1,0:T(8,128)S(1)}, u32[]{:S(2)}, u32[]{:S(2)}) collective-permute-start(f32[128,128]{1,0:T(8,128)S(1)} %get-tuple-element.9), channel_id=1, source_target_pairs={{0,256},{1,257},{2,258},{3,259},{4,260},{5,261},{6,262},{7,263},{8... | collective-permute-start | bytes 196616 | tf_op jit(solution)/shard_map/ppermute | solution.py:37
  3.3 16.0 %collective-permute-start.7 = (f32[128,128]{1,0:T(8,128)S(1)}, f32[128,128]{1,0:T(8,128)S(1)}, u32[]{:S(2)}, u32[]{:S(2)}) collective-permute-start(f32[128,128]{1,0:T(8,128)S(1)} %get-tuple-element.9), channel_id=1, source_target_pairs={{0,128},{1,129},{2,130},{3,131},{4,132},{5,133},{6,134},{7,135},{8... | collective-permute-start | bytes 196616 | tf_op jit(solution)/shard_map/ppermute | solution.py:37
  4.0 17.3 %collective-permute-start = (f32[512,128]{1,0:T(8,128)S(1)}, f32[512,128]{1,0:T(8,128)S(1)}, u32[]{:S(2)}, u32[]{:S(2)}) collective-permute-start(f32[512,128]{1,0:T(8,128)S(1)} %slice.30), channel_id=1, source_target_pairs={{0,256},{1,257},{2,258},{3,259},{4,260},{5,261},{6,262},{7,263},{8... | collective-permute-start | bytes 786440 | tf_op jit(solution)/shard_map/ppermute | solution.py:16
  5.9 37.1 %collective-permute-start.18 = (f32[128,264]{1,0:T(8,128)S(1)}, f32[128,264]{1,0:T(8,128)S(1)}, u32[]{:S(2)}, u32[]{:S(2)}) collective-permute-start(f32[128,264]{1,0:T(8,128)S(1)} %pad_maximum_fusion), channel_id=1, source_target_pairs={{0,12},{16,28},{32,44},{48,60},{64,76},{80,92},{96,108},{112,124},... | collective-permute-start | bytes 405512 | tf_op jit(solution)/shard_map/ppermute | solution.py:37
  19.3 2.8 %collective-permute-start.8 = (f32[128,128]{1,0:T(8,128)S(1)}, f32[128,128]{1,0:T(8,128)S(1)}, u32[]{:S(2)}, u32[]{:S(2)}) collective-permute-start(f32[128,128]{1,0:T(8,128)S(1)} %select_select_fusion.4), channel_id=1, source_target_pairs={{0,96},{128,224},{256,352},{384,480},{1,97},{129,225},{257,353},{3... | collective-permute-start | bytes 196616 | tf_op jit(solution)/shard_map/ppermute | solution.py:37
  19.9 5.8 %collective-permute-start.9 = (f32[128,128]{1,0:T(8,128)S(1)}, f32[128,128]{1,0:T(8,128)S(1)}, u32[]{:S(2)}, u32[]{:S(2)}) collective-permute-start(f32[128,128]{1,0:T(8,128)S(1)} %select_select_fusion.4), channel_id=1, source_target_pairs={{0,64},{128,192},{256,320},{384,448},{1,65},{129,193},{257,321},{3... | collective-permute-start | bytes 196616 | tf_op jit(solution)/shard_map/ppermute | solution.py:37
  20.6 6.5 %collective-permute-start.10 = (f32[128,128]{1,0:T(8,128)S(1)}, f32[128,128]{1,0:T(8,128)S(1)}, u32[]{:S(2)}, u32[]{:S(2)}) collective-permute-start(f32[128,128]{1,0:T(8,128)S(1)} %select_select_fusion.4), channel_id=1, source_target_pairs={{0,32},{128,160},{256,288},{384,416},{1,33},{129,161},{257,289},{3... | collective-permute-start | bytes 196616 | tf_op jit(solution)/shard_map/ppermute | solution.py:37
  21.3 7.1 %collective-permute-start.1 = (f32[512,128]{1,0:T(8,128)S(1)}, f32[512,128]{1,0:T(8,128)S(1)}, u32[]{:S(2)}, u32[]{:S(2)}) collective-permute-start(f32[512,128]{1,0:T(8,128)S(1)} %broadcast_select_fusion.3), channel_id=1, source_target_pairs={{0,128},{256,384},{1,129},{257,385},{2,130},{258,386},{3,131},{259... | collective-permute-start | bytes 786440 | tf_op jit(solution)/shard_map/ppermute | solution.py:16
  22.1 22.2 %collective-permute-start.19 = (f32[128,264]{1,0:T(8,128)S(1)}, f32[128,264]{1,0:T(8,128)S(1)}, u32[]{:S(2)}, u32[]{:S(2)}) collective-permute-start(f32[128,264]{1,0:T(8,128)S(1)} %pad_maximum_fusion), channel_id=1, source_target_pairs={{0,8},{16,24},{32,40},{48,56},{64,72},{80,88},{96,104},{112,120},{... | collective-permute-start | bytes 405512 | tf_op jit(solution)/shard_map/ppermute | solution.py:37
  25.8 19.2 %collective-permute-start.20 = (f32[128,264]{1,0:T(8,128)S(1)}, f32[128,264]{1,0:T(8,128)S(1)}, u32[]{:S(2)}, u32[]{:S(2)}) collective-permute-start(f32[128,264]{1,0:T(8,128)S(1)} %pad_maximum_fusion), channel_id=1, source_target_pairs={{0,4},{16,20},{32,36},{48,52},{64,68},{80,84},{96,100},{112,116},{... | collective-permute-start | bytes 405512 | tf_op jit(solution)/shard_map/ppermute | solution.py:37
  27.1 13.2 %collective-permute-start.11 = (f32[128,128]{1,0:T(8,128)S(1)}, f32[128,128]{1,0:T(8,128)S(1)}, u32[]{:S(2)}, u32[]{:S(2)}) collective-permute-start(f32[128,128]{1,0:T(8,128)S(1)} %select_select_fusion.3), channel_id=1, source_target_pairs={{0,16},{32,48},{64,80},{96,112},{128,144},{160,176},{192,208},{224... | collective-permute-start | bytes 196616 | tf_op jit(solution)/shard_map/ppermute | solution.py:37
  28.5 13.1 %collective-permute-start.2 = (f32[512,128]{1,0:T(8,128)S(1)}, f32[512,128]{1,0:T(8,128)S(1)}, u32[]{:S(2)}, u32[]{:S(2)}) collective-permute-start(f32[512,128]{1,0:T(8,128)S(1)} %broadcast_select_fusion.4), channel_id=1, source_target_pairs={{0,64},{128,192},{256,320},{384,448},{1,65},{129,193},{257,321},{3... | collective-permute-start | bytes 786440 | tf_op jit(solution)/shard_map/ppermute | solution.py:16
  40.3 6.0 %collective-permute-start.12 = (f32[128,128]{1,0:T(8,128)S(1)}, f32[128,128]{1,0:T(8,128)S(1)}, u32[]{:S(2)}, u32[]{:S(2)}) collective-permute-start(f32[128,128]{1,0:T(8,128)S(1)} %broadcast_select_fusion.8), channel_id=1, source_target_pairs={{0,12},{16,28},{32,44},{48,60},{64,76},{80,92},{96,108},{112,124},... | collective-permute-start | bytes 196616 | tf_op jit(solution)/shard_map/ppermute | solution.py:37
  41.6 6.0 %collective-permute-start.13 = (f32[128,128]{1,0:T(8,128)S(1)}, f32[128,128]{1,0:T(8,128)S(1)}, u32[]{:S(2)}, u32[]{:S(2)}) collective-permute-start(f32[128,128]{1,0:T(8,128)S(1)} %broadcast_select_fusion.8), channel_id=1, source_target_pairs={{0,8},{16,24},{32,40},{48,56},{64,72},{80,88},{96,104},{112,120},{... | collective-permute-start | bytes 196616 | tf_op jit(solution)/shard_map/ppermute | solution.py:37
  43.0 4.7 %collective-permute-start.14 = (f32[128,128]{1,0:T(8,128)S(1)}, f32[128,128]{1,0:T(8,128)S(1)}, u32[]{:S(2)}, u32[]{:S(2)}) collective-permute-start(f32[128,128]{1,0:T(8,128)S(1)} %broadcast_select_fusion.8), channel_id=1, source_target_pairs={{0,4},{16,20},{32,36},{48,52},{64,68},{80,84},{96,100},{112,116},{... | collective-permute-start | bytes 196616 | tf_op jit(solution)/shard_map/ppermute | solution.py:37
  44.3 6.0 %collective-permute-start.3 = (f32[512,128]{1,0:T(8,128)S(1)}, f32[512,128]{1,0:T(8,128)S(1)}, u32[]{:S(2)}, u32[]{:S(2)}) collective-permute-start(f32[512,128]{1,0:T(8,128)S(1)} %broadcast_select_fusion.5), channel_id=1, source_target_pairs={{0,32},{64,96},{128,160},{192,224},{256,288},{320,352},{384,416},{... | collective-permute-start | bytes 786440 | tf_op jit(solution)/shard_map/ppermute | solution.py:16
  45.0 12.4 %collective-permute-start.21 = (f32[128,264]{1,0:T(8,128)S(1)}, f32[128,264]{1,0:T(8,128)S(1)}, u32[]{:S(2)}, u32[]{:S(2)}) collective-permute-start(f32[128,264]{1,0:T(8,128)S(1)} %select_select_fusion), channel_id=1, source_target_pairs={{0,3},{4,7},{8,11},{12,15},{16,19},{20,23},{24,27},{28,31},{32,35}... | collective-permute-start | bytes 405512 | tf_op jit(solution)/shard_map/ppermute | solution.py:37
  46.3 11.1 %collective-permute-start.22 = (f32[128,264]{1,0:T(8,128)S(1)}, f32[128,264]{1,0:T(8,128)S(1)}, u32[]{:S(2)}, u32[]{:S(2)}) collective-permute-start(f32[128,264]{1,0:T(8,128)S(1)} %select_select_fusion), channel_id=1, source_target_pairs={{0,2},{4,6},{8,10},{12,14},{16,18},{20,22},{24,26},{28,30},{32,34}... | collective-permute-start | bytes 405512 | tf_op jit(solution)/shard_map/ppermute | solution.py:37
  47.7 6.9 %collective-permute-start.15 = (f32[128,128]{1,0:T(8,128)S(1)}, f32[128,128]{1,0:T(8,128)S(1)}, u32[]{:S(2)}, u32[]{:S(2)}) collective-permute-start(f32[128,128]{1,0:T(8,128)S(1)} %select_select_fusion.2), channel_id=1, source_target_pairs={{0,3},{4,7},{8,11},{12,15},{16,19},{20,23},{24,27},{28,31},{32,35}... | collective-permute-start | bytes 196616 | tf_op jit(solution)/shard_map/ppermute | solution.py:37
  49.0 7.0 %collective-permute-start.16 = (f32[128,128]{1,0:T(8,128)S(1)}, f32[128,128]{1,0:T(8,128)S(1)}, u32[]{:S(2)}, u32[]{:S(2)}) collective-permute-start(f32[128,128]{1,0:T(8,128)S(1)} %select_select_fusion.2), channel_id=1, source_target_pairs={{0,2},{4,6},{8,10},{12,14},{16,18},{20,22},{24,26},{28,30},{32,34}... | collective-permute-start | bytes 196616 | tf_op jit(solution)/shard_map/ppermute | solution.py:37
  50.3 7.1 %collective-permute-start.17 = (f32[128,128]{1,0:T(8,128)S(1)}, f32[128,128]{1,0:T(8,128)S(1)}, u32[]{:S(2)}, u32[]{:S(2)}) collective-permute-start(f32[128,128]{1,0:T(8,128)S(1)} %select_select_fusion.2), channel_id=1, source_target_pairs={{0,1},{4,5},{8,9},{12,13},{16,17},{20,21},{24,25},{28,29},{32,33},... | collective-permute-start | bytes 196616 | tf_op jit(solution)/shard_map/ppermute | solution.py:37
  54.6 7.0 %collective-permute-start.23 = (f32[128,264]{1,0:T(8,128)S(1)}, f32[128,264]{1,0:T(8,128)S(1)}, u32[]{:S(2)}, u32[]{:S(2)}) collective-permute-start(f32[128,264]{1,0:T(8,128)S(1)} %select_select_fusion), channel_id=1, source_target_pairs={{0,1},{4,5},{8,9},{12,13},{16,17},{20,21},{24,25},{28,29},{32,33},... | collective-permute-start | bytes 405512 | tf_op jit(solution)/shard_map/ppermute | solution.py:37
  56.0 9.5 %collective-permute-start.4 = (f32[512,128]{1,0:T(8,128)S(1)}, f32[512,128]{1,0:T(8,128)S(1)}, u32[]{:S(2)}, u32[]{:S(2)}) collective-permute-start(f32[512,128]{1,0:T(8,128)S(1)} %broadcast_select_fusion.6), channel_id=1, source_target_pairs={{0,16},{32,48},{64,80},{96,112},{128,144},{160,176},{192,208},{224... | collective-permute-start | bytes 786440 | tf_op jit(solution)/shard_map/ppermute | solution.py:16
  (5 other events, 9.7 us)

commit v20 on v16

--- a/solution.py
+++ b/solution.py
@@ -91,7 +91,7 @@
 
     holder = (row_id == 0) & (col_id == 0)
     corner, inverse = lax.cond(holder, factor, skip, local[:block, :block])
-    inverse = spread_wide(spread_wide(inverse, "col"), "row")
+    inverse = spread(spread_wide(inverse, "col"), "row")
     left = spread(local[:, :block], "col")
     top = jnp.concatenate([local[:block], right_sides[:, 0, 0, :].T], axis=1)
     top = spread(top, "row")

time: 66 us -> 65.8 us (level)
  the two profiles are of different devices: /device:TPU:1 before, /device:TPU:352 now
where the time goes in v20:
time: 65.8 us; the launch traced here: 65.1 us
  waiting for transfers between devices  28.9 us (44%)
  starting transfers between devices  27.3 us (41%)
  local copies, waits for them, and re-layouts  3.26 us (5%)
  other arithmetic  2.7 us (4%)
  matrix products  1.75 us (3%)
  between operations  1.15 us (2%)
    ppermute x13, waiting for transfers between devices, spread(): arrived = lax.ppermute(block, axis, pairs)  26.2 us
    ppermute x13, starting transfers between devices, spread(): arrived = lax.ppermute(block, axis, pairs)  14.7 us
    ppermute x7, starting transfers between devices, spread_wide(): arrived = lax.ppermute(block, axis, pairs)  12.7 us
    ppermute x7, waiting for transfers between devices, spread_wide(): arrived = lax.ppermute(block, axis, pairs)  2.67 us
    select_n x1, other arithmetic, on_device(): jnp.where((global_cols == 0)[None, None, :, None], column[:, :, None, :],...  1.52 us
  transfers between devices with their start and end apart: 20, of which 8 were waited for; matrix products, arithmetic and copies ran while one was open for 2% of the time, Pallas kernels for 0%

profile of v20, /device:TPU:352, one launch (start us, length us, event | category | flops | bytes accessed | tf_op | source)
XLA Modules:
  0.0 65.1 jit_solution(10993375688143960767)
XLA Ops:
  0.7 1.1 %copy.18 = f32[64,8,2,128]{3,1,2,0:T(8,128)S(1)} copy(f32[64,8,2,128]{3,2,1,0:T(2,128)} %bitcast.28) | data formatting | bytes 1048576
  1.8 4.9 %collective-permute-start.5 = (f32[128,128]{1,0:T(8,128)S(1)}, f32[128,128]{1,0:T(8,128)S(1)}, u32[]{:S(2)}, u32[]{:S(2)}) collective-permute-start(f32[128,128]{1,0:T(8,128)S(1)} %get-tuple-element.9), channel_id=1, source_target_pairs={{0,384},{1,385},{2,386},{3,387},{4,388},{5,389},{6,390},{7,391},{8... | collective-permute-start | bytes 196616 | tf_op jit(solution)/shard_map/ppermute | solution.py:37
  6.8 1.3 %collective-permute-start.6 = (f32[128,128]{1,0:T(8,128)S(1)}, f32[128,128]{1,0:T(8,128)S(1)}, u32[]{:S(2)}, u32[]{:S(2)}) collective-permute-start(f32[128,128]{1,0:T(8,128)S(1)} %get-tuple-element.9), channel_id=1, source_target_pairs={{0,256},{1,257},{2,258},{3,259},{4,260},{5,261},{6,262},{7,263},{8... | collective-permute-start | bytes 196616 | tf_op jit(solution)/shard_map/ppermute | solution.py:37
  8.1 1.3 %collective-permute-start.7 = (f32[128,128]{1,0:T(8,128)S(1)}, f32[128,128]{1,0:T(8,128)S(1)}, u32[]{:S(2)}, u32[]{:S(2)}) collective-permute-start(f32[128,128]{1,0:T(8,128)S(1)} %get-tuple-element.9), channel_id=1, source_target_pairs={{0,128},{1,129},{2,130},{3,131},{4,132},{5,133},{6,134},{7,135},{8... | collective-permute-start | bytes 196616 | tf_op jit(solution)/shard_map/ppermute | solution.py:37
  11.3 1.3 %collective-permute-start = (f32[512,128]{1,0:T(8,128)S(1)}, f32[512,128]{1,0:T(8,128)S(1)}, u32[]{:S(2)}, u32[]{:S(2)}) collective-permute-start(f32[512,128]{1,0:T(8,128)S(1)} %slice.30), channel_id=1, source_target_pairs={{0,256},{1,257},{2,258},{3,259},{4,260},{5,261},{6,262},{7,263},{8... | collective-permute-start | bytes 786440 | tf_op jit(solution)/shard_map/ppermute | solution.py:16
  12.7 1.3 %collective-permute-start.10 = (f32[128,128]{1,0:T(8,128)S(1)}, f32[128,128]{1,0:T(8,128)S(1)}, u32[]{:S(2)}, u32[]{:S(2)}) collective-permute-start(f32[128,128]{1,0:T(8,128)S(1)} %select_select_fusion.1), channel_id=1, source_target_pairs={{0,32},{128,160},{256,288},{384,416},{1,33},{129,161},{257,289},{3... | collective-permute-start | bytes 196616 | tf_op jit(solution)/shard_map/ppermute | solution.py:37
  14.0 1.3 %collective-permute-start.8 = (f32[128,128]{1,0:T(8,128)S(1)}, f32[128,128]{1,0:T(8,128)S(1)}, u32[]{:S(2)}, u32[]{:S(2)}) collective-permute-start(f32[128,128]{1,0:T(8,128)S(1)} %select_select_fusion.1), channel_id=1, source_target_pairs={{0,96},{128,224},{256,352},{384,480},{1,97},{129,225},{257,353},{3... | collective-permute-start | bytes 196616 | tf_op jit(solution)/shard_map/ppermute | solution.py:37
  15.3 1.3 %collective-permute-start.9 = (f32[128,128]{1,0:T(8,128)S(1)}, f32[128,128]{1,0:T(8,128)S(1)}, u32[]{:S(2)}, u32[]{:S(2)}) collective-permute-start(f32[128,128]{1,0:T(8,128)S(1)} %select_select_fusion.1), channel_id=1, source_target_pairs={{0,64},{128,192},{256,320},{384,448},{1,65},{129,193},{257,321},{3... | collective-permute-start | bytes 196616 | tf_op jit(solution)/shard_map/ppermute | solution.py:37
  17.2 1.3 %collective-permute-done.9 = f32[128,128]{1,0:T(8,128)S(1)} collective-permute-done((f32[128,128]{1,0:T(8,128)S(1)}, f32[128,128]{1,0:T(8,128)S(1)}, u32[]{:S(2)}, u32[]{:S(2)}) %collective-permute-start.9) | collective-permute-done | bytes 65568 | tf_op jit(solution)/shard_map/ppermute | solution.py:37
  18.5 1.3 %collective-permute-start.11 = (f32[128,128]{1,0:T(8,128)S(1)}, f32[128,128]{1,0:T(8,128)S(1)}, u32[]{:S(2)}, u32[]{:S(2)}) collective-permute-start(f32[128,128]{1,0:T(8,128)S(1)} %select_select_fusion), channel_id=1, source_target_pairs={{0,16},{32,48},{64,80},{96,112},{128,144},{160,176},{192,208},{224... | collective-permute-start | bytes 196616 | tf_op jit(solution)/shard_map/ppermute | solution.py:37
  19.9 0.8 %collective-permute-done.11 = f32[128,128]{1,0:T(8,128)S(1)} collective-permute-done((f32[128,128]{1,0:T(8,128)S(1)}, f32[128,128]{1,0:T(8,128)S(1)}, u32[]{:S(2)}, u32[]{:S(2)}) %collective-permute-start.11) | collective-permute-done | bytes 65568 | tf_op jit(solution)/shard_map/ppermute | solution.py:37
  21.4 2.8 %collective-permute-start.1 = (f32[512,128]{1,0:T(8,128)S(1)}, f32[512,128]{1,0:T(8,128)S(1)}, u32[]{:S(2)}, u32[]{:S(2)}) collective-permute-start(f32[512,128]{1,0:T(8,128)S(1)} %broadcast_select_fusion.3), channel_id=1, source_target_pairs={{0,128},{256,384},{1,129},{257,385},{2,130},{258,386},{3,131},{259... | collective-permute-start | bytes 786440 | tf_op jit(solution)/shard_map/ppermute | solution.py:16
  25.7 2.4 %collective-permute-done.1 = f32[512,128]{1,0:T(8,128)S(1)} collective-permute-done((f32[512,128]{1,0:T(8,128)S(1)}, f32[512,128]{1,0:T(8,128)S(1)}, u32[]{:S(2)}, u32[]{:S(2)}) %collective-permute-start.1) | collective-permute-done | bytes 262176 | tf_op jit(solution)/shard_map/ppermute | solution.py:16
  28.2 1.3 %collective-permute-start.2 = (f32[512,128]{1,0:T(8,128)S(1)}, f32[512,128]{1,0:T(8,128)S(1)}, u32[]{:S(2)}, u32[]{:S(2)}) collective-permute-start(f32[512,128]{1,0:T(8,128)S(1)} %broadcast_select_fusion.4), channel_id=1, source_target_pairs={{0,64},{128,192},{256,320},{384,448},{1,65},{129,193},{257,321},{3... | collective-permute-start | bytes 786440 | tf_op jit(solution)/shard_map/ppermute | solution.py:16
  30.9 2.4 %collective-permute-done.2 = f32[512,128]{1,0:T(8,128)S(1)} collective-permute-done((f32[512,128]{1,0:T(8,128)S(1)}, f32[512,128]{1,0:T(8,128)S(1)}, u32[]{:S(2)}, u32[]{:S(2)}) %collective-permute-start.2) | collective-permute-done | bytes 262176 | tf_op jit(solution)/shard_map/ppermute | solution.py:16
  33.4 1.3 %collective-permute-start.3 = (f32[512,128]{1,0:T(8,128)S(1)}, f32[512,128]{1,0:T(8,128)S(1)}, u32[]{:S(2)}, u32[]{:S(2)}) collective-permute-start(f32[512,128]{1,0:T(8,128)S(1)} %broadcast_select_fusion.5), channel_id=1, source_target_pairs={{0,32},{64,96},{128,160},{192,224},{256,288},{320,352},{384,416},{... | collective-permute-start | bytes 786440 | tf_op jit(solution)/shard_map/ppermute | solution.py:16
  34.7 1.3 %collective-permute-start.15 = (f32[128,128]{1,0:T(8,128)S(1)}, f32[128,128]{1,0:T(8,128)S(1)}, u32[]{:S(2)}, u32[]{:S(2)}) collective-permute-start(f32[128,128]{1,0:T(8,128)S(1)} %broadcast_select_fusion.14), channel_id=1, source_target_pairs={{0,1},{2,3},{4,5},{6,7},{8,9},{10,11},{12,13},{14,15},{16,17},{18,... | collective-permute-start | bytes 196616 | tf_op jit(solution)/shard_map/ppermute | solution.py:16
  36.1 1.3 %collective-permute-start.19 = (f32[128,264]{1,0:T(8,128)S(1)}, f32[128,264]{1,0:T(8,128)S(1)}, u32[]{:S(2)}, u32[]{:S(2)}) collective-permute-start(f32[128,264]{1,0:T(8,128)S(1)} %broadcast_select_fusion.9), channel_id=1, source_target_pairs={{0,1},{2,3},{4,5},{6,7},{8,9},{10,11},{12,13},{14,15},{16,17},{18,... | collective-permute-start | bytes 405512 | tf_op jit(solution)/shard_map/ppermute | solution.py:16
  37.4 1.2 %collective-permute-done.3 = f32[512,128]{1,0:T(8,128)S(1)} collective-permute-done((f32[512,128]{1,0:T(8,128)S(1)}, f32[512,128]{1,0:T(8,128)S(1)}, u32[]{:S(2)}, u32[]{:S(2)}) %collective-permute-start.3) | collective-permute-done | bytes 262176 | tf_op jit(solution)/shard_map/ppermute | solution.py:16
  38.6 1.3 %collective-permute-start.4 = (f32[512,128]{1,0:T(8,128)S(1)}, f32[512,128]{1,0:T(8,128)S(1)}, u32[]{:S(2)}, u32[]{:S(2)}) collective-permute-start(f32[512,128]{1,0:T(8,128)S(1)} %broadcast_select_fusion.6), channel_id=1, source_target_pairs={{0,16},{32,48},{64,80},{96,112},{128,144},{160,176},{192,208},{224... | collective-permute-start | bytes 786440 | tf_op jit(solution)/shard_map/ppermute | solution.py:16
  40.0 17.4 %collective-permute-done.15 = f32[128,128]{1,0:T(8,128)S(1)} collective-permute-done((f32[128,128]{1,0:T(8,128)S(1)}, f32[128,128]{1,0:T(8,128)S(1)}, u32[]{:S(2)}, u32[]{:S(2)}) %collective-permute-start.15) | collective-permute-done | bytes 65568 | tf_op jit(solution)/shard_map/ppermute | solution.py:16
  57.4 2.7 %collective-permute-done.19 = f32[128,264]{1,0:T(8,128)S(1)} collective-permute-done((f32[128,264]{1,0:T(8,128)S(1)}, f32[128,264]{1,0:T(8,128)S(1)}, u32[]{:S(2)}, u32[]{:S(2)}) %collective-permute-start.19) | collective-permute-done | bytes 135200 | tf_op jit(solution)/shard_map/ppermute | solution.py:16
  62.8 0.7 %broadcast_select_fusion.10 = f32[8,4,1,128]{3,2,1,0:T(1,128)} fusion(pred[4]{0:T(512)(128)(4,1)S(1)} %get-tuple-element.13, f32[8,4,1,128]{3,0,1,2:T(8,128)S(1)} %fusion, f32[8,128]{1,0:T(8,128)S(1)} %slice-done), kind=kLoop, calls=%fused_computation.26 | loop fusion | flops 4096 | bytes 36868 | tf_op jit(solution)/shard_map/jit(_where)/select_n | solution.py:130
  63.6 1.5 %broadcast_select_fusion = f32[4,1,128,2,1,128]{5,4,3,2,1,0:T(1,128)} fusion(pred[2]{0:T(512)(128)(4,1)S(1)} %fusion.9, f32[4,1,128,2,1,128]{5,4,3,2,1,0:T(1,128)S(1)} %bitcast.33, pred[4,2]{1,0:T(4,128)(4,1)S(1)} %broadcast_and_fusion, f32[4,128,128]{2,1,0:T(8,128)S(1)} %broadcast_select_fusion.2), kind=kLoop, calls=%fused_computation.3 | loop fusion | flops 262144 | bytes 1310730 | tf_op jit(solution)/shard_map/jit(_where)/select_n | solution.py:122
  (61 shorter events, 9.0 us)
Async XLA Ops:
  0.6 8.7 %copy-start = (f32[4,1,128,2,1,128]{5,4,3,2,1,0:T(1,128)S(1)}, f32[4,1,128,2,1,128]{5,4,3,2,1,0:T(1,128)}, u32[]{:S(2)}) copy-start(f32[4,1,128,2,1,128]{5,4,3,2,1,0:T(1,128)} %param.4) | copy-start | bytes 1572868
  1.8 10.8 %collective-permute-start.5 = (f32[128,128]{1,0:T(8,128)S(1)}, f32[128,128]{1,0:T(8,128)S(1)}, u32[]{:S(2)}, u32[]{:S(2)}) collective-permute-start(f32[128,128]{1,0:T(8,128)S(1)} %get-tuple-element.9), channel_id=1, source_target_pairs={{0,384},{1,385},{2,386},{3,387},{4,388},{5,389},{6,390},{7,391},{8... | collective-permute-start | bytes 196616 | tf_op jit(solution)/shard_map/ppermute | solution.py:37
  6.8 5.9 %collective-permute-start.6 = (f32[128,128]{1,0:T(8,128)S(1)}, f32[128,128]{1,0:T(8,128)S(1)}, u32[]{:S(2)}, u32[]{:S(2)}) collective-permute-start(f32[128,128]{1,0:T(8,128)S(1)} %get-tuple-element.9), channel_id=1, source_target_pairs={{0,256},{1,257},{2,258},{3,259},{4,260},{5,261},{6,262},{7,263},{8... | collective-permute-start | bytes 196616 | tf_op jit(solution)/shard_map/ppermute | solution.py:37
  8.1 4.6 %collective-permute-start.7 = (f32[128,128]{1,0:T(8,128)S(1)}, f32[128,128]{1,0:T(8,128)S(1)}, u32[]{:S(2)}, u32[]{:S(2)}) collective-permute-start(f32[128,128]{1,0:T(8,128)S(1)} %get-tuple-element.9), channel_id=1, source_target_pairs={{0,128},{1,129},{2,130},{3,131},{4,132},{5,133},{6,134},{7,135},{8... | collective-permute-start | bytes 196616 | tf_op jit(solution)/shard_map/ppermute | solution.py:37
  10.6 13.7 %collective-permute-start.16 = (f32[128,264]{1,0:T(8,128)S(1)}, f32[128,264]{1,0:T(8,128)S(1)}, u32[]{:S(2)}, u32[]{:S(2)}) collective-permute-start(f32[128,264]{1,0:T(8,128)S(1)} %pad_maximum_fusion), channel_id=1, source_target_pairs={{0,8},{16,24},{32,40},{48,56},{64,72},{80,88},{96,104},{112,120},{... | collective-permute-start | bytes 405512 | tf_op jit(solution)/shard_map/ppermute | solution.py:16
  11.3 10.1 %collective-permute-start = (f32[512,128]{1,0:T(8,128)S(1)}, f32[512,128]{1,0:T(8,128)S(1)}, u32[]{:S(2)}, u32[]{:S(2)}) collective-permute-start(f32[512,128]{1,0:T(8,128)S(1)} %slice.30), channel_id=1, source_target_pairs={{0,256},{1,257},{2,258},{3,259},{4,260},{5,261},{6,262},{7,263},{8... | collective-permute-start | bytes 786440 | tf_op jit(solution)/shard_map/ppermute | solution.py:16
  12.7 3.9 %collective-permute-start.10 = (f32[128,128]{1,0:T(8,128)S(1)}, f32[128,128]{1,0:T(8,128)S(1)}, u32[]{:S(2)}, u32[]{:S(2)}) collective-permute-start(f32[128,128]{1,0:T(8,128)S(1)} %select_select_fusion.1), channel_id=1, source_target_pairs={{0,32},{128,160},{256,288},{384,416},{1,33},{129,161},{257,289},{3... | collective-permute-start | bytes 196616 | tf_op jit(solution)/shard_map/ppermute | solution.py:37
  14.0 3.2 %collective-permute-start.8 = (f32[128,128]{1,0:T(8,128)S(1)}, f32[128,128]{1,0:T(8,128)S(1)}, u32[]{:S(2)}, u32[]{:S(2)}) collective-permute-start(f32[128,128]{1,0:T(8,128)S(1)} %select_select_fusion.1), channel_id=1, source_target_pairs={{0,96},{128,224},{256,352},{384,480},{1,97},{129,225},{257,353},{3... | collective-permute-start | bytes 196616 | tf_op jit(solution)/shard_map/ppermute | solution.py:37
  15.3 3.2 %collective-permute-start.9 = (f32[128,128]{1,0:T(8,128)S(1)}, f32[128,128]{1,0:T(8,128)S(1)}, u32[]{:S(2)}, u32[]{:S(2)}) collective-permute-start(f32[128,128]{1,0:T(8,128)S(1)} %select_select_fusion.1), channel_id=1, source_target_pairs={{0,64},{128,192},{256,320},{384,448},{1,65},{129,193},{257,321},{3... | collective-permute-start | bytes 196616 | tf_op jit(solution)/shard_map/ppermute | solution.py:37
  18.5 2.2 %collective-permute-start.11 = (f32[128,128]{1,0:T(8,128)S(1)}, f32[128,128]{1,0:T(8,128)S(1)}, u32[]{:S(2)}, u32[]{:S(2)}) collective-permute-start(f32[128,128]{1,0:T(8,128)S(1)} %select_select_fusion), channel_id=1, source_target_pairs={{0,16},{32,48},{64,80},{96,112},{128,144},{160,176},{192,208},{224... | collective-permute-start | bytes 196616 | tf_op jit(solution)/shard_map/ppermute | solution.py:37
  20.7 4.3 %collective-permute-start.12 = (f32[128,128]{1,0:T(8,128)S(1)}, f32[128,128]{1,0:T(8,128)S(1)}, u32[]{:S(2)}, u32[]{:S(2)}) collective-permute-start(f32[128,128]{1,0:T(8,128)S(1)} %broadcast_select_fusion.11), channel_id=1, source_target_pairs={{0,8},{16,24},{32,40},{48,56},{64,72},{80,88},{96,104},{112,120},{... | collective-permute-start | bytes 196616 | tf_op jit(solution)/shard_map/ppermute | solution.py:16
  21.4 6.7 %collective-permute-start.1 = (f32[512,128]{1,0:T(8,128)S(1)}, f32[512,128]{1,0:T(8,128)S(1)}, u32[]{:S(2)}, u32[]{:S(2)}) collective-permute-start(f32[512,128]{1,0:T(8,128)S(1)} %broadcast_select_fusion.3), channel_id=1, source_target_pairs={{0,128},{256,384},{1,129},{257,385},{2,130},{258,386},{3,131},{259... | collective-permute-start | bytes 786440 | tf_op jit(solution)/shard_map/ppermute | solution.py:16
  24.3 5.2 %collective-permute-start.17 = (f32[128,264]{1,0:T(8,128)S(1)}, f32[128,264]{1,0:T(8,128)S(1)}, u32[]{:S(2)}, u32[]{:S(2)}) collective-permute-start(f32[128,264]{1,0:T(8,128)S(1)} %broadcast_select_fusion.7), channel_id=1, source_target_pairs={{0,4},{8,12},{16,20},{24,28},{32,36},{40,44},{48,52},{56,60},{64,6... | collective-permute-start | bytes 405512 | tf_op jit(solution)/shard_map/ppermute | solution.py:16
  25.0 5.2 %collective-permute-start.13 = (f32[128,128]{1,0:T(8,128)S(1)}, f32[128,128]{1,0:T(8,128)S(1)}, u32[]{:S(2)}, u32[]{:S(2)}) collective-permute-start(f32[128,128]{1,0:T(8,128)S(1)} %broadcast_select_fusion.12), channel_id=1, source_target_pairs={{0,4},{8,12},{16,20},{24,28},{32,36},{40,44},{48,52},{56,60},{64,6... | collective-permute-start | bytes 196616 | tf_op jit(solution)/shard_map/ppermute | solution.py:16
  28.2 5.2 %collective-permute-start.2 = (f32[512,128]{1,0:T(8,128)S(1)}, f32[512,128]{1,0:T(8,128)S(1)}, u32[]{:S(2)}, u32[]{:S(2)}) collective-permute-start(f32[512,128]{1,0:T(8,128)S(1)} %broadcast_select_fusion.4), channel_id=1, source_target_pairs={{0,64},{128,192},{256,320},{384,448},{1,65},{129,193},{257,321},{3... | collective-permute-start | bytes 786440 | tf_op jit(solution)/shard_map/ppermute | solution.py:16
  29.5 6.5 %collective-permute-start.18 = (f32[128,264]{1,0:T(8,128)S(1)}, f32[128,264]{1,0:T(8,128)S(1)}, u32[]{:S(2)}, u32[]{:S(2)}) collective-permute-start(f32[128,264]{1,0:T(8,128)S(1)} %broadcast_select_fusion.8), channel_id=1, source_target_pairs={{0,2},{4,6},{8,10},{12,14},{16,18},{20,22},{24,26},{28,30},{32,34}... | collective-permute-start | bytes 405512 | tf_op jit(solution)/shard_map/ppermute | solution.py:16
  30.3 4.5 %collective-permute-start.14 = (f32[128,128]{1,0:T(8,128)S(1)}, f32[128,128]{1,0:T(8,128)S(1)}, u32[]{:S(2)}, u32[]{:S(2)}) collective-permute-start(f32[128,128]{1,0:T(8,128)S(1)} %broadcast_select_fusion.13), channel_id=1, source_target_pairs={{0,2},{4,6},{8,10},{12,14},{16,18},{20,22},{24,26},{28,30},{32,34}... | collective-permute-start | bytes 196616 | tf_op jit(solution)/shard_map/ppermute | solution.py:16
  33.4 5.2 %collective-permute-start.3 = (f32[512,128]{1,0:T(8,128)S(1)}, f32[512,128]{1,0:T(8,128)S(1)}, u32[]{:S(2)}, u32[]{:S(2)}) collective-permute-start(f32[512,128]{1,0:T(8,128)S(1)} %broadcast_select_fusion.5), channel_id=1, source_target_pairs={{0,32},{64,96},{128,160},{192,224},{256,288},{320,352},{384,416},{... | collective-permute-start | bytes 786440 | tf_op jit(solution)/shard_map/ppermute | solution.py:16
  34.7 22.7 %collective-permute-start.15 = (f32[128,128]{1,0:T(8,128)S(1)}, f32[128,128]{1,0:T(8,128)S(1)}, u32[]{:S(2)}, u32[]{:S(2)}) collective-permute-start(f32[128,128]{1,0:T(8,128)S(1)} %broadcast_select_fusion.14), channel_id=1, source_target_pairs={{0,1},{2,3},{4,5},{6,7},{8,9},{10,11},{12,13},{14,15},{16,17},{18,... | collective-permute-start | bytes 196616 | tf_op jit(solution)/shard_map/ppermute | solution.py:16
  36.1 24.1 %collective-permute-start.19 = (f32[128,264]{1,0:T(8,128)S(1)}, f32[128,264]{1,0:T(8,128)S(1)}, u32[]{:S(2)}, u32[]{:S(2)}) collective-permute-start(f32[128,264]{1,0:T(8,128)S(1)} %broadcast_select_fusion.9), channel_id=1, source_target_pairs={{0,1},{2,3},{4,5},{6,7},{8,9},{10,11},{12,13},{14,15},{16,17},{18,... | collective-permute-start | bytes 405512 | tf_op jit(solution)/shard_map/ppermute | solution.py:16
  38.6 22.1 %collective-permute-start.4 = (f32[512,128]{1,0:T(8,128)S(1)}, f32[512,128]{1,0:T(8,128)S(1)}, u32[]{:S(2)}, u32[]{:S(2)}) collective-permute-start(f32[512,128]{1,0:T(8,128)S(1)} %broadcast_select_fusion.6), channel_id=1, source_target_pairs={{0,16},{32,48},{64,80},{96,112},{128,144},{160,176},{192,208},{224... | collective-permute-start | bytes 786440 | tf_op jit(solution)/shard_map/ppermute | solution.py:16
  60.7 1.0 %copy-start.1 = (f32[264,128]{1,0:T(8,128)}, f32[264,128]{1,0:T(8,128)S(1)}, u32[]{:S(2)}) copy-start(f32[264,128]{1,0:T(8,128)S(1)} %fusion.3) | copy-start | bytes 405508
  61.1 0.7 %copy-start.2 = (f32[8,4,1,128]{3,2,1,0:T(1,128)S(1)}, f32[8,4,1,128]{3,2,1,0:T(1,128)}, u32[]{:S(2)}) copy-start(f32[8,4,1,128]{3,2,1,0:T(1,128)} %param.5) | copy-start | bytes 49156
  62.1 0.7 %slice-start = ((f32[264,128]{1,0:T(8,128)}), f32[8,128]{1,0:T(8,128)S(1)}, s32[]{:S(2)}) async-start(f32[264,128]{1,0:T(8,128)} %copy-done.1), calls=%async_computation | async-start | bytes 8192 | tf_op jit(solution)/shard_map/slice | solution.py:106
  (1 other events, 0.7 us)
